TPU v7x, 32 devices: a whole 2x2x4 slice. The times are simulated.
32 devices in a mesh: shots: 2 (over y), gx: 4 (over z), gy: 4 (over x, core).
Axes of the slice: x: 2, y: 2, z: 4, core: 2. Of those that a mesh axis runs over, the one named last changes fastest.
Arguments:
- p_now: float32 [64, 64, 128], P(('shots', 'gx'), 'gy'), parts along dimension 0, may hold values from -6 to 6
- q_now: float32 [64, 64, 128], P(('shots', 'gx'), 'gy'), parts along dimension 0, may hold values from -6 to 6
- p_prev: float32 [64, 64, 128], P(('shots', 'gx'), 'gy'), parts along dimension 0, may hold values from -6 to 6
- q_prev: float32 [64, 64, 128], P(('shots', 'gx'), 'gy'), parts along dimension 0, may hold values from -6 to 6
- speed: float32 [32, 64, 128], P('gx', 'gy'), may hold values from 0.05 to 0.2
- epsilon: float32 [32, 64, 128], P('gx', 'gy'), may hold values from 0.05 to 0.35
- delta: float32 [32, 64, 128], P('gx', 'gy'), may hold values from 0 to 0.3
- theta: float32 [32, 64, 128], P('gx', 'gy'), may hold values from -1 to 1
- phi: float32 [32, 64, 128], P('gx', 'gy'), may hold values from -3.140625 to 3.140625
- snapshots: bfloat16 [2, 64, 64, 128], P(None, ('shots', 'gx'), 'gy'), parts along dimension 1, may hold values from -6 to 6
- traces: float32 [1024, 4096], P(None, ('shots', 'gx', 'gy')), parts along dimension 1, may hold values from -6 to 6
- time_steps: int32 [4], P('shots'), parts along dimension 0, may hold values from 0 to 1023
- rec_owner: int32 [4096, 1], P(('shots', 'gx', 'gy')), parts along dimension 0, may hold values from 0 to 3; in each aligned block of 128 rows (0 to 127, 128 to 255, ...) at most 64 rows name the same one
- rec_local: int32 [4096], P(('shots', 'gx', 'gy')), parts along dimension 0, may hold values from 0 to 16383
Outputs:
- p_next: float32 [64, 64, 128], P(('shots', 'gx'), 'gy'), parts along dimension 0
- q_next: float32 [64, 64, 128], P(('shots', 'gx'), 'gy'), parts along dimension 0
- p_mid: float32 [64, 64, 128], P(('shots', 'gx'), 'gy'), parts along dimension 0
- q_mid: float32 [64, 64, 128], P(('shots', 'gx'), 'gy'), parts along dimension 0
- image: float32 [64, 64, 128], P(('shots', 'gx'), 'gy'), parts along dimension 0
There are 2 independent parts, one for each index of `shots`. A program takes and returns all parts, laid end to end along the dimension named above; an argument that names none is the same for every part. Nothing has to cross between parts.
Inputs may be any that keep to these rules, and one draw needn't show every extreme that they name: `rec_owner`: the 128 receivers of one device (aligned blocks of 128 rows) name any one owner at most 64 times, a bound that some block reaches. `rec_local`: A receiver's cell lies in the band of the second dimension that the device holding the receiver covers.
All inputs are finite; a program needn't handle non-finite values.
Results may differ from a plain program's by a relative error of at most 0.0003.
Values sent between devices are 32-bit elements; how exact they have to be, the bound alone decides.
No kernel may reach another device: no remote copies, remote signals or barrier semaphores. Data moves between devices by JAX's collectives and lax.ppermute only.
A program may use at most 64 MiB of HBM per device.

v0:
```python
import jax
import jax.numpy as jnp
from jax import lax
from jax.sharding import PartitionSpec as P

second_coef = (-205.0 / 72.0, 8.0 / 5.0, -1.0 / 5.0, 8.0 / 315.0, -1.0 / 560.0)
first_coef = (4.0 / 5.0, -1.0 / 5.0, 4.0 / 105.0, -1.0 / 280.0)


def padded_2(cells, sides, width):
    for axis, dim in sides:
        count = lax.axis_size(axis)
        ends = count - 1
        head = lax.slice_in_dim(cells, 0, width, axis=dim)
        tail = lax.slice_in_dim(cells, cells.shape[dim] - width, cells.shape[dim], axis=dim)
        cells = jnp.concatenate(
            [
                lax.ppermute(tail, axis, [(i, (i + 1) % count) for i in range(ends)]),
                cells,
                lax.ppermute(head, axis, [((i + 1) % count, i) for i in range(ends)]),
            ],
            axis=dim,
        )
    return cells


def derivatives(padded, sx, sy, sz):

    def part(dx, dy, dz):
        return padded[:, 4 + dx : 4 + dx + sx, 4 + dy : 4 + dy + sy, 4 + dz : 4 + dz + sz]

    centre = part(0, 0, 0)
    dxx = second_coef[0] * centre
    dyy = second_coef[0] * centre
    dzz = second_coef[0] * centre
    for k in range(1, 5):
        dxx = dxx + second_coef[k] * (part(k, 0, 0) + part(-k, 0, 0))
        dyy = dyy + second_coef[k] * (part(0, k, 0) + part(0, -k, 0))
        dzz = dzz + second_coef[k] * (part(0, 0, k) + part(0, 0, -k))
    dy_wide = 0.0
    dz_xwide = 0.0
    dz_ywide = 0.0
    for k in range(1, 5):
        weight = first_coef[k - 1]
        dy_wide = dy_wide + weight * (
            padded[:, :, 4 + k : 4 + k + sy, 4 : 4 + sz]
            - padded[:, :, 4 - k : 4 - k + sy, 4 : 4 + sz]
        )
        dz_xwide = dz_xwide + weight * (
            padded[:, :, 4 : 4 + sy, 4 + k : 4 + k + sz]
            - padded[:, :, 4 : 4 + sy, 4 - k : 4 - k + sz]
        )
        dz_ywide = dz_ywide + weight * (
            padded[:, 4 : 4 + sx, :, 4 + k : 4 + k + sz]
            - padded[:, 4 : 4 + sx, :, 4 - k : 4 - k + sz]
        )
    dxy = 0.0
    dxz = 0.0
    dyz = 0.0
    for k in range(1, 5):
        weight = first_coef[k - 1]
        dxy = dxy + weight * (dy_wide[:, 4 + k : 4 + k + sx] - dy_wide[:, 4 - k : 4 - k + sx])
        dxz = dxz + weight * (dz_xwide[:, 4 + k : 4 + k + sx] - dz_xwide[:, 4 - k : 4 - k + sx])
        dyz = dyz + weight * (
            dz_ywide[:, :, 4 + k : 4 + k + sy] - dz_ywide[:, :, 4 - k : 4 - k + sy]
        )
    return (centre, dxx, dyy, dzz, dxy, dxz, dyz)


def advance(padded, previous, speed, epsilon, delta, theta, phi, source):
    sx, sy, sz = (previous.shape[1], previous.shape[2], previous.shape[3])
    centre, dxx, dyy, dzz, dxy, dxz, dyz = derivatives(padded, sx, sy, sz)
    axis_x = jnp.sin(theta) * jnp.cos(phi)
    axis_y = jnp.sin(theta) * jnp.sin(phi)
    axis_z = jnp.cos(theta)
    rotated = (
        axis_x * axis_x * dxx
        + axis_y * axis_y * dyy
        + axis_z * axis_z * dzz
        + 2.0 * axis_x * axis_y * dxy
        + 2.0 * axis_x * axis_z * dxz
        + 2.0 * axis_y * axis_z * dyz
    )
    remainder = dxx + dyy + dzz - rotated
    root_delta = jnp.sqrt(1.0 + 2.0 * delta)
    p_new = (
        2.0 * centre[0]
        - previous[0]
        + speed * ((1.0 + 2.0 * epsilon) * remainder[0] + root_delta * rotated[1])
        + source
    )
    q_new = (
        2.0 * centre[1] - previous[1] + speed * (root_delta * remainder[0] + rotated[1]) + source
    )
    return jnp.stack([p_new, q_new])


def pad_depth(fields):
    return jnp.pad(fields, ((0, 0), (0, 0), (0, 0), (4, 4)))


def widened(fields):
    return pad_depth(padded_2(fields, (("gx", 1), ("gy", 2)), 4))


def local(
    p_now,
    q_now,
    p_prev,
    q_prev,
    speed,
    epsilon,
    delta,
    theta,
    phi,
    snapshots,
    traces,
    time_steps,
    rec_owner,
    rec_local,
):
    sx, sy, sz = p_now.shape
    cells = sx * sy * sz
    groups = lax.axis_size("gx")
    held = rec_local.shape[0]
    samples = jnp.take(traces, time_steps, axis=0)
    owner = rec_owner[:, 0]
    capacity = 2 * held // groups
    onehot = (owner[:, None] == jnp.arange(groups, dtype=jnp.int32)[None, :]).astype(jnp.int32)
    running = jnp.cumsum(onehot, axis=0)
    rank = jnp.sum(onehot * running, axis=1) - 1
    position = owner * capacity + rank
    payload = jnp.concatenate([samples, rec_local.astype(jnp.float32)[None, :]], axis=0)
    slots = jnp.zeros((3, groups * capacity), jnp.float32).at[:, position].set(payload)
    slots = slots.reshape(3, groups, capacity)
    arrived = lax.all_to_all(slots, "gx", split_axis=1, concat_axis=1, tiled=True)
    values = arrived[0:2].reshape(2, groups * capacity)
    target = arrived[2].reshape(groups * capacity).astype(jnp.int32)
    sources = jnp.zeros((2, cells), jnp.float32).at[:, target].add(values).reshape(2, sx, sy, sz)
    current = jnp.stack([p_now, q_now])
    earlier = jnp.stack([p_prev, q_prev])
    middle = advance(widened(current), earlier, speed, epsilon, delta, theta, phi, sources[0])
    final = advance(widened(middle), current, speed, epsilon, delta, theta, phi, sources[1])
    image = (
        snapshots[0].astype(jnp.float32) * middle[0] + snapshots[1].astype(jnp.float32) * final[0]
    )
    return (final[0], final[1], middle[0], middle[1], image)


def solution(mesh):
    return jax.shard_map(
        local,
        mesh=mesh,
        in_specs=(
            P(("shots", "gx"), "gy", None),
            P(("shots", "gx"), "gy", None),
            P(("shots", "gx"), "gy", None),
            P(("shots", "gx"), "gy", None),
            P("gx", "gy", None),
            P("gx", "gy", None),
            P("gx", "gy", None),
            P("gx", "gy", None),
            P("gx", "gy", None),
            P(None, ("shots", "gx"), "gy", None),
            P(None, ("shots", "gx", "gy")),
            P("shots"),
            P(("shots", "gx", "gy"), None),
            P(("shots", "gx", "gy")),
        ),
        out_specs=(
            P(("shots", "gx"), "gy", None),
            P(("shots", "gx"), "gy", None),
            P(("shots", "gx"), "gy", None),
            P(("shots", "gx"), "gy", None),
            P(("shots", "gx"), "gy", None),
        ),
        check_vma=False,
    )
```

profile of v0, /device:TPU:30, one launch (start us, length us, event | category | flops | bytes accessed | tf_op | source)
XLA Modules:
  0.0 71.3 jit_solution(5272176775762559091)
XLA Ops:
  0.6 0.0 copy-start
  0.6 0.7 %compare_select_fusion.1 = s32[2]{0:T(128)S(1)} fusion(s32[2]{0:T(128)} %param.25), kind=kLoop, calls=%fused_computation.299 | loop fusion | flops 6 | bytes 16 | tf_op jit(solution)/shard_map/jit(_take)/jit(_where)/select_n | solution.py:126
  1.4 0.7 compare_and_fusion
  2.0 0.7 %fusion.156 = s32[128,4]{1,0:T(8,128)S(1)} fusion(s32[128]{0:T(128)} %bitcast.80), kind=kLoop, calls=%fused_computation.286 | loop fusion | flops 1024 | bytes 2560 | tf_op jit(solution)/shard_map/convert_element_type | solution.py:129
  2.8 0.2 reduce_window_sum.11
  2.9 0.8 %select_reduce_fusion = s32[128]{0:T(128)S(1)} fusion(s32[128,4]{1,0:T(8,128)S(1)} %reduce_window_sum.11, s32[128]{0:T(128)} %bitcast.81), kind=kLoop, calls=%fused_computation.284 | loop fusion | flops 1408 | bytes 3072 | tf_op jit(solution)/shard_map/reduce_sum | solution.py:131
  3.8 0.7 fusion.160
  4.4 0.7 convert_bitcast_fusion
  5.1 0.6 gather_fusion
  5.7 0.1 broadcast_select_fusion
  5.8 0.1 copy.25
  5.9 0.9 %scatter_custom_fusion = f32[3,256]{0,1:T(8,128)S(1)} fusion(s32[128]{0:T(128)S(1)} %fusion.160, f32[128,3]{1,0:T(8,128)S(1)} %copy.25, f32[]{:T(128)} %constant.26.clone.1), kind=kCustom, calls=%fused_computation.287 | custom fusion | bytes 3076 | tf_op jit(solution)/shard_map/scatter | solution.py:134
  6.8 0.1 copy.26
  6.9 0.7 reshape.111
  7.6 5.1 %all-to-all-start = ((f32[4,1,192]{2,1,0:T(1,128)}), f32[4,1,192]{2,1,0:T(1,128)S(1)}, u32[]{:S(2)}, u32[]{:S(2)}) async-start(f32[4,1,192]{2,1,0:T(1,128)} %reshape.111), calls=%async_computation | async-start | bytes 8192 | tf_op jit(solution)/shard_map/all_to_all | solution.py:136
  12.7 0.8 %fusion.152 = (f32[2,4,16,128]{3,2,1,0:T(8,128)S(1)}, f32[2,4,16,128]{3,2,1,0:T(8,128)S(1)}) fusion(f32[1,8,16,128]{3,2,1,0:T(8,128)} %bitcast.59, f32[1,8,16,128]{3,2,1,0:T(8,128)} %bitcast.47), kind=kLoop, calls=%fused_computation.259 | loop fusion | flops 32768 | bytes 262144 | tf_op jit(solution)/shard_map/stack | solution.py:140
  13.5 2.5 %collective-permute-start = (f32[2,4,16,128]{3,2,1,0:T(8,128)S(1)}, f32[2,4,16,128]{3,2,1,0:T(8,128)S(1)}, u32[]{:S(2)}, u32[]{:S(2)}) collective-permute-start(f32[2,4,16,128]{3,2,1,0:T(8,128)S(1)} %get-tuple-element.42), channel_id=1, source_target_pairs={{4,0},{8,4},{12,8},{5,1},{9,5},{13,9},{6,2},{10,6},{14,10},{7,3},{... | collective-permute-start | bytes 196616 | tf_op jit(solution)/shard_map/ppermute | solution.py:20
  16.0 1.3 %collective-permute-start.1 = (f32[2,4,16,128]{3,2,1,0:T(8,128)S(1)}, f32[2,4,16,128]{3,2,1,0:T(8,128)S(1)}, u32[]{:S(2)}, u32[]{:S(2)}) collective-permute-start(f32[2,4,16,128]{3,2,1,0:T(8,128)S(1)} %get-tuple-element.41), channel_id=1, source_target_pairs={{0,4},{4,8},{8,12},{1,5},{5,9},{9,13},{2,6},{6,10},{10,14},{3,7},{... | collective-permute-start | bytes 196616 | tf_op jit(solution)/shard_map/ppermute | solution.py:18
  17.3 1.1 %fusion.171 = (f32[8,16,128]{2,1,0:T(8,128)S(1)}, f32[8,16,128]{2,1,0:T(8,128)S(1)}) fusion(f32[8,16,128]{2,1,0:T(8,128)} %param.21), kind=kLoop, calls=%fused_computation.311 | loop fusion | bytes 196608 | tf_op jit(solution)/shard_map/sin | solution.py:73
  18.3 1.1 %fusion.161 = (f32[8,16,128]{2,1,0:T(8,128)S(1)}, f32[8,16,128]{2,1,0:T(8,128)S(1)}, f32[8,16,128]{2,1,0:T(8,128)S(1)}, f32[8,16,128]{2,1,0:T(8,128)S(1)}, f32[8...) fusion(f32[8,16,128]{2,1,0:T(8,128)S(1)} %get-tuple-element.44, f32[8,16,128]{2,1,0:T(8,128)} %param.22, ...), kind=kLoop, calls=%fused_computation.309 | loop fusion | flops 163840 | bytes 589824 | tf_op jit(solution)/shard_map/mul | solution.py:77
  19.4 0.0 all-to-all-done
  19.5 0.5 broadcast.301
  20.0 0.7 reduce.8
  20.6 0.1 reshape.112
  20.8 0.1 convert_element_type.37
  20.8 0.1 reshape.90
  20.9 0.1 copy.28
  21.1 5.7 %scatter_custom_fusion.1 = f32[2,16384]{0,1:T(8,128)} fusion(s32[256]{0:T(256)S(1)} %bitcast.82, f32[256,2]{1,0:T(8,128)S(1)} %copy.28, f32[]{:T(128)} %constant.26.clone.1), kind=kCustom, calls=%fused_computation.5 | custom fusion | flops 512 | bytes 131076 | tf_op jit(solution)/shard_map/scatter-add | solution.py:139
  26.8 12.3 %slice_reduce_fusion.1 = (f32[16384]{0:T(1024)S(1)}, f32[16384]{0:T(1024)S(1)}) fusion(f32[2,16384]{0,1:T(8,128)} %scatter_custom_fusion.1), kind=kLoop, calls=%fused_computation.4 | loop fusion | bytes 262144 | tf_op jit(solution)/shard_map/slice | solution.py:142
  39.1 0.0 collective-permute-done
  39.1 1.9 %collective-permute-start.2 = (f32[2,16,4,128]{3,2,1,0:T(4,128)S(1)}, f32[2,16,4,128]{3,2,1,0:T(4,128)S(1)}, u32[]{:S(2)}, u32[]{:S(2)}) collective-permute-start(f32[2,16,4,128]{3,2,1,0:T(4,128)S(1)} %get-tuple-element.27), channel_id=1, source_target_pairs={{1,0},{2,1},{3,2},{5,4},{6,5},{7,6},{9,8},{10,9},{11,10},{13,12},{... | collective-permute-start | bytes 196616 | tf_op jit(solution)/shard_map/ppermute | solution.py:20
  41.1 0.0 copy-start.5
  41.1 0.0 copy-start.6
  41.1 0.0 copy-start.8
  41.1 2.5 %collective-permute-start.3 = (f32[2,16,4,128]{3,2,1,0:T(4,128)S(1)}, f32[2,16,4,128]{3,2,1,0:T(4,128)S(1)}, u32[]{:S(2)}, u32[]{:S(2)}) collective-permute-start(f32[2,16,4,128]{3,2,1,0:T(4,128)S(1)} %get-tuple-element.26), channel_id=1, source_target_pairs={{0,1},{1,2},{2,3},{4,5},{5,6},{6,7},{8,9},{9,10},{10,11},{12,13},{... | collective-permute-start | bytes 196616 | tf_op jit(solution)/shard_map/ppermute | solution.py:18
  43.7 0.0 copy-start.7
  43.7 0.0 copy-start.9
  43.7 0.0 collective-permute-done.2
  43.7 3.1 %collective-permute-done.3 = f32[2,16,4,128]{3,2,1,0:T(4,128)S(1)} collective-permute-done((f32[2,16,4,128]{3,2,1,0:T(4,128)S(1)}, f32[2,16,4,128]{3,2,1,0:T(4,128)S(1)}, u32[]{:S(2)}, u32[]{:S(2)}) %collective-permute-start.3) | collective-permute-done | bytes 65568 | tf_op jit(solution)/shard_map/ppermute | solution.py:18
  46.8 0.4 select_maximum_fusion.5
  47.2 0.4 fusion.39
  47.7 0.1 pad_maximum_fusion
  47.7 0.7 fusion.18
  48.4 0.6 fusion.101
  49.0 0.1 add_add_fusion.2
  49.1 0.0 copy-start.2
  49.1 0.1 add_add_fusion.3
  49.2 0.0 copy-start.4
  49.2 4.6 %collective-permute-start.4 = (f32[2,4,16,128]{3,2,1,0:T(8,128)S(1)}, f32[2,4,16,128]{3,2,1,0:T(8,128)S(1)}, u32[]{:S(2)}, u32[]{:S(2)}) collective-permute-start(f32[2,4,16,128]{3,2,1,0:T(8,128)S(1)} %get-tuple-element.33), channel_id=1, source_target_pairs={{4,0},{8,4},{12,8},{5,1},{9,5},{13,9},{6,2},{10,6},{14,10},{7,3},{... | collective-permute-start | bytes 196616 | tf_op jit(solution)/shard_map/ppermute | solution.py:20
  53.8 1.3 %collective-permute-start.5 = (f32[2,4,16,128]{3,2,1,0:T(8,128)S(1)}, f32[2,4,16,128]{3,2,1,0:T(8,128)S(1)}, u32[]{:S(2)}, u32[]{:S(2)}) collective-permute-start(f32[2,4,16,128]{3,2,1,0:T(8,128)S(1)} %get-tuple-element.32), channel_id=1, source_target_pairs={{0,4},{4,8},{8,12},{1,5},{5,9},{9,13},{2,6},{6,10},{10,14},{3,7},{... | collective-permute-start | bytes 196616 | tf_op jit(solution)/shard_map/ppermute | solution.py:18
  55.1 0.6 collective-permute-done.4
  55.7 4.3 %collective-permute-done.5 = f32[2,4,16,128]{3,2,1,0:T(8,128)S(1)} collective-permute-done((f32[2,4,16,128]{3,2,1,0:T(8,128)S(1)}, f32[2,4,16,128]{3,2,1,0:T(8,128)S(1)}, u32[]{:S(2)}, u32[]{:S(2)}) %collective-permute-start.5) | collective-permute-done | bytes 65568 | tf_op jit(solution)/shard_map/ppermute | solution.py:18
  60.0 1.9 %collective-permute-start.6 = (f32[2,16,4,128]{3,2,1,0:T(4,128)S(1)}, f32[2,16,4,128]{3,2,1,0:T(4,128)S(1)}, u32[]{:S(2)}, u32[]{:S(2)}) collective-permute-start(f32[2,16,4,128]{3,2,1,0:T(4,128)S(1)} %get-tuple-element.23), channel_id=1, source_target_pairs={{1,0},{2,1},{3,2},{5,4},{6,5},{7,6},{9,8},{10,9},{11,10},{13,12},{... | collective-permute-start | bytes 196616 | tf_op jit(solution)/shard_map/ppermute | solution.py:20
  61.9 0.0 copy-start.10
  61.9 2.5 %collective-permute-start.7 = (f32[2,16,4,128]{3,2,1,0:T(4,128)S(1)}, f32[2,16,4,128]{3,2,1,0:T(4,128)S(1)}, u32[]{:S(2)}, u32[]{:S(2)}) collective-permute-start(f32[2,16,4,128]{3,2,1,0:T(4,128)S(1)} %get-tuple-element.22), channel_id=1, source_target_pairs={{0,1},{1,2},{2,3},{4,5},{5,6},{6,7},{8,9},{9,10},{10,11},{12,13},{... | collective-permute-start | bytes 196616 | tf_op jit(solution)/shard_map/ppermute | solution.py:18
  64.5 3.1 %collective-permute-done.7 = f32[2,16,4,128]{3,2,1,0:T(4,128)S(1)} collective-permute-done((f32[2,16,4,128]{3,2,1,0:T(4,128)S(1)}, f32[2,16,4,128]{3,2,1,0:T(4,128)S(1)}, u32[]{:S(2)}, u32[]{:S(2)}) %collective-permute-start.7) | collective-permute-done | bytes 65568 | tf_op jit(solution)/shard_map/ppermute | solution.py:18
  67.6 0.4 select_maximum_fusion
  68.1 0.4 fusion.32
  68.5 0.5 fusion.4
  69.0 0.1 pad_maximum_fusion.1
  69.1 0.2 fusion.11
  69.3 0.6 fusion.50
  69.9 0.7 %fusion.155 = (f32[8,16,128]{2,1,0:T(8,128)}, f32[8,16,128]{2,1,0:T(8,128)}, f32[8,16,128]{2,1,0:T(8,128)S(1)}) fusion(f32[8,16,128]{2,1,0:T(8,128)S(1)} %add_add_fusion.3, bf16[2,8,16,128]{3,2,1,0:T(8,128)(2,1)S(1)} %copy-done.10, f32[8,16,128]{2,1,0:T(8,128)S(1)} %bitcast.73, f32[8,16,128]{2,1,0:T(8,128)S(1)} %copy-done.5, ...), kind=kLoop, calls=%fused_computation.279 | loop fusion | flops 327680 | bytes 983040 | tf_op jit(solution)/shard_map/add | solution.py:145
  70.6 0.7 add_add_fusion
  (26 shorter events, 0.2 us)
Async XLA Ops:
  0.6 4.5 %copy-start = (f32[1024,128]{1,0:T(8,128)S(1)}, f32[1024,128]{1,0:T(8,128)}, u32[]{:S(2)}) copy-start(f32[1024,128]{1,0:T(8,128)} %param.24) | copy-start | bytes 1572868
  7.6 11.9 %all-to-all-start = ((f32[4,1,192]{2,1,0:T(1,128)}), f32[4,1,192]{2,1,0:T(1,128)S(1)}, u32[]{:S(2)}, u32[]{:S(2)}) async-start(f32[4,1,192]{2,1,0:T(1,128)} %reshape.111), calls=%async_computation | async-start | bytes 8192 | tf_op jit(solution)/shard_map/all_to_all | solution.py:136
  13.5 25.6 %collective-permute-start = (f32[2,4,16,128]{3,2,1,0:T(8,128)S(1)}, f32[2,4,16,128]{3,2,1,0:T(8,128)S(1)}, u32[]{:S(2)}, u32[]{:S(2)}) collective-permute-start(f32[2,4,16,128]{3,2,1,0:T(8,128)S(1)} %get-tuple-element.42), channel_id=1, source_target_pairs={{4,0},{8,4},{12,8},{5,1},{9,5},{13,9},{6,2},{10,6},{14,10},{7,3},{... | collective-permute-start | bytes 196616 | tf_op jit(solution)/shard_map/ppermute | solution.py:20
  16.0 23.1 %collective-permute-start.1 = (f32[2,4,16,128]{3,2,1,0:T(8,128)S(1)}, f32[2,4,16,128]{3,2,1,0:T(8,128)S(1)}, u32[]{:S(2)}, u32[]{:S(2)}) collective-permute-start(f32[2,4,16,128]{3,2,1,0:T(8,128)S(1)} %get-tuple-element.41), channel_id=1, source_target_pairs={{0,4},{4,8},{8,12},{1,5},{5,9},{9,13},{2,6},{6,10},{10,14},{3,7},{... | collective-permute-start | bytes 196616 | tf_op jit(solution)/shard_map/ppermute | solution.py:18
  26.8 12.3 %copy-start.1 = (f32[8,16,128]{2,1,0:T(8,128)S(1)}, f32[8,16,128]{2,1,0:T(8,128)}, u32[]{:S(2)}) copy-start(f32[8,16,128]{2,1,0:T(8,128)} %param.15) | copy-start | bytes 196612
  26.8 12.3 %copy-start.3 = (f32[8,16,128]{2,1,0:T(8,128)S(1)}, f32[8,16,128]{2,1,0:T(8,128)}, u32[]{:S(2)}) copy-start(f32[8,16,128]{2,1,0:T(8,128)} %param.14) | copy-start | bytes 196612
  39.1 4.6 %collective-permute-start.2 = (f32[2,16,4,128]{3,2,1,0:T(4,128)S(1)}, f32[2,16,4,128]{3,2,1,0:T(4,128)S(1)}, u32[]{:S(2)}, u32[]{:S(2)}) collective-permute-start(f32[2,16,4,128]{3,2,1,0:T(4,128)S(1)} %get-tuple-element.27), channel_id=1, source_target_pairs={{1,0},{2,1},{3,2},{5,4},{6,5},{7,6},{9,8},{10,9},{11,10},{13,12},{... | collective-permute-start | bytes 196616 | tf_op jit(solution)/shard_map/ppermute | solution.py:20
  41.1 7.9 %copy-start.5 = (f32[8,16,128]{2,1,0:T(8,128)S(1)}, f32[8,16,128]{2,1,0:T(8,128)}, u32[]{:S(2)}) copy-start(f32[8,16,128]{2,1,0:T(8,128)} %param.18) | copy-start | bytes 196612
  41.1 7.9 %copy-start.6 = (f32[8,16,128]{2,1,0:T(8,128)S(1)}, f32[8,16,128]{2,1,0:T(8,128)}, u32[]{:S(2)}) copy-start(f32[8,16,128]{2,1,0:T(8,128)} %param.20) | copy-start | bytes 196612
  41.1 7.9 %copy-start.8 = (f32[8,16,128]{2,1,0:T(8,128)S(1)}, f32[8,16,128]{2,1,0:T(8,128)}, u32[]{:S(2)}) copy-start(f32[8,16,128]{2,1,0:T(8,128)} %param.17) | copy-start | bytes 196612
  41.1 5.7 %collective-permute-start.3 = (f32[2,16,4,128]{3,2,1,0:T(4,128)S(1)}, f32[2,16,4,128]{3,2,1,0:T(4,128)S(1)}, u32[]{:S(2)}, u32[]{:S(2)}) collective-permute-start(f32[2,16,4,128]{3,2,1,0:T(4,128)S(1)} %get-tuple-element.26), channel_id=1, source_target_pairs={{0,1},{1,2},{2,3},{4,5},{5,6},{6,7},{8,9},{9,10},{10,11},{12,13},{... | collective-permute-start | bytes 196616 | tf_op jit(solution)/shard_map/ppermute | solution.py:18
  43.7 5.4 %copy-start.7 = (f32[8,16,128]{2,1,0:T(8,128)S(1)}, f32[8,16,128]{2,1,0:T(8,128)}, u32[]{:S(2)}) copy-start(f32[8,16,128]{2,1,0:T(8,128)} %param.19) | copy-start | bytes 196612
  43.7 5.4 %copy-start.9 = (f32[8,16,128]{2,1,0:T(8,128)S(1)}, f32[8,16,128]{2,1,0:T(8,128)}, u32[]{:S(2)}) copy-start(f32[8,16,128]{2,1,0:T(8,128)} %param.16) | copy-start | bytes 196612
  49.1 21.5 %copy-start.2 = (f32[8,16,128]{2,1,0:T(8,128)}, f32[8,16,128]{2,1,0:T(8,128)S(1)}, u32[]{:S(2)}) copy-start(f32[8,16,128]{2,1,0:T(8,128)S(1)} %get-tuple-element.14) | copy-start | bytes 196612
  49.2 20.7 %copy-start.4 = (f32[8,16,128]{2,1,0:T(8,128)}, f32[8,16,128]{2,1,0:T(8,128)S(1)}, u32[]{:S(2)}) copy-start(f32[8,16,128]{2,1,0:T(8,128)S(1)} %add_add_fusion.3) | copy-start | bytes 196612
  49.2 6.5 %collective-permute-start.4 = (f32[2,4,16,128]{3,2,1,0:T(8,128)S(1)}, f32[2,4,16,128]{3,2,1,0:T(8,128)S(1)}, u32[]{:S(2)}, u32[]{:S(2)}) collective-permute-start(f32[2,4,16,128]{3,2,1,0:T(8,128)S(1)} %get-tuple-element.33), channel_id=1, source_target_pairs={{4,0},{8,4},{12,8},{5,1},{9,5},{13,9},{6,2},{10,6},{14,10},{7,3},{... | collective-permute-start | bytes 196616 | tf_op jit(solution)/shard_map/ppermute | solution.py:20
  53.8 6.2 %collective-permute-start.5 = (f32[2,4,16,128]{3,2,1,0:T(8,128)S(1)}, f32[2,4,16,128]{3,2,1,0:T(8,128)S(1)}, u32[]{:S(2)}, u32[]{:S(2)}) collective-permute-start(f32[2,4,16,128]{3,2,1,0:T(8,128)S(1)} %get-tuple-element.32), channel_id=1, source_target_pairs={{0,4},{4,8},{8,12},{1,5},{5,9},{9,13},{2,6},{6,10},{10,14},{3,7},{... | collective-permute-start | bytes 196616 | tf_op jit(solution)/shard_map/ppermute | solution.py:18
  60.0 4.5 %collective-permute-start.6 = (f32[2,16,4,128]{3,2,1,0:T(4,128)S(1)}, f32[2,16,4,128]{3,2,1,0:T(4,128)S(1)}, u32[]{:S(2)}, u32[]{:S(2)}) collective-permute-start(f32[2,16,4,128]{3,2,1,0:T(4,128)S(1)} %get-tuple-element.23), channel_id=1, source_target_pairs={{1,0},{2,1},{3,2},{5,4},{6,5},{7,6},{9,8},{10,9},{11,10},{13,12},{... | collective-permute-start | bytes 196616 | tf_op jit(solution)/shard_map/ppermute | solution.py:20
  61.9 8.0 %copy-start.10 = (bf16[2,8,16,128]{3,2,1,0:T(8,128)(2,1)S(1)}, bf16[2,8,16,128]{3,2,1,0:T(8,128)(2,1)}, u32[]{:S(2)}) copy-start(bf16[2,8,16,128]{3,2,1,0:T(8,128)(2,1)} %param.23) | copy-start | bytes 196612
  61.9 5.7 %collective-permute-start.7 = (f32[2,16,4,128]{3,2,1,0:T(4,128)S(1)}, f32[2,16,4,128]{3,2,1,0:T(4,128)S(1)}, u32[]{:S(2)}, u32[]{:S(2)}) collective-permute-start(f32[2,16,4,128]{3,2,1,0:T(4,128)S(1)} %get-tuple-element.22), channel_id=1, source_target_pairs={{0,1},{1,2},{2,3},{4,5},{5,6},{6,7},{8,9},{9,10},{10,11},{12,13},{... | collective-permute-start | bytes 196616 | tf_op jit(solution)/shard_map/ppermute | solution.py:18
where the time goes:
time: 72.1 us; the launch traced here: 71.3 us
  starting transfers between devices  23.6 us (33%)
  other arithmetic  18.8 us (26%)
  local copies, waits for them, and re-layouts  16.7 us (23%)
  waiting for transfers between devices  11.1 us (15%)
  between operations  1.04 us (1%)
    slice x1, local copies, waits for them, and re-layouts, local(): sources[0]  12.3 us
    ppermute x4, starting transfers between devices, padded_2(): lax.ppermute(head, axis, [((i + 1) % count, i) for i in range(ends)])  10.9 us
    ppermute x4, waiting for transfers between devices, padded_2(): lax.ppermute(tail, axis, [(i, (i + 1) % count) for i in range(ends)])  10.5 us
    ppermute x4, starting transfers between devices, padded_2(): lax.ppermute(tail, axis, [(i, (i + 1) % count) for i in range(ends)])  7.66 us
    scatter-add x1, other arithmetic, local(): jnp.zeros((2, cells), jnp.float32).at[:, target].add(values)  5.68 us
    all_to_all x1, starting transfers between devices, local(): lax.all_to_all(slots, 'gx', split_axis=1, concat_axis=1, tiled=True)  5.09 us
  transfers between devices with their start and end apart: 9, of which 4 were waited for; matrix products, arithmetic and copies ran while one was open for 32% of the time, Pallas kernels for 0%

commit v1 on v0

--- a/solution.py
+++ b/solution.py
@@ -103,6 +103,32 @@
     return pad_depth(padded_2(fields, (("gx", 1), ("gy", 2)), 4))
 
 
+def receiver_sources(traces, time_steps, rec_owner, rec_local, shape):
+    sx, sy, sz = shape
+    groups = lax.axis_size("gx")
+    held = rec_local.shape[0]
+    samples = [lax.dynamic_index_in_dim(traces, time_steps[k], 0, keepdims=False) for k in range(2)]
+    payload = jnp.stack(
+        samples + [rec_local.astype(jnp.float32), rec_owner[:, 0].astype(jnp.float32)]
+    )
+    sent = jnp.broadcast_to(payload[None], (groups, 4, held))
+    arrived = lax.all_to_all(sent, "gx", split_axis=0, concat_axis=0, tiled=True)
+    arrived = jnp.transpose(arrived, (1, 0, 2)).reshape(4, groups * held)
+    mine = arrived[3].astype(jnp.int32) == lax.axis_index("gx")
+    cell = arrived[2].astype(jnp.int32)
+    plane = cell // sz
+    depth = cell % sz
+    values = jnp.where(mine[None, :], arrived[0:2], 0.0)
+    picks = (plane[None, :] == jnp.arange(sx * sy, dtype=jnp.int32)[:, None]).astype(jnp.float32)
+    spread = values[:, None, :] * picks[None, :, :]
+    columns = (depth[:, None] == jnp.arange(sz, dtype=jnp.int32)[None, :]).astype(jnp.float32)
+    sources = jnp.einsum(
+        "cpr,rz->cpz", spread, columns, precision=lax.Precision.HIGHEST,
+        preferred_element_type=jnp.float32,
+    )
+    return sources.reshape(2, sx, sy, sz)
+
+
 def local(
     p_now,
     q_now,
@@ -119,24 +145,7 @@
     rec_owner,
     rec_local,
 ):
-    sx, sy, sz = p_now.shape
-    cells = sx * sy * sz
-    groups = lax.axis_size("gx")
-    held = rec_local.shape[0]
-    samples = jnp.take(traces, time_steps, axis=0)
-    owner = rec_owner[:, 0]
-    capacity = 2 * held // groups
-    onehot = (owner[:, None] == jnp.arange(groups, dtype=jnp.int32)[None, :]).astype(jnp.int32)
-    running = jnp.cumsum(onehot, axis=0)
-    rank = jnp.sum(onehot * running, axis=1) - 1
-    position = owner * capacity + rank
-    payload = jnp.concatenate([samples, rec_local.astype(jnp.float32)[None, :]], axis=0)
-    slots = jnp.zeros((3, groups * capacity), jnp.float32).at[:, position].set(payload)
-    slots = slots.reshape(3, groups, capacity)
-    arrived = lax.all_to_all(slots, "gx", split_axis=1, concat_axis=1, tiled=True)
-    values = arrived[0:2].reshape(2, groups * capacity)
-    target = arrived[2].reshape(groups * capacity).astype(jnp.int32)
-    sources = jnp.zeros((2, cells), jnp.float32).at[:, target].add(values).reshape(2, sx, sy, sz)
+    sources = receiver_sources(traces, time_steps, rec_owner, rec_local, p_now.shape)
     current = jnp.stack([p_now, q_now])
     earlier = jnp.stack([p_prev, q_prev])
     middle = advance(widened(current), earlier, speed, epsilon, delta, theta, phi, sources[0])

time: 72.1 us -> 59.7 us (0.83)
  the two profiles are of different devices: /device:TPU:30 before, /device:TPU:1 now
where the time goes in v1:
time: 59.7 us; the launch traced here: 59 us
  starting transfers between devices  27.4 us (46%)
  waiting for transfers between devices  13.5 us (23%)
  other arithmetic  8.46 us (14%)
  between operations  4.87 us (8%)
  local copies, waits for them, and re-layouts  4.3 us (7%)
    ppermute x4, starting transfers between devices, padded_2(): lax.ppermute(tail, axis, [(i, (i + 1) % count) for i in range(ends)])  15.4 us
    ppermute x4, waiting for transfers between devices, padded_2(): lax.ppermute(head, axis, [((i + 1) % count, i) for i in range(ends)])  13.5 us
    ppermute x4, starting transfers between devices, padded_2(): lax.ppermute(head, axis, [((i + 1) % count, i) for i in range(ends)])  6.56 us
    all_to_all x1, starting transfers between devices, receiver_sources(): lax.all_to_all(sent, 'gx', split_axis=0, concat_axis=0, tiled=True)  5.42 us
    unnamed x24, local copies, waits for them, and re-layouts  1.42 us
    slice x1, local copies, waits for them, and re-layouts, receiver_sources(): time_steps[k]  1.31 us
    add x2, other arithmetic, derivatives(): dz_xwide + weight * (padded[:, :, 4:4 + sy, 4 + k:4 + k + sz] - padded[:,...  1.24 us
  transfers between devices with their start and end apart: 9, of which 4 were waited for; matrix products, arithmetic and copies ran while one was open for 3% of the time, Pallas kernels for 0%

profile of v1, /device:TPU:1, one launch (start us, length us, event | category | flops | bytes accessed | tf_op | source)
XLA Modules:
  0.0 59.0 jit_solution(16232336924576089874)
XLA Ops:
  0.6 0.0 copy-start
  0.6 1.3 %fusion.176 = (s32[1]{0:T(128)}, s32[1]{0:T(128)}) fusion(s32[2]{0:T(128)} %param.25), kind=kLoop, calls=%fused_computation.316 | loop fusion | bytes 16 | tf_op jit(solution)/shard_map/slice | solution.py:110
  4.5 0.7 %convert_bitcast_fusion = f32[1,128]{1,0:T(1,128)S(1)} fusion(s32[128,1]{0,1:T(1,128)} %param.26), kind=kLoop, calls=%fused_computation.308 | loop fusion | flops 128 | bytes 1024 | tf_op jit(solution)/shard_map/convert_element_type | solution.py:112
  5.2 0.7 %convert_bitcast_fusion.1 = f32[1,128]{1,0:T(1,128)S(1)} fusion(s32[128]{0:T(128)} %param.27), kind=kLoop, calls=%fused_computation.309 | loop fusion | flops 128 | bytes 1024 | tf_op jit(solution)/shard_map/stack | solution.py:111
  7.2 0.7 %constant_dynamic-slice_fusion.1 = (f32[1,128]{1,0:T(1,128)S(1)}, f32[1,128]{1,0:T(1,128)S(1)}) fusion(f32[1024,128]{1,0:T(8,128)} %param.24, s32[]{:T(128)S(6)} %select_n.35, s32[]{:T(128)S(6)} %select_n.36), kind=kLoop, calls=%fused_computation.311 | loop fusion | bytes 2056 | tf_op jit(solution)/shard_map/jit(dynamic_index_in_dim)/dynamic_slice | solution.py:110
  7.9 0.6 %broadcast_in_dim.14 = f32[4,4,128]{2,1,0:T(4,128)} broadcast(f32[4,128]{1,0:T(4,128)S(1)} %pad_maximum_fusion.14), dimensions={1,2} | broadcast | bytes 10240 | tf_op jit(solution)/shard_map/broadcast_in_dim | solution.py:114
  8.5 5.4 %all-to-all-start = ((f32[4,4,128]{2,1,0:T(4,128)}), f32[4,4,128]{2,1,0:T(4,128)S(1)}, u32[]{:S(2)}, u32[]{:S(2)}) async-start(f32[4,4,128]{2,1,0:T(4,128)} %broadcast_in_dim.14), calls=%async_computation | async-start | bytes 16384 | tf_op jit(solution)/shard_map/all_to_all | solution.py:115
  13.9 0.0 copy-done
  13.9 0.0 copy-start.7
  13.9 0.8 %fusion.158 = (f32[2,4,16,128]{3,2,1,0:T(8,128)S(1)}, f32[2,4,16,128]{3,2,1,0:T(8,128)S(1)}) fusion(f32[1,8,16,128]{3,2,1,0:T(8,128)} %bitcast.59, f32[1,8,16,128]{3,2,1,0:T(8,128)S(1)} %bitcast.47), kind=kLoop, calls=%fused_computation.261 | loop fusion | flops 32768 | bytes 262144 | tf_op jit(solution)/shard_map/stack | solution.py:149
  14.7 3.4 %collective-permute-start.1 = (f32[2,4,16,128]{3,2,1,0:T(8,128)S(1)}, f32[2,4,16,128]{3,2,1,0:T(8,128)S(1)}, u32[]{:S(2)}, u32[]{:S(2)}) collective-permute-start(f32[2,4,16,128]{3,2,1,0:T(8,128)S(1)} %get-tuple-element.43), channel_id=1, source_target_pairs={{0,4},{4,8},{8,12},{1,5},{5,9},{9,13},{2,6},{6,10},{10,14},{3,7},{... | collective-permute-start | bytes 196616 | tf_op jit(solution)/shard_map/ppermute | solution.py:18
  18.1 0.0 copy-start.8
  18.1 1.4 %collective-permute-start = (f32[2,4,16,128]{3,2,1,0:T(8,128)S(1)}, f32[2,4,16,128]{3,2,1,0:T(8,128)S(1)}, u32[]{:S(2)}, u32[]{:S(2)}) collective-permute-start(f32[2,4,16,128]{3,2,1,0:T(8,128)S(1)} %get-tuple-element.44), channel_id=1, source_target_pairs={{4,0},{8,4},{12,8},{5,1},{9,5},{13,9},{6,2},{10,6},{14,10},{7,3},{... | collective-permute-start | bytes 196616 | tf_op jit(solution)/shard_map/ppermute | solution.py:20
  19.6 0.0 copy-done.7
  19.6 0.2 fusion.175
  19.8 0.0 copy-done.8
  19.8 0.3 fusion.164
  20.1 0.0 all-to-all-done
  20.2 0.5 fusion.1
  20.7 0.0 copy-start.2
  20.7 0.0 collective-permute-done.1
  20.7 2.5 %collective-permute-done = f32[2,4,16,128]{3,2,1,0:T(8,128)S(1)} collective-permute-done((f32[2,4,16,128]{3,2,1,0:T(8,128)S(1)}, f32[2,4,16,128]{3,2,1,0:T(8,128)S(1)}, u32[]{:S(2)}, u32[]{:S(2)}) %collective-permute-start) | collective-permute-done | bytes 65568 | tf_op jit(solution)/shard_map/ppermute | solution.py:20
  23.3 0.0 copy-done.2
  23.3 5.7 %collective-permute-start.3 = (f32[2,16,4,128]{3,2,1,0:T(4,128)S(1)}, f32[2,16,4,128]{3,2,1,0:T(4,128)S(1)}, u32[]{:S(2)}, u32[]{:S(2)}) collective-permute-start(f32[2,16,4,128]{3,2,1,0:T(4,128)S(1)} %get-tuple-element.26), channel_id=1, source_target_pairs={{0,1},{1,2},{2,3},{4,5},{5,6},{6,7},{8,9},{9,10},{10,11},{12,13},{... | collective-permute-start | bytes 196616 | tf_op jit(solution)/shard_map/ppermute | solution.py:18
  29.0 1.9 %collective-permute-start.2 = (f32[2,16,4,128]{3,2,1,0:T(4,128)S(1)}, f32[2,16,4,128]{3,2,1,0:T(4,128)S(1)}, u32[]{:S(2)}, u32[]{:S(2)}) collective-permute-start(f32[2,16,4,128]{3,2,1,0:T(4,128)S(1)} %get-tuple-element.27), channel_id=1, source_target_pairs={{1,0},{2,1},{3,2},{5,4},{6,5},{7,6},{9,8},{10,9},{11,10},{13,12},{... | collective-permute-start | bytes 196616 | tf_op jit(solution)/shard_map/ppermute | solution.py:20
  30.9 0.0 collective-permute-done.3
  31.0 3.6 %collective-permute-done.2 = f32[2,16,4,128]{3,2,1,0:T(4,128)S(1)} collective-permute-done((f32[2,16,4,128]{3,2,1,0:T(4,128)S(1)}, f32[2,16,4,128]{3,2,1,0:T(4,128)S(1)}, u32[]{:S(2)}, u32[]{:S(2)}) %collective-permute-start.2) | collective-permute-done | bytes 65568 | tf_op jit(solution)/shard_map/ppermute | solution.py:20
  34.6 0.4 select_maximum_fusion.5
  35.0 0.4 fusion.44
  35.4 0.1 pad_maximum_fusion
  35.5 0.7 %fusion.18 = (f32[2,16,16,128]{3,2,1,0:T(8,128)S(1)}, f32[2,16,16,128]{3,2,1,0:T(8,128)S(1)}) fusion(f32[2,16,24,136]{3,2,1,0:T(8,128)S(1)} %select_maximum_fusion.5, f32[2,16,20,128]{3,2,1,0:T(8,128)S(1)} %get-tuple-element.25, f32[2,16,20,128]{3,2,1,0:T(8,128)S(1)} %get-tuple-element.24), kind=kLoop, calls=%fused_computation.43 | loop fusion | flops 1441792 | bytes 4718592 | tf_op jit(solution)/shard_map/add | solution.py:49
  36.2 0.0 copy-start.4
  36.2 0.0 copy-start.5
  36.2 0.0 copy-start.9
  36.2 0.6 fusion.106
  36.8 0.2 copy-done.4
  37.0 0.0 copy-done.5
  37.1 0.0 copy-done.9
  37.1 0.1 add_add_fusion.2
  37.1 0.0 copy-start.1
  37.2 0.8 %copy-done.6 = f32[8,16,128]{2,1,0:T(8,128)S(1)} copy-done((f32[8,16,128]{2,1,0:T(8,128)S(1)}, f32[8,16,128]{2,1,0:T(8,128)}, u32[]{:S(2)}) %copy-start.6) | copy-done | bytes 65560
  37.9 0.0 copy-done.10
  38.0 0.1 add_add_fusion.3
  38.0 0.0 copy-start.3
  38.0 3.1 %collective-permute-start.5 = (f32[2,4,16,128]{3,2,1,0:T(8,128)S(1)}, f32[2,4,16,128]{3,2,1,0:T(8,128)S(1)}, u32[]{:S(2)}, u32[]{:S(2)}) collective-permute-start(f32[2,4,16,128]{3,2,1,0:T(8,128)S(1)} %get-tuple-element.32), channel_id=1, source_target_pairs={{0,4},{4,8},{8,12},{1,5},{5,9},{9,13},{2,6},{6,10},{10,14},{3,7},{... | collective-permute-start | bytes 196616 | tf_op jit(solution)/shard_map/ppermute | solution.py:18
  41.1 1.3 %collective-permute-start.4 = (f32[2,4,16,128]{3,2,1,0:T(8,128)S(1)}, f32[2,4,16,128]{3,2,1,0:T(8,128)S(1)}, u32[]{:S(2)}, u32[]{:S(2)}) collective-permute-start(f32[2,4,16,128]{3,2,1,0:T(8,128)S(1)} %get-tuple-element.33), channel_id=1, source_target_pairs={{4,0},{8,4},{12,8},{5,1},{9,5},{13,9},{6,2},{10,6},{14,10},{7,3},{... | collective-permute-start | bytes 196616 | tf_op jit(solution)/shard_map/ppermute | solution.py:20
  42.4 0.0 collective-permute-done.5
  42.5 3.7 %collective-permute-done.4 = f32[2,4,16,128]{3,2,1,0:T(8,128)S(1)} collective-permute-done((f32[2,4,16,128]{3,2,1,0:T(8,128)S(1)}, f32[2,4,16,128]{3,2,1,0:T(8,128)S(1)}, u32[]{:S(2)}, u32[]{:S(2)}) %collective-permute-start.4) | collective-permute-done | bytes 65568 | tf_op jit(solution)/shard_map/ppermute | solution.py:20
  46.2 3.3 %collective-permute-start.7 = (f32[2,16,4,128]{3,2,1,0:T(4,128)S(1)}, f32[2,16,4,128]{3,2,1,0:T(4,128)S(1)}, u32[]{:S(2)}, u32[]{:S(2)}) collective-permute-start(f32[2,16,4,128]{3,2,1,0:T(4,128)S(1)} %get-tuple-element.22), channel_id=1, source_target_pairs={{0,1},{1,2},{2,3},{4,5},{5,6},{6,7},{8,9},{9,10},{10,11},{12,13},{... | collective-permute-start | bytes 196616 | tf_op jit(solution)/shard_map/ppermute | solution.py:18
  49.5 1.9 %collective-permute-start.6 = (f32[2,16,4,128]{3,2,1,0:T(4,128)S(1)}, f32[2,16,4,128]{3,2,1,0:T(4,128)S(1)}, u32[]{:S(2)}, u32[]{:S(2)}) collective-permute-start(f32[2,16,4,128]{3,2,1,0:T(4,128)S(1)} %get-tuple-element.23), channel_id=1, source_target_pairs={{1,0},{2,1},{3,2},{5,4},{6,5},{7,6},{9,8},{10,9},{11,10},{13,12},{... | collective-permute-start | bytes 196616 | tf_op jit(solution)/shard_map/ppermute | solution.py:20
  51.5 0.0 collective-permute-done.7
  51.5 3.6 %collective-permute-done.6 = f32[2,16,4,128]{3,2,1,0:T(4,128)S(1)} collective-permute-done((f32[2,16,4,128]{3,2,1,0:T(4,128)S(1)}, f32[2,16,4,128]{3,2,1,0:T(4,128)S(1)}, u32[]{:S(2)}, u32[]{:S(2)}) %collective-permute-start.6) | collective-permute-done | bytes 65568 | tf_op jit(solution)/shard_map/ppermute | solution.py:20
  55.1 0.4 select_maximum_fusion
  55.5 0.4 fusion.37
  55.9 0.5 fusion.4
  56.5 0.1 pad_maximum_fusion.1
  56.5 0.2 fusion.11
  56.7 0.0 copy-start.11
  56.8 0.6 fusion.55
  57.3 0.0 copy-done.3
  57.3 0.3 copy-done.11
  57.6 0.7 %fusion.161 = (f32[8,16,128]{2,1,0:T(8,128)}, f32[8,16,128]{2,1,0:T(8,128)}, f32[8,16,128]{2,1,0:T(8,128)S(1)}) fusion(f32[8,16,128]{2,1,0:T(8,128)S(1)} %add_add_fusion.3, bf16[2,8,16,128]{3,2,1,0:T(8,128)(2,1)S(1)} %copy-done.11, f32[8,16,128]{2,1,0:T(8,128)S(1)} %bitcast.73, f32[8,16,128]{2,1,0:T(8,128)S(1)} %copy-done.4, ...), kind=kLoop, calls=%fused_computation.281 | loop fusion | flops 327680 | bytes 983040 | tf_op jit(solution)/shard_map/add | solution.py:154
  58.3 0.0 copy-done.1
  58.3 0.7 %add_add_fusion = f32[8,16,128]{2,1,0:T(8,128)} fusion(f32[8,16,128]{2,1,0:T(8,128)S(1)} %bitcast.74, f32[8,16,128]{2,1,0:T(8,128)S(1)} %copy-done.4, f32[8,16,128]{2,1,0:T(8,128)S(1)} %get-tuple-element.7, f32[8,16,128]{2,1,0:T(8,128)S(1)} %copy-done, f32[8,16,128]{2,1,0:T(8,128)S(1)} %get-tuple-element.12, f32[2,8,16,128]{3,2,1,0:T(8,128)S(1)} %get-tuple-element.8, ...), kind=kLoop, calls=%fused_computation.283 | loop fusion | flops 147456 | bytes 524288 | tf_op jit(solution)/shard_map/add | solution.py:93
  (14 shorter events, 0.2 us)
Async XLA Ops:
  0.6 13.3 %copy-start = (f32[8,16,128]{2,1,0:T(8,128)S(1)}, f32[8,16,128]{2,1,0:T(8,128)}, u32[]{:S(2)}) copy-start(f32[8,16,128]{2,1,0:T(8,128)} %param.15) | copy-start | bytes 196612
  8.5 11.6 %all-to-all-start = ((f32[4,4,128]{2,1,0:T(4,128)}), f32[4,4,128]{2,1,0:T(4,128)S(1)}, u32[]{:S(2)}, u32[]{:S(2)}) async-start(f32[4,4,128]{2,1,0:T(4,128)} %broadcast_in_dim.14), calls=%async_computation | async-start | bytes 16384 | tf_op jit(solution)/shard_map/all_to_all | solution.py:115
  13.9 5.6 %copy-start.7 = (f32[8,16,128]{2,1,0:T(8,128)S(1)}, f32[8,16,128]{2,1,0:T(8,128)}, u32[]{:S(2)}) copy-start(f32[8,16,128]{2,1,0:T(8,128)} %param.21) | copy-start | bytes 196612
  14.7 6.0 %collective-permute-start.1 = (f32[2,4,16,128]{3,2,1,0:T(8,128)S(1)}, f32[2,4,16,128]{3,2,1,0:T(8,128)S(1)}, u32[]{:S(2)}, u32[]{:S(2)}) collective-permute-start(f32[2,4,16,128]{3,2,1,0:T(8,128)S(1)} %get-tuple-element.43), channel_id=1, source_target_pairs={{0,4},{4,8},{8,12},{1,5},{5,9},{9,13},{2,6},{6,10},{10,14},{3,7},{... | collective-permute-start | bytes 196616 | tf_op jit(solution)/shard_map/ppermute | solution.py:18
  18.1 1.7 %copy-start.8 = (f32[8,16,128]{2,1,0:T(8,128)S(1)}, f32[8,16,128]{2,1,0:T(8,128)}, u32[]{:S(2)}) copy-start(f32[8,16,128]{2,1,0:T(8,128)} %param.22) | copy-start | bytes 196612
  18.1 5.1 %collective-permute-start = (f32[2,4,16,128]{3,2,1,0:T(8,128)S(1)}, f32[2,4,16,128]{3,2,1,0:T(8,128)S(1)}, u32[]{:S(2)}, u32[]{:S(2)}) collective-permute-start(f32[2,4,16,128]{3,2,1,0:T(8,128)S(1)} %get-tuple-element.44), channel_id=1, source_target_pairs={{4,0},{8,4},{12,8},{5,1},{9,5},{13,9},{6,2},{10,6},{14,10},{7,3},{... | collective-permute-start | bytes 196616 | tf_op jit(solution)/shard_map/ppermute | solution.py:20
  20.7 2.6 %copy-start.2 = (f32[8,16,128]{2,1,0:T(8,128)S(1)}, f32[8,16,128]{2,1,0:T(8,128)}, u32[]{:S(2)}) copy-start(f32[8,16,128]{2,1,0:T(8,128)} %param.14) | copy-start | bytes 196612
  23.3 7.6 %collective-permute-start.3 = (f32[2,16,4,128]{3,2,1,0:T(4,128)S(1)}, f32[2,16,4,128]{3,2,1,0:T(4,128)S(1)}, u32[]{:S(2)}, u32[]{:S(2)}) collective-permute-start(f32[2,16,4,128]{3,2,1,0:T(4,128)S(1)} %get-tuple-element.26), channel_id=1, source_target_pairs={{0,1},{1,2},{2,3},{4,5},{5,6},{6,7},{8,9},{9,10},{10,11},{12,13},{... | collective-permute-start | bytes 196616 | tf_op jit(solution)/shard_map/ppermute | solution.py:18
  29.0 5.6 %collective-permute-start.2 = (f32[2,16,4,128]{3,2,1,0:T(4,128)S(1)}, f32[2,16,4,128]{3,2,1,0:T(4,128)S(1)}, u32[]{:S(2)}, u32[]{:S(2)}) collective-permute-start(f32[2,16,4,128]{3,2,1,0:T(4,128)S(1)} %get-tuple-element.27), channel_id=1, source_target_pairs={{1,0},{2,1},{3,2},{5,4},{6,5},{7,6},{9,8},{10,9},{11,10},{13,12},{... | collective-permute-start | bytes 196616 | tf_op jit(solution)/shard_map/ppermute | solution.py:20
  36.2 0.8 %copy-start.4 = (f32[8,16,128]{2,1,0:T(8,128)S(1)}, f32[8,16,128]{2,1,0:T(8,128)}, u32[]{:S(2)}) copy-start(f32[8,16,128]{2,1,0:T(8,128)} %param.18) | copy-start | bytes 196612
  36.2 0.9 %copy-start.5 = (f32[8,16,128]{2,1,0:T(8,128)S(1)}, f32[8,16,128]{2,1,0:T(8,128)}, u32[]{:S(2)}) copy-start(f32[8,16,128]{2,1,0:T(8,128)} %param.20) | copy-start | bytes 196612
  36.2 0.9 %copy-start.9 = (f32[8,16,128]{2,1,0:T(8,128)S(1)}, f32[8,16,128]{2,1,0:T(8,128)}, u32[]{:S(2)}) copy-start(f32[8,16,128]{2,1,0:T(8,128)} %param.17) | copy-start | bytes 196612
  37.1 0.8 %copy-start.6 = (f32[8,16,128]{2,1,0:T(8,128)S(1)}, f32[8,16,128]{2,1,0:T(8,128)}, u32[]{:S(2)}) copy-start(f32[8,16,128]{2,1,0:T(8,128)} %param.19) | copy-start | bytes 196612
  37.1 0.9 %copy-start.10 = (f32[8,16,128]{2,1,0:T(8,128)S(1)}, f32[8,16,128]{2,1,0:T(8,128)}, u32[]{:S(2)}) copy-start(f32[8,16,128]{2,1,0:T(8,128)} %param.16) | copy-start | bytes 196612
  37.1 21.2 %copy-start.1 = (f32[8,16,128]{2,1,0:T(8,128)}, f32[8,16,128]{2,1,0:T(8,128)S(1)}, u32[]{:S(2)}) copy-start(f32[8,16,128]{2,1,0:T(8,128)S(1)} %get-tuple-element.12) | copy-start | bytes 196612
  38.0 19.3 %copy-start.3 = (f32[8,16,128]{2,1,0:T(8,128)}, f32[8,16,128]{2,1,0:T(8,128)S(1)}, u32[]{:S(2)}) copy-start(f32[8,16,128]{2,1,0:T(8,128)S(1)} %add_add_fusion.3) | copy-start | bytes 196612
  38.0 4.4 %collective-permute-start.5 = (f32[2,4,16,128]{3,2,1,0:T(8,128)S(1)}, f32[2,4,16,128]{3,2,1,0:T(8,128)S(1)}, u32[]{:S(2)}, u32[]{:S(2)}) collective-permute-start(f32[2,4,16,128]{3,2,1,0:T(8,128)S(1)} %get-tuple-element.32), channel_id=1, source_target_pairs={{0,4},{4,8},{8,12},{1,5},{5,9},{9,13},{2,6},{6,10},{10,14},{3,7},{... | collective-permute-start | bytes 196616 | tf_op jit(solution)/shard_map/ppermute | solution.py:18
  41.1 5.0 %collective-permute-start.4 = (f32[2,4,16,128]{3,2,1,0:T(8,128)S(1)}, f32[2,4,16,128]{3,2,1,0:T(8,128)S(1)}, u32[]{:S(2)}, u32[]{:S(2)}) collective-permute-start(f32[2,4,16,128]{3,2,1,0:T(8,128)S(1)} %get-tuple-element.33), channel_id=1, source_target_pairs={{4,0},{8,4},{12,8},{5,1},{9,5},{13,9},{6,2},{10,6},{14,10},{7,3},{... | collective-permute-start | bytes 196616 | tf_op jit(solution)/shard_map/ppermute | solution.py:20
  46.2 5.3 %collective-permute-start.7 = (f32[2,16,4,128]{3,2,1,0:T(4,128)S(1)}, f32[2,16,4,128]{3,2,1,0:T(4,128)S(1)}, u32[]{:S(2)}, u32[]{:S(2)}) collective-permute-start(f32[2,16,4,128]{3,2,1,0:T(4,128)S(1)} %get-tuple-element.22), channel_id=1, source_target_pairs={{0,1},{1,2},{2,3},{4,5},{5,6},{6,7},{8,9},{9,10},{10,11},{12,13},{... | collective-permute-start | bytes 196616 | tf_op jit(solution)/shard_map/ppermute | solution.py:18
  49.5 5.6 %collective-permute-start.6 = (f32[2,16,4,128]{3,2,1,0:T(4,128)S(1)}, f32[2,16,4,128]{3,2,1,0:T(4,128)S(1)}, u32[]{:S(2)}, u32[]{:S(2)}) collective-permute-start(f32[2,16,4,128]{3,2,1,0:T(4,128)S(1)} %get-tuple-element.23), channel_id=1, source_target_pairs={{1,0},{2,1},{3,2},{5,4},{6,5},{7,6},{9,8},{10,9},{11,10},{13,12},{... | collective-permute-start | bytes 196616 | tf_op jit(solution)/shard_map/ppermute | solution.py:20
  56.7 0.8 %copy-start.11 = (bf16[2,8,16,128]{3,2,1,0:T(8,128)(2,1)S(1)}, bf16[2,8,16,128]{3,2,1,0:T(8,128)(2,1)}, u32[]{:S(2)}) copy-start(bf16[2,8,16,128]{3,2,1,0:T(8,128)(2,1)} %param.23) | copy-start | bytes 196612

commit v2 on v1

--- a/solution.py
+++ b/solution.py
@@ -111,9 +111,17 @@
     payload = jnp.stack(
         samples + [rec_local.astype(jnp.float32), rec_owner[:, 0].astype(jnp.float32)]
     )
-    sent = jnp.broadcast_to(payload[None], (groups, 4, held))
-    arrived = lax.all_to_all(sent, "gx", split_axis=0, concat_axis=0, tiled=True)
-    arrived = jnp.transpose(arrived, (1, 0, 2)).reshape(4, groups * held)
+    if groups & (groups - 1) == 0:
+        arrived = payload
+        step = 1
+        while step < groups:
+            partner = lax.ppermute(arrived, "gx", [(i, i ^ step) for i in range(groups)])
+            arrived = jnp.concatenate([arrived, partner], axis=1)
+            step *= 2
+    else:
+        sent = jnp.broadcast_to(payload[None], (groups, 4, held))
+        arrived = lax.all_to_all(sent, "gx", split_axis=0, concat_axis=0, tiled=True)
+        arrived = jnp.transpose(arrived, (1, 0, 2)).reshape(4, groups * held)
     mine = arrived[3].astype(jnp.int32) == lax.axis_index("gx")
     cell = arrived[2].astype(jnp.int32)
     plane = cell // sz

time: 59.7 us -> 57 us (0.955)
  other arithmetic: 8.46 us -> 7.21 us
  starting transfers between devices: 27.4 us -> 26.2 us
  waiting for transfers between devices: 13.5 us -> 12.4 us
  local copies, waits for them, and re-layouts: 4.3 us -> 5.15 us
    ppermute x0 -> x2, starting transfers between devices: none -> 6.62 us  [receiver_sources(): lax.ppermute(arrived, 'gx', [(i, i ^ step) for i in range(groups)])]
    all_to_all x1 -> x0, starting transfers between devices: 5.42 us -> none  [receiver_sources(): lax.all_to_all(sent, 'gx', split_axis=0, concat_axis=0, tiled=True)]
    ppermute x4, starting transfers between devices: 15.4 us -> 13 us  [padded_2(): lax.ppermute(tail, axis, [(i, (i + 1) % count) for i in range(ends)])]
    ppermute x4, waiting for transfers between devices: 13.5 us -> 11.2 us  [padded_2(): lax.ppermute(head, axis, [((i + 1) % count, i) for i in range(ends)])]
    unnamed x24 -> x28, local copies, waits for them, and re-layouts: 1.42 us -> 2.88 us
    ppermute x0 -> x2, waiting for transfers between devices: none -> 1.16 us  [receiver_sources(): lax.ppermute(arrived, 'gx', [(i, i ^ step) for i in range(groups)])]
    convert_element_type x1, other arithmetic: 0.66 us -> 0.01 us  [receiver_sources(): rec_owner[:, 0].astype(jnp.float32)]
    another operation x2, other arithmetic: 0.67 us -> 0.01 us  [receiver_sources(): jnp.stack(samples + [rec_local.astype(jnp.float32), rec_owner[:, 0].astyp...]
  transfers between devices with their start and end apart: 9 -> 10, of which waited for: 4 -> 4; matrix products, arithmetic and copies ran while one was open for 3% -> 4% of each run, Pallas kernels for 0% -> 0%
where the time goes in v2:
time: 57 us; the launch traced here: 56.3 us
  starting transfers between devices  26.2 us (46%)
  waiting for transfers between devices  12.4 us (22%)
  other arithmetic  7.21 us (13%)
  local copies, waits for them, and re-layouts  5.15 us (9%)
  between operations  4.92 us (9%)
    ppermute x4, starting transfers between devices, padded_2(): lax.ppermute(tail, axis, [(i, (i + 1) % count) for i in range(ends)])  13 us
    ppermute x4, waiting for transfers between devices, padded_2(): lax.ppermute(head, axis, [((i + 1) % count, i) for i in range(ends)])  11.2 us
    ppermute x2, starting transfers between devices, receiver_sources(): lax.ppermute(arrived, 'gx', [(i, i ^ step) for i in range(groups)])  6.62 us
    ppermute x4, starting transfers between devices, padded_2(): lax.ppermute(head, axis, [((i + 1) % count, i) for i in range(ends)])  6.56 us
    unnamed x28, local copies, waits for them, and re-layouts  2.88 us
    slice x1, local copies, waits for them, and re-layouts, receiver_sources(): time_steps[k]  1.31 us
    add x2, other arithmetic, derivatives(): dz_xwide + weight * (padded[:, :, 4:4 + sy, 4 + k:4 + k + sz] - padded[:,...  1.24 us
    ppermute x2, waiting for transfers between devices, receiver_sources(): lax.ppermute(arrived, 'gx', [(i, i ^ step) for i in range(groups)])  1.16 us
  transfers between devices with their start and end apart: 10, of which 4 were waited for; matrix products, arithmetic and copies ran while one was open for 4% of the time, Pallas kernels for 0%

profile of v2, /device:TPU:1, one launch (start us, length us, event | category | flops | bytes accessed | tf_op | source)
XLA Modules:
  0.0 56.3 jit_solution(6877721376248750339)
XLA Ops:
  0.6 1.3 %fusion.175 = (s32[1]{0:T(128)}, s32[1]{0:T(128)}) fusion(s32[2]{0:T(128)} %param.25), kind=kLoop, calls=%fused_computation.317 | loop fusion | bytes 16 | tf_op jit(solution)/shard_map/slice | solution.py:110
  3.9 0.0 copy-start.12
  4.6 0.0 copy-done.12
  4.6 0.0 copy-start.13
  4.6 0.6 %copy-done.13 = s32[128]{0:T(128)S(1)} copy-done((s32[128]{0:T(128)S(1)}, s32[128]{0:T(128)}, u32[]{:S(2)}) %copy-start.13) | copy-done | bytes 536
  6.5 0.7 %constant_dynamic-slice_fusion.1 = (f32[1,128]{1,0:T(1,128)S(1)}, f32[1,128]{1,0:T(1,128)S(1)}) fusion(f32[1024,128]{1,0:T(8,128)} %param.24, s32[]{:T(128)S(6)} %select_n.30, s32[]{:T(128)S(6)} %select_n.31), kind=kLoop, calls=%fused_computation.312 | loop fusion | bytes 2056 | tf_op jit(solution)/shard_map/jit(dynamic_index_in_dim)/dynamic_slice | solution.py:110
  7.3 2.2 %collective-permute-start.4 = (f32[4,128]{1,0:T(4,128)S(1)}, f32[4,128]{1,0:T(4,128)S(1)}, u32[]{:S(2)}, u32[]{:S(2)}) collective-permute-start(f32[4,128]{1,0:T(4,128)S(1)} %pad_maximum_fusion.16), channel_id=1, source_target_pairs={{0,4},{4,0},{8,12},{12,8},{1,5},{5,1},{9,13},{13,9},{2,6},{6,2},{1... | collective-permute-start | bytes 6152 | tf_op jit(solution)/shard_map/ppermute | solution.py:118
  9.5 0.8 %fusion.158 = (f32[2,4,16,128]{3,2,1,0:T(8,128)S(1)}, f32[2,4,16,128]{3,2,1,0:T(8,128)S(1)}) fusion(f32[1,8,16,128]{3,2,1,0:T(8,128)} %bitcast.54, f32[1,8,16,128]{3,2,1,0:T(8,128)} %bitcast.42), kind=kLoop, calls=%fused_computation.261 | loop fusion | flops 32768 | bytes 262144 | tf_op jit(solution)/shard_map/stack | solution.py:157
  10.3 1.9 %collective-permute-start.1 = (f32[2,4,16,128]{3,2,1,0:T(8,128)S(1)}, f32[2,4,16,128]{3,2,1,0:T(8,128)S(1)}, u32[]{:S(2)}, u32[]{:S(2)}) collective-permute-start(f32[2,4,16,128]{3,2,1,0:T(8,128)S(1)} %get-tuple-element.45), channel_id=1, source_target_pairs={{0,4},{4,8},{8,12},{1,5},{5,9},{9,13},{2,6},{6,10},{10,14},{3,7},{... | collective-permute-start | bytes 196616 | tf_op jit(solution)/shard_map/ppermute | solution.py:18
  12.2 0.0 copy-start.8
  12.3 1.4 %collective-permute-start = (f32[2,4,16,128]{3,2,1,0:T(8,128)S(1)}, f32[2,4,16,128]{3,2,1,0:T(8,128)S(1)}, u32[]{:S(2)}, u32[]{:S(2)}) collective-permute-start(f32[2,4,16,128]{3,2,1,0:T(8,128)S(1)} %get-tuple-element.46), channel_id=1, source_target_pairs={{4,0},{8,4},{12,8},{5,1},{9,5},{13,9},{6,2},{10,6},{14,10},{7,3},{... | collective-permute-start | bytes 196616 | tf_op jit(solution)/shard_map/ppermute | solution.py:20
  13.7 0.0 copy-done.7
  13.7 0.2 fusion.174
  13.9 0.0 collective-permute-done.4
  14.0 4.4 %collective-permute-start.5 = (f32[4,256]{1,0:T(4,128)S(1)}, f32[4,256]{1,0:T(4,128)S(1)}, u32[]{:S(2)}, u32[]{:S(2)}) collective-permute-start(f32[4,256]{1,0:T(4,128)S(1)} %pad_maximum_fusion.15), channel_id=1, source_target_pairs={{0,8},{4,12},{8,0},{12,4},{1,9},{5,13},{9,1},{13,5},{2,10},{6,14},... | collective-permute-start | bytes 12296 | tf_op jit(solution)/shard_map/ppermute | solution.py:118
  18.4 0.0 copy-done.8
  18.4 0.3 fusion.163
  18.7 1.2 %collective-permute-done.5 = f32[4,256]{1,0:T(4,128)S(1)} collective-permute-done((f32[4,256]{1,0:T(4,128)S(1)}, f32[4,256]{1,0:T(4,128)S(1)}, u32[]{:S(2)}, u32[]{:S(2)}) %collective-permute-start.5) | collective-permute-done | bytes 4128 | tf_op jit(solution)/shard_map/ppermute | solution.py:118
  20.0 0.5 fusion.1
  20.4 0.0 copy-start
  20.5 0.0 copy-start.2
  20.5 0.0 collective-permute-done.1
  20.5 0.0 collective-permute-done
  20.5 0.8 %copy-done = f32[8,16,128]{2,1,0:T(8,128)S(1)} copy-done((f32[8,16,128]{2,1,0:T(8,128)S(1)}, f32[8,16,128]{2,1,0:T(8,128)}, u32[]{:S(2)}) %copy-start) | copy-done | bytes 65560
  21.3 0.0 copy-done.2
  21.3 5.3 %collective-permute-start.3 = (f32[2,16,4,128]{3,2,1,0:T(4,128)S(1)}, f32[2,16,4,128]{3,2,1,0:T(4,128)S(1)}, u32[]{:S(2)}, u32[]{:S(2)}) collective-permute-start(f32[2,16,4,128]{3,2,1,0:T(4,128)S(1)} %get-tuple-element.28), channel_id=1, source_target_pairs={{0,1},{1,2},{2,3},{4,5},{5,6},{6,7},{8,9},{9,10},{10,11},{12,13},{... | collective-permute-start | bytes 196616 | tf_op jit(solution)/shard_map/ppermute | solution.py:18
  26.6 1.9 %collective-permute-start.2 = (f32[2,16,4,128]{3,2,1,0:T(4,128)S(1)}, f32[2,16,4,128]{3,2,1,0:T(4,128)S(1)}, u32[]{:S(2)}, u32[]{:S(2)}) collective-permute-start(f32[2,16,4,128]{3,2,1,0:T(4,128)S(1)} %get-tuple-element.29), channel_id=1, source_target_pairs={{1,0},{2,1},{3,2},{5,4},{6,5},{7,6},{9,8},{10,9},{11,10},{13,12},{... | collective-permute-start | bytes 196616 | tf_op jit(solution)/shard_map/ppermute | solution.py:20
  28.6 0.0 collective-permute-done.3
  28.6 3.6 %collective-permute-done.2 = f32[2,16,4,128]{3,2,1,0:T(4,128)S(1)} collective-permute-done((f32[2,16,4,128]{3,2,1,0:T(4,128)S(1)}, f32[2,16,4,128]{3,2,1,0:T(4,128)S(1)}, u32[]{:S(2)}, u32[]{:S(2)}) %collective-permute-start.2) | collective-permute-done | bytes 65568 | tf_op jit(solution)/shard_map/ppermute | solution.py:20
  32.2 0.4 select_maximum_fusion.5
  32.6 0.4 fusion.44
  33.1 0.1 pad_maximum_fusion
  33.1 0.7 %fusion.18 = (f32[2,16,16,128]{3,2,1,0:T(8,128)S(1)}, f32[2,16,16,128]{3,2,1,0:T(8,128)S(1)}) fusion(f32[2,16,24,136]{3,2,1,0:T(8,128)S(1)} %select_maximum_fusion.5, f32[2,16,20,128]{3,2,1,0:T(8,128)S(1)} %get-tuple-element.27, f32[2,16,20,128]{3,2,1,0:T(8,128)S(1)} %get-tuple-element.26), kind=kLoop, calls=%fused_computation.43 | loop fusion | flops 1441792 | bytes 4718592 | tf_op jit(solution)/shard_map/add | solution.py:49
  33.8 0.0 copy-start.4
  33.8 0.0 copy-start.5
  33.9 0.0 copy-start.9
  33.9 0.6 fusion.106
  34.4 0.2 copy-done.4
  34.7 0.0 copy-done.5
  34.7 0.0 copy-done.9
  34.8 0.1 add_add_fusion.2
  34.8 0.0 copy-start.1
  34.8 0.8 %copy-done.6 = f32[8,16,128]{2,1,0:T(8,128)S(1)} copy-done((f32[8,16,128]{2,1,0:T(8,128)S(1)}, f32[8,16,128]{2,1,0:T(8,128)}, u32[]{:S(2)}) %copy-start.6) | copy-done | bytes 65560
  35.6 0.0 copy-done.10
  35.6 0.1 add_add_fusion.3
  35.7 0.0 copy-start.3
  35.7 2.8 %collective-permute-start.7 = (f32[2,4,16,128]{3,2,1,0:T(8,128)S(1)}, f32[2,4,16,128]{3,2,1,0:T(8,128)S(1)}, u32[]{:S(2)}, u32[]{:S(2)}) collective-permute-start(f32[2,4,16,128]{3,2,1,0:T(8,128)S(1)} %get-tuple-element.34), channel_id=1, source_target_pairs={{0,4},{4,8},{8,12},{1,5},{5,9},{9,13},{2,6},{6,10},{10,14},{3,7},{... | collective-permute-start | bytes 196616 | tf_op jit(solution)/shard_map/ppermute | solution.py:18
  38.5 1.3 %collective-permute-start.6 = (f32[2,4,16,128]{3,2,1,0:T(8,128)S(1)}, f32[2,4,16,128]{3,2,1,0:T(8,128)S(1)}, u32[]{:S(2)}, u32[]{:S(2)}) collective-permute-start(f32[2,4,16,128]{3,2,1,0:T(8,128)S(1)} %get-tuple-element.35), channel_id=1, source_target_pairs={{4,0},{8,4},{12,8},{5,1},{9,5},{13,9},{6,2},{10,6},{14,10},{7,3},{... | collective-permute-start | bytes 196616 | tf_op jit(solution)/shard_map/ppermute | solution.py:20
  39.8 0.0 collective-permute-done.7
  39.8 4.0 %collective-permute-done.6 = f32[2,4,16,128]{3,2,1,0:T(8,128)S(1)} collective-permute-done((f32[2,4,16,128]{3,2,1,0:T(8,128)S(1)}, f32[2,4,16,128]{3,2,1,0:T(8,128)S(1)}, u32[]{:S(2)}, u32[]{:S(2)}) %collective-permute-start.6) | collective-permute-done | bytes 65568 | tf_op jit(solution)/shard_map/ppermute | solution.py:20
  43.8 3.0 %collective-permute-start.9 = (f32[2,16,4,128]{3,2,1,0:T(4,128)S(1)}, f32[2,16,4,128]{3,2,1,0:T(4,128)S(1)}, u32[]{:S(2)}, u32[]{:S(2)}) collective-permute-start(f32[2,16,4,128]{3,2,1,0:T(4,128)S(1)} %get-tuple-element.24), channel_id=1, source_target_pairs={{0,1},{1,2},{2,3},{4,5},{5,6},{6,7},{8,9},{9,10},{10,11},{12,13},{... | collective-permute-start | bytes 196616 | tf_op jit(solution)/shard_map/ppermute | solution.py:18
  46.8 1.9 %collective-permute-start.8 = (f32[2,16,4,128]{3,2,1,0:T(4,128)S(1)}, f32[2,16,4,128]{3,2,1,0:T(4,128)S(1)}, u32[]{:S(2)}, u32[]{:S(2)}) collective-permute-start(f32[2,16,4,128]{3,2,1,0:T(4,128)S(1)} %get-tuple-element.25), channel_id=1, source_target_pairs={{1,0},{2,1},{3,2},{5,4},{6,5},{7,6},{9,8},{10,9},{11,10},{13,12},{... | collective-permute-start | bytes 196616 | tf_op jit(solution)/shard_map/ppermute | solution.py:20
  48.8 0.0 collective-permute-done.9
  48.8 3.6 %collective-permute-done.8 = f32[2,16,4,128]{3,2,1,0:T(4,128)S(1)} collective-permute-done((f32[2,16,4,128]{3,2,1,0:T(4,128)S(1)}, f32[2,16,4,128]{3,2,1,0:T(4,128)S(1)}, u32[]{:S(2)}, u32[]{:S(2)}) %collective-permute-start.8) | collective-permute-done | bytes 65568 | tf_op jit(solution)/shard_map/ppermute | solution.py:20
  52.4 0.4 select_maximum_fusion
  52.8 0.4 fusion.37
  53.2 0.5 fusion.4
  53.8 0.1 pad_maximum_fusion.1
  53.9 0.2 fusion.11
  54.1 0.0 copy-start.11
  54.1 0.6 fusion.55
  54.7 0.3 copy-done.11
  54.9 0.7 %fusion.161 = (f32[8,16,128]{2,1,0:T(8,128)}, f32[8,16,128]{2,1,0:T(8,128)}, f32[8,16,128]{2,1,0:T(8,128)S(1)}) fusion(f32[8,16,128]{2,1,0:T(8,128)S(1)} %add_add_fusion.3, bf16[2,8,16,128]{3,2,1,0:T(8,128)(2,1)S(1)} %copy-done.11, f32[8,16,128]{2,1,0:T(8,128)S(1)} %bitcast.68, f32[8,16,128]{2,1,0:T(8,128)S(1)} %copy-done.4, ...), kind=kLoop, calls=%fused_computation.281 | loop fusion | flops 327680 | bytes 983040 | tf_op jit(solution)/shard_map/add | solution.py:162
  55.6 0.7 %add_add_fusion = f32[8,16,128]{2,1,0:T(8,128)} fusion(f32[8,16,128]{2,1,0:T(8,128)S(1)} %bitcast.69, f32[8,16,128]{2,1,0:T(8,128)S(1)} %copy-done.4, f32[8,16,128]{2,1,0:T(8,128)S(1)} %get-tuple-element.7, f32[8,16,128]{2,1,0:T(8,128)S(1)} %copy-done, f32[8,16,128]{2,1,0:T(8,128)S(1)} %get-tuple-element.12, f32[2,8,16,128]{3,2,1,0:T(8,128)S(1)} %get-tuple-element.8, ...), kind=kLoop, calls=%fused_computation.283 | loop fusion | flops 147456 | bytes 524288 | tf_op jit(solution)/shard_map/add | solution.py:93
  (21 shorter events, 0.3 us)
Async XLA Ops:
  3.9 0.7 %copy-start.12 = (s32[128,1]{0,1:T(1,128)S(1)}, s32[128,1]{0,1:T(1,128)}, u32[]{:S(2)}) copy-start(s32[128,1]{0,1:T(1,128)} %param.26) | copy-start | bytes 1540
  4.6 0.7 %copy-start.13 = (s32[128]{0:T(128)S(1)}, s32[128]{0:T(128)}, u32[]{:S(2)}) copy-start(s32[128]{0:T(128)} %param.27) | copy-start | bytes 1540
  7.3 6.7 %collective-permute-start.4 = (f32[4,128]{1,0:T(4,128)S(1)}, f32[4,128]{1,0:T(4,128)S(1)}, u32[]{:S(2)}, u32[]{:S(2)}) collective-permute-start(f32[4,128]{1,0:T(4,128)S(1)} %pad_maximum_fusion.16), channel_id=1, source_target_pairs={{0,4},{4,0},{8,12},{12,8},{1,5},{5,1},{9,13},{13,9},{2,6},{6,2},{1... | collective-permute-start | bytes 6152 | tf_op jit(solution)/shard_map/ppermute | solution.py:118
  9.5 4.2 %copy-start.7 = (f32[8,16,128]{2,1,0:T(8,128)S(1)}, f32[8,16,128]{2,1,0:T(8,128)}, u32[]{:S(2)}) copy-start(f32[8,16,128]{2,1,0:T(8,128)} %param.21) | copy-start | bytes 196612
  10.3 10.2 %collective-permute-start.1 = (f32[2,4,16,128]{3,2,1,0:T(8,128)S(1)}, f32[2,4,16,128]{3,2,1,0:T(8,128)S(1)}, u32[]{:S(2)}, u32[]{:S(2)}) collective-permute-start(f32[2,4,16,128]{3,2,1,0:T(8,128)S(1)} %get-tuple-element.45), channel_id=1, source_target_pairs={{0,4},{4,8},{8,12},{1,5},{5,9},{9,13},{2,6},{6,10},{10,14},{3,7},{... | collective-permute-start | bytes 196616 | tf_op jit(solution)/shard_map/ppermute | solution.py:18
  12.2 6.2 %copy-start.8 = (f32[8,16,128]{2,1,0:T(8,128)S(1)}, f32[8,16,128]{2,1,0:T(8,128)}, u32[]{:S(2)}) copy-start(f32[8,16,128]{2,1,0:T(8,128)} %param.22) | copy-start | bytes 196612
  12.3 8.2 %collective-permute-start = (f32[2,4,16,128]{3,2,1,0:T(8,128)S(1)}, f32[2,4,16,128]{3,2,1,0:T(8,128)S(1)}, u32[]{:S(2)}, u32[]{:S(2)}) collective-permute-start(f32[2,4,16,128]{3,2,1,0:T(8,128)S(1)} %get-tuple-element.46), channel_id=1, source_target_pairs={{4,0},{8,4},{12,8},{5,1},{9,5},{13,9},{6,2},{10,6},{14,10},{7,3},{... | collective-permute-start | bytes 196616 | tf_op jit(solution)/shard_map/ppermute | solution.py:20
  14.0 5.9 %collective-permute-start.5 = (f32[4,256]{1,0:T(4,128)S(1)}, f32[4,256]{1,0:T(4,128)S(1)}, u32[]{:S(2)}, u32[]{:S(2)}) collective-permute-start(f32[4,256]{1,0:T(4,128)S(1)} %pad_maximum_fusion.15), channel_id=1, source_target_pairs={{0,8},{4,12},{8,0},{12,4},{1,9},{5,13},{9,1},{13,5},{2,10},{6,14},... | collective-permute-start | bytes 12296 | tf_op jit(solution)/shard_map/ppermute | solution.py:118
  20.4 0.8 %copy-start = (f32[8,16,128]{2,1,0:T(8,128)S(1)}, f32[8,16,128]{2,1,0:T(8,128)}, u32[]{:S(2)}) copy-start(f32[8,16,128]{2,1,0:T(8,128)} %param.15) | copy-start | bytes 196612
  20.5 0.9 %copy-start.2 = (f32[8,16,128]{2,1,0:T(8,128)S(1)}, f32[8,16,128]{2,1,0:T(8,128)}, u32[]{:S(2)}) copy-start(f32[8,16,128]{2,1,0:T(8,128)} %param.14) | copy-start | bytes 196612
  21.3 7.3 %collective-permute-start.3 = (f32[2,16,4,128]{3,2,1,0:T(4,128)S(1)}, f32[2,16,4,128]{3,2,1,0:T(4,128)S(1)}, u32[]{:S(2)}, u32[]{:S(2)}) collective-permute-start(f32[2,16,4,128]{3,2,1,0:T(4,128)S(1)} %get-tuple-element.28), channel_id=1, source_target_pairs={{0,1},{1,2},{2,3},{4,5},{5,6},{6,7},{8,9},{9,10},{10,11},{12,13},{... | collective-permute-start | bytes 196616 | tf_op jit(solution)/shard_map/ppermute | solution.py:18
  26.6 5.6 %collective-permute-start.2 = (f32[2,16,4,128]{3,2,1,0:T(4,128)S(1)}, f32[2,16,4,128]{3,2,1,0:T(4,128)S(1)}, u32[]{:S(2)}, u32[]{:S(2)}) collective-permute-start(f32[2,16,4,128]{3,2,1,0:T(4,128)S(1)} %get-tuple-element.29), channel_id=1, source_target_pairs={{1,0},{2,1},{3,2},{5,4},{6,5},{7,6},{9,8},{10,9},{11,10},{13,12},{... | collective-permute-start | bytes 196616 | tf_op jit(solution)/shard_map/ppermute | solution.py:20
  33.8 0.8 %copy-start.4 = (f32[8,16,128]{2,1,0:T(8,128)S(1)}, f32[8,16,128]{2,1,0:T(8,128)}, u32[]{:S(2)}) copy-start(f32[8,16,128]{2,1,0:T(8,128)} %param.18) | copy-start | bytes 196612
  33.8 0.9 %copy-start.5 = (f32[8,16,128]{2,1,0:T(8,128)S(1)}, f32[8,16,128]{2,1,0:T(8,128)}, u32[]{:S(2)}) copy-start(f32[8,16,128]{2,1,0:T(8,128)} %param.20) | copy-start | bytes 196612
  33.9 0.9 %copy-start.9 = (f32[8,16,128]{2,1,0:T(8,128)S(1)}, f32[8,16,128]{2,1,0:T(8,128)}, u32[]{:S(2)}) copy-start(f32[8,16,128]{2,1,0:T(8,128)} %param.17) | copy-start | bytes 196612
  34.7 0.8 %copy-start.6 = (f32[8,16,128]{2,1,0:T(8,128)S(1)}, f32[8,16,128]{2,1,0:T(8,128)}, u32[]{:S(2)}) copy-start(f32[8,16,128]{2,1,0:T(8,128)} %param.19) | copy-start | bytes 196612
  34.7 0.9 %copy-start.10 = (f32[8,16,128]{2,1,0:T(8,128)S(1)}, f32[8,16,128]{2,1,0:T(8,128)}, u32[]{:S(2)}) copy-start(f32[8,16,128]{2,1,0:T(8,128)} %param.16) | copy-start | bytes 196612
  34.8 20.8 %copy-start.1 = (f32[8,16,128]{2,1,0:T(8,128)}, f32[8,16,128]{2,1,0:T(8,128)S(1)}, u32[]{:S(2)}) copy-start(f32[8,16,128]{2,1,0:T(8,128)S(1)} %get-tuple-element.12) | copy-start | bytes 196612
  35.7 19.0 %copy-start.3 = (f32[8,16,128]{2,1,0:T(8,128)}, f32[8,16,128]{2,1,0:T(8,128)S(1)}, u32[]{:S(2)}) copy-start(f32[8,16,128]{2,1,0:T(8,128)S(1)} %add_add_fusion.3) | copy-start | bytes 196612
  35.7 4.1 %collective-permute-start.7 = (f32[2,4,16,128]{3,2,1,0:T(8,128)S(1)}, f32[2,4,16,128]{3,2,1,0:T(8,128)S(1)}, u32[]{:S(2)}, u32[]{:S(2)}) collective-permute-start(f32[2,4,16,128]{3,2,1,0:T(8,128)S(1)} %get-tuple-element.34), channel_id=1, source_target_pairs={{0,4},{4,8},{8,12},{1,5},{5,9},{9,13},{2,6},{6,10},{10,14},{3,7},{... | collective-permute-start | bytes 196616 | tf_op jit(solution)/shard_map/ppermute | solution.py:18
  38.5 5.3 %collective-permute-start.6 = (f32[2,4,16,128]{3,2,1,0:T(8,128)S(1)}, f32[2,4,16,128]{3,2,1,0:T(8,128)S(1)}, u32[]{:S(2)}, u32[]{:S(2)}) collective-permute-start(f32[2,4,16,128]{3,2,1,0:T(8,128)S(1)} %get-tuple-element.35), channel_id=1, source_target_pairs={{4,0},{8,4},{12,8},{5,1},{9,5},{13,9},{6,2},{10,6},{14,10},{7,3},{... | collective-permute-start | bytes 196616 | tf_op jit(solution)/shard_map/ppermute | solution.py:20
  43.8 5.0 %collective-permute-start.9 = (f32[2,16,4,128]{3,2,1,0:T(4,128)S(1)}, f32[2,16,4,128]{3,2,1,0:T(4,128)S(1)}, u32[]{:S(2)}, u32[]{:S(2)}) collective-permute-start(f32[2,16,4,128]{3,2,1,0:T(4,128)S(1)} %get-tuple-element.24), channel_id=1, source_target_pairs={{0,1},{1,2},{2,3},{4,5},{5,6},{6,7},{8,9},{9,10},{10,11},{12,13},{... | collective-permute-start | bytes 196616 | tf_op jit(solution)/shard_map/ppermute | solution.py:18
  46.8 5.6 %collective-permute-start.8 = (f32[2,16,4,128]{3,2,1,0:T(4,128)S(1)}, f32[2,16,4,128]{3,2,1,0:T(4,128)S(1)}, u32[]{:S(2)}, u32[]{:S(2)}) collective-permute-start(f32[2,16,4,128]{3,2,1,0:T(4,128)S(1)} %get-tuple-element.25), channel_id=1, source_target_pairs={{1,0},{2,1},{3,2},{5,4},{6,5},{7,6},{9,8},{10,9},{11,10},{13,12},{... | collective-permute-start | bytes 196616 | tf_op jit(solution)/shard_map/ppermute | solution.py:20
  54.1 0.8 %copy-start.11 = (bf16[2,8,16,128]{3,2,1,0:T(8,128)(2,1)S(1)}, bf16[2,8,16,128]{3,2,1,0:T(8,128)(2,1)}, u32[]{:S(2)}) copy-start(bf16[2,8,16,128]{3,2,1,0:T(8,128)(2,1)} %param.23) | copy-start | bytes 196612

commit v3 on v2

--- a/solution.py
+++ b/solution.py
@@ -99,12 +99,14 @@
     return jnp.pad(fields, ((0, 0), (0, 0), (0, 0), (4, 4)))
 
 
-def widened(fields):
-    return pad_depth(padded_2(fields, (("gx", 1), ("gy", 2)), 4))
-
-
-def receiver_sources(traces, time_steps, rec_owner, rec_local, shape):
-    sx, sy, sz = shape
+def from_neighbours(low_part, high_part, axis):
+    count = lax.axis_size(axis)
+    below = lax.ppermute(low_part, axis, [(i, i + 1) for i in range(count - 1)])
+    above = lax.ppermute(high_part, axis, [(i + 1, i) for i in range(count - 1)])
+    return below, above
+
+
+def gather_column(traces, time_steps, rec_owner, rec_local):
     groups = lax.axis_size("gx")
     held = rec_local.shape[0]
     samples = [lax.dynamic_index_in_dim(traces, time_steps[k], 0, keepdims=False) for k in range(2)]
@@ -118,23 +120,28 @@
             partner = lax.ppermute(arrived, "gx", [(i, i ^ step) for i in range(groups)])
             arrived = jnp.concatenate([arrived, partner], axis=1)
             step *= 2
-    else:
-        sent = jnp.broadcast_to(payload[None], (groups, 4, held))
-        arrived = lax.all_to_all(sent, "gx", split_axis=0, concat_axis=0, tiled=True)
-        arrived = jnp.transpose(arrived, (1, 0, 2)).reshape(4, groups * held)
-    mine = arrived[3].astype(jnp.int32) == lax.axis_index("gx")
+        return arrived
+    sent = jnp.broadcast_to(payload[None], (groups, 4, held))
+    arrived = lax.all_to_all(sent, "gx", split_axis=0, concat_axis=0, tiled=True)
+    return jnp.transpose(arrived, (1, 0, 2)).reshape(4, groups * held)
+
+
+def sources_over(arrived, values, shape, first, rows):
+    sx, sy, sz = shape
     cell = arrived[2].astype(jnp.int32)
-    plane = cell // sz
+    owner = arrived[3].astype(jnp.int32)
+    row = (owner - lax.axis_index("gx")) * sx + cell // (sy * sz) - first
+    inside = (row >= 0) & (row < rows)
+    plane = jnp.where(inside, row * sy + cell // sz % sy, -1)
     depth = cell % sz
-    values = jnp.where(mine[None, :], arrived[0:2], 0.0)
-    picks = (plane[None, :] == jnp.arange(sx * sy, dtype=jnp.int32)[:, None]).astype(jnp.float32)
+    picks = (plane[None, :] == jnp.arange(rows * sy, dtype=jnp.int32)[:, None]).astype(jnp.float32)
     spread = values[:, None, :] * picks[None, :, :]
     columns = (depth[:, None] == jnp.arange(sz, dtype=jnp.int32)[None, :]).astype(jnp.float32)
     sources = jnp.einsum(
         "cpr,rz->cpz", spread, columns, precision=lax.Precision.HIGHEST,
         preferred_element_type=jnp.float32,
     )
-    return sources.reshape(2, sx, sy, sz)
+    return sources.reshape(values.shape[0], rows, sy, sz)
 
 
 def local(
@@ -153,11 +160,41 @@
     rec_owner,
     rec_local,
 ):
-    sources = receiver_sources(traces, time_steps, rec_owner, rec_local, p_now.shape)
+    sx, sy, sz = p_now.shape
+    assert sx >= 8
     current = jnp.stack([p_now, q_now])
     earlier = jnp.stack([p_prev, q_prev])
-    middle = advance(widened(current), earlier, speed, epsilon, delta, theta, phi, sources[0])
-    final = advance(widened(middle), current, speed, epsilon, delta, theta, phi, sources[1])
+    params = jnp.stack([speed, epsilon, delta, theta, phi])
+    def slabs(parts):
+        return jnp.concatenate([part.reshape(-1, sy, sz) for part in parts], axis=0)
+
+    low_part = slabs([current[:, sx - 8 :], earlier[:, sx - 4 :], params[:, sx - 4 :]])
+    high_part = slabs([current[:, :8], earlier[:, :4], params[:, :4]])
+    below, above = from_neighbours(low_part, high_part, "gx")
+
+    def unpack(got):
+        return (
+            got[0:16].reshape(2, 8, sy, sz),
+            got[16:24].reshape(2, 4, sy, sz),
+            got[24:44].reshape(5, 4, sy, sz),
+        )
+
+    (now_lo, prev_lo, params_lo), (now_hi, prev_hi, params_hi) = unpack(below), unpack(above)
+    now_x = jnp.concatenate([now_lo, current, now_hi], axis=1)
+    prev_x = jnp.concatenate([prev_lo, earlier, prev_hi], axis=1)
+    params_x = jnp.concatenate([params_lo, params, params_hi], axis=1)
+    lo_y, hi_y = from_neighbours(now_x[:, :, sy - 4 :], now_x[:, :, :4], "gy")
+    now_xy = pad_depth(jnp.concatenate([lo_y, now_x, hi_y], axis=2))
+
+    arrived = gather_column(traces, time_steps, rec_owner, rec_local)
+    source_0 = sources_over(arrived, arrived[0:1], (sx, sy, sz), -4, sx + 8)[0]
+    source_1 = sources_over(arrived, arrived[1:2], (sx, sy, sz), 0, sx)[0]
+
+    mid_x = advance(now_xy, prev_x, *params_x, source_0)
+    middle = mid_x[:, 4 : 4 + sx]
+    lo_m, hi_m = from_neighbours(mid_x[:, :, sy - 4 :], mid_x[:, :, :4], "gy")
+    mid_xy = pad_depth(jnp.concatenate([lo_m, mid_x, hi_m], axis=2))
+    final = advance(mid_xy, current, speed, epsilon, delta, theta, phi, source_1)
     image = (
         snapshots[0].astype(jnp.float32) * middle[0] + snapshots[1].astype(jnp.float32) * final[0]
     )

time: 57 us -> 52.5 us (0.921)
  the two profiles are of different devices: /device:TPU:1 before, /device:TPU:30 now
where the time goes in v3:
time: 52.5 us; the launch traced here: 51.7 us
  starting transfers between devices  16.1 us (31%)
  waiting for transfers between devices  12.5 us (24%)
  other arithmetic  10.2 us (19%)
  local copies, waits for them, and re-layouts  6.98 us (13%)
  between operations  4.99 us (10%)
  matrix products  0.89 us (2%)
    ppermute x2, waiting for transfers between devices, gather_column(): lax.ppermute(arrived, 'gx', [(i, i ^ step) for i in range(groups)])  7.42 us
    ppermute x3, starting transfers between devices, from_neighbours(): lax.ppermute(high_part, axis, [(i + 1, i) for i in range(count - 1)])  7.34 us
    ppermute x3, starting transfers between devices, from_neighbours(): below = lax.ppermute(low_part, axis, [(i, i + 1) for i in range(count - 1)])  6.1 us
    ppermute x3, waiting for transfers between devices, from_neighbours(): below = lax.ppermute(low_part, axis, [(i, i + 1) for i in range(count - 1)])  5.11 us
    unnamed x24, local copies, waits for them, and re-layouts  3.75 us
    ppermute x2, starting transfers between devices, gather_column(): lax.ppermute(arrived, 'gx', [(i, i ^ step) for i in range(groups)])  2.65 us
    add x2, other arithmetic, advance(): axis_x * axis_x * dxx + axis_y * axis_y * dyy + axis_z * axis_z * dzz  1.61 us
    add x2, other arithmetic, derivatives(): dz_xwide + weight * (padded[:, :, 4:4 + sy, 4 + k:4 + k + sz] - padded[:,...  1.58 us
  transfers between devices with their start and end apart: 8, of which 3 were waited for; matrix products, arithmetic and copies ran while one was open for 13% of the time, Pallas kernels for 0%

profile of v3, /device:TPU:30, one launch (start us, length us, event | category | flops | bytes accessed | tf_op | source)
XLA Modules:
  0.0 51.7 jit_solution(2628478196916645479)
XLA Ops:
  0.6 0.0 copy-start.1
  0.6 0.0 copy-start
  0.7 0.0 copy-start.7
  0.7 0.0 copy-start.8
  0.7 1.3 %fusion.224 = (s32[1]{0:T(128)}, s32[1]{0:T(128)}) fusion(s32[2]{0:T(128)} %param.25), kind=kLoop, calls=%fused_computation.397 | loop fusion | bytes 16 | tf_op jit(solution)/shard_map/slice | solution.py:112
  4.6 0.7 %convert_bitcast_fusion = f32[1,128]{1,0:T(1,128)S(1)} fusion(s32[128,1]{0,1:T(1,128)} %param.26), kind=kLoop, calls=%fused_computation.385 | loop fusion | flops 128 | bytes 1024 | tf_op jit(solution)/shard_map/convert_element_type | solution.py:114
  5.2 0.7 %convert_bitcast_fusion.1 = f32[1,128]{1,0:T(1,128)S(1)} fusion(s32[128]{0:T(128)} %param.27), kind=kLoop, calls=%fused_computation.386 | loop fusion | flops 128 | bytes 1024 | tf_op jit(solution)/shard_map/stack | solution.py:113
  7.2 0.7 %constant_dynamic-slice_fusion.1 = (f32[1,128]{1,0:T(1,128)S(1)}, f32[1,128]{1,0:T(1,128)S(1)}) fusion(f32[1024,128]{1,0:T(8,128)} %param.24, s32[]{:T(128)S(6)} %select_n.55, s32[]{:T(128)S(6)} %select_n.56), kind=kLoop, calls=%fused_computation.388 | loop fusion | bytes 2056 | tf_op jit(solution)/shard_map/jit(dynamic_index_in_dim)/dynamic_slice | solution.py:112
  7.9 0.5 collective-permute-start.4
  8.4 0.8 %bitcast_dynamic-update-slice_fusion.4 = f32[5,8,16,128]{3,2,1,0:T(8,128)S(1)} fusion(f32[8,16,128]{2,1,0:T(8,128)} %param.18), kind=kLoop, calls=%fused_computation.349 | loop fusion | bytes 131072
  9.3 0.8 %bitcast_dynamic-update-slice_fusion.3 = f32[5,8,16,128]{3,2,1,0:T(8,128)S(1)} fusion(f32[5,8,16,128]{3,2,1,0:T(8,128)S(1)} %bitcast_dynamic-update-slice_fusion.4, f32[8,16,128]{2,1,0:T(8,128)} %param.19), kind=kLoop, calls=%fused_computation.348 | loop fusion | bytes 131072
  10.1 0.8 %bitcast_dynamic-update-slice_fusion.2 = f32[5,8,16,128]{3,2,1,0:T(8,128)S(1)} fusion(f32[5,8,16,128]{3,2,1,0:T(8,128)S(1)} %bitcast_dynamic-update-slice_fusion.3, f32[8,16,128]{2,1,0:T(8,128)} %param.20), kind=kLoop, calls=%fused_computation.347 | loop fusion | bytes 131072
  11.0 0.8 %bitcast_dynamic-update-slice_fusion.1 = f32[5,8,16,128]{3,2,1,0:T(8,128)S(1)} fusion(f32[5,8,16,128]{3,2,1,0:T(8,128)S(1)} %bitcast_dynamic-update-slice_fusion.2, f32[8,16,128]{2,1,0:T(8,128)} %param.21), kind=kLoop, calls=%fused_computation.346 | loop fusion | bytes 131072
  11.8 0.8 %bitcast_dynamic-update-slice_fusion = f32[5,8,16,128]{3,2,1,0:T(8,128)S(1)} fusion(f32[5,8,16,128]{3,2,1,0:T(8,128)S(1)} %bitcast_dynamic-update-slice_fusion.1, f32[8,16,128]{2,1,0:T(8,128)} %param.22), kind=kLoop, calls=%fused_computation.345 | loop fusion | bytes 131072 | tf_op jit(solution)/shard_map/stack | solution.py:167
  12.7 0.0 copy-start.5
  12.7 0.0 copy-done.1
  12.7 0.0 copy-done
  12.7 0.0 copy-done.7
  12.8 0.0 copy-done.8
  12.8 0.1 fusion.26
  12.8 3.5 %collective-permute-start.1 = (f32[44,16,128]{2,1,0:T(8,128)S(1)}, f32[44,16,128]{2,1,0:T(8,128)S(1)}, u32[]{:S(2)}, u32[]{:S(2)}) collective-permute-start(f32[44,16,128]{2,1,0:T(8,128)S(1)} %get-tuple-element.50), channel_id=1, source_target_pairs={{4,0},{8,4},{12,8},{5,1},{9,5},{13,9},{6,2},{10,6},{14,10},{7,3},{... | collective-permute-start | bytes 1081352 | tf_op jit(solution)/shard_map/ppermute | solution.py:105
  16.3 1.3 %collective-permute-start = (f32[44,16,128]{2,1,0:T(8,128)S(1)}, f32[44,16,128]{2,1,0:T(8,128)S(1)}, u32[]{:S(2)}, u32[]{:S(2)}) collective-permute-start(f32[44,16,128]{2,1,0:T(8,128)S(1)} %get-tuple-element.49), channel_id=1, source_target_pairs={{0,4},{4,8},{8,12},{1,5},{5,9},{9,13},{2,6},{6,10},{10,14},{3,7},{... | collective-permute-start | bytes 1081352 | tf_op jit(solution)/shard_map/ppermute | solution.py:104
  17.7 0.2 fusion.222
  17.9 0.3 fusion.209
  18.2 0.0 collective-permute-done.4
  18.2 2.1 %collective-permute-start.5 = (f32[4,256]{1,0:T(4,128)S(1)}, f32[4,256]{1,0:T(4,128)S(1)}, u32[]{:S(2)}, u32[]{:S(2)}) collective-permute-start(f32[4,256]{1,0:T(4,128)S(1)} %pad_maximum_fusion.11), channel_id=1, source_target_pairs={{0,8},{4,12},{8,0},{12,4},{1,9},{5,13},{9,1},{13,5},{2,10},{6,14},... | collective-permute-start | bytes 12296 | tf_op jit(solution)/shard_map/ppermute | solution.py:120
  20.4 7.4 %collective-permute-done.5 = f32[4,256]{1,0:T(4,128)S(1)} collective-permute-done((f32[4,256]{1,0:T(4,128)S(1)}, f32[4,256]{1,0:T(4,128)S(1)}, u32[]{:S(2)}, u32[]{:S(2)}) %collective-permute-start.5) | collective-permute-done | bytes 4128 | tf_op jit(solution)/shard_map/ppermute | solution.py:120
  27.9 0.5 fusion.2
  28.4 0.0 collective-permute-done.1
  28.4 0.0 collective-permute-done
  28.6 1.9 %collective-permute-start.2 = (f32[2,24,4,128]{3,2,1,0:T(4,128)S(1)}, f32[2,24,4,128]{3,2,1,0:T(4,128)S(1)}, u32[]{:S(2)}, u32[]{:S(2)}) collective-permute-start(f32[2,24,4,128]{3,2,1,0:T(4,128)S(1)} %get-tuple-element.35), channel_id=1, source_target_pairs={{1,0},{2,1},{3,2},{5,4},{6,5},{7,6},{9,8},{10,9},{11,10},{13,12},{... | collective-permute-start | bytes 294920 | tf_op jit(solution)/shard_map/ppermute | solution.py:105
  30.5 2.4 %collective-permute-start.3 = (f32[2,24,4,128]{3,2,1,0:T(4,128)S(1)}, f32[2,24,4,128]{3,2,1,0:T(4,128)S(1)}, u32[]{:S(2)}, u32[]{:S(2)}) collective-permute-start(f32[2,24,4,128]{3,2,1,0:T(4,128)S(1)} %get-tuple-element.34), channel_id=1, source_target_pairs={{0,1},{1,2},{2,3},{4,5},{5,6},{6,7},{8,9},{9,10},{10,11},{12,13},{... | collective-permute-start | bytes 294920 | tf_op jit(solution)/shard_map/ppermute | solution.py:104
  32.9 0.1 pad_maximum_fusion
  33.0 1.0 %multiply_bitcast_fusion.5 = (f32[16,16,128]{2,1,0:T(8,128)S(1)}, f32[16,16,128]{2,1,0:T(8,128)S(1)}, f32[16,16,128]{2,1,0:T(8,128)S(1)}, f32[16,16,128]{2,1,0:T...) fusion(f32[5,16,16,128]{3,2,1,0:T(8,128)S(1)} %pad_maximum_fusion), kind=kLoop, calls=%fused_computation.327 | loop fusion | flops 327680 | bytes 1048576 | tf_op jit(solution)/shard_map/mul | solution.py:77
  34.1 0.0 collective-permute-done.2
  34.1 2.3 %collective-permute-done.3 = f32[2,24,4,128]{3,2,1,0:T(4,128)S(1)} collective-permute-done((f32[2,24,4,128]{3,2,1,0:T(4,128)S(1)}, f32[2,24,4,128]{3,2,1,0:T(4,128)S(1)}, u32[]{:S(2)}, u32[]{:S(2)}) %collective-permute-start.3) | collective-permute-done | bytes 98336 | tf_op jit(solution)/shard_map/ppermute | solution.py:104
  36.4 0.6 %select_maximum_fusion = f32[2,24,24,136]{3,2,1,0:T(8,128)S(1)} fusion(f32[2,24,4,128]{3,2,1,0:T(4,128)S(1)} %collective-permute-done.2, f32[2,24,4,128]{3,2,1,0:T(4,128)S(1)} %collective-permute-done.3, f32[2,8,16,128]{3,2,1,0:T(8,128)S(1)} %bitcast.126, f32[2,8,16,128]{3,2,1,0:T(8,128)S(1)} %bitcast.130, f32[1,8,16,128]{3,2,1,0:T(8,128)S(1)} %bitcast.140, ...), kind=kLoop, calls=%fused_computation.4 | loop fusion | flops 2193408 | bytes 1216512 | tf_op jit(solution)/shard_map/concatenate | solution.py:187
  37.0 0.8 %fusion.6 = f32[2,16,24,128]{3,2,1,0:T(8,128)S(1)} fusion(f32[2,24,24,136]{3,2,1,0:T(8,128)S(1)} %select_maximum_fusion), kind=kLoop, calls=%fused_computation.44 | loop fusion | flops 1081344 | bytes 3538944 | tf_op jit(solution)/shard_map/add | solution.py:53
  37.8 0.1 pad_maximum_fusion.1
  37.9 1.0 %fusion.13 = (f32[2,24,16,128]{3,2,1,0:T(8,128)S(1)}, f32[2,24,16,128]{3,2,1,0:T(8,128)S(1)}) fusion(f32[2,24,24,136]{3,2,1,0:T(8,128)S(1)} %select_maximum_fusion, f32[2,24,20,128]{3,2,1,0:T(8,128)S(1)} %get-tuple-element.33, f32[2,24,20,128]{3,2,1,0:T(8,128)S(1)} %get-tuple-element.32), kind=kLoop, calls=%fused_computation.55 | loop fusion | flops 2162688 | bytes 7077888 | tf_op jit(solution)/shard_map/add | solution.py:49
  38.9 1.0 %fusion.45 = (f32[2,16,16,128]{3,2,1,0:T(8,128)S(1)}, f32[2,16,16,128]{3,2,1,0:T(8,128)S(1)}, f32[2,16,16,128]{3,2,1,0:T(8,128)S(1)}, f32[2,16,16,128]{3,2,1,0:T(8,128)S(1)}) fusion(f32[2,16,24,128]{3,2,1,0:T(8,128)S(1)} %fusion.6, f32[2,24,16,128]{3,2,1,0:T(8,128)S(1)} %get-tuple-element.61, f32[2,24,16,128]{3,2,1,0:T(8,128)S(1)} %get-tuple-element.62, ...), kind=kLoop, calls=%fused_computation.106 | loop fusion | flops 5570560 | bytes 14548992 | tf_op jit(solution)/shard_map/add | solution.py:77
  40.0 0.1 fusion.178
  40.1 0.1 fusion.190
  40.2 1.9 %collective-permute-start.6 = (f32[2,16,4,128]{3,2,1,0:T(4,128)S(1)}, f32[2,16,4,128]{3,2,1,0:T(4,128)S(1)}, u32[]{:S(2)}, u32[]{:S(2)}) collective-permute-start(f32[2,16,4,128]{3,2,1,0:T(4,128)S(1)} %get-tuple-element.41), channel_id=1, source_target_pairs={{1,0},{2,1},{3,2},{5,4},{6,5},{7,6},{9,8},{10,9},{11,10},{13,12},{... | collective-permute-start | bytes 196616 | tf_op jit(solution)/shard_map/ppermute | solution.py:105
  42.1 2.4 %collective-permute-start.7 = (f32[2,16,4,128]{3,2,1,0:T(4,128)S(1)}, f32[2,16,4,128]{3,2,1,0:T(4,128)S(1)}, u32[]{:S(2)}, u32[]{:S(2)}) collective-permute-start(f32[2,16,4,128]{3,2,1,0:T(4,128)S(1)} %get-tuple-element.40), channel_id=1, source_target_pairs={{0,1},{1,2},{2,3},{4,5},{5,6},{6,7},{8,9},{9,10},{10,11},{12,13},{... | collective-permute-start | bytes 196616 | tf_op jit(solution)/shard_map/ppermute | solution.py:104
  44.6 0.4 fusion.93
  44.9 0.0 collective-permute-done.6
  44.9 2.8 %collective-permute-done.7 = f32[2,16,4,128]{3,2,1,0:T(4,128)S(1)} collective-permute-done((f32[2,16,4,128]{3,2,1,0:T(4,128)S(1)}, f32[2,16,4,128]{3,2,1,0:T(4,128)S(1)}, u32[]{:S(2)}, u32[]{:S(2)}) %collective-permute-start.7) | collective-permute-done | bytes 65568 | tf_op jit(solution)/shard_map/ppermute | solution.py:104
  47.7 0.4 select_maximum_fusion.5
  48.1 0.4 fusion.104
  48.6 0.5 %fusion.29 = f32[2,16,16,128]{3,2,1,0:T(8,128)S(1)} fusion(f32[2,16,24,136]{3,2,1,0:T(8,128)S(1)} %select_maximum_fusion.5), kind=kLoop, calls=%fused_computation.82 | loop fusion | flops 720896 | bytes 2359296 | tf_op jit(solution)/shard_map/add | solution.py:49
  49.1 0.1 pad_maximum_fusion.5
  49.2 0.2 fusion.36
  49.4 0.0 copy-start.2
  49.4 0.0 copy-start.3
  49.4 0.0 copy-start.6
  49.4 0.0 copy-start.9
  49.4 0.6 %fusion.135 = (f32[2,8,16,128]{3,2,1,0:T(8,128)S(1)}, f32[2,8,16,128]{3,2,1,0:T(8,128)S(1)}, f32[2,8,16,128]{3,2,1,0:T(8,128)S(1)}, f32[2,8,16,128]{3,2,1,0:T(8,128)S(1)}) fusion(f32[2,8,24,128]{3,2,1,0:T(8,128)S(1)} %fusion.104, f32[2,16,16,128]{3,2,1,0:T(8,128)S(1)} %fusion.29, f32[2,16,16,128]{3,2,1,0:T(8,128)S(1)} %fusion.36, ...), kind=kLoop, calls=%fused_computation.225 | loop fusion | flops 3080192 | bytes 6422528 | tf_op jit(solution)/shard_map/add | solution.py:77
  50.0 0.2 copy-done.2
  50.2 0.0 copy-done.3
  50.3 0.0 copy-done.6
  50.3 0.0 copy-done.9
  50.3 0.7 %fusion.201 = (f32[8,16,128]{2,1,0:T(8,128)}, f32[8,16,128]{2,1,0:T(8,128)}, f32[8,16,128]{2,1,0:T(8,128)}, f32[8,16,128]{2,1,0:T(8,128)S(1)}) fusion(bf16[2,8,16,128]{3,2,1,0:T(8,128)(2,1)S(1)} %copy-done.9, f32[8,16,128]{2,1,0:T(8,128)S(1)} %fusion.93, f32[8,16,128]{2,1,0:T(8,128)S(1)} %copy-done.2, f32[2,8,16,128]{3,2,1,0:T(8,128)S(1)} %get-tuple-element.11, ...), kind=kLoop, calls=%fused_computation.343 | loop fusion | flops 327680 | bytes 1048576 | tf_op jit(solution)/shard_map/add | solution.py:199
  51.1 0.7 %add_add_fusion = (f32[8,16,128]{2,1,0:T(8,128)}, f32[8,16,128]{2,1,0:T(8,128)}) fusion(f32[8,16,128]{2,1,0:T(8,128)S(1)} %fusion.93, f32[8,16,128]{2,1,0:T(8,128)S(1)} %copy-done.2, f32[8,16,128]{2,1,0:T(8,128)S(1)} %get-tuple-element.8, f32[8,16,128]{2,1,0:T(8,128)S(1)} %copy-done.1, f32[2,8,16,128]{3,2,1,0:T(8,128)S(1)} %get-tuple-element.11, ...), kind=kLoop, calls=%fused_computation.350 | loop fusion | flops 147456 | bytes 589824 | tf_op jit(solution)/shard_map/add | solution.py:93
  (25 shorter events, 0.3 us)
Async XLA Ops:
  0.6 12.1 %copy-start.1 = (f32[8,16,128]{2,1,0:T(8,128)S(1)}, f32[8,16,128]{2,1,0:T(8,128)}, u32[]{:S(2)}) copy-start(f32[8,16,128]{2,1,0:T(8,128)} %param.15) | copy-start | bytes 196612
  0.6 12.1 %copy-start = (f32[8,16,128]{2,1,0:T(8,128)S(1)}, f32[8,16,128]{2,1,0:T(8,128)}, u32[]{:S(2)}) copy-start(f32[8,16,128]{2,1,0:T(8,128)} %param.14) | copy-start | bytes 196612
  0.7 12.1 %copy-start.7 = (f32[8,16,128]{2,1,0:T(8,128)S(1)}, f32[8,16,128]{2,1,0:T(8,128)}, u32[]{:S(2)}) copy-start(f32[8,16,128]{2,1,0:T(8,128)} %param.16) | copy-start | bytes 196612
  0.7 12.1 %copy-start.8 = (f32[8,16,128]{2,1,0:T(8,128)S(1)}, f32[8,16,128]{2,1,0:T(8,128)}, u32[]{:S(2)}) copy-start(f32[8,16,128]{2,1,0:T(8,128)} %param.17) | copy-start | bytes 196612
  7.9 10.3 %collective-permute-start.4 = (f32[4,128]{1,0:T(4,128)S(1)}, f32[4,128]{1,0:T(4,128)S(1)}, u32[]{:S(2)}, u32[]{:S(2)}) collective-permute-start(f32[4,128]{1,0:T(4,128)S(1)} %pad_maximum_fusion.12), channel_id=1, source_target_pairs={{0,4},{4,0},{8,12},{12,8},{1,5},{5,1},{9,13},{13,9},{2,6},{6,2},{1... | collective-permute-start | bytes 6152 | tf_op jit(solution)/shard_map/ppermute | solution.py:120
  12.7 5.0 %copy-start.4 = (f32[8,16,128]{2,1,0:T(8,128)S(1)}, f32[8,16,128]{2,1,0:T(8,128)}, u32[]{:S(2)}) copy-start(f32[8,16,128]{2,1,0:T(8,128)} %param.21) | copy-start | bytes 196612
  12.7 5.2 %copy-start.5 = (f32[8,16,128]{2,1,0:T(8,128)S(1)}, f32[8,16,128]{2,1,0:T(8,128)}, u32[]{:S(2)}) copy-start(f32[8,16,128]{2,1,0:T(8,128)} %param.22) | copy-start | bytes 196612
  12.8 15.6 %collective-permute-start.1 = (f32[44,16,128]{2,1,0:T(8,128)S(1)}, f32[44,16,128]{2,1,0:T(8,128)S(1)}, u32[]{:S(2)}, u32[]{:S(2)}) collective-permute-start(f32[44,16,128]{2,1,0:T(8,128)S(1)} %get-tuple-element.50), channel_id=1, source_target_pairs={{4,0},{8,4},{12,8},{5,1},{9,5},{13,9},{6,2},{10,6},{14,10},{7,3},{... | collective-permute-start | bytes 1081352 | tf_op jit(solution)/shard_map/ppermute | solution.py:105
  16.3 12.1 %collective-permute-start = (f32[44,16,128]{2,1,0:T(8,128)S(1)}, f32[44,16,128]{2,1,0:T(8,128)S(1)}, u32[]{:S(2)}, u32[]{:S(2)}) collective-permute-start(f32[44,16,128]{2,1,0:T(8,128)S(1)} %get-tuple-element.49), channel_id=1, source_target_pairs={{0,4},{4,8},{8,12},{1,5},{5,9},{9,13},{2,6},{6,10},{10,14},{3,7},{... | collective-permute-start | bytes 1081352 | tf_op jit(solution)/shard_map/ppermute | solution.py:104
  18.2 9.6 %collective-permute-start.5 = (f32[4,256]{1,0:T(4,128)S(1)}, f32[4,256]{1,0:T(4,128)S(1)}, u32[]{:S(2)}, u32[]{:S(2)}) collective-permute-start(f32[4,256]{1,0:T(4,128)S(1)} %pad_maximum_fusion.11), channel_id=1, source_target_pairs={{0,8},{4,12},{8,0},{12,4},{1,9},{5,13},{9,1},{13,5},{2,10},{6,14},... | collective-permute-start | bytes 12296 | tf_op jit(solution)/shard_map/ppermute | solution.py:120
  28.6 5.5 %collective-permute-start.2 = (f32[2,24,4,128]{3,2,1,0:T(4,128)S(1)}, f32[2,24,4,128]{3,2,1,0:T(4,128)S(1)}, u32[]{:S(2)}, u32[]{:S(2)}) collective-permute-start(f32[2,24,4,128]{3,2,1,0:T(4,128)S(1)} %get-tuple-element.35), channel_id=1, source_target_pairs={{1,0},{2,1},{3,2},{5,4},{6,5},{7,6},{9,8},{10,9},{11,10},{13,12},{... | collective-permute-start | bytes 294920 | tf_op jit(solution)/shard_map/ppermute | solution.py:105
  30.5 5.9 %collective-permute-start.3 = (f32[2,24,4,128]{3,2,1,0:T(4,128)S(1)}, f32[2,24,4,128]{3,2,1,0:T(4,128)S(1)}, u32[]{:S(2)}, u32[]{:S(2)}) collective-permute-start(f32[2,24,4,128]{3,2,1,0:T(4,128)S(1)} %get-tuple-element.34), channel_id=1, source_target_pairs={{0,1},{1,2},{2,3},{4,5},{5,6},{6,7},{8,9},{9,10},{10,11},{12,13},{... | collective-permute-start | bytes 294920 | tf_op jit(solution)/shard_map/ppermute | solution.py:104
  40.2 4.7 %collective-permute-start.6 = (f32[2,16,4,128]{3,2,1,0:T(4,128)S(1)}, f32[2,16,4,128]{3,2,1,0:T(4,128)S(1)}, u32[]{:S(2)}, u32[]{:S(2)}) collective-permute-start(f32[2,16,4,128]{3,2,1,0:T(4,128)S(1)} %get-tuple-element.41), channel_id=1, source_target_pairs={{1,0},{2,1},{3,2},{5,4},{6,5},{7,6},{9,8},{10,9},{11,10},{13,12},{... | collective-permute-start | bytes 196616 | tf_op jit(solution)/shard_map/ppermute | solution.py:105
  42.1 5.6 %collective-permute-start.7 = (f32[2,16,4,128]{3,2,1,0:T(4,128)S(1)}, f32[2,16,4,128]{3,2,1,0:T(4,128)S(1)}, u32[]{:S(2)}, u32[]{:S(2)}) collective-permute-start(f32[2,16,4,128]{3,2,1,0:T(4,128)S(1)} %get-tuple-element.40), channel_id=1, source_target_pairs={{0,1},{1,2},{2,3},{4,5},{5,6},{6,7},{8,9},{9,10},{10,11},{12,13},{... | collective-permute-start | bytes 196616 | tf_op jit(solution)/shard_map/ppermute | solution.py:104
  49.4 0.8 %copy-start.2 = (f32[8,16,128]{2,1,0:T(8,128)S(1)}, f32[8,16,128]{2,1,0:T(8,128)}, u32[]{:S(2)}) copy-start(f32[8,16,128]{2,1,0:T(8,128)} %param.18) | copy-start | bytes 196612
  49.4 0.9 %copy-start.3 = (f32[8,16,128]{2,1,0:T(8,128)S(1)}, f32[8,16,128]{2,1,0:T(8,128)}, u32[]{:S(2)}) copy-start(f32[8,16,128]{2,1,0:T(8,128)} %param.20) | copy-start | bytes 196612
  49.4 0.9 %copy-start.6 = (f32[8,16,128]{2,1,0:T(8,128)S(1)}, f32[8,16,128]{2,1,0:T(8,128)}, u32[]{:S(2)}) copy-start(f32[8,16,128]{2,1,0:T(8,128)} %param.19) | copy-start | bytes 196612
  49.4 0.9 %copy-start.9 = (bf16[2,8,16,128]{3,2,1,0:T(8,128)(2,1)S(1)}, bf16[2,8,16,128]{3,2,1,0:T(8,128)(2,1)}, u32[]{:S(2)}) copy-start(bf16[2,8,16,128]{3,2,1,0:T(8,128)(2,1)} %param.23) | copy-start | bytes 196612

commit v4 on v3

--- a/solution.py
+++ b/solution.py
@@ -109,9 +109,13 @@
 def gather_column(traces, time_steps, rec_owner, rec_local):
     groups = lax.axis_size("gx")
     held = rec_local.shape[0]
-    samples = [lax.dynamic_index_in_dim(traces, time_steps[k], 0, keepdims=False) for k in range(2)]
-    payload = jnp.stack(
-        samples + [rec_local.astype(jnp.float32), rec_owner[:, 0].astype(jnp.float32)]
+    steps = jnp.arange(traces.shape[0], dtype=jnp.int32)
+    chosen = (time_steps[:, None] == steps[None, :]).astype(jnp.float32)
+    samples = jnp.dot(
+        chosen, traces, precision=lax.Precision.HIGHEST, preferred_element_type=jnp.float32
+    )
+    payload = jnp.concatenate(
+        [samples, rec_local.astype(jnp.float32)[None], rec_owner[:, 0].astype(jnp.float32)[None]]
     )
     if groups & (groups - 1) == 0:
         arrived = payload
@@ -161,15 +165,18 @@
     rec_local,
 ):
     sx, sy, sz = p_now.shape
-    assert sx >= 8
+    assert sx == 8
     current = jnp.stack([p_now, q_now])
     earlier = jnp.stack([p_prev, q_prev])
-    params = jnp.stack([speed, epsilon, delta, theta, phi])
+    params = (speed, epsilon, delta, theta, phi)
+
     def slabs(parts):
         return jnp.concatenate([part.reshape(-1, sy, sz) for part in parts], axis=0)
 
-    low_part = slabs([current[:, sx - 8 :], earlier[:, sx - 4 :], params[:, sx - 4 :]])
-    high_part = slabs([current[:, :8], earlier[:, :4], params[:, :4]])
+    low_part = slabs(
+        [p_now, q_now, p_prev[sx - 4 :], q_prev[sx - 4 :]] + [f[sx - 4 :] for f in params]
+    )
+    high_part = slabs([p_now, q_now, p_prev[:4], q_prev[:4]] + [f[:4] for f in params])
     below, above = from_neighbours(low_part, high_part, "gx")
 
     def unpack(got):
@@ -182,7 +189,9 @@
     (now_lo, prev_lo, params_lo), (now_hi, prev_hi, params_hi) = unpack(below), unpack(above)
     now_x = jnp.concatenate([now_lo, current, now_hi], axis=1)
     prev_x = jnp.concatenate([prev_lo, earlier, prev_hi], axis=1)
-    params_x = jnp.concatenate([params_lo, params, params_hi], axis=1)
+    params_x = [
+        jnp.concatenate([params_lo[k], params[k], params_hi[k]], axis=0) for k in range(5)
+    ]
     lo_y, hi_y = from_neighbours(now_x[:, :, sy - 4 :], now_x[:, :, :4], "gy")
     now_xy = pad_depth(jnp.concatenate([lo_y, now_x, hi_y], axis=2))
 

time: 52.5 us -> 46.8 us (0.89)
  local copies, waits for them, and re-layouts: 6.98 us -> 2.43 us
  between operations: 4.99 us -> 1.18 us
  waiting for transfers between devices: 12.5 us -> 13.7 us
  other arithmetic: 10.2 us -> 11.2 us
  matrix products: 0.89 us -> 1.84 us
    unnamed x24 -> x32, local copies, waits for them, and re-layouts: 3.75 us -> 2.08 us
    slice x4 -> x2, local copies, waits for them, and re-layouts: 1.36 us -> 0.03 us  [the longest x1 0.01 us: local(): params_lo[k]]
    ppermute x3, waiting for transfers between devices: 5.11 us -> 6.23 us  [from_neighbours(): below = lax.ppermute(low_part, axis, [(i, i + 1) for i in range(count - 1)])]
    mul x0 -> x1, other arithmetic: none -> 1 us  [advance(): axis_y * axis_y * dyy]
    dot_general x0 -> x1, matrix products: none -> 0.95 us  [gather_column(): jnp.dot(chosen, traces, precision=lax.Precision.HIGHEST, preferred_elemen...]
    another operation x1 -> x0, local copies, waits for them, and re-layouts: 0.84 us -> none  [local(): params = jnp.stack([speed, epsilon, delta, theta, phi])]
    dynamic_slice x1 -> x0, local copies, waits for them, and re-layouts: 0.71 us -> none  [gather_column(): lax.dynamic_index_in_dim(traces, time_steps[k], 0, keepdims=False)]
    another operation x4 -> x0, other arithmetic: 0.69 us -> none  [the longest x2 0.67 us: gather_column(): jnp.stack(samples + [rec_local.astype(jnp.float32), rec_owner[:, 0].astyp...]
  transfers between devices with their start and end apart: 8 -> 8, of which waited for: 3 -> 3; matrix products, arithmetic and copies ran while one was open for 13% -> 7% of each run, Pallas kernels for 0% -> 0%
where the time goes in v4:
time: 46.8 us; the launch traced here: 46.4 us
  starting transfers between devices  16.1 us (34%)
  waiting for transfers between devices  13.7 us (29%)
  other arithmetic  11.2 us (24%)
  local copies, waits for them, and re-layouts  2.43 us (5%)
  matrix products  1.84 us (4%)
  between operations  1.18 us (3%)
    ppermute x2, waiting for transfers between devices, gather_column(): lax.ppermute(arrived, 'gx', [(i, i ^ step) for i in range(groups)])  7.45 us
    ppermute x3, starting transfers between devices, from_neighbours(): lax.ppermute(high_part, axis, [(i + 1, i) for i in range(count - 1)])  7.34 us
    ppermute x3, waiting for transfers between devices, from_neighbours(): below = lax.ppermute(low_part, axis, [(i, i + 1) for i in range(count - 1)])  6.23 us
    ppermute x3, starting transfers between devices, from_neighbours(): below = lax.ppermute(low_part, axis, [(i, i + 1) for i in range(count - 1)])  6.1 us
    ppermute x2, starting transfers between devices, gather_column(): lax.ppermute(arrived, 'gx', [(i, i ^ step) for i in range(groups)])  2.65 us
    unnamed x32, local copies, waits for them, and re-layouts  2.08 us
    add x2, other arithmetic, advance(): axis_x * axis_x * dxx + axis_y * axis_y * dyy + axis_z * axis_z * dzz  1.61 us
    add x2, other arithmetic, derivatives(): dz_xwide + weight * (padded[:, :, 4:4 + sy, 4 + k:4 + k + sz] - padded[:,...  1.58 us
  transfers between devices with their start and end apart: 8, of which 3 were waited for; matrix products, arithmetic and copies ran while one was open for 7% of the time, Pallas kernels for 0%

profile of v4, /device:TPU:30, one launch (start us, length us, event | category | flops | bytes accessed | tf_op | source)
XLA Modules:
  0.0 46.4 jit_solution(4660373710159969886)
XLA Ops:
  0.6 0.0 copy-start
  0.7 0.0 copy-start.8
  0.7 0.0 copy-start.9
  0.7 0.0 copy-start.3
  0.7 0.0 copy-start.7
  0.7 0.0 copy-start.4
  0.7 0.0 copy-start.5
  0.7 0.0 copy-start.6
  0.7 0.7 %convert_bitcast_fusion = f32[1,128]{1,0:T(1,128)S(1)} fusion(s32[128,1]{0,1:T(1,128)} %param.26), kind=kLoop, calls=%fused_computation.390 | loop fusion | flops 128 | bytes 1024 | tf_op jit(solution)/shard_map/convert_element_type | solution.py:118
  1.4 0.7 %convert_bitcast_fusion.1 = f32[1,128]{1,0:T(1,128)S(1)} fusion(s32[128]{0:T(128)} %param.27), kind=kLoop, calls=%fused_computation.391 | loop fusion | flops 128 | bytes 1024 | tf_op jit(solution)/shard_map/broadcast_in_dim | solution.py:118
  2.1 0.0 copy-done
  2.1 0.9 %fusion.200 = f32[2,128]{1,0:T(2,128)S(1)} fusion(f32[1024,128]{1,0:T(8,128)S(1)} %copy-done, s32[2]{0:T(128)} %param.25), kind=kOutput, calls=%fused_computation.359 | convolution fusion | flops 3147776 | bytes 525320 | tf_op jit(solution)/shard_map/dot_general | solution.py:114
  3.1 0.5 %collective-permute-start.4 = (f32[4,128]{1,0:T(4,128)S(1)}, f32[4,128]{1,0:T(4,128)S(1)}, u32[]{:S(2)}, u32[]{:S(2)}) collective-permute-start(f32[4,128]{1,0:T(4,128)S(1)} %pad_maximum_fusion.10), channel_id=1, source_target_pairs={{0,4},{4,0},{8,12},{12,8},{1,5},{5,1},{9,13},{13,9},{2,6},{6,2},{1... | collective-permute-start | bytes 6152 | tf_op jit(solution)/shard_map/ppermute | solution.py:124
  3.6 0.8 %constant_dynamic-update-slice_fusion.17 = f32[44,16,128]{2,1,0:T(8,128)S(1)} fusion(f32[8,16,128]{2,1,0:T(8,128)} %param.14), kind=kLoop, calls=%fused_computation.357 | loop fusion | bytes 131072
  4.4 0.8 %constant_dynamic-update-slice_fusion.16 = f32[44,16,128]{2,1,0:T(8,128)S(1)} fusion(f32[44,16,128]{2,1,0:T(8,128)S(1)} %constant_dynamic-update-slice_fusion.17, f32[8,16,128]{2,1,0:T(8,128)} %param.15), kind=kLoop, calls=%fused_computation.356 | loop fusion | bytes 131072
  5.3 0.0 copy-done.8
  5.3 0.0 copy-done.9
  5.4 0.0 copy-done.3
  5.4 0.0 copy-done.7
  5.4 0.0 copy-done.4
  5.4 0.0 copy-done.5
  5.5 0.0 copy-done.6
  5.5 3.5 %collective-permute-start.1 = (f32[44,16,128]{2,1,0:T(8,128)S(1)}, f32[44,16,128]{2,1,0:T(8,128)S(1)}, u32[]{:S(2)}, u32[]{:S(2)}) collective-permute-start(f32[44,16,128]{2,1,0:T(8,128)S(1)} %get-tuple-element.59), channel_id=1, source_target_pairs={{4,0},{8,4},{12,8},{5,1},{9,5},{13,9},{6,2},{10,6},{14,10},{7,3},{... | collective-permute-start | bytes 1081352 | tf_op jit(solution)/shard_map/ppermute | solution.py:105
  9.0 1.3 %collective-permute-start = (f32[44,16,128]{2,1,0:T(8,128)S(1)}, f32[44,16,128]{2,1,0:T(8,128)S(1)}, u32[]{:S(2)}, u32[]{:S(2)}) collective-permute-start(f32[44,16,128]{2,1,0:T(8,128)S(1)} %get-tuple-element.58), channel_id=1, source_target_pairs={{0,4},{4,8},{8,12},{1,5},{5,9},{9,13},{2,6},{6,10},{10,14},{3,7},{... | collective-permute-start | bytes 1081352 | tf_op jit(solution)/shard_map/ppermute | solution.py:104
  10.3 0.2 fusion.227
  10.6 0.3 fusion.211
  10.8 0.0 collective-permute-done.4
  10.9 2.1 %collective-permute-start.5 = (f32[4,256]{1,0:T(4,128)S(1)}, f32[4,256]{1,0:T(4,128)S(1)}, u32[]{:S(2)}, u32[]{:S(2)}) collective-permute-start(f32[4,256]{1,0:T(4,128)S(1)} %pad_maximum_fusion.9), channel_id=1, source_target_pairs={{0,8},{4,12},{8,0},{12,4},{1,9},{5,13},{9,1},{13,5},{2,10},{6,14},... | collective-permute-start | bytes 12296 | tf_op jit(solution)/shard_map/ppermute | solution.py:124
  13.0 7.4 %collective-permute-done.5 = f32[4,256]{1,0:T(4,128)S(1)} collective-permute-done((f32[4,256]{1,0:T(4,128)S(1)}, f32[4,256]{1,0:T(4,128)S(1)}, u32[]{:S(2)}, u32[]{:S(2)}) %collective-permute-start.5) | collective-permute-done | bytes 4128 | tf_op jit(solution)/shard_map/ppermute | solution.py:124
  20.5 0.5 %fusion.2 = f32[16,16,128]{2,1,0:T(8,128)S(1)} fusion(f32[512]{0:T(512)S(1)} %bitcast.96, s32[16,16]{1,0:T(8,128)S(1)} %multiply_add_fusion, s32[512]{0:T(512)S(1)} %bitcast.97, s32[512]{0:T(512)S(1)} %add_select_fusion), kind=kOutput, calls=%fused_computation.36 | convolution fusion | flops 201654272 | bytes 138240 | tf_op jit(solution)/shard_map/cpr,rz->cpz/dot_general | solution.py:144
  21.1 0.0 copy-start.1
  21.1 0.0 copy-start.2
  21.1 0.0 collective-permute-done.1
  21.1 0.0 collective-permute-done
  21.2 1.0 %fusion.213 = (f32[16,16,128]{2,1,0:T(8,128)S(1)}, f32[16,16,128]{2,1,0:T(8,128)S(1)}, f32[16,16,128]{2,1,0:T(8,128)S(1)}) fusion(f32[4,16,128]{2,1,0:T(8,128)S(1)} %get-tuple-element.35, f32[8,16,128]{2,1,0:T(8,128)S(1)} %copy-done.6, f32[4,16,128]{2,1,0:T(8,128)S(1)} %get-tuple-element.30, f32[4,16,128]{2,1,0:T(8,128)S(1)} %get-tuple-element.36, ...), kind=kLoop, calls=%fused_computation.396 | loop fusion | flops 360448 | bytes 655360 | tf_op jit(solution)/shard_map/mul | solution.py:77
  22.2 1.0 %fusion.214 = (f32[16,16,128]{2,1,0:T(8,128)S(1)}, f32[16,16,128]{2,1,0:T(8,128)S(1)}, f32[16,16,128]{2,1,0:T(8,128)S(1)}) fusion(f32[4,16,128]{2,1,0:T(8,128)S(1)} %get-tuple-element.35, f32[8,16,128]{2,1,0:T(8,128)S(1)} %copy-done.6, f32[4,16,128]{2,1,0:T(8,128)S(1)} %get-tuple-element.30, f32[4,16,128]{2,1,0:T(8,128)S(1)} %get-tuple-element.36, ...), kind=kLoop, calls=%fused_computation.397 | loop fusion | flops 327680 | bytes 655360 | tf_op jit(solution)/shard_map/mul | solution.py:78
  23.2 0.0 copy-done.1
  23.2 0.0 copy-done.2
  23.3 1.9 %collective-permute-start.2 = (f32[2,24,4,128]{3,2,1,0:T(4,128)S(1)}, f32[2,24,4,128]{3,2,1,0:T(4,128)S(1)}, u32[]{:S(2)}, u32[]{:S(2)}) collective-permute-start(f32[2,24,4,128]{3,2,1,0:T(4,128)S(1)} %get-tuple-element.27), channel_id=1, source_target_pairs={{1,0},{2,1},{3,2},{5,4},{6,5},{7,6},{9,8},{10,9},{11,10},{13,12},{... | collective-permute-start | bytes 294920 | tf_op jit(solution)/shard_map/ppermute | solution.py:105
  25.2 2.4 %collective-permute-start.3 = (f32[2,24,4,128]{3,2,1,0:T(4,128)S(1)}, f32[2,24,4,128]{3,2,1,0:T(4,128)S(1)}, u32[]{:S(2)}, u32[]{:S(2)}) collective-permute-start(f32[2,24,4,128]{3,2,1,0:T(4,128)S(1)} %get-tuple-element.26), channel_id=1, source_target_pairs={{0,1},{1,2},{2,3},{4,5},{5,6},{6,7},{8,9},{9,10},{10,11},{12,13},{... | collective-permute-start | bytes 294920 | tf_op jit(solution)/shard_map/ppermute | solution.py:104
  27.7 0.0 collective-permute-done.2
  27.7 3.5 %collective-permute-done.3 = f32[2,24,4,128]{3,2,1,0:T(4,128)S(1)} collective-permute-done((f32[2,24,4,128]{3,2,1,0:T(4,128)S(1)}, f32[2,24,4,128]{3,2,1,0:T(4,128)S(1)}, u32[]{:S(2)}, u32[]{:S(2)}) %collective-permute-start.3) | collective-permute-done | bytes 98336 | tf_op jit(solution)/shard_map/ppermute | solution.py:104
  31.2 0.6 %select_maximum_fusion = f32[2,24,24,136]{3,2,1,0:T(8,128)S(1)} fusion(f32[2,24,4,128]{3,2,1,0:T(4,128)S(1)} %collective-permute-done.2, f32[2,24,4,128]{3,2,1,0:T(4,128)S(1)} %collective-permute-done.3, f32[2,8,16,128]{3,2,1,0:T(8,128)S(1)} %bitcast.74, f32[2,8,16,128]{3,2,1,0:T(8,128)S(1)} %bitcast.78, f32[1,8,16,128]{3,2,1,0:T(8,128)S(1)} %bitcast.86, ...), kind=kLoop, calls=%fused_computation.4 | loop fusion | flops 2193408 | bytes 1216512 | tf_op jit(solution)/shard_map/concatenate | solution.py:196
  31.8 0.8 %fusion.6 = f32[2,16,24,128]{3,2,1,0:T(8,128)S(1)} fusion(f32[2,24,24,136]{3,2,1,0:T(8,128)S(1)} %select_maximum_fusion), kind=kLoop, calls=%fused_computation.41 | loop fusion | flops 1081344 | bytes 3538944 | tf_op jit(solution)/shard_map/add | solution.py:53
  32.5 0.1 pad_maximum_fusion
  32.6 1.0 %fusion.13 = (f32[2,24,16,128]{3,2,1,0:T(8,128)S(1)}, f32[2,24,16,128]{3,2,1,0:T(8,128)S(1)}) fusion(f32[2,24,24,136]{3,2,1,0:T(8,128)S(1)} %select_maximum_fusion, f32[2,24,20,128]{3,2,1,0:T(8,128)S(1)} %get-tuple-element.25, f32[2,24,20,128]{3,2,1,0:T(8,128)S(1)} %get-tuple-element.24), kind=kLoop, calls=%fused_computation.52 | loop fusion | flops 2162688 | bytes 7077888 | tf_op jit(solution)/shard_map/add | solution.py:49
  33.7 1.0 %fusion.43 = (f32[2,16,16,128]{3,2,1,0:T(8,128)S(1)}, f32[2,16,16,128]{3,2,1,0:T(8,128)S(1)}, f32[2,16,16,128]{3,2,1,0:T(8,128)S(1)}, f32[2,16,16,128]{3,2,1,0:T(8,128)S(1)}) fusion(f32[2,16,24,128]{3,2,1,0:T(8,128)S(1)} %fusion.6, f32[2,24,16,128]{3,2,1,0:T(8,128)S(1)} %get-tuple-element.73, f32[2,24,16,128]{3,2,1,0:T(8,128)S(1)} %get-tuple-element.74, ...), kind=kLoop, calls=%fused_computation.101 | loop fusion | flops 5570560 | bytes 14548992 | tf_op jit(solution)/shard_map/add | solution.py:77
  34.7 0.1 fusion.176
  34.8 0.1 fusion.181
  35.0 1.9 %collective-permute-start.6 = (f32[2,16,4,128]{3,2,1,0:T(4,128)S(1)}, f32[2,16,4,128]{3,2,1,0:T(4,128)S(1)}, u32[]{:S(2)}, u32[]{:S(2)}) collective-permute-start(f32[2,16,4,128]{3,2,1,0:T(4,128)S(1)} %get-tuple-element.41), channel_id=1, source_target_pairs={{1,0},{2,1},{3,2},{5,4},{6,5},{7,6},{9,8},{10,9},{11,10},{13,12},{... | collective-permute-start | bytes 196616 | tf_op jit(solution)/shard_map/ppermute | solution.py:105
  36.9 2.4 %collective-permute-start.7 = (f32[2,16,4,128]{3,2,1,0:T(4,128)S(1)}, f32[2,16,4,128]{3,2,1,0:T(4,128)S(1)}, u32[]{:S(2)}, u32[]{:S(2)}) collective-permute-start(f32[2,16,4,128]{3,2,1,0:T(4,128)S(1)} %get-tuple-element.40), channel_id=1, source_target_pairs={{0,1},{1,2},{2,3},{4,5},{5,6},{6,7},{8,9},{9,10},{10,11},{12,13},{... | collective-permute-start | bytes 196616 | tf_op jit(solution)/shard_map/ppermute | solution.py:104
  39.3 0.4 fusion.91
  39.7 0.0 collective-permute-done.6
  39.7 2.8 %collective-permute-done.7 = f32[2,16,4,128]{3,2,1,0:T(4,128)S(1)} collective-permute-done((f32[2,16,4,128]{3,2,1,0:T(4,128)S(1)}, f32[2,16,4,128]{3,2,1,0:T(4,128)S(1)}, u32[]{:S(2)}, u32[]{:S(2)}) %collective-permute-start.7) | collective-permute-done | bytes 65568 | tf_op jit(solution)/shard_map/ppermute | solution.py:104
  42.5 0.4 select_maximum_fusion.5
  42.9 0.4 fusion.102
  43.3 0.5 %fusion.27 = f32[2,16,16,128]{3,2,1,0:T(8,128)S(1)} fusion(f32[2,16,24,136]{3,2,1,0:T(8,128)S(1)} %select_maximum_fusion.5), kind=kLoop, calls=%fused_computation.77 | loop fusion | flops 720896 | bytes 2359296 | tf_op jit(solution)/shard_map/add | solution.py:49
  43.9 0.1 pad_maximum_fusion.2
  43.9 0.2 fusion.34
  44.2 0.0 copy-start.10
  44.2 0.6 %fusion.133 = (f32[2,8,16,128]{3,2,1,0:T(8,128)S(1)}, f32[2,8,16,128]{3,2,1,0:T(8,128)S(1)}, f32[2,8,16,128]{3,2,1,0:T(8,128)S(1)}, f32[2,8,16,128]{3,2,1,0:T(8,128)S(1)}) fusion(f32[2,8,24,128]{3,2,1,0:T(8,128)S(1)} %fusion.102, f32[2,16,16,128]{3,2,1,0:T(8,128)S(1)} %fusion.27, f32[2,16,16,128]{3,2,1,0:T(8,128)S(1)} %fusion.34, ...), kind=kLoop, calls=%fused_computation.220 | loop fusion | flops 3080192 | bytes 6422528 | tf_op jit(solution)/shard_map/add | solution.py:77
  44.7 0.3 copy-done.10
  45.0 0.7 %fusion.198 = (f32[8,16,128]{2,1,0:T(8,128)}, f32[8,16,128]{2,1,0:T(8,128)}, f32[8,16,128]{2,1,0:T(8,128)}, f32[8,16,128]{2,1,0:T(8,128)S(1)}) fusion(bf16[2,8,16,128]{3,2,1,0:T(8,128)(2,1)S(1)} %copy-done.10, f32[8,16,128]{2,1,0:T(8,128)S(1)} %fusion.91, f32[8,16,128]{2,1,0:T(8,128)S(1)} %copy-done.3, f32[2,8,16,128]{3,2,1,0:T(8,128)S(1)} %get-tuple-element.11, ...), kind=kLoop, calls=%fused_computation.330 | loop fusion | flops 327680 | bytes 1048576 | tf_op jit(solution)/shard_map/add | solution.py:208
  45.7 0.7 %add_add_fusion = (f32[8,16,128]{2,1,0:T(8,128)}, f32[8,16,128]{2,1,0:T(8,128)}) fusion(f32[8,16,128]{2,1,0:T(8,128)S(1)} %fusion.91, f32[8,16,128]{2,1,0:T(8,128)S(1)} %copy-done.3, f32[8,16,128]{2,1,0:T(8,128)S(1)} %get-tuple-element.8, f32[8,16,128]{2,1,0:T(8,128)S(1)} %copy-done.2, f32[2,8,16,128]{3,2,1,0:T(8,128)S(1)} %get-tuple-element.11, ...), kind=kLoop, calls=%fused_computation.332 | loop fusion | flops 147456 | bytes 589824 | tf_op jit(solution)/shard_map/add | solution.py:93
  (28 shorter events, 0.4 us)
Async XLA Ops:
  0.6 1.5 %copy-start = (f32[1024,128]{1,0:T(8,128)S(1)}, f32[1024,128]{1,0:T(8,128)}, u32[]{:S(2)}) copy-start(f32[1024,128]{1,0:T(8,128)} %param.24) | copy-start | bytes 1572868
  0.7 4.7 %copy-start.8 = (f32[8,16,128]{2,1,0:T(8,128)S(1)}, f32[8,16,128]{2,1,0:T(8,128)}, u32[]{:S(2)}) copy-start(f32[8,16,128]{2,1,0:T(8,128)} %param.16) | copy-start | bytes 196612
  0.7 4.7 %copy-start.9 = (f32[8,16,128]{2,1,0:T(8,128)S(1)}, f32[8,16,128]{2,1,0:T(8,128)}, u32[]{:S(2)}) copy-start(f32[8,16,128]{2,1,0:T(8,128)} %param.17) | copy-start | bytes 196612
  0.7 4.7 %copy-start.3 = (f32[8,16,128]{2,1,0:T(8,128)S(1)}, f32[8,16,128]{2,1,0:T(8,128)}, u32[]{:S(2)}) copy-start(f32[8,16,128]{2,1,0:T(8,128)} %param.18) | copy-start | bytes 196612
  0.7 4.7 %copy-start.7 = (f32[8,16,128]{2,1,0:T(8,128)S(1)}, f32[8,16,128]{2,1,0:T(8,128)}, u32[]{:S(2)}) copy-start(f32[8,16,128]{2,1,0:T(8,128)} %param.19) | copy-start | bytes 196612
  0.7 4.7 %copy-start.4 = (f32[8,16,128]{2,1,0:T(8,128)S(1)}, f32[8,16,128]{2,1,0:T(8,128)}, u32[]{:S(2)}) copy-start(f32[8,16,128]{2,1,0:T(8,128)} %param.20) | copy-start | bytes 196612
  0.7 4.7 %copy-start.5 = (f32[8,16,128]{2,1,0:T(8,128)S(1)}, f32[8,16,128]{2,1,0:T(8,128)}, u32[]{:S(2)}) copy-start(f32[8,16,128]{2,1,0:T(8,128)} %param.21) | copy-start | bytes 196612
  0.7 4.8 %copy-start.6 = (f32[8,16,128]{2,1,0:T(8,128)S(1)}, f32[8,16,128]{2,1,0:T(8,128)}, u32[]{:S(2)}) copy-start(f32[8,16,128]{2,1,0:T(8,128)} %param.22) | copy-start | bytes 196612
  3.1 7.8 %collective-permute-start.4 = (f32[4,128]{1,0:T(4,128)S(1)}, f32[4,128]{1,0:T(4,128)S(1)}, u32[]{:S(2)}, u32[]{:S(2)}) collective-permute-start(f32[4,128]{1,0:T(4,128)S(1)} %pad_maximum_fusion.10), channel_id=1, source_target_pairs={{0,4},{4,0},{8,12},{12,8},{1,5},{5,1},{9,13},{13,9},{2,6},{6,2},{1... | collective-permute-start | bytes 6152 | tf_op jit(solution)/shard_map/ppermute | solution.py:124
  5.5 15.6 %collective-permute-start.1 = (f32[44,16,128]{2,1,0:T(8,128)S(1)}, f32[44,16,128]{2,1,0:T(8,128)S(1)}, u32[]{:S(2)}, u32[]{:S(2)}) collective-permute-start(f32[44,16,128]{2,1,0:T(8,128)S(1)} %get-tuple-element.59), channel_id=1, source_target_pairs={{4,0},{8,4},{12,8},{5,1},{9,5},{13,9},{6,2},{10,6},{14,10},{7,3},{... | collective-permute-start | bytes 1081352 | tf_op jit(solution)/shard_map/ppermute | solution.py:105
  9.0 12.1 %collective-permute-start = (f32[44,16,128]{2,1,0:T(8,128)S(1)}, f32[44,16,128]{2,1,0:T(8,128)S(1)}, u32[]{:S(2)}, u32[]{:S(2)}) collective-permute-start(f32[44,16,128]{2,1,0:T(8,128)S(1)} %get-tuple-element.58), channel_id=1, source_target_pairs={{0,4},{4,8},{8,12},{1,5},{5,9},{9,13},{2,6},{6,10},{10,14},{3,7},{... | collective-permute-start | bytes 1081352 | tf_op jit(solution)/shard_map/ppermute | solution.py:104
  10.9 9.6 %collective-permute-start.5 = (f32[4,256]{1,0:T(4,128)S(1)}, f32[4,256]{1,0:T(4,128)S(1)}, u32[]{:S(2)}, u32[]{:S(2)}) collective-permute-start(f32[4,256]{1,0:T(4,128)S(1)} %pad_maximum_fusion.9), channel_id=1, source_target_pairs={{0,8},{4,12},{8,0},{12,4},{1,9},{5,13},{9,1},{13,5},{2,10},{6,14},... | collective-permute-start | bytes 12296 | tf_op jit(solution)/shard_map/ppermute | solution.py:124
  21.1 2.1 %copy-start.1 = (f32[8,16,128]{2,1,0:T(8,128)S(1)}, f32[8,16,128]{2,1,0:T(8,128)}, u32[]{:S(2)}) copy-start(f32[8,16,128]{2,1,0:T(8,128)} %param.14) | copy-start | bytes 196612
  21.1 2.1 %copy-start.2 = (f32[8,16,128]{2,1,0:T(8,128)S(1)}, f32[8,16,128]{2,1,0:T(8,128)}, u32[]{:S(2)}) copy-start(f32[8,16,128]{2,1,0:T(8,128)} %param.15) | copy-start | bytes 196612
  23.3 4.4 %collective-permute-start.2 = (f32[2,24,4,128]{3,2,1,0:T(4,128)S(1)}, f32[2,24,4,128]{3,2,1,0:T(4,128)S(1)}, u32[]{:S(2)}, u32[]{:S(2)}) collective-permute-start(f32[2,24,4,128]{3,2,1,0:T(4,128)S(1)} %get-tuple-element.27), channel_id=1, source_target_pairs={{1,0},{2,1},{3,2},{5,4},{6,5},{7,6},{9,8},{10,9},{11,10},{13,12},{... | collective-permute-start | bytes 294920 | tf_op jit(solution)/shard_map/ppermute | solution.py:105
  25.2 5.9 %collective-permute-start.3 = (f32[2,24,4,128]{3,2,1,0:T(4,128)S(1)}, f32[2,24,4,128]{3,2,1,0:T(4,128)S(1)}, u32[]{:S(2)}, u32[]{:S(2)}) collective-permute-start(f32[2,24,4,128]{3,2,1,0:T(4,128)S(1)} %get-tuple-element.26), channel_id=1, source_target_pairs={{0,1},{1,2},{2,3},{4,5},{5,6},{6,7},{8,9},{9,10},{10,11},{12,13},{... | collective-permute-start | bytes 294920 | tf_op jit(solution)/shard_map/ppermute | solution.py:104
  35.0 4.7 %collective-permute-start.6 = (f32[2,16,4,128]{3,2,1,0:T(4,128)S(1)}, f32[2,16,4,128]{3,2,1,0:T(4,128)S(1)}, u32[]{:S(2)}, u32[]{:S(2)}) collective-permute-start(f32[2,16,4,128]{3,2,1,0:T(4,128)S(1)} %get-tuple-element.41), channel_id=1, source_target_pairs={{1,0},{2,1},{3,2},{5,4},{6,5},{7,6},{9,8},{10,9},{11,10},{13,12},{... | collective-permute-start | bytes 196616 | tf_op jit(solution)/shard_map/ppermute | solution.py:105
  36.9 5.6 %collective-permute-start.7 = (f32[2,16,4,128]{3,2,1,0:T(4,128)S(1)}, f32[2,16,4,128]{3,2,1,0:T(4,128)S(1)}, u32[]{:S(2)}, u32[]{:S(2)}) collective-permute-start(f32[2,16,4,128]{3,2,1,0:T(4,128)S(1)} %get-tuple-element.40), channel_id=1, source_target_pairs={{0,1},{1,2},{2,3},{4,5},{5,6},{6,7},{8,9},{9,10},{10,11},{12,13},{... | collective-permute-start | bytes 196616 | tf_op jit(solution)/shard_map/ppermute | solution.py:104
  44.2 0.8 %copy-start.10 = (bf16[2,8,16,128]{3,2,1,0:T(8,128)(2,1)S(1)}, bf16[2,8,16,128]{3,2,1,0:T(8,128)(2,1)}, u32[]{:S(2)}) copy-start(bf16[2,8,16,128]{3,2,1,0:T(8,128)(2,1)} %param.23) | copy-start | bytes 196612

commit v5 on v4

--- a/solution.py
+++ b/solution.py
@@ -106,20 +106,28 @@
     return below, above
 
 
-def gather_column(traces, time_steps, rec_owner, rec_local):
-    groups = lax.axis_size("gx")
-    held = rec_local.shape[0]
+def receiver_payload(traces, time_steps, rec_owner, rec_local):
     steps = jnp.arange(traces.shape[0], dtype=jnp.int32)
     chosen = (time_steps[:, None] == steps[None, :]).astype(jnp.float32)
     samples = jnp.dot(
         chosen, traces, precision=lax.Precision.HIGHEST, preferred_element_type=jnp.float32
     )
-    payload = jnp.concatenate(
+    return jnp.concatenate(
         [samples, rec_local.astype(jnp.float32)[None], rec_owner[:, 0].astype(jnp.float32)[None]]
     )
-    if groups & (groups - 1) == 0:
-        arrived = payload
-        step = 1
+
+
+def gather_column(payload, below, above):
+    groups = lax.axis_size("gx")
+    held = payload.shape[1]
+    if groups & (groups - 1) == 0 and groups >= 2:
+        even = lax.axis_index("gx") % 2 == 0
+        arrived = jnp.where(
+            even,
+            jnp.concatenate([payload, above], axis=1),
+            jnp.concatenate([below, payload], axis=1),
+        )
+        step = 2
         while step < groups:
             partner = lax.ppermute(arrived, "gx", [(i, i ^ step) for i in range(groups)])
             arrived = jnp.concatenate([arrived, partner], axis=1)
@@ -173,10 +181,17 @@
     def slabs(parts):
         return jnp.concatenate([part.reshape(-1, sy, sz) for part in parts], axis=0)
 
+    payload = receiver_payload(traces, time_steps, rec_owner, rec_local)
+    held = payload.shape[1]
+    extra = -(-4 * held // (sy * sz))
+    riding = jnp.pad(payload.reshape(-1), (0, extra * sy * sz - 4 * held)).reshape(extra, sy, sz)
     low_part = slabs(
         [p_now, q_now, p_prev[sx - 4 :], q_prev[sx - 4 :]] + [f[sx - 4 :] for f in params]
-    )
-    high_part = slabs([p_now, q_now, p_prev[:4], q_prev[:4]] + [f[:4] for f in params])
+        + [riding]
+    )
+    high_part = slabs(
+        [p_now, q_now, p_prev[:4], q_prev[:4]] + [f[:4] for f in params] + [riding]
+    )
     below, above = from_neighbours(low_part, high_part, "gx")
 
     def unpack(got):
@@ -184,9 +199,13 @@
             got[0:16].reshape(2, 8, sy, sz),
             got[16:24].reshape(2, 4, sy, sz),
             got[24:44].reshape(5, 4, sy, sz),
-        )
-
-    (now_lo, prev_lo, params_lo), (now_hi, prev_hi, params_hi) = unpack(below), unpack(above)
+            got[44:].reshape(-1)[: 4 * held].reshape(4, held),
+        )
+
+    (now_lo, prev_lo, params_lo, rec_lo), (now_hi, prev_hi, params_hi, rec_hi) = (
+        unpack(below),
+        unpack(above),
+    )
     now_x = jnp.concatenate([now_lo, current, now_hi], axis=1)
     prev_x = jnp.concatenate([prev_lo, earlier, prev_hi], axis=1)
     params_x = [
@@ -195,7 +214,7 @@
     lo_y, hi_y = from_neighbours(now_x[:, :, sy - 4 :], now_x[:, :, :4], "gy")
     now_xy = pad_depth(jnp.concatenate([lo_y, now_x, hi_y], axis=2))
 
-    arrived = gather_column(traces, time_steps, rec_owner, rec_local)
+    arrived = gather_column(payload, rec_lo, rec_hi)
     source_0 = sources_over(arrived, arrived[0:1], (sx, sy, sz), -4, sx + 8)[0]
     source_1 = sources_over(arrived, arrived[1:2], (sx, sy, sz), 0, sx)[0]
 

time: 46.8 us -> 49.5 us (1.058)
  the two profiles are of different devices: /device:TPU:30 before, /device:TPU:1 now
where the time goes in v5:
time: 49.5 us; the launch traced here: 49 us
  starting transfers between devices  22.4 us (45%)
  other arithmetic  11.1 us (22%)
  waiting for transfers between devices  8.46 us (17%)
  local copies, waits for them, and re-layouts  4.02 us (8%)
  matrix products  1.84 us (4%)
  between operations  1.16 us (2%)
    ppermute x3, starting transfers between devices, from_neighbours(): below = lax.ppermute(low_part, axis, [(i, i + 1) for i in range(count - 1)])  12 us
    ppermute x3, starting transfers between devices, from_neighbours(): lax.ppermute(high_part, axis, [(i + 1, i) for i in range(count - 1)])  7.27 us
    ppermute x3, waiting for transfers between devices, from_neighbours(): lax.ppermute(high_part, axis, [(i + 1, i) for i in range(count - 1)])  5.8 us
    unnamed x33, local copies, waits for them, and re-layouts  3.68 us
    ppermute x1, starting transfers between devices, gather_column(): lax.ppermute(arrived, 'gx', [(i, i ^ step) for i in range(groups)])  3.12 us
    ppermute x3, waiting for transfers between devices, from_neighbours(): below = lax.ppermute(low_part, axis, [(i, i + 1) for i in range(count - 1)])  2.65 us
    add x2, other arithmetic, advance(): axis_x * axis_x * dxx + axis_y * axis_y * dyy + axis_z * axis_z * dzz  1.61 us
    add x2, other arithmetic, derivatives(): dz_xwide + weight * (padded[:, :, 4:4 + sy, 4 + k:4 + k + sz] - padded[:,...  1.58 us
  transfers between devices with their start and end apart: 7, of which 4 were waited for; matrix products, arithmetic and copies ran while one was open for 3% of the time, Pallas kernels for 0%

profile of v5, /device:TPU:1, one launch (start us, length us, event | category | flops | bytes accessed | tf_op | source)
XLA Modules:
  0.0 49.0 jit_solution(10263953872474281460)
XLA Ops:
  0.6 0.0 copy-start
  0.6 0.0 copy-start.9
  0.7 0.0 copy-start.3
  0.7 0.0 copy-start.7
  0.7 0.0 copy-start.4
  0.7 0.0 copy-start.5
  0.7 0.0 copy-start.6
  0.7 0.9 %constant_dynamic-update-slice_fusion.19 = f32[45,16,128]{2,1,0:T(8,128)S(1)} fusion(f32[8,16,128]{2,1,0:T(8,128)} %param.14), kind=kLoop, calls=%fused_computation.359 | loop fusion | bytes 131072
  1.6 0.8 %constant_dynamic-update-slice_fusion.18 = f32[45,16,128]{2,1,0:T(8,128)S(1)} fusion(f32[45,16,128]{2,1,0:T(8,128)S(1)} %constant_dynamic-update-slice_fusion.19, f32[8,16,128]{2,1,0:T(8,128)} %param.15), kind=kLoop, calls=%fused_computation.358 | loop fusion | bytes 131072
  2.5 0.8 %constant_dynamic-update-slice_fusion.7 = f32[45,16,128]{2,1,0:T(8,128)S(1)} fusion(f32[45,16,128]{2,1,0:T(8,128)S(1)} %constant_dynamic-update-slice_fusion.18, f32[8,16,128]{2,1,0:T(8,128)} %param.16), kind=kLoop, calls=%fused_computation.347 | loop fusion | bytes 65536
  3.3 0.8 %constant_dynamic-update-slice_fusion.17 = f32[45,16,128]{2,1,0:T(8,128)S(1)} fusion(f32[45,16,128]{2,1,0:T(8,128)S(1)} %copy.21, f32[8,16,128]{2,1,0:T(8,128)} %param.16), kind=kLoop, calls=%fused_computation.357 | loop fusion | bytes 65536
  4.0 0.7 %convert_bitcast_fusion = f32[1,128]{1,0:T(1,128)S(1)} fusion(s32[128,1]{0,1:T(1,128)} %param.26), kind=kLoop, calls=%fused_computation.400 | loop fusion | flops 128 | bytes 1024 | tf_op jit(solution)/shard_map/convert_element_type | solution.py:116
  4.7 0.7 %convert_bitcast_fusion.1 = f32[1,128]{1,0:T(1,128)S(1)} fusion(s32[128]{0:T(128)} %param.27), kind=kLoop, calls=%fused_computation.401 | loop fusion | flops 128 | bytes 1024 | tf_op jit(solution)/shard_map/broadcast_in_dim | solution.py:116
  5.3 0.0 copy-done
  5.3 0.9 %fusion.200 = f32[2,128]{1,0:T(2,128)S(1)} fusion(f32[1024,128]{1,0:T(8,128)S(1)} %copy-done, s32[2]{0:T(128)} %param.25), kind=kOutput, calls=%fused_computation.361 | convolution fusion | flops 3147776 | bytes 525320 | tf_op jit(solution)/shard_map/dot_general | solution.py:112
  6.3 0.0 copy-done.9
  6.3 0.0 copy-done.3
  6.3 0.0 copy-done.7
  6.4 0.0 copy-done.4
  6.4 0.0 copy-done.5
  6.4 0.0 copy-done.6
  6.5 1.3 %collective-permute-start.1 = (f32[45,16,128]{2,1,0:T(8,128)S(1)}, f32[45,16,128]{2,1,0:T(8,128)S(1)}, u32[]{:S(2)}, u32[]{:S(2)}) collective-permute-start(f32[45,16,128]{2,1,0:T(8,128)S(1)} %get-tuple-element.74), channel_id=1, source_target_pairs={{4,0},{8,4},{12,8},{5,1},{9,5},{13,9},{6,2},{10,6},{14,10},{7,3},{... | collective-permute-start | bytes 1105928 | tf_op jit(solution)/shard_map/ppermute | solution.py:105
  7.8 4.7 %collective-permute-start = (f32[45,16,128]{2,1,0:T(8,128)S(1)}, f32[45,16,128]{2,1,0:T(8,128)S(1)}, u32[]{:S(2)}, u32[]{:S(2)}) collective-permute-start(f32[45,16,128]{2,1,0:T(8,128)S(1)} %get-tuple-element.73), channel_id=1, source_target_pairs={{0,4},{4,8},{8,12},{1,5},{5,9},{9,13},{2,6},{6,10},{10,14},{3,7},{... | collective-permute-start | bytes 1105928 | tf_op jit(solution)/shard_map/ppermute | solution.py:104
  12.5 0.2 fusion.228
  12.7 0.3 fusion.212
  13.0 5.8 %collective-permute-done.1 = f32[45,16,128]{2,1,0:T(8,128)S(1)} collective-permute-done((f32[45,16,128]{2,1,0:T(8,128)S(1)}, f32[45,16,128]{2,1,0:T(8,128)S(1)}, u32[]{:S(2)}, u32[]{:S(2)}) %collective-permute-start.1) | collective-permute-done | bytes 368672 | tf_op jit(solution)/shard_map/ppermute | solution.py:105
  18.8 0.0 copy-start.1
  18.8 0.0 copy-start.2
  18.8 0.8 %collective-permute-done = f32[45,16,128]{2,1,0:T(8,128)S(1)} collective-permute-done((f32[45,16,128]{2,1,0:T(8,128)S(1)}, f32[45,16,128]{2,1,0:T(8,128)S(1)}, u32[]{:S(2)}, u32[]{:S(2)}) %collective-permute-start) | collective-permute-done | bytes 368672 | tf_op jit(solution)/shard_map/ppermute | solution.py:104
  19.7 1.0 %fusion.214 = (f32[16,16,128]{2,1,0:T(8,128)S(1)}, f32[16,16,128]{2,1,0:T(8,128)S(1)}, f32[16,16,128]{2,1,0:T(8,128)S(1)}) fusion(f32[4,16,128]{2,1,0:T(8,128)S(1)} %get-tuple-element.36, f32[8,16,128]{2,1,0:T(8,128)S(1)} %copy-done.6, f32[4,16,128]{2,1,0:T(8,128)S(1)} %get-tuple-element.31, f32[4,16,128]{2,1,0:T(8,128)S(1)} %get-tuple-element.37, ...), kind=kLoop, calls=%fused_computation.406 | loop fusion | flops 360448 | bytes 655360 | tf_op jit(solution)/shard_map/mul | solution.py:77
  20.7 0.0 copy-start.8
  20.7 1.0 %fusion.215 = (f32[16,16,128]{2,1,0:T(8,128)S(1)}, f32[16,16,128]{2,1,0:T(8,128)S(1)}, f32[16,16,128]{2,1,0:T(8,128)S(1)}) fusion(f32[4,16,128]{2,1,0:T(8,128)S(1)} %get-tuple-element.36, f32[8,16,128]{2,1,0:T(8,128)S(1)} %copy-done.6, f32[4,16,128]{2,1,0:T(8,128)S(1)} %get-tuple-element.31, f32[4,16,128]{2,1,0:T(8,128)S(1)} %get-tuple-element.37, ...), kind=kLoop, calls=%fused_computation.407 | loop fusion | flops 327680 | bytes 655360 | tf_op jit(solution)/shard_map/mul | solution.py:78
  21.8 3.1 %collective-permute-start.4 = (f32[4,256]{1,0:T(4,128)S(1)}, f32[4,256]{1,0:T(4,128)S(1)}, u32[]{:S(2)}, u32[]{:S(2)}) collective-permute-start(f32[4,256]{1,0:T(4,128)S(1)} %maximum_select_fusion), channel_id=1, source_target_pairs={{0,8},{4,12},{8,0},{12,4},{1,9},{5,13},{9,1},{13,5},{2,10},{6,14},... | collective-permute-start | bytes 12296 | tf_op jit(solution)/shard_map/ppermute | solution.py:132
  24.9 0.0 copy-done.1
  24.9 0.0 copy-done.2
  25.0 4.1 %collective-permute-start.2 = (f32[2,24,4,128]{3,2,1,0:T(4,128)S(1)}, f32[2,24,4,128]{3,2,1,0:T(4,128)S(1)}, u32[]{:S(2)}, u32[]{:S(2)}) collective-permute-start(f32[2,24,4,128]{3,2,1,0:T(4,128)S(1)} %get-tuple-element.28), channel_id=1, source_target_pairs={{1,0},{2,1},{3,2},{5,4},{6,5},{7,6},{9,8},{10,9},{11,10},{13,12},{... | collective-permute-start | bytes 294920 | tf_op jit(solution)/shard_map/ppermute | solution.py:105
  29.1 3.0 %collective-permute-start.3 = (f32[2,24,4,128]{3,2,1,0:T(4,128)S(1)}, f32[2,24,4,128]{3,2,1,0:T(4,128)S(1)}, u32[]{:S(2)}, u32[]{:S(2)}) collective-permute-start(f32[2,24,4,128]{3,2,1,0:T(4,128)S(1)} %get-tuple-element.27), channel_id=1, source_target_pairs={{0,1},{1,2},{2,3},{4,5},{5,6},{6,7},{8,9},{9,10},{10,11},{12,13},{... | collective-permute-start | bytes 294920 | tf_op jit(solution)/shard_map/ppermute | solution.py:104
  32.1 0.0 copy-done.8
  32.2 0.0 collective-permute-done.4
  32.2 0.5 %fusion.2 = f32[16,16,128]{2,1,0:T(8,128)S(1)} fusion(f32[512]{0:T(512)S(1)} %bitcast.106, s32[16,16]{1,0:T(8,128)S(1)} %multiply_add_fusion, s32[512]{0:T(512)S(1)} %bitcast.104, s32[512]{0:T(512)S(1)} %add_select_fusion), kind=kOutput, calls=%fused_computation.36 | convolution fusion | flops 201654272 | bytes 138240 | tf_op jit(solution)/shard_map/cpr,rz->cpz/dot_general | solution.py:152
  32.8 0.0 collective-permute-done.2
  32.8 0.9 %collective-permute-done.3 = f32[2,24,4,128]{3,2,1,0:T(4,128)S(1)} collective-permute-done((f32[2,24,4,128]{3,2,1,0:T(4,128)S(1)}, f32[2,24,4,128]{3,2,1,0:T(4,128)S(1)}, u32[]{:S(2)}, u32[]{:S(2)}) %collective-permute-start.3) | collective-permute-done | bytes 98336 | tf_op jit(solution)/shard_map/ppermute | solution.py:104
  33.7 0.6 %select_maximum_fusion = f32[2,24,24,136]{3,2,1,0:T(8,128)S(1)} fusion(f32[2,24,4,128]{3,2,1,0:T(4,128)S(1)} %collective-permute-done.2, f32[2,24,4,128]{3,2,1,0:T(4,128)S(1)} %collective-permute-done.3, f32[2,8,16,128]{3,2,1,0:T(8,128)S(1)} %bitcast.83, f32[2,8,16,128]{3,2,1,0:T(8,128)S(1)} %bitcast.87, f32[1,8,16,128]{3,2,1,0:T(8,128)S(1)} %bitcast.95, ...), kind=kLoop, calls=%fused_computation.4 | loop fusion | flops 2193408 | bytes 1216512 | tf_op jit(solution)/shard_map/concatenate | solution.py:215
  34.3 0.8 %fusion.6 = f32[2,16,24,128]{3,2,1,0:T(8,128)S(1)} fusion(f32[2,24,24,136]{3,2,1,0:T(8,128)S(1)} %select_maximum_fusion), kind=kLoop, calls=%fused_computation.41 | loop fusion | flops 1081344 | bytes 3538944 | tf_op jit(solution)/shard_map/add | solution.py:53
  35.1 0.1 pad_maximum_fusion
  35.2 1.0 %fusion.13 = (f32[2,24,16,128]{3,2,1,0:T(8,128)S(1)}, f32[2,24,16,128]{3,2,1,0:T(8,128)S(1)}) fusion(f32[2,24,24,136]{3,2,1,0:T(8,128)S(1)} %select_maximum_fusion, f32[2,24,20,128]{3,2,1,0:T(8,128)S(1)} %get-tuple-element.26, f32[2,24,20,128]{3,2,1,0:T(8,128)S(1)} %get-tuple-element.25), kind=kLoop, calls=%fused_computation.52 | loop fusion | flops 2162688 | bytes 7077888 | tf_op jit(solution)/shard_map/add | solution.py:49
  36.2 1.0 %fusion.43 = (f32[2,16,16,128]{3,2,1,0:T(8,128)S(1)}, f32[2,16,16,128]{3,2,1,0:T(8,128)S(1)}, f32[2,16,16,128]{3,2,1,0:T(8,128)S(1)}, f32[2,16,16,128]{3,2,1,0:T(8,128)S(1)}) fusion(f32[2,16,24,128]{3,2,1,0:T(8,128)S(1)} %fusion.6, f32[2,24,16,128]{3,2,1,0:T(8,128)S(1)} %get-tuple-element.75, f32[2,24,16,128]{3,2,1,0:T(8,128)S(1)} %get-tuple-element.76, ...), kind=kLoop, calls=%fused_computation.101 | loop fusion | flops 5570560 | bytes 14548992 | tf_op jit(solution)/shard_map/add | solution.py:77
  37.3 0.1 fusion.176
  37.4 0.1 fusion.181
  37.5 1.9 %collective-permute-start.5 = (f32[2,16,4,128]{3,2,1,0:T(4,128)S(1)}, f32[2,16,4,128]{3,2,1,0:T(4,128)S(1)}, u32[]{:S(2)}, u32[]{:S(2)}) collective-permute-start(f32[2,16,4,128]{3,2,1,0:T(4,128)S(1)} %get-tuple-element.42), channel_id=1, source_target_pairs={{1,0},{2,1},{3,2},{5,4},{6,5},{7,6},{9,8},{10,9},{11,10},{13,12},{... | collective-permute-start | bytes 196616 | tf_op jit(solution)/shard_map/ppermute | solution.py:105
  39.4 4.3 %collective-permute-start.6 = (f32[2,16,4,128]{3,2,1,0:T(4,128)S(1)}, f32[2,16,4,128]{3,2,1,0:T(4,128)S(1)}, u32[]{:S(2)}, u32[]{:S(2)}) collective-permute-start(f32[2,16,4,128]{3,2,1,0:T(4,128)S(1)} %get-tuple-element.41), channel_id=1, source_target_pairs={{0,1},{1,2},{2,3},{4,5},{5,6},{6,7},{8,9},{9,10},{10,11},{12,13},{... | collective-permute-start | bytes 196616 | tf_op jit(solution)/shard_map/ppermute | solution.py:104
  43.8 0.4 fusion.91
  44.1 0.0 collective-permute-done.5
  44.2 0.9 %collective-permute-done.6 = f32[2,16,4,128]{3,2,1,0:T(4,128)S(1)} collective-permute-done((f32[2,16,4,128]{3,2,1,0:T(4,128)S(1)}, f32[2,16,4,128]{3,2,1,0:T(4,128)S(1)}, u32[]{:S(2)}, u32[]{:S(2)}) %collective-permute-start.6) | collective-permute-done | bytes 65568 | tf_op jit(solution)/shard_map/ppermute | solution.py:104
  45.1 0.4 select_maximum_fusion.5
  45.5 0.4 fusion.102
  45.9 0.5 %fusion.27 = f32[2,16,16,128]{3,2,1,0:T(8,128)S(1)} fusion(f32[2,16,24,136]{3,2,1,0:T(8,128)S(1)} %select_maximum_fusion.5), kind=kLoop, calls=%fused_computation.77 | loop fusion | flops 720896 | bytes 2359296 | tf_op jit(solution)/shard_map/add | solution.py:49
  46.5 0.1 pad_maximum_fusion.2
  46.5 0.2 fusion.34
  46.7 0.0 copy-start.10
  46.8 0.6 %fusion.133 = (f32[2,8,16,128]{3,2,1,0:T(8,128)S(1)}, f32[2,8,16,128]{3,2,1,0:T(8,128)S(1)}, f32[2,8,16,128]{3,2,1,0:T(8,128)S(1)}, f32[2,8,16,128]{3,2,1,0:T(8,128)S(1)}) fusion(f32[2,8,24,128]{3,2,1,0:T(8,128)S(1)} %fusion.102, f32[2,16,16,128]{3,2,1,0:T(8,128)S(1)} %fusion.27, f32[2,16,16,128]{3,2,1,0:T(8,128)S(1)} %fusion.34, ...), kind=kLoop, calls=%fused_computation.220 | loop fusion | flops 3080192 | bytes 6422528 | tf_op jit(solution)/shard_map/add | solution.py:77
  47.3 0.3 copy-done.10
  47.6 0.7 %fusion.198 = (f32[8,16,128]{2,1,0:T(8,128)}, f32[8,16,128]{2,1,0:T(8,128)}, f32[8,16,128]{2,1,0:T(8,128)}, f32[8,16,128]{2,1,0:T(8,128)S(1)}) fusion(bf16[2,8,16,128]{3,2,1,0:T(8,128)(2,1)S(1)} %copy-done.10, f32[8,16,128]{2,1,0:T(8,128)S(1)} %fusion.91, f32[8,16,128]{2,1,0:T(8,128)S(1)} %copy-done.3, f32[2,8,16,128]{3,2,1,0:T(8,128)S(1)} %get-tuple-element.11, ...), kind=kLoop, calls=%fused_computation.330 | loop fusion | flops 327680 | bytes 1048576 | tf_op jit(solution)/shard_map/add | solution.py:227
  48.3 0.7 %add_add_fusion = (f32[8,16,128]{2,1,0:T(8,128)}, f32[8,16,128]{2,1,0:T(8,128)}) fusion(f32[8,16,128]{2,1,0:T(8,128)S(1)} %fusion.91, f32[8,16,128]{2,1,0:T(8,128)S(1)} %copy-done.3, f32[8,16,128]{2,1,0:T(8,128)S(1)} %get-tuple-element.8, f32[8,16,128]{2,1,0:T(8,128)S(1)} %copy-done.2, f32[2,8,16,128]{3,2,1,0:T(8,128)S(1)} %get-tuple-element.11, ...), kind=kLoop, calls=%fused_computation.332 | loop fusion | flops 147456 | bytes 589824 | tf_op jit(solution)/shard_map/add | solution.py:93
  (28 shorter events, 0.4 us)
Async XLA Ops:
  0.6 4.7 %copy-start = (f32[1024,128]{1,0:T(8,128)S(1)}, f32[1024,128]{1,0:T(8,128)}, u32[]{:S(2)}) copy-start(f32[1024,128]{1,0:T(8,128)} %param.24) | copy-start | bytes 1572868
  0.6 5.6 %copy-start.9 = (f32[8,16,128]{2,1,0:T(8,128)S(1)}, f32[8,16,128]{2,1,0:T(8,128)}, u32[]{:S(2)}) copy-start(f32[8,16,128]{2,1,0:T(8,128)} %param.17) | copy-start | bytes 196612
  0.7 5.7 %copy-start.3 = (f32[8,16,128]{2,1,0:T(8,128)S(1)}, f32[8,16,128]{2,1,0:T(8,128)}, u32[]{:S(2)}) copy-start(f32[8,16,128]{2,1,0:T(8,128)} %param.18) | copy-start | bytes 196612
  0.7 5.7 %copy-start.7 = (f32[8,16,128]{2,1,0:T(8,128)S(1)}, f32[8,16,128]{2,1,0:T(8,128)}, u32[]{:S(2)}) copy-start(f32[8,16,128]{2,1,0:T(8,128)} %param.19) | copy-start | bytes 196612
  0.7 5.7 %copy-start.4 = (f32[8,16,128]{2,1,0:T(8,128)S(1)}, f32[8,16,128]{2,1,0:T(8,128)}, u32[]{:S(2)}) copy-start(f32[8,16,128]{2,1,0:T(8,128)} %param.20) | copy-start | bytes 196612
  0.7 5.7 %copy-start.5 = (f32[8,16,128]{2,1,0:T(8,128)S(1)}, f32[8,16,128]{2,1,0:T(8,128)}, u32[]{:S(2)}) copy-start(f32[8,16,128]{2,1,0:T(8,128)} %param.21) | copy-start | bytes 196612
  0.7 5.7 %copy-start.6 = (f32[8,16,128]{2,1,0:T(8,128)S(1)}, f32[8,16,128]{2,1,0:T(8,128)}, u32[]{:S(2)}) copy-start(f32[8,16,128]{2,1,0:T(8,128)} %param.22) | copy-start | bytes 196612
  6.5 12.3 %collective-permute-start.1 = (f32[45,16,128]{2,1,0:T(8,128)S(1)}, f32[45,16,128]{2,1,0:T(8,128)S(1)}, u32[]{:S(2)}, u32[]{:S(2)}) collective-permute-start(f32[45,16,128]{2,1,0:T(8,128)S(1)} %get-tuple-element.74), channel_id=1, source_target_pairs={{4,0},{8,4},{12,8},{5,1},{9,5},{13,9},{6,2},{10,6},{14,10},{7,3},{... | collective-permute-start | bytes 1105928 | tf_op jit(solution)/shard_map/ppermute | solution.py:105
  7.8 11.9 %collective-permute-start = (f32[45,16,128]{2,1,0:T(8,128)S(1)}, f32[45,16,128]{2,1,0:T(8,128)S(1)}, u32[]{:S(2)}, u32[]{:S(2)}) collective-permute-start(f32[45,16,128]{2,1,0:T(8,128)S(1)} %get-tuple-element.73), channel_id=1, source_target_pairs={{0,4},{4,8},{8,12},{1,5},{5,9},{9,13},{2,6},{6,10},{10,14},{3,7},{... | collective-permute-start | bytes 1105928 | tf_op jit(solution)/shard_map/ppermute | solution.py:104
  18.8 6.1 %copy-start.1 = (f32[8,16,128]{2,1,0:T(8,128)S(1)}, f32[8,16,128]{2,1,0:T(8,128)}, u32[]{:S(2)}) copy-start(f32[8,16,128]{2,1,0:T(8,128)} %param.14) | copy-start | bytes 196612
  18.8 6.1 %copy-start.2 = (f32[8,16,128]{2,1,0:T(8,128)S(1)}, f32[8,16,128]{2,1,0:T(8,128)}, u32[]{:S(2)}) copy-start(f32[8,16,128]{2,1,0:T(8,128)} %param.15) | copy-start | bytes 196612
  20.7 11.4 %copy-start.8 = (f32[8,16,128]{2,1,0:T(8,128)S(1)}, f32[8,16,128]{2,1,0:T(8,128)}, u32[]{:S(2)}) copy-start(f32[8,16,128]{2,1,0:T(8,128)} %param.16) | copy-start | bytes 196612
  21.8 10.4 %collective-permute-start.4 = (f32[4,256]{1,0:T(4,128)S(1)}, f32[4,256]{1,0:T(4,128)S(1)}, u32[]{:S(2)}, u32[]{:S(2)}) collective-permute-start(f32[4,256]{1,0:T(4,128)S(1)} %maximum_select_fusion), channel_id=1, source_target_pairs={{0,8},{4,12},{8,0},{12,4},{1,9},{5,13},{9,1},{13,5},{2,10},{6,14},... | collective-permute-start | bytes 12296 | tf_op jit(solution)/shard_map/ppermute | solution.py:132
  25.0 7.8 %collective-permute-start.2 = (f32[2,24,4,128]{3,2,1,0:T(4,128)S(1)}, f32[2,24,4,128]{3,2,1,0:T(4,128)S(1)}, u32[]{:S(2)}, u32[]{:S(2)}) collective-permute-start(f32[2,24,4,128]{3,2,1,0:T(4,128)S(1)} %get-tuple-element.28), channel_id=1, source_target_pairs={{1,0},{2,1},{3,2},{5,4},{6,5},{7,6},{9,8},{10,9},{11,10},{13,12},{... | collective-permute-start | bytes 294920 | tf_op jit(solution)/shard_map/ppermute | solution.py:105
  29.1 4.6 %collective-permute-start.3 = (f32[2,24,4,128]{3,2,1,0:T(4,128)S(1)}, f32[2,24,4,128]{3,2,1,0:T(4,128)S(1)}, u32[]{:S(2)}, u32[]{:S(2)}) collective-permute-start(f32[2,24,4,128]{3,2,1,0:T(4,128)S(1)} %get-tuple-element.27), channel_id=1, source_target_pairs={{0,1},{1,2},{2,3},{4,5},{5,6},{6,7},{8,9},{9,10},{10,11},{12,13},{... | collective-permute-start | bytes 294920 | tf_op jit(solution)/shard_map/ppermute | solution.py:104
  37.5 6.6 %collective-permute-start.5 = (f32[2,16,4,128]{3,2,1,0:T(4,128)S(1)}, f32[2,16,4,128]{3,2,1,0:T(4,128)S(1)}, u32[]{:S(2)}, u32[]{:S(2)}) collective-permute-start(f32[2,16,4,128]{3,2,1,0:T(4,128)S(1)} %get-tuple-element.42), channel_id=1, source_target_pairs={{1,0},{2,1},{3,2},{5,4},{6,5},{7,6},{9,8},{10,9},{11,10},{13,12},{... | collective-permute-start | bytes 196616 | tf_op jit(solution)/shard_map/ppermute | solution.py:105
  39.4 5.6 %collective-permute-start.6 = (f32[2,16,4,128]{3,2,1,0:T(4,128)S(1)}, f32[2,16,4,128]{3,2,1,0:T(4,128)S(1)}, u32[]{:S(2)}, u32[]{:S(2)}) collective-permute-start(f32[2,16,4,128]{3,2,1,0:T(4,128)S(1)} %get-tuple-element.41), channel_id=1, source_target_pairs={{0,1},{1,2},{2,3},{4,5},{5,6},{6,7},{8,9},{9,10},{10,11},{12,13},{... | collective-permute-start | bytes 196616 | tf_op jit(solution)/shard_map/ppermute | solution.py:104
  46.7 0.8 %copy-start.10 = (bf16[2,8,16,128]{3,2,1,0:T(8,128)(2,1)S(1)}, bf16[2,8,16,128]{3,2,1,0:T(8,128)(2,1)}, u32[]{:S(2)}) copy-start(bf16[2,8,16,128]{3,2,1,0:T(8,128)(2,1)} %param.23) | copy-start | bytes 196612

commit v6 on v4

--- a/solution.py
+++ b/solution.py
@@ -106,7 +106,7 @@
     return below, above
 
 
-def gather_column(traces, time_steps, rec_owner, rec_local):
+def gather_column(traces, time_steps, rec_owner, rec_local, after):
     groups = lax.axis_size("gx")
     held = rec_local.shape[0]
     steps = jnp.arange(traces.shape[0], dtype=jnp.int32)
@@ -121,6 +121,8 @@
         arrived = payload
         step = 1
         while step < groups:
+            if step == 2:
+                arrived = arrived + 0.0 * after
             partner = lax.ppermute(arrived, "gx", [(i, i ^ step) for i in range(groups)])
             arrived = jnp.concatenate([arrived, partner], axis=1)
             step *= 2
@@ -195,7 +197,7 @@
     lo_y, hi_y = from_neighbours(now_x[:, :, sy - 4 :], now_x[:, :, :4], "gy")
     now_xy = pad_depth(jnp.concatenate([lo_y, now_x, hi_y], axis=2))
 
-    arrived = gather_column(traces, time_steps, rec_owner, rec_local)
+    arrived = gather_column(traces, time_steps, rec_owner, rec_local, lo_y[0, 0, 0, 0] + hi_y[0, 0, 0, 0])
     source_0 = sources_over(arrived, arrived[0:1], (sx, sy, sz), -4, sx + 8)[0]
     source_1 = sources_over(arrived, arrived[1:2], (sx, sy, sz), 0, sx)[0]
 

time: 46.8 us -> 52.8 us (1.13)
  the two profiles are of different devices: /device:TPU:30 before, /device:TPU:1 now
where the time goes in v6:
time: 52.8 us; the launch traced here: 52.3 us
  starting transfers between devices  23.3 us (44%)
  other arithmetic  11.1 us (21%)
  waiting for transfers between devices  10.2 us (19%)
  local copies, waits for them, and re-layouts  3.45 us (7%)
  between operations  2.47 us (5%)
  matrix products  1.84 us (3%)
    ppermute x3, starting transfers between devices, from_neighbours(): below = lax.ppermute(low_part, axis, [(i, i + 1) for i in range(count - 1)])  12.8 us
    ppermute x3, waiting for transfers between devices, from_neighbours(): lax.ppermute(high_part, axis, [(i + 1, i) for i in range(count - 1)])  8.4 us
    ppermute x2, starting transfers between devices, gather_column(): lax.ppermute(arrived, 'gx', [(i, i ^ step) for i in range(groups)])  5.31 us
    ppermute x3, starting transfers between devices, from_neighbours(): lax.ppermute(high_part, axis, [(i + 1, i) for i in range(count - 1)])  5.13 us
    unnamed x32, local copies, waits for them, and re-layouts  2.08 us
    ppermute x3, waiting for transfers between devices, from_neighbours(): below = lax.ppermute(low_part, axis, [(i, i + 1) for i in range(count - 1)])  1.77 us
    add x2, other arithmetic, advance(): axis_x * axis_x * dxx + axis_y * axis_y * dyy + axis_z * axis_z * dzz  1.61 us
    add x2, other arithmetic, derivatives(): dz_xwide + weight * (padded[:, :, 4:4 + sy, 4 + k:4 + k + sz] - padded[:,...  1.58 us
  transfers between devices with their start and end apart: 8, of which 4 were waited for; matrix products, arithmetic and copies ran while one was open for 18% of the time, Pallas kernels for 0%

profile of v6, /device:TPU:1, one launch (start us, length us, event | category | flops | bytes accessed | tf_op | source)
XLA Modules:
  0.0 52.3 jit_solution(11984200553968343020)
XLA Ops:
  0.6 0.0 copy-start
  0.7 0.0 copy-start.8
  0.7 0.0 copy-start.9
  0.7 0.0 copy-start.3
  0.7 0.0 copy-start.7
  0.7 0.0 copy-start.4
  0.7 0.0 copy-start.5
  0.7 0.0 copy-start.6
  0.7 0.7 %convert_bitcast_fusion = f32[1,128]{1,0:T(1,128)S(1)} fusion(s32[128,1]{0,1:T(1,128)} %param.26), kind=kLoop, calls=%fused_computation.396 | loop fusion | flops 128 | bytes 1024 | tf_op jit(solution)/shard_map/convert_element_type | solution.py:118
  1.4 0.7 %convert_bitcast_fusion.1 = f32[1,128]{1,0:T(1,128)S(1)} fusion(s32[128]{0:T(128)} %param.27), kind=kLoop, calls=%fused_computation.397 | loop fusion | flops 128 | bytes 1024 | tf_op jit(solution)/shard_map/broadcast_in_dim | solution.py:118
  2.1 0.0 copy-done
  2.1 0.9 %fusion.200 = f32[2,128]{1,0:T(2,128)S(1)} fusion(f32[1024,128]{1,0:T(8,128)S(1)} %copy-done, s32[2]{0:T(128)} %param.25), kind=kOutput, calls=%fused_computation.359 | convolution fusion | flops 3147776 | bytes 525320 | tf_op jit(solution)/shard_map/dot_general | solution.py:114
  3.1 2.2 %collective-permute-start.4 = (f32[4,128]{1,0:T(4,128)S(1)}, f32[4,128]{1,0:T(4,128)S(1)}, u32[]{:S(2)}, u32[]{:S(2)}) collective-permute-start(f32[4,128]{1,0:T(4,128)S(1)} %pad_maximum_fusion.9), channel_id=1, source_target_pairs={{0,4},{4,0},{8,12},{12,8},{1,5},{5,1},{9,13},{13,9},{2,6},{6,2},{1... | collective-permute-start | bytes 6152 | tf_op jit(solution)/shard_map/ppermute | solution.py:126
  5.3 0.8 %constant_dynamic-update-slice_fusion.17 = f32[44,16,128]{2,1,0:T(8,128)S(1)} fusion(f32[8,16,128]{2,1,0:T(8,128)} %param.14), kind=kLoop, calls=%fused_computation.357 | loop fusion | bytes 131072
  6.1 0.8 %constant_dynamic-update-slice_fusion.16 = f32[44,16,128]{2,1,0:T(8,128)S(1)} fusion(f32[44,16,128]{2,1,0:T(8,128)S(1)} %constant_dynamic-update-slice_fusion.17, f32[8,16,128]{2,1,0:T(8,128)} %param.15), kind=kLoop, calls=%fused_computation.356 | loop fusion | bytes 131072
  7.0 0.0 copy-done.8
  7.0 0.0 copy-done.9
  7.0 0.0 copy-done.3
  7.1 0.0 copy-done.7
  7.1 0.0 copy-done.4
  7.1 0.0 copy-done.5
  7.1 0.0 copy-done.6
  7.2 1.3 %collective-permute-start.1 = (f32[44,16,128]{2,1,0:T(8,128)S(1)}, f32[44,16,128]{2,1,0:T(8,128)S(1)}, u32[]{:S(2)}, u32[]{:S(2)}) collective-permute-start(f32[44,16,128]{2,1,0:T(8,128)S(1)} %get-tuple-element.60), channel_id=1, source_target_pairs={{4,0},{8,4},{12,8},{5,1},{9,5},{13,9},{6,2},{10,6},{14,10},{7,3},{... | collective-permute-start | bytes 1081352 | tf_op jit(solution)/shard_map/ppermute | solution.py:105
  8.5 4.0 %collective-permute-start = (f32[44,16,128]{2,1,0:T(8,128)S(1)}, f32[44,16,128]{2,1,0:T(8,128)S(1)}, u32[]{:S(2)}, u32[]{:S(2)}) collective-permute-start(f32[44,16,128]{2,1,0:T(8,128)S(1)} %get-tuple-element.59), channel_id=1, source_target_pairs={{0,4},{4,8},{8,12},{1,5},{5,9},{9,13},{2,6},{6,10},{10,14},{3,7},{... | collective-permute-start | bytes 1081352 | tf_op jit(solution)/shard_map/ppermute | solution.py:104
  12.5 0.2 fusion.228
  12.7 0.3 fusion.212
  13.0 0.0 copy-start.1
  13.0 0.0 copy-start.2
  13.1 5.0 %collective-permute-done.1 = f32[44,16,128]{2,1,0:T(8,128)S(1)} collective-permute-done((f32[44,16,128]{2,1,0:T(8,128)S(1)}, f32[44,16,128]{2,1,0:T(8,128)S(1)}, u32[]{:S(2)}, u32[]{:S(2)}) %collective-permute-start.1) | collective-permute-done | bytes 360480 | tf_op jit(solution)/shard_map/ppermute | solution.py:105
  18.0 0.9 %collective-permute-done = f32[44,16,128]{2,1,0:T(8,128)S(1)} collective-permute-done((f32[44,16,128]{2,1,0:T(8,128)S(1)}, f32[44,16,128]{2,1,0:T(8,128)S(1)}, u32[]{:S(2)}, u32[]{:S(2)}) %collective-permute-start) | collective-permute-done | bytes 360480 | tf_op jit(solution)/shard_map/ppermute | solution.py:104
  18.9 1.0 %fusion.214 = (f32[16,16,128]{2,1,0:T(8,128)S(1)}, f32[16,16,128]{2,1,0:T(8,128)S(1)}, f32[16,16,128]{2,1,0:T(8,128)S(1)}) fusion(f32[4,16,128]{2,1,0:T(8,128)S(1)} %get-tuple-element.36, f32[8,16,128]{2,1,0:T(8,128)S(1)} %copy-done.6, f32[4,16,128]{2,1,0:T(8,128)S(1)} %get-tuple-element.31, f32[4,16,128]{2,1,0:T(8,128)S(1)} %get-tuple-element.37, ...), kind=kLoop, calls=%fused_computation.402 | loop fusion | flops 360448 | bytes 655360 | tf_op jit(solution)/shard_map/mul | solution.py:77
  19.9 1.0 %fusion.215 = (f32[16,16,128]{2,1,0:T(8,128)S(1)}, f32[16,16,128]{2,1,0:T(8,128)S(1)}, f32[16,16,128]{2,1,0:T(8,128)S(1)}) fusion(f32[4,16,128]{2,1,0:T(8,128)S(1)} %get-tuple-element.36, f32[8,16,128]{2,1,0:T(8,128)S(1)} %copy-done.6, f32[4,16,128]{2,1,0:T(8,128)S(1)} %get-tuple-element.31, f32[4,16,128]{2,1,0:T(8,128)S(1)} %get-tuple-element.37, ...), kind=kLoop, calls=%fused_computation.403 | loop fusion | flops 327680 | bytes 655360 | tf_op jit(solution)/shard_map/mul | solution.py:78
  21.1 5.2 %collective-permute-start.3 = (f32[2,24,4,128]{3,2,1,0:T(4,128)S(1)}, f32[2,24,4,128]{3,2,1,0:T(4,128)S(1)}, u32[]{:S(2)}, u32[]{:S(2)}) collective-permute-start(f32[2,24,4,128]{3,2,1,0:T(4,128)S(1)} %get-tuple-element.28), channel_id=1, source_target_pairs={{0,1},{1,2},{2,3},{4,5},{5,6},{6,7},{8,9},{9,10},{10,11},{12,13},{... | collective-permute-start | bytes 294920 | tf_op jit(solution)/shard_map/ppermute | solution.py:104
  26.3 1.9 %collective-permute-start.2 = (f32[2,24,4,128]{3,2,1,0:T(4,128)S(1)}, f32[2,24,4,128]{3,2,1,0:T(4,128)S(1)}, u32[]{:S(2)}, u32[]{:S(2)}) collective-permute-start(f32[2,24,4,128]{3,2,1,0:T(4,128)S(1)} %get-tuple-element.27), channel_id=1, source_target_pairs={{1,0},{2,1},{3,2},{5,4},{6,5},{7,6},{9,8},{10,9},{11,10},{13,12},{... | collective-permute-start | bytes 294920 | tf_op jit(solution)/shard_map/ppermute | solution.py:105
  28.2 0.0 collective-permute-done.3
  28.3 0.5 slice.1024
  28.8 3.4 %collective-permute-done.2 = f32[2,24,4,128]{3,2,1,0:T(4,128)S(1)} collective-permute-done((f32[2,24,4,128]{3,2,1,0:T(4,128)S(1)}, f32[2,24,4,128]{3,2,1,0:T(4,128)S(1)}, u32[]{:S(2)}, u32[]{:S(2)}) %collective-permute-start.2) | collective-permute-done | bytes 98336 | tf_op jit(solution)/shard_map/ppermute | solution.py:105
  32.2 0.5 slice.1025
  34.0 0.0 collective-permute-done.4
  34.0 3.1 %collective-permute-start.5 = (f32[4,256]{1,0:T(4,128)S(1)}, f32[4,256]{1,0:T(4,128)S(1)}, u32[]{:S(2)}, u32[]{:S(2)}) collective-permute-start(f32[4,256]{1,0:T(4,128)S(1)} %maximum_add_fusion.1), channel_id=1, source_target_pairs={{0,8},{4,12},{8,0},{12,4},{1,9},{5,13},{9,1},{13,5},{2,10},{6,14},... | collective-permute-start | bytes 12296 | tf_op jit(solution)/shard_map/ppermute | solution.py:126
  37.2 0.6 %select_maximum_fusion = f32[2,24,24,136]{3,2,1,0:T(8,128)S(1)} fusion(f32[2,24,4,128]{3,2,1,0:T(4,128)S(1)} %collective-permute-done.2, f32[2,24,4,128]{3,2,1,0:T(4,128)S(1)} %collective-permute-done.3, f32[2,8,16,128]{3,2,1,0:T(8,128)S(1)} %bitcast.75, f32[2,8,16,128]{3,2,1,0:T(8,128)S(1)} %bitcast.79, f32[1,8,16,128]{3,2,1,0:T(8,128)S(1)} %bitcast.87, ...), kind=kLoop, calls=%fused_computation.4 | loop fusion | flops 2193408 | bytes 1216512 | tf_op jit(solution)/shard_map/concatenate | solution.py:198
  37.7 0.8 %fusion.6 = f32[2,16,24,128]{3,2,1,0:T(8,128)S(1)} fusion(f32[2,24,24,136]{3,2,1,0:T(8,128)S(1)} %select_maximum_fusion), kind=kLoop, calls=%fused_computation.41 | loop fusion | flops 1081344 | bytes 3538944 | tf_op jit(solution)/shard_map/add | solution.py:53
  38.5 0.1 pad_maximum_fusion
  38.6 1.0 %fusion.13 = (f32[2,24,16,128]{3,2,1,0:T(8,128)S(1)}, f32[2,24,16,128]{3,2,1,0:T(8,128)S(1)}) fusion(f32[2,24,24,136]{3,2,1,0:T(8,128)S(1)} %select_maximum_fusion, f32[2,24,20,128]{3,2,1,0:T(8,128)S(1)} %get-tuple-element.26, f32[2,24,20,128]{3,2,1,0:T(8,128)S(1)} %get-tuple-element.25), kind=kLoop, calls=%fused_computation.52 | loop fusion | flops 2162688 | bytes 7077888 | tf_op jit(solution)/shard_map/add | solution.py:49
  39.7 1.0 %fusion.43 = (f32[2,16,16,128]{3,2,1,0:T(8,128)S(1)}, f32[2,16,16,128]{3,2,1,0:T(8,128)S(1)}, f32[2,16,16,128]{3,2,1,0:T(8,128)S(1)}, f32[2,16,16,128]{3,2,1,0:T(8,128)S(1)}) fusion(f32[2,16,24,128]{3,2,1,0:T(8,128)S(1)} %fusion.6, f32[2,24,16,128]{3,2,1,0:T(8,128)S(1)} %get-tuple-element.73, f32[2,24,16,128]{3,2,1,0:T(8,128)S(1)} %get-tuple-element.74, ...), kind=kLoop, calls=%fused_computation.101 | loop fusion | flops 5570560 | bytes 14548992 | tf_op jit(solution)/shard_map/add | solution.py:77
  40.7 0.0 collective-permute-done.5
  40.8 0.5 fusion.2
  41.3 0.1 fusion.176
  41.4 0.1 fusion.181
  41.6 1.9 %collective-permute-start.6 = (f32[2,16,4,128]{3,2,1,0:T(4,128)S(1)}, f32[2,16,4,128]{3,2,1,0:T(4,128)S(1)}, u32[]{:S(2)}, u32[]{:S(2)}) collective-permute-start(f32[2,16,4,128]{3,2,1,0:T(4,128)S(1)} %get-tuple-element.42), channel_id=1, source_target_pairs={{1,0},{2,1},{3,2},{5,4},{6,5},{7,6},{9,8},{10,9},{11,10},{13,12},{... | collective-permute-start | bytes 196616 | tf_op jit(solution)/shard_map/ppermute | solution.py:105
  43.5 3.6 %collective-permute-start.7 = (f32[2,16,4,128]{3,2,1,0:T(4,128)S(1)}, f32[2,16,4,128]{3,2,1,0:T(4,128)S(1)}, u32[]{:S(2)}, u32[]{:S(2)}) collective-permute-start(f32[2,16,4,128]{3,2,1,0:T(4,128)S(1)} %get-tuple-element.41), channel_id=1, source_target_pairs={{0,1},{1,2},{2,3},{4,5},{5,6},{6,7},{8,9},{9,10},{10,11},{12,13},{... | collective-permute-start | bytes 196616 | tf_op jit(solution)/shard_map/ppermute | solution.py:104
  47.1 0.4 fusion.91
  47.5 0.0 collective-permute-done.6
  47.5 0.9 %collective-permute-done.7 = f32[2,16,4,128]{3,2,1,0:T(4,128)S(1)} collective-permute-done((f32[2,16,4,128]{3,2,1,0:T(4,128)S(1)}, f32[2,16,4,128]{3,2,1,0:T(4,128)S(1)}, u32[]{:S(2)}, u32[]{:S(2)}) %collective-permute-start.7) | collective-permute-done | bytes 65568 | tf_op jit(solution)/shard_map/ppermute | solution.py:104
  48.4 0.4 select_maximum_fusion.5
  48.9 0.4 fusion.102
  49.3 0.5 %fusion.27 = f32[2,16,16,128]{3,2,1,0:T(8,128)S(1)} fusion(f32[2,16,24,136]{3,2,1,0:T(8,128)S(1)} %select_maximum_fusion.5), kind=kLoop, calls=%fused_computation.77 | loop fusion | flops 720896 | bytes 2359296 | tf_op jit(solution)/shard_map/add | solution.py:49
  49.8 0.1 pad_maximum_fusion.2
  49.9 0.2 fusion.34
  50.1 0.0 copy-start.10
  50.1 0.6 %fusion.133 = (f32[2,8,16,128]{3,2,1,0:T(8,128)S(1)}, f32[2,8,16,128]{3,2,1,0:T(8,128)S(1)}, f32[2,8,16,128]{3,2,1,0:T(8,128)S(1)}, f32[2,8,16,128]{3,2,1,0:T(8,128)S(1)}) fusion(f32[2,8,24,128]{3,2,1,0:T(8,128)S(1)} %fusion.102, f32[2,16,16,128]{3,2,1,0:T(8,128)S(1)} %fusion.27, f32[2,16,16,128]{3,2,1,0:T(8,128)S(1)} %fusion.34, ...), kind=kLoop, calls=%fused_computation.220 | loop fusion | flops 3080192 | bytes 6422528 | tf_op jit(solution)/shard_map/add | solution.py:77
  50.7 0.3 copy-done.10
  51.0 0.7 %fusion.198 = (f32[8,16,128]{2,1,0:T(8,128)}, f32[8,16,128]{2,1,0:T(8,128)}, f32[8,16,128]{2,1,0:T(8,128)}, f32[8,16,128]{2,1,0:T(8,128)S(1)}) fusion(bf16[2,8,16,128]{3,2,1,0:T(8,128)(2,1)S(1)} %copy-done.10, f32[8,16,128]{2,1,0:T(8,128)S(1)} %fusion.91, f32[8,16,128]{2,1,0:T(8,128)S(1)} %copy-done.3, f32[2,8,16,128]{3,2,1,0:T(8,128)S(1)} %get-tuple-element.11, ...), kind=kLoop, calls=%fused_computation.330 | loop fusion | flops 327680 | bytes 1048576 | tf_op jit(solution)/shard_map/add | solution.py:210
  51.7 0.7 %add_add_fusion = (f32[8,16,128]{2,1,0:T(8,128)}, f32[8,16,128]{2,1,0:T(8,128)}) fusion(f32[8,16,128]{2,1,0:T(8,128)S(1)} %fusion.91, f32[8,16,128]{2,1,0:T(8,128)S(1)} %copy-done.3, f32[8,16,128]{2,1,0:T(8,128)S(1)} %get-tuple-element.8, f32[8,16,128]{2,1,0:T(8,128)S(1)} %copy-done.2, f32[2,8,16,128]{3,2,1,0:T(8,128)S(1)} %get-tuple-element.11, ...), kind=kLoop, calls=%fused_computation.332 | loop fusion | flops 147456 | bytes 589824 | tf_op jit(solution)/shard_map/add | solution.py:93
  (29 shorter events, 0.4 us)
Async XLA Ops:
  0.6 1.5 %copy-start = (f32[1024,128]{1,0:T(8,128)S(1)}, f32[1024,128]{1,0:T(8,128)}, u32[]{:S(2)}) copy-start(f32[1024,128]{1,0:T(8,128)} %param.24) | copy-start | bytes 1572868
  0.7 6.3 %copy-start.8 = (f32[8,16,128]{2,1,0:T(8,128)S(1)}, f32[8,16,128]{2,1,0:T(8,128)}, u32[]{:S(2)}) copy-start(f32[8,16,128]{2,1,0:T(8,128)} %param.16) | copy-start | bytes 196612
  0.7 6.4 %copy-start.9 = (f32[8,16,128]{2,1,0:T(8,128)S(1)}, f32[8,16,128]{2,1,0:T(8,128)}, u32[]{:S(2)}) copy-start(f32[8,16,128]{2,1,0:T(8,128)} %param.17) | copy-start | bytes 196612
  0.7 6.4 %copy-start.3 = (f32[8,16,128]{2,1,0:T(8,128)S(1)}, f32[8,16,128]{2,1,0:T(8,128)}, u32[]{:S(2)}) copy-start(f32[8,16,128]{2,1,0:T(8,128)} %param.18) | copy-start | bytes 196612
  0.7 6.4 %copy-start.7 = (f32[8,16,128]{2,1,0:T(8,128)S(1)}, f32[8,16,128]{2,1,0:T(8,128)}, u32[]{:S(2)}) copy-start(f32[8,16,128]{2,1,0:T(8,128)} %param.19) | copy-start | bytes 196612
  0.7 6.4 %copy-start.4 = (f32[8,16,128]{2,1,0:T(8,128)S(1)}, f32[8,16,128]{2,1,0:T(8,128)}, u32[]{:S(2)}) copy-start(f32[8,16,128]{2,1,0:T(8,128)} %param.20) | copy-start | bytes 196612
  0.7 6.4 %copy-start.5 = (f32[8,16,128]{2,1,0:T(8,128)S(1)}, f32[8,16,128]{2,1,0:T(8,128)}, u32[]{:S(2)}) copy-start(f32[8,16,128]{2,1,0:T(8,128)} %param.21) | copy-start | bytes 196612
  0.7 6.4 %copy-start.6 = (f32[8,16,128]{2,1,0:T(8,128)S(1)}, f32[8,16,128]{2,1,0:T(8,128)}, u32[]{:S(2)}) copy-start(f32[8,16,128]{2,1,0:T(8,128)} %param.22) | copy-start | bytes 196612
  3.1 30.9 %collective-permute-start.4 = (f32[4,128]{1,0:T(4,128)S(1)}, f32[4,128]{1,0:T(4,128)S(1)}, u32[]{:S(2)}, u32[]{:S(2)}) collective-permute-start(f32[4,128]{1,0:T(4,128)S(1)} %pad_maximum_fusion.9), channel_id=1, source_target_pairs={{0,4},{4,0},{8,12},{12,8},{1,5},{5,1},{9,13},{13,9},{2,6},{6,2},{1... | collective-permute-start | bytes 6152 | tf_op jit(solution)/shard_map/ppermute | solution.py:126
  7.2 10.9 %collective-permute-start.1 = (f32[44,16,128]{2,1,0:T(8,128)S(1)}, f32[44,16,128]{2,1,0:T(8,128)S(1)}, u32[]{:S(2)}, u32[]{:S(2)}) collective-permute-start(f32[44,16,128]{2,1,0:T(8,128)S(1)} %get-tuple-element.60), channel_id=1, source_target_pairs={{4,0},{8,4},{12,8},{5,1},{9,5},{13,9},{6,2},{10,6},{14,10},{7,3},{... | collective-permute-start | bytes 1081352 | tf_op jit(solution)/shard_map/ppermute | solution.py:105
  8.5 10.4 %collective-permute-start = (f32[44,16,128]{2,1,0:T(8,128)S(1)}, f32[44,16,128]{2,1,0:T(8,128)S(1)}, u32[]{:S(2)}, u32[]{:S(2)}) collective-permute-start(f32[44,16,128]{2,1,0:T(8,128)S(1)} %get-tuple-element.59), channel_id=1, source_target_pairs={{0,4},{4,8},{8,12},{1,5},{5,9},{9,13},{2,6},{6,10},{10,14},{3,7},{... | collective-permute-start | bytes 1081352 | tf_op jit(solution)/shard_map/ppermute | solution.py:104
  13.0 7.9 %copy-start.1 = (f32[8,16,128]{2,1,0:T(8,128)S(1)}, f32[8,16,128]{2,1,0:T(8,128)}, u32[]{:S(2)}) copy-start(f32[8,16,128]{2,1,0:T(8,128)} %param.14) | copy-start | bytes 196612
  13.0 7.9 %copy-start.2 = (f32[8,16,128]{2,1,0:T(8,128)S(1)}, f32[8,16,128]{2,1,0:T(8,128)}, u32[]{:S(2)}) copy-start(f32[8,16,128]{2,1,0:T(8,128)} %param.15) | copy-start | bytes 196612
  21.1 7.2 %collective-permute-start.3 = (f32[2,24,4,128]{3,2,1,0:T(4,128)S(1)}, f32[2,24,4,128]{3,2,1,0:T(4,128)S(1)}, u32[]{:S(2)}, u32[]{:S(2)}) collective-permute-start(f32[2,24,4,128]{3,2,1,0:T(4,128)S(1)} %get-tuple-element.28), channel_id=1, source_target_pairs={{0,1},{1,2},{2,3},{4,5},{5,6},{6,7},{8,9},{9,10},{10,11},{12,13},{... | collective-permute-start | bytes 294920 | tf_op jit(solution)/shard_map/ppermute | solution.py:104
  26.3 5.9 %collective-permute-start.2 = (f32[2,24,4,128]{3,2,1,0:T(4,128)S(1)}, f32[2,24,4,128]{3,2,1,0:T(4,128)S(1)}, u32[]{:S(2)}, u32[]{:S(2)}) collective-permute-start(f32[2,24,4,128]{3,2,1,0:T(4,128)S(1)} %get-tuple-element.27), channel_id=1, source_target_pairs={{1,0},{2,1},{3,2},{5,4},{6,5},{7,6},{9,8},{10,9},{11,10},{13,12},{... | collective-permute-start | bytes 294920 | tf_op jit(solution)/shard_map/ppermute | solution.py:105
  34.0 6.7 %collective-permute-start.5 = (f32[4,256]{1,0:T(4,128)S(1)}, f32[4,256]{1,0:T(4,128)S(1)}, u32[]{:S(2)}, u32[]{:S(2)}) collective-permute-start(f32[4,256]{1,0:T(4,128)S(1)} %maximum_add_fusion.1), channel_id=1, source_target_pairs={{0,8},{4,12},{8,0},{12,4},{1,9},{5,13},{9,1},{13,5},{2,10},{6,14},... | collective-permute-start | bytes 12296 | tf_op jit(solution)/shard_map/ppermute | solution.py:126
  41.6 6.0 %collective-permute-start.6 = (f32[2,16,4,128]{3,2,1,0:T(4,128)S(1)}, f32[2,16,4,128]{3,2,1,0:T(4,128)S(1)}, u32[]{:S(2)}, u32[]{:S(2)}) collective-permute-start(f32[2,16,4,128]{3,2,1,0:T(4,128)S(1)} %get-tuple-element.42), channel_id=1, source_target_pairs={{1,0},{2,1},{3,2},{5,4},{6,5},{7,6},{9,8},{10,9},{11,10},{13,12},{... | collective-permute-start | bytes 196616 | tf_op jit(solution)/shard_map/ppermute | solution.py:105
  43.5 5.0 %collective-permute-start.7 = (f32[2,16,4,128]{3,2,1,0:T(4,128)S(1)}, f32[2,16,4,128]{3,2,1,0:T(4,128)S(1)}, u32[]{:S(2)}, u32[]{:S(2)}) collective-permute-start(f32[2,16,4,128]{3,2,1,0:T(4,128)S(1)} %get-tuple-element.41), channel_id=1, source_target_pairs={{0,1},{1,2},{2,3},{4,5},{5,6},{6,7},{8,9},{9,10},{10,11},{12,13},{... | collective-permute-start | bytes 196616 | tf_op jit(solution)/shard_map/ppermute | solution.py:104
  50.1 0.8 %copy-start.10 = (bf16[2,8,16,128]{3,2,1,0:T(8,128)(2,1)S(1)}, bf16[2,8,16,128]{3,2,1,0:T(8,128)(2,1)}, u32[]{:S(2)}) copy-start(bf16[2,8,16,128]{3,2,1,0:T(8,128)(2,1)} %param.23) | copy-start | bytes 196612

commit v7 on v4

--- a/solution.py
+++ b/solution.py
@@ -173,20 +173,20 @@
     def slabs(parts):
         return jnp.concatenate([part.reshape(-1, sy, sz) for part in parts], axis=0)
 
-    low_part = slabs(
-        [p_now, q_now, p_prev[sx - 4 :], q_prev[sx - 4 :]] + [f[sx - 4 :] for f in params]
-    )
-    high_part = slabs([p_now, q_now, p_prev[:4], q_prev[:4]] + [f[:4] for f in params])
-    below, above = from_neighbours(low_part, high_part, "gx")
+    now_lo, now_hi = from_neighbours(
+        slabs([p_now, q_now]).reshape(2, 8, sy, sz), slabs([p_now, q_now]).reshape(2, 8, sy, sz),
+        "gx",
+    )
+    rest_lo, rest_hi = from_neighbours(
+        slabs([p_prev[sx - 4 :], q_prev[sx - 4 :]] + [f[sx - 4 :] for f in params]),
+        slabs([p_prev[:4], q_prev[:4]] + [f[:4] for f in params]),
+        "gx",
+    )
 
     def unpack(got):
-        return (
-            got[0:16].reshape(2, 8, sy, sz),
-            got[16:24].reshape(2, 4, sy, sz),
-            got[24:44].reshape(5, 4, sy, sz),
-        )
-
-    (now_lo, prev_lo, params_lo), (now_hi, prev_hi, params_hi) = unpack(below), unpack(above)
+        return got[0:8].reshape(2, 4, sy, sz), got[8:28].reshape(5, 4, sy, sz)
+
+    (prev_lo, params_lo), (prev_hi, params_hi) = unpack(rest_lo), unpack(rest_hi)
     now_x = jnp.concatenate([now_lo, current, now_hi], axis=1)
     prev_x = jnp.concatenate([prev_lo, earlier, prev_hi], axis=1)
     params_x = [

time: 46.8 us -> 55.3 us (1.18)
  the two profiles are of different devices: /device:TPU:30 before, /device:TPU:1 now
where the time goes in v7:
time: 55.3 us; the launch traced here: 54.5 us
  starting transfers between devices  29.4 us (53%)
  other arithmetic  10.7 us (19%)
  local copies, waits for them, and re-layouts  6.86 us (12%)
  waiting for transfers between devices  5.14 us (9%)
  matrix products  1.18 us (2%)
  between operations  1.17 us (2%)
    ppermute x4, starting transfers between devices, from_neighbours(): below = lax.ppermute(low_part, axis, [(i, i + 1) for i in range(count - 1)])  14.9 us
    ppermute x4, starting transfers between devices, from_neighbours(): lax.ppermute(high_part, axis, [(i + 1, i) for i in range(count - 1)])  10 us
    unnamed x34, local copies, waits for them, and re-layouts  5.77 us
    ppermute x2, starting transfers between devices, gather_column(): lax.ppermute(arrived, 'gx', [(i, i ^ step) for i in range(groups)])  4.51 us
    ppermute x2, waiting for transfers between devices, gather_column(): lax.ppermute(arrived, 'gx', [(i, i ^ step) for i in range(groups)])  4.21 us
    add x2, other arithmetic, advance(): axis_x * axis_x * dxx + axis_y * axis_y * dyy + axis_z * axis_z * dzz  1.61 us
    add x2, other arithmetic, derivatives(): dz_xwide + weight * (padded[:, :, 4:4 + sy, 4 + k:4 + k + sz] - padded[:,...  1.58 us
    mul x2, other arithmetic, advance(): axis_x * axis_x * dxx + axis_y * axis_y * dyy + axis_z * axis_z * dzz  1.26 us
  transfers between devices with their start and end apart: 10, of which 3 were waited for; matrix products, arithmetic and copies ran while one was open for 17% of the time, Pallas kernels for 0%

profile of v7, /device:TPU:1, one launch (start us, length us, event | category | flops | bytes accessed | tf_op | source)
XLA Modules:
  0.0 54.5 jit_solution(1922739052814618014)
XLA Ops:
  0.6 0.0 copy-start
  0.6 0.0 copy-start.5
  0.7 0.0 copy-start.6
  0.7 0.0 copy-start.12
  0.7 0.0 copy-start.13
  0.7 0.0 copy-start.11
  0.7 1.0 %pad_maximum_fusion.4 = f32[16,16,128]{2,1,0:T(8,128)S(1)} fusion(f32[8,16,128]{2,1,0:T(8,128)} %param.15, f32[8,16,128]{2,1,0:T(8,128)} %param.14), kind=kLoop, calls=%fused_computation.296 | loop fusion | flops 32768 | bytes 262144 | tf_op jit(solution)/shard_map/concatenate | solution.py:174
  1.7 4.0 %collective-permute-start = (f32[2,8,16,128]{3,2,1,0:T(8,128)S(1)}, f32[2,8,16,128]{3,2,1,0:T(8,128)S(1)}, u32[]{:S(2)}, u32[]{:S(2)}) collective-permute-start(f32[2,8,16,128]{3,2,1,0:T(8,128)S(1)} %bitcast.84), channel_id=1, source_target_pairs={{0,4},{4,8},{8,12},{1,5},{5,9},{9,13},{2,6},{6,10},{10,14},{3,7},{... | collective-permute-start | bytes 393224 | tf_op jit(solution)/shard_map/ppermute | solution.py:104
  5.7 1.3 %collective-permute-start.1 = (f32[2,8,16,128]{3,2,1,0:T(8,128)S(1)}, f32[2,8,16,128]{3,2,1,0:T(8,128)S(1)}, u32[]{:S(2)}, u32[]{:S(2)}) collective-permute-start(f32[2,8,16,128]{3,2,1,0:T(8,128)S(1)} %bitcast.85), channel_id=1, source_target_pairs={{4,0},{8,4},{12,8},{5,1},{9,5},{13,9},{6,2},{10,6},{14,10},{7,3},{... | collective-permute-start | bytes 393224 | tf_op jit(solution)/shard_map/ppermute | solution.py:105
  7.0 0.8 %slice_dynamic-update-slice_fusion.13 = (f32[28,16,128]{2,1,0:T(8,128)S(1)}, f32[28,16,128]{2,1,0:T(8,128)S(1)}) fusion(f32[8,16,128]{2,1,0:T(8,128)} %param.16), kind=kLoop, calls=%fused_computation.355 | loop fusion | bytes 131072
  7.8 0.8 %slice_dynamic-update-slice_fusion.12 = (f32[28,16,128]{2,1,0:T(8,128)S(1)}, f32[28,16,128]{2,1,0:T(8,128)S(1)}) fusion(f32[28,16,128]{2,1,0:T(8,128)S(1)} %get-tuple-element.70, f32[8,16,128]{2,1,0:T(8,128)} %param.17, f32[28,16,128]{2,1,0:T(8,128)S(1)} %get-tuple-element.71), kind=kLoop, calls=%fused_computation.354 | loop fusion | bytes 131072
  8.6 0.8 %slice_dynamic-update-slice_fusion.11 = (f32[28,16,128]{2,1,0:T(8,128)S(1)}, f32[28,16,128]{2,1,0:T(8,128)S(1)}) fusion(f32[28,16,128]{2,1,0:T(8,128)S(1)} %get-tuple-element.68, f32[8,16,128]{2,1,0:T(8,128)} %param.18, f32[28,16,128]{2,1,0:T(8,128)S(1)} %get-tuple-element.69), kind=kLoop, calls=%fused_computation.353 | loop fusion | bytes 131072
  9.4 0.8 %slice_dynamic-update-slice_fusion.10 = (f32[28,16,128]{2,1,0:T(8,128)S(1)}, f32[28,16,128]{2,1,0:T(8,128)S(1)}) fusion(f32[28,16,128]{2,1,0:T(8,128)S(1)} %get-tuple-element.66, f32[8,16,128]{2,1,0:T(8,128)} %param.19, f32[28,16,128]{2,1,0:T(8,128)S(1)} %get-tuple-element.67), kind=kLoop, calls=%fused_computation.352 | loop fusion | bytes 131072
  10.1 0.8 %slice_dynamic-update-slice_fusion.9 = (f32[28,16,128]{2,1,0:T(8,128)S(1)}, f32[28,16,128]{2,1,0:T(8,128)S(1)}) fusion(f32[28,16,128]{2,1,0:T(8,128)S(1)} %get-tuple-element.64, f32[8,16,128]{2,1,0:T(8,128)} %param.20, f32[28,16,128]{2,1,0:T(8,128)S(1)} %get-tuple-element.65), kind=kLoop, calls=%fused_computation.351 | loop fusion | bytes 131072
  11.0 0.8 %slice_dynamic-update-slice_fusion.8 = (f32[28,16,128]{2,1,0:T(8,128)S(1)}, f32[28,16,128]{2,1,0:T(8,128)S(1)}) fusion(f32[28,16,128]{2,1,0:T(8,128)S(1)} %get-tuple-element.62, f32[8,16,128]{2,1,0:T(8,128)} %param.21, f32[28,16,128]{2,1,0:T(8,128)S(1)} %get-tuple-element.63), kind=kLoop, calls=%fused_computation.350 | loop fusion | bytes 131072
  11.7 0.8 %slice_dynamic-update-slice_fusion.7 = (f32[28,16,128]{2,1,0:T(8,128)S(1)}, f32[28,16,128]{2,1,0:T(8,128)S(1)}) fusion(f32[28,16,128]{2,1,0:T(8,128)S(1)} %get-tuple-element.60, f32[8,16,128]{2,1,0:T(8,128)} %param.22, f32[28,16,128]{2,1,0:T(8,128)S(1)} %get-tuple-element.61), kind=kLoop, calls=%fused_computation.349 | loop fusion | bytes 131072 | tf_op jit(solution)/shard_map/concatenate | solution.py:174
  12.5 4.0 %collective-permute-start.2 = (f32[28,16,128]{2,1,0:T(8,128)S(1)}, f32[28,16,128]{2,1,0:T(8,128)S(1)}, u32[]{:S(2)}, u32[]{:S(2)}) collective-permute-start(f32[28,16,128]{2,1,0:T(8,128)S(1)} %get-tuple-element.58), channel_id=1, source_target_pairs={{0,4},{4,8},{8,12},{1,5},{5,9},{9,13},{2,6},{6,10},{10,14},{3,7},{... | collective-permute-start | bytes 688136 | tf_op jit(solution)/shard_map/ppermute | solution.py:104
  16.5 1.3 %collective-permute-start.3 = (f32[28,16,128]{2,1,0:T(8,128)S(1)}, f32[28,16,128]{2,1,0:T(8,128)S(1)}, u32[]{:S(2)}, u32[]{:S(2)}) collective-permute-start(f32[28,16,128]{2,1,0:T(8,128)S(1)} %get-tuple-element.59), channel_id=1, source_target_pairs={{4,0},{8,4},{12,8},{5,1},{9,5},{13,9},{6,2},{10,6},{14,10},{7,3},{... | collective-permute-start | bytes 688136 | tf_op jit(solution)/shard_map/ppermute | solution.py:105
  17.9 0.3 fusion.200
  18.2 2.1 %collective-permute-start.6 = (f32[4,128]{1,0:T(4,128)S(1)}, f32[4,128]{1,0:T(4,128)S(1)}, u32[]{:S(2)}, u32[]{:S(2)}) collective-permute-start(f32[4,128]{1,0:T(4,128)S(1)} %pad_maximum_fusion.11), channel_id=1, source_target_pairs={{0,4},{4,0},{8,12},{12,8},{1,5},{5,1},{9,13},{13,9},{2,6},{6,2},{1... | collective-permute-start | bytes 6152 | tf_op jit(solution)/shard_map/ppermute | solution.py:124
  20.3 0.2 fusion.227
  20.6 0.3 fusion.211
  20.9 3.2 %collective-permute-done.6 = f32[4,128]{1,0:T(4,128)S(1)} collective-permute-done((f32[4,128]{1,0:T(4,128)S(1)}, f32[4,128]{1,0:T(4,128)S(1)}, u32[]{:S(2)}, u32[]{:S(2)}) %collective-permute-start.6) | collective-permute-done | bytes 2080 | tf_op jit(solution)/shard_map/ppermute | solution.py:124
  24.0 2.4 %collective-permute-start.7 = (f32[4,256]{1,0:T(4,128)S(1)}, f32[4,256]{1,0:T(4,128)S(1)}, u32[]{:S(2)}, u32[]{:S(2)}) collective-permute-start(f32[4,256]{1,0:T(4,128)S(1)} %pad_maximum_fusion.10), channel_id=1, source_target_pairs={{0,8},{4,12},{8,0},{12,4},{1,9},{5,13},{9,1},{13,5},{2,10},{6,14},... | collective-permute-start | bytes 12296 | tf_op jit(solution)/shard_map/ppermute | solution.py:124
  26.4 1.1 %collective-permute-done.7 = f32[4,256]{1,0:T(4,128)S(1)} collective-permute-done((f32[4,256]{1,0:T(4,128)S(1)}, f32[4,256]{1,0:T(4,128)S(1)}, u32[]{:S(2)}, u32[]{:S(2)}) %collective-permute-start.7) | collective-permute-done | bytes 4128 | tf_op jit(solution)/shard_map/ppermute | solution.py:124
  27.6 0.5 fusion.2
  28.1 0.0 collective-permute-done
  28.1 0.0 collective-permute-done.1
  28.2 5.5 %collective-permute-start.4 = (f32[2,24,4,128]{3,2,1,0:T(4,128)S(1)}, f32[2,24,4,128]{3,2,1,0:T(4,128)S(1)}, u32[]{:S(2)}, u32[]{:S(2)}) collective-permute-start(f32[2,24,4,128]{3,2,1,0:T(4,128)S(1)} %get-tuple-element.27), channel_id=1, source_target_pairs={{1,0},{2,1},{3,2},{5,4},{6,5},{7,6},{9,8},{10,9},{11,10},{13,12},{... | collective-permute-start | bytes 294920 | tf_op jit(solution)/shard_map/ppermute | solution.py:105
  33.7 3.0 %collective-permute-start.5 = (f32[2,24,4,128]{3,2,1,0:T(4,128)S(1)}, f32[2,24,4,128]{3,2,1,0:T(4,128)S(1)}, u32[]{:S(2)}, u32[]{:S(2)}) collective-permute-start(f32[2,24,4,128]{3,2,1,0:T(4,128)S(1)} %get-tuple-element.26), channel_id=1, source_target_pairs={{0,1},{1,2},{2,3},{4,5},{5,6},{6,7},{8,9},{9,10},{10,11},{12,13},{... | collective-permute-start | bytes 294920 | tf_op jit(solution)/shard_map/ppermute | solution.py:104
  36.8 0.0 collective-permute-done.2
  36.8 0.0 collective-permute-done.3
  36.8 1.0 %fusion.214 = (f32[16,16,128]{2,1,0:T(8,128)S(1)}, f32[16,16,128]{2,1,0:T(8,128)S(1)}, f32[16,16,128]{2,1,0:T(8,128)S(1)}) fusion(f32[4,16,128]{2,1,0:T(8,128)S(1)} %get-tuple-element.44, f32[8,16,128]{2,1,0:T(8,128)S(1)} %copy-done.6, f32[4,16,128]{2,1,0:T(8,128)S(1)} %get-tuple-element.39, f32[4,16,128]{2,1,0:T(8,128)S(1)} %get-tuple-element.45, ...), kind=kLoop, calls=%fused_computation.394 | loop fusion | flops 327680 | bytes 655360 | tf_op jit(solution)/shard_map/mul | solution.py:78
  37.8 1.0 %fusion.213 = (f32[16,16,128]{2,1,0:T(8,128)S(1)}, f32[16,16,128]{2,1,0:T(8,128)S(1)}, f32[16,16,128]{2,1,0:T(8,128)S(1)}) fusion(f32[4,16,128]{2,1,0:T(8,128)S(1)} %get-tuple-element.44, f32[8,16,128]{2,1,0:T(8,128)S(1)} %copy-done.6, f32[4,16,128]{2,1,0:T(8,128)S(1)} %get-tuple-element.39, f32[4,16,128]{2,1,0:T(8,128)S(1)} %get-tuple-element.45, ...), kind=kLoop, calls=%fused_computation.393 | loop fusion | flops 360448 | bytes 655360 | tf_op jit(solution)/shard_map/mul | solution.py:77
  38.8 0.0 collective-permute-done.4
  38.8 0.0 collective-permute-done.5
  38.8 0.6 %select_maximum_fusion = f32[2,24,24,136]{3,2,1,0:T(8,128)S(1)} fusion(f32[2,24,4,128]{3,2,1,0:T(4,128)S(1)} %collective-permute-done.4, f32[2,24,4,128]{3,2,1,0:T(4,128)S(1)} %collective-permute-done.5, f32[2,8,16,128]{3,2,1,0:T(8,128)S(1)} %collective-permute-done.1, f32[2,8,16,128]{3,2,1,0:T(8,128)S(1)} %collective-permute-done, ...), kind=kLoop, calls=%fused_computation.4 | loop fusion | flops 2193408 | bytes 1216512 | tf_op jit(solution)/shard_map/concatenate | solution.py:196
  39.4 0.8 %fusion.6 = f32[2,16,24,128]{3,2,1,0:T(8,128)S(1)} fusion(f32[2,24,24,136]{3,2,1,0:T(8,128)S(1)} %select_maximum_fusion), kind=kLoop, calls=%fused_computation.41 | loop fusion | flops 1081344 | bytes 3538944 | tf_op jit(solution)/shard_map/add | solution.py:53
  40.2 0.1 pad_maximum_fusion
  40.3 0.0 copy-start.8
  40.3 0.0 copy-start.9
  40.3 1.0 %fusion.13 = (f32[2,24,16,128]{3,2,1,0:T(8,128)S(1)}, f32[2,24,16,128]{3,2,1,0:T(8,128)S(1)}) fusion(f32[2,24,24,136]{3,2,1,0:T(8,128)S(1)} %select_maximum_fusion, f32[2,24,20,128]{3,2,1,0:T(8,128)S(1)} %get-tuple-element.25, f32[2,24,20,128]{3,2,1,0:T(8,128)S(1)} %get-tuple-element.24), kind=kLoop, calls=%fused_computation.52 | loop fusion | flops 2162688 | bytes 7077888 | tf_op jit(solution)/shard_map/add | solution.py:49
  41.5 0.0 copy-start.3
  41.5 0.0 copy-start.4
  41.5 1.0 %fusion.43 = (f32[2,16,16,128]{3,2,1,0:T(8,128)S(1)}, f32[2,16,16,128]{3,2,1,0:T(8,128)S(1)}, f32[2,16,16,128]{3,2,1,0:T(8,128)S(1)}, f32[2,16,16,128]{3,2,1,0:T(8,128)S(1)}) fusion(f32[2,16,24,128]{3,2,1,0:T(8,128)S(1)} %fusion.6, f32[2,24,16,128]{3,2,1,0:T(8,128)S(1)} %get-tuple-element.75, f32[2,24,16,128]{3,2,1,0:T(8,128)S(1)} %get-tuple-element.76, ...), kind=kLoop, calls=%fused_computation.101 | loop fusion | flops 5570560 | bytes 14548992 | tf_op jit(solution)/shard_map/add | solution.py:77
  42.5 0.0 copy-start.7
  42.6 0.1 fusion.176
  42.7 0.7 %copy-done.7 = f32[8,16,128]{2,1,0:T(8,128)S(1)} copy-done((f32[8,16,128]{2,1,0:T(8,128)S(1)}, f32[8,16,128]{2,1,0:T(8,128)}, u32[]{:S(2)}) %copy-start.7) | copy-done | bytes 65560
  43.4 0.1 fusion.181
  43.5 1.9 %collective-permute-start.8 = (f32[2,16,4,128]{3,2,1,0:T(4,128)S(1)}, f32[2,16,4,128]{3,2,1,0:T(4,128)S(1)}, u32[]{:S(2)}, u32[]{:S(2)}) collective-permute-start(f32[2,16,4,128]{3,2,1,0:T(4,128)S(1)} %get-tuple-element.31), channel_id=1, source_target_pairs={{1,0},{2,1},{3,2},{5,4},{6,5},{7,6},{9,8},{10,9},{11,10},{13,12},{... | collective-permute-start | bytes 196616 | tf_op jit(solution)/shard_map/ppermute | solution.py:105
  45.4 3.8 %collective-permute-start.9 = (f32[2,16,4,128]{3,2,1,0:T(4,128)S(1)}, f32[2,16,4,128]{3,2,1,0:T(4,128)S(1)}, u32[]{:S(2)}, u32[]{:S(2)}) collective-permute-start(f32[2,16,4,128]{3,2,1,0:T(4,128)S(1)} %get-tuple-element.30), channel_id=1, source_target_pairs={{0,1},{1,2},{2,3},{4,5},{5,6},{6,7},{8,9},{9,10},{10,11},{12,13},{... | collective-permute-start | bytes 196616 | tf_op jit(solution)/shard_map/ppermute | solution.py:104
  49.3 0.4 fusion.91
  49.6 0.0 collective-permute-done.8
  49.7 0.9 %collective-permute-done.9 = f32[2,16,4,128]{3,2,1,0:T(4,128)S(1)} collective-permute-done((f32[2,16,4,128]{3,2,1,0:T(4,128)S(1)}, f32[2,16,4,128]{3,2,1,0:T(4,128)S(1)}, u32[]{:S(2)}, u32[]{:S(2)}) %collective-permute-start.9) | collective-permute-done | bytes 65568 | tf_op jit(solution)/shard_map/ppermute | solution.py:104
  50.6 0.4 select_maximum_fusion.5
  51.0 0.5 fusion.27
  51.5 0.4 fusion.102
  52.0 0.1 pad_maximum_fusion.2
  52.0 0.2 fusion.34
  52.2 0.0 copy-start.10
  52.3 0.6 %fusion.133 = (f32[2,8,16,128]{3,2,1,0:T(8,128)S(1)}, f32[2,8,16,128]{3,2,1,0:T(8,128)S(1)}, f32[2,8,16,128]{3,2,1,0:T(8,128)S(1)}, f32[2,8,16,128]{3,2,1,0:T(8,128)S(1)}) fusion(f32[2,8,24,128]{3,2,1,0:T(8,128)S(1)} %fusion.102, f32[2,16,16,128]{3,2,1,0:T(8,128)S(1)} %fusion.27, f32[2,16,16,128]{3,2,1,0:T(8,128)S(1)} %fusion.34, ...), kind=kLoop, calls=%fused_computation.220 | loop fusion | flops 3080192 | bytes 6422528 | tf_op jit(solution)/shard_map/add | solution.py:77
  52.8 0.3 copy-done.10
  53.1 0.7 %fusion.198 = (f32[8,16,128]{2,1,0:T(8,128)}, f32[8,16,128]{2,1,0:T(8,128)}, f32[8,16,128]{2,1,0:T(8,128)}, f32[8,16,128]{2,1,0:T(8,128)S(1)}) fusion(bf16[2,8,16,128]{3,2,1,0:T(8,128)(2,1)S(1)} %copy-done.10, f32[8,16,128]{2,1,0:T(8,128)S(1)} %fusion.91, f32[8,16,128]{2,1,0:T(8,128)S(1)} %copy-done.3, f32[2,8,16,128]{3,2,1,0:T(8,128)S(1)} %get-tuple-element.11, ...), kind=kLoop, calls=%fused_computation.331 | loop fusion | flops 327680 | bytes 1048576 | tf_op jit(solution)/shard_map/add | solution.py:208
  53.8 0.7 %add_add_fusion = (f32[8,16,128]{2,1,0:T(8,128)}, f32[8,16,128]{2,1,0:T(8,128)}) fusion(f32[8,16,128]{2,1,0:T(8,128)S(1)} %fusion.91, f32[8,16,128]{2,1,0:T(8,128)S(1)} %copy-done.3, f32[8,16,128]{2,1,0:T(8,128)S(1)} %get-tuple-element.8, f32[8,16,128]{2,1,0:T(8,128)S(1)} %copy-done.2, f32[2,8,16,128]{3,2,1,0:T(8,128)S(1)} %get-tuple-element.11, ...), kind=kLoop, calls=%fused_computation.333 | loop fusion | flops 147456 | bytes 589824 | tf_op jit(solution)/shard_map/add | solution.py:93
  (33 shorter events, 0.3 us)
Async XLA Ops:
  0.6 17.2 %copy-start = (f32[1024,128]{1,0:T(8,128)S(1)}, f32[1024,128]{1,0:T(8,128)}, u32[]{:S(2)}) copy-start(f32[1024,128]{1,0:T(8,128)} %param.24) | copy-start | bytes 1572868
  0.6 19.7 %copy-start.5 = (f32[8,16,128]{2,1,0:T(8,128)S(1)}, f32[8,16,128]{2,1,0:T(8,128)}, u32[]{:S(2)}) copy-start(f32[8,16,128]{2,1,0:T(8,128)} %param.21) | copy-start | bytes 196612
  0.7 19.9 %copy-start.6 = (f32[8,16,128]{2,1,0:T(8,128)S(1)}, f32[8,16,128]{2,1,0:T(8,128)}, u32[]{:S(2)}) copy-start(f32[8,16,128]{2,1,0:T(8,128)} %param.22) | copy-start | bytes 196612
  0.7 17.2 %copy-start.12 = (s32[128,1]{0,1:T(1,128)S(1)}, s32[128,1]{0,1:T(1,128)}, u32[]{:S(2)}) copy-start(s32[128,1]{0,1:T(1,128)} %param.26) | copy-start | bytes 1540
  0.7 17.2 %copy-start.13 = (s32[128]{0:T(128)S(1)}, s32[128]{0:T(128)}, u32[]{:S(2)}) copy-start(s32[128]{0:T(128)} %param.27) | copy-start | bytes 1540
  0.7 17.2 %copy-start.11 = (s32[2]{0:T(128)S(1)}, s32[2]{0:T(128)}, u32[]{:S(2)}) copy-start(s32[2]{0:T(128)} %param.25) | copy-start | bytes 28
  1.7 26.4 %collective-permute-start = (f32[2,8,16,128]{3,2,1,0:T(8,128)S(1)}, f32[2,8,16,128]{3,2,1,0:T(8,128)S(1)}, u32[]{:S(2)}, u32[]{:S(2)}) collective-permute-start(f32[2,8,16,128]{3,2,1,0:T(8,128)S(1)} %bitcast.84), channel_id=1, source_target_pairs={{0,4},{4,8},{8,12},{1,5},{5,9},{9,13},{2,6},{6,10},{10,14},{3,7},{... | collective-permute-start | bytes 393224 | tf_op jit(solution)/shard_map/ppermute | solution.py:104
  5.7 22.4 %collective-permute-start.1 = (f32[2,8,16,128]{3,2,1,0:T(8,128)S(1)}, f32[2,8,16,128]{3,2,1,0:T(8,128)S(1)}, u32[]{:S(2)}, u32[]{:S(2)}) collective-permute-start(f32[2,8,16,128]{3,2,1,0:T(8,128)S(1)} %bitcast.85), channel_id=1, source_target_pairs={{4,0},{8,4},{12,8},{5,1},{9,5},{13,9},{6,2},{10,6},{14,10},{7,3},{... | collective-permute-start | bytes 393224 | tf_op jit(solution)/shard_map/ppermute | solution.py:105
  10.1 18.0 %copy-start.1 = (f32[8,16,128]{2,1,0:T(8,128)S(1)}, f32[8,16,128]{2,1,0:T(8,128)}, u32[]{:S(2)}) copy-start(f32[8,16,128]{2,1,0:T(8,128)} %param.14) | copy-start | bytes 196612
  10.1 18.0 %copy-start.2 = (f32[8,16,128]{2,1,0:T(8,128)S(1)}, f32[8,16,128]{2,1,0:T(8,128)}, u32[]{:S(2)}) copy-start(f32[8,16,128]{2,1,0:T(8,128)} %param.15) | copy-start | bytes 196612
  12.5 24.2 %collective-permute-start.2 = (f32[28,16,128]{2,1,0:T(8,128)S(1)}, f32[28,16,128]{2,1,0:T(8,128)S(1)}, u32[]{:S(2)}, u32[]{:S(2)}) collective-permute-start(f32[28,16,128]{2,1,0:T(8,128)S(1)} %get-tuple-element.58), channel_id=1, source_target_pairs={{0,4},{4,8},{8,12},{1,5},{5,9},{9,13},{2,6},{6,10},{10,14},{3,7},{... | collective-permute-start | bytes 688136 | tf_op jit(solution)/shard_map/ppermute | solution.py:104
  16.5 20.3 %collective-permute-start.3 = (f32[28,16,128]{2,1,0:T(8,128)S(1)}, f32[28,16,128]{2,1,0:T(8,128)S(1)}, u32[]{:S(2)}, u32[]{:S(2)}) collective-permute-start(f32[28,16,128]{2,1,0:T(8,128)S(1)} %get-tuple-element.59), channel_id=1, source_target_pairs={{4,0},{8,4},{12,8},{5,1},{9,5},{13,9},{6,2},{10,6},{14,10},{7,3},{... | collective-permute-start | bytes 688136 | tf_op jit(solution)/shard_map/ppermute | solution.py:105
  18.2 5.8 %collective-permute-start.6 = (f32[4,128]{1,0:T(4,128)S(1)}, f32[4,128]{1,0:T(4,128)S(1)}, u32[]{:S(2)}, u32[]{:S(2)}) collective-permute-start(f32[4,128]{1,0:T(4,128)S(1)} %pad_maximum_fusion.11), channel_id=1, source_target_pairs={{0,4},{4,0},{8,12},{12,8},{1,5},{5,1},{9,13},{13,9},{2,6},{6,2},{1... | collective-permute-start | bytes 6152 | tf_op jit(solution)/shard_map/ppermute | solution.py:124
  24.0 3.4 %collective-permute-start.7 = (f32[4,256]{1,0:T(4,128)S(1)}, f32[4,256]{1,0:T(4,128)S(1)}, u32[]{:S(2)}, u32[]{:S(2)}) collective-permute-start(f32[4,256]{1,0:T(4,128)S(1)} %pad_maximum_fusion.10), channel_id=1, source_target_pairs={{0,8},{4,12},{8,0},{12,4},{1,9},{5,13},{9,1},{13,5},{2,10},{6,14},... | collective-permute-start | bytes 12296 | tf_op jit(solution)/shard_map/ppermute | solution.py:124
  28.2 10.6 %collective-permute-start.4 = (f32[2,24,4,128]{3,2,1,0:T(4,128)S(1)}, f32[2,24,4,128]{3,2,1,0:T(4,128)S(1)}, u32[]{:S(2)}, u32[]{:S(2)}) collective-permute-start(f32[2,24,4,128]{3,2,1,0:T(4,128)S(1)} %get-tuple-element.27), channel_id=1, source_target_pairs={{1,0},{2,1},{3,2},{5,4},{6,5},{7,6},{9,8},{10,9},{11,10},{13,12},{... | collective-permute-start | bytes 294920 | tf_op jit(solution)/shard_map/ppermute | solution.py:105
  33.7 5.1 %collective-permute-start.5 = (f32[2,24,4,128]{3,2,1,0:T(4,128)S(1)}, f32[2,24,4,128]{3,2,1,0:T(4,128)S(1)}, u32[]{:S(2)}, u32[]{:S(2)}) collective-permute-start(f32[2,24,4,128]{3,2,1,0:T(4,128)S(1)} %get-tuple-element.26), channel_id=1, source_target_pairs={{0,1},{1,2},{2,3},{4,5},{5,6},{6,7},{8,9},{9,10},{10,11},{12,13},{... | collective-permute-start | bytes 294920 | tf_op jit(solution)/shard_map/ppermute | solution.py:104
  40.3 1.1 %copy-start.8 = (f32[8,16,128]{2,1,0:T(8,128)S(1)}, f32[8,16,128]{2,1,0:T(8,128)}, u32[]{:S(2)}) copy-start(f32[8,16,128]{2,1,0:T(8,128)} %param.16) | copy-start | bytes 196612
  40.3 1.1 %copy-start.9 = (f32[8,16,128]{2,1,0:T(8,128)S(1)}, f32[8,16,128]{2,1,0:T(8,128)}, u32[]{:S(2)}) copy-start(f32[8,16,128]{2,1,0:T(8,128)} %param.17) | copy-start | bytes 196612
  41.5 1.1 %copy-start.3 = (f32[8,16,128]{2,1,0:T(8,128)S(1)}, f32[8,16,128]{2,1,0:T(8,128)}, u32[]{:S(2)}) copy-start(f32[8,16,128]{2,1,0:T(8,128)} %param.18) | copy-start | bytes 196612
  41.5 1.1 %copy-start.4 = (f32[8,16,128]{2,1,0:T(8,128)S(1)}, f32[8,16,128]{2,1,0:T(8,128)}, u32[]{:S(2)}) copy-start(f32[8,16,128]{2,1,0:T(8,128)} %param.20) | copy-start | bytes 196612
  42.5 0.8 %copy-start.7 = (f32[8,16,128]{2,1,0:T(8,128)S(1)}, f32[8,16,128]{2,1,0:T(8,128)}, u32[]{:S(2)}) copy-start(f32[8,16,128]{2,1,0:T(8,128)} %param.19) | copy-start | bytes 196612
  43.5 6.2 %collective-permute-start.8 = (f32[2,16,4,128]{3,2,1,0:T(4,128)S(1)}, f32[2,16,4,128]{3,2,1,0:T(4,128)S(1)}, u32[]{:S(2)}, u32[]{:S(2)}) collective-permute-start(f32[2,16,4,128]{3,2,1,0:T(4,128)S(1)} %get-tuple-element.31), channel_id=1, source_target_pairs={{1,0},{2,1},{3,2},{5,4},{6,5},{7,6},{9,8},{10,9},{11,10},{13,12},{... | collective-permute-start | bytes 196616 | tf_op jit(solution)/shard_map/ppermute | solution.py:105
  45.4 5.1 %collective-permute-start.9 = (f32[2,16,4,128]{3,2,1,0:T(4,128)S(1)}, f32[2,16,4,128]{3,2,1,0:T(4,128)S(1)}, u32[]{:S(2)}, u32[]{:S(2)}) collective-permute-start(f32[2,16,4,128]{3,2,1,0:T(4,128)S(1)} %get-tuple-element.30), channel_id=1, source_target_pairs={{0,1},{1,2},{2,3},{4,5},{5,6},{6,7},{8,9},{9,10},{10,11},{12,13},{... | collective-permute-start | bytes 196616 | tf_op jit(solution)/shard_map/ppermute | solution.py:104
  52.2 0.8 %copy-start.10 = (bf16[2,8,16,128]{3,2,1,0:T(8,128)(2,1)S(1)}, bf16[2,8,16,128]{3,2,1,0:T(8,128)(2,1)}, u32[]{:S(2)}) copy-start(bf16[2,8,16,128]{3,2,1,0:T(8,128)(2,1)} %param.23) | copy-start | bytes 196612

commit v8 on v4

--- a/solution.py
+++ b/solution.py
@@ -67,26 +67,32 @@
     return (centre, dxx, dyy, dzz, dxy, dxz, dyz)
 
 
-def advance(padded, previous, speed, epsilon, delta, theta, phi, source):
-    sx, sy, sz = (previous.shape[1], previous.shape[2], previous.shape[3])
-    centre, dxx, dyy, dzz, dxy, dxz, dyz = derivatives(padded, sx, sy, sz)
+def coefficients(epsilon, delta, theta, phi):
     axis_x = jnp.sin(theta) * jnp.cos(phi)
     axis_y = jnp.sin(theta) * jnp.sin(phi)
     axis_z = jnp.cos(theta)
-    rotated = (
-        axis_x * axis_x * dxx
-        + axis_y * axis_y * dyy
-        + axis_z * axis_z * dzz
-        + 2.0 * axis_x * axis_y * dxy
-        + 2.0 * axis_x * axis_z * dxz
-        + 2.0 * axis_y * axis_z * dyz
-    )
+    return (
+        axis_x * axis_x,
+        axis_y * axis_y,
+        axis_z * axis_z,
+        2.0 * axis_x * axis_y,
+        2.0 * axis_x * axis_z,
+        2.0 * axis_y * axis_z,
+        1.0 + 2.0 * epsilon,
+        jnp.sqrt(1.0 + 2.0 * delta),
+    )
+
+
+def advance(padded, previous, speed, coefs, source):
+    sx, sy, sz = (previous.shape[1], previous.shape[2], previous.shape[3])
+    centre, dxx, dyy, dzz, dxy, dxz, dyz = derivatives(padded, sx, sy, sz)
+    nxx, nyy, nzz, nxy, nxz, nyz, stretch, root_delta = coefs
+    rotated = nxx * dxx + nyy * dyy + nzz * dzz + nxy * dxy + nxz * dxz + nyz * dyz
     remainder = dxx + dyy + dzz - rotated
-    root_delta = jnp.sqrt(1.0 + 2.0 * delta)
     p_new = (
         2.0 * centre[0]
         - previous[0]
-        + speed * ((1.0 + 2.0 * epsilon) * remainder[0] + root_delta * rotated[1])
+        + speed * (stretch * remainder[0] + root_delta * rotated[1])
         + source
     )
     q_new = (
@@ -189,9 +195,11 @@
     (now_lo, prev_lo, params_lo), (now_hi, prev_hi, params_hi) = unpack(below), unpack(above)
     now_x = jnp.concatenate([now_lo, current, now_hi], axis=1)
     prev_x = jnp.concatenate([prev_lo, earlier, prev_hi], axis=1)
-    params_x = [
-        jnp.concatenate([params_lo[k], params[k], params_hi[k]], axis=0) for k in range(5)
-    ]
+    coefs = coefficients(epsilon, delta, theta, phi)
+    coefs_lo = coefficients(*params_lo[1:5])
+    coefs_hi = coefficients(*params_hi[1:5])
+    coefs_x = [jnp.concatenate(parts, axis=0) for parts in zip(coefs_lo, coefs, coefs_hi)]
+    speed_x = jnp.concatenate([params_lo[0], speed, params_hi[0]], axis=0)
     lo_y, hi_y = from_neighbours(now_x[:, :, sy - 4 :], now_x[:, :, :4], "gy")
     now_xy = pad_depth(jnp.concatenate([lo_y, now_x, hi_y], axis=2))
 
@@ -199,11 +207,11 @@
     source_0 = sources_over(arrived, arrived[0:1], (sx, sy, sz), -4, sx + 8)[0]
     source_1 = sources_over(arrived, arrived[1:2], (sx, sy, sz), 0, sx)[0]
 
-    mid_x = advance(now_xy, prev_x, *params_x, source_0)
+    mid_x = advance(now_xy, prev_x, speed_x, coefs_x, source_0)
     middle = mid_x[:, 4 : 4 + sx]
     lo_m, hi_m = from_neighbours(mid_x[:, :, sy - 4 :], mid_x[:, :, :4], "gy")
     mid_xy = pad_depth(jnp.concatenate([lo_m, mid_x, hi_m], axis=2))
-    final = advance(mid_xy, current, speed, epsilon, delta, theta, phi, source_1)
+    final = advance(mid_xy, current, speed, coefs, source_1)
     image = (
         snapshots[0].astype(jnp.float32) * middle[0] + snapshots[1].astype(jnp.float32) * final[0]
     )

time: 46.8 us -> 44.9 us (0.959)
  other arithmetic: 11.2 us -> 9.75 us
  waiting for transfers between devices: 13.7 us -> 13 us
    mul x3 -> x1, other arithmetic: 2.26 us -> 0.27 us  [coefficients(): axis_x * axis_x]
    ppermute x3, waiting for transfers between devices: 6.23 us -> 5.61 us  [from_neighbours(): below = lax.ppermute(low_part, axis, [(i, i + 1) for i in range(count - 1)])]
    add x2 -> x4, other arithmetic: 1.61 us -> 2.14 us  [the longest x2 1.61 us: advance(): nxx * dxx + nyy * dyy + nzz * dzz + nxy * dxy + nxz * dxz + nyz * dyz]
  transfers between devices with their start and end apart: 8 -> 8, of which waited for: 3 -> 3; matrix products, arithmetic and copies ran while one was open for 7% -> 9% of each run, Pallas kernels for 0% -> 0%
where the time goes in v8:
time: 44.9 us; the launch traced here: 44.4 us
  starting transfers between devices  16.2 us (36%)
  waiting for transfers between devices  13 us (29%)
  other arithmetic  9.75 us (22%)
  local copies, waits for them, and re-layouts  2.4 us (5%)
  matrix products  1.84 us (4%)
  between operations  1.19 us (3%)
    ppermute x3, starting transfers between devices, from_neighbours(): lax.ppermute(high_part, axis, [(i + 1, i) for i in range(count - 1)])  7.48 us
    ppermute x2, waiting for transfers between devices, gather_column(): lax.ppermute(arrived, 'gx', [(i, i ^ step) for i in range(groups)])  7.41 us
    ppermute x3, starting transfers between devices, from_neighbours(): below = lax.ppermute(low_part, axis, [(i, i + 1) for i in range(count - 1)])  6.1 us
    ppermute x3, waiting for transfers between devices, from_neighbours(): below = lax.ppermute(low_part, axis, [(i, i + 1) for i in range(count - 1)])  5.61 us
    ppermute x2, starting transfers between devices, gather_column(): lax.ppermute(arrived, 'gx', [(i, i ^ step) for i in range(groups)])  2.65 us
    unnamed x32, local copies, waits for them, and re-layouts  2.08 us
    add x2, other arithmetic, advance(): nxx * dxx + nyy * dyy + nzz * dzz + nxy * dxy + nxz * dxz + nyz * dyz  1.61 us
    add x2, other arithmetic, derivatives(): dz_xwide + weight * (padded[:, :, 4:4 + sy, 4 + k:4 + k + sz] - padded[:,...  1.58 us
  transfers between devices with their start and end apart: 8, of which 3 were waited for; matrix products, arithmetic and copies ran while one was open for 9% of the time, Pallas kernels for 0%

profile of v8, /device:TPU:30, one launch (start us, length us, event | category | flops | bytes accessed | tf_op | source)
XLA Modules:
  0.0 44.4 jit_solution(5194009299521718598)
XLA Ops:
  0.6 0.0 copy-start
  0.7 0.0 copy-start.8
  0.7 0.0 copy-start.9
  0.7 0.0 copy-start.3
  0.7 0.0 copy-start.5
  0.7 0.0 copy-start.4
  0.7 0.0 copy-start.6
  0.7 0.0 copy-start.7
  0.7 0.7 %convert_bitcast_fusion = f32[1,128]{1,0:T(1,128)S(1)} fusion(s32[128,1]{0,1:T(1,128)} %param.26), kind=kLoop, calls=%fused_computation.409 | loop fusion | flops 128 | bytes 1024 | tf_op jit(solution)/shard_map/convert_element_type | solution.py:124
  1.4 0.7 %convert_bitcast_fusion.1 = f32[1,128]{1,0:T(1,128)S(1)} fusion(s32[128]{0:T(128)} %param.27), kind=kLoop, calls=%fused_computation.410 | loop fusion | flops 128 | bytes 1024 | tf_op jit(solution)/shard_map/broadcast_in_dim | solution.py:124
  2.1 0.0 copy-done
  2.1 0.9 %fusion.201 = f32[2,128]{1,0:T(2,128)S(1)} fusion(f32[1024,128]{1,0:T(8,128)S(1)} %copy-done, s32[2]{0:T(128)} %param.25), kind=kOutput, calls=%fused_computation.378 | convolution fusion | flops 3147776 | bytes 525320 | tf_op jit(solution)/shard_map/dot_general | solution.py:120
  3.1 0.5 %collective-permute-start.4 = (f32[4,128]{1,0:T(4,128)S(1)}, f32[4,128]{1,0:T(4,128)S(1)}, u32[]{:S(2)}, u32[]{:S(2)}) collective-permute-start(f32[4,128]{1,0:T(4,128)S(1)} %pad_maximum_fusion.15), channel_id=1, source_target_pairs={{0,4},{4,0},{8,12},{12,8},{1,5},{5,1},{9,13},{13,9},{2,6},{6,2},{1... | collective-permute-start | bytes 6152 | tf_op jit(solution)/shard_map/ppermute | solution.py:130
  3.6 0.8 %constant_dynamic-update-slice_fusion.17 = f32[44,16,128]{2,1,0:T(8,128)S(1)} fusion(f32[8,16,128]{2,1,0:T(8,128)} %param.14), kind=kLoop, calls=%fused_computation.351 | loop fusion | bytes 131072
  4.4 0.8 %constant_dynamic-update-slice_fusion.16 = f32[44,16,128]{2,1,0:T(8,128)S(1)} fusion(f32[44,16,128]{2,1,0:T(8,128)S(1)} %constant_dynamic-update-slice_fusion.17, f32[8,16,128]{2,1,0:T(8,128)} %param.15), kind=kLoop, calls=%fused_computation.350 | loop fusion | bytes 131072
  5.3 0.0 copy-done.8
  5.3 0.0 copy-done.9
  5.4 0.0 copy-done.3
  5.4 0.0 copy-done.5
  5.4 0.0 copy-done.4
  5.4 0.0 copy-done.6
  5.5 0.0 copy-done.7
  5.5 0.0 copy-start.1
  5.5 0.0 copy-start.2
  5.5 3.6 %collective-permute-start.1 = (f32[44,16,128]{2,1,0:T(8,128)S(1)}, f32[44,16,128]{2,1,0:T(8,128)S(1)}, u32[]{:S(2)}, u32[]{:S(2)}) collective-permute-start(f32[44,16,128]{2,1,0:T(8,128)S(1)} %get-tuple-element.61), channel_id=1, source_target_pairs={{4,0},{8,4},{12,8},{5,1},{9,5},{13,9},{6,2},{10,6},{14,10},{7,3},{... | collective-permute-start | bytes 1081352 | tf_op jit(solution)/shard_map/ppermute | solution.py:111
  9.2 1.3 %collective-permute-start = (f32[44,16,128]{2,1,0:T(8,128)S(1)}, f32[44,16,128]{2,1,0:T(8,128)S(1)}, u32[]{:S(2)}, u32[]{:S(2)}) collective-permute-start(f32[44,16,128]{2,1,0:T(8,128)S(1)} %get-tuple-element.60), channel_id=1, source_target_pairs={{0,4},{4,8},{8,12},{1,5},{5,9},{9,13},{2,6},{6,10},{10,14},{3,7},{... | collective-permute-start | bytes 1081352 | tf_op jit(solution)/shard_map/ppermute | solution.py:110
  10.5 0.2 fusion.228
  10.8 0.3 fusion.212
  11.0 0.0 collective-permute-done.4
  11.1 2.1 %collective-permute-start.5 = (f32[4,256]{1,0:T(4,128)S(1)}, f32[4,256]{1,0:T(4,128)S(1)}, u32[]{:S(2)}, u32[]{:S(2)}) collective-permute-start(f32[4,256]{1,0:T(4,128)S(1)} %pad_maximum_fusion.14), channel_id=1, source_target_pairs={{0,8},{4,12},{8,0},{12,4},{1,9},{5,13},{9,1},{13,5},{2,10},{6,14},... | collective-permute-start | bytes 12296 | tf_op jit(solution)/shard_map/ppermute | solution.py:130
  13.2 7.4 %collective-permute-done.5 = f32[4,256]{1,0:T(4,128)S(1)} collective-permute-done((f32[4,256]{1,0:T(4,128)S(1)}, f32[4,256]{1,0:T(4,128)S(1)}, u32[]{:S(2)}, u32[]{:S(2)}) %collective-permute-start.5) | collective-permute-done | bytes 4128 | tf_op jit(solution)/shard_map/ppermute | solution.py:130
  20.7 0.5 %fusion.2 = f32[16,16,128]{2,1,0:T(8,128)S(1)} fusion(f32[512]{0:T(512)S(1)} %bitcast.96, s32[16,16]{1,0:T(8,128)S(1)} %multiply_add_fusion.1, s32[512]{0:T(512)S(1)} %bitcast.97, s32[512]{0:T(512)S(1)} %add_select_fusion), kind=kOutput, calls=%fused_computation.36 | convolution fusion | flops 201654272 | bytes 138240 | tf_op jit(solution)/shard_map/cpr,rz->cpz/dot_general | solution.py:150
  21.2 0.0 collective-permute-done.1
  21.3 0.0 collective-permute-done
  21.3 0.0 copy-done.1
  21.3 0.0 copy-done.2
  21.4 1.9 %collective-permute-start.2 = (f32[2,24,4,128]{3,2,1,0:T(4,128)S(1)}, f32[2,24,4,128]{3,2,1,0:T(4,128)S(1)}, u32[]{:S(2)}, u32[]{:S(2)}) collective-permute-start(f32[2,24,4,128]{3,2,1,0:T(4,128)S(1)} %get-tuple-element.27), channel_id=1, source_target_pairs={{1,0},{2,1},{3,2},{5,4},{6,5},{7,6},{9,8},{10,9},{11,10},{13,12},{... | collective-permute-start | bytes 294920 | tf_op jit(solution)/shard_map/ppermute | solution.py:111
  23.3 2.4 %collective-permute-start.3 = (f32[2,24,4,128]{3,2,1,0:T(4,128)S(1)}, f32[2,24,4,128]{3,2,1,0:T(4,128)S(1)}, u32[]{:S(2)}, u32[]{:S(2)}) collective-permute-start(f32[2,24,4,128]{3,2,1,0:T(4,128)S(1)} %get-tuple-element.26), channel_id=1, source_target_pairs={{0,1},{1,2},{2,3},{4,5},{5,6},{6,7},{8,9},{9,10},{10,11},{12,13},{... | collective-permute-start | bytes 294920 | tf_op jit(solution)/shard_map/ppermute | solution.py:110
  25.8 0.3 fusion.197
  26.1 0.3 fusion.198
  26.4 0.0 collective-permute-done.2
  26.4 2.8 %collective-permute-done.3 = f32[2,24,4,128]{3,2,1,0:T(4,128)S(1)} collective-permute-done((f32[2,24,4,128]{3,2,1,0:T(4,128)S(1)}, f32[2,24,4,128]{3,2,1,0:T(4,128)S(1)}, u32[]{:S(2)}, u32[]{:S(2)}) %collective-permute-start.3) | collective-permute-done | bytes 98336 | tf_op jit(solution)/shard_map/ppermute | solution.py:110
  29.3 0.6 %select_maximum_fusion = f32[2,24,24,136]{3,2,1,0:T(8,128)S(1)} fusion(f32[2,24,4,128]{3,2,1,0:T(4,128)S(1)} %collective-permute-done.2, f32[2,24,4,128]{3,2,1,0:T(4,128)S(1)} %collective-permute-done.3, f32[2,8,16,128]{3,2,1,0:T(8,128)S(1)} %bitcast.74, f32[2,8,16,128]{3,2,1,0:T(8,128)S(1)} %bitcast.78, f32[1,8,16,128]{3,2,1,0:T(8,128)S(1)} %bitcast.86, ...), kind=kLoop, calls=%fused_computation.4 | loop fusion | flops 2193408 | bytes 1216512 | tf_op jit(solution)/shard_map/concatenate | solution.py:204
  29.8 0.8 %fusion.6 = f32[2,16,24,128]{3,2,1,0:T(8,128)S(1)} fusion(f32[2,24,24,136]{3,2,1,0:T(8,128)S(1)} %select_maximum_fusion), kind=kLoop, calls=%fused_computation.41 | loop fusion | flops 1081344 | bytes 3538944 | tf_op jit(solution)/shard_map/add | solution.py:53
  30.6 0.1 pad_maximum_fusion
  30.7 1.0 %fusion.13 = (f32[2,24,16,128]{3,2,1,0:T(8,128)S(1)}, f32[2,24,16,128]{3,2,1,0:T(8,128)S(1)}) fusion(f32[2,24,24,136]{3,2,1,0:T(8,128)S(1)} %select_maximum_fusion, f32[2,24,20,128]{3,2,1,0:T(8,128)S(1)} %get-tuple-element.25, f32[2,24,20,128]{3,2,1,0:T(8,128)S(1)} %get-tuple-element.24), kind=kLoop, calls=%fused_computation.52 | loop fusion | flops 2162688 | bytes 7077888 | tf_op jit(solution)/shard_map/add | solution.py:49
  31.8 1.0 %fusion.43 = (f32[2,16,16,128]{3,2,1,0:T(8,128)S(1)}, f32[2,16,16,128]{3,2,1,0:T(8,128)S(1)}, f32[2,16,16,128]{3,2,1,0:T(8,128)S(1)}, f32[2,16,16,128]{3,2,1,0:T(8,128)S(1)}) fusion(f32[2,16,24,128]{3,2,1,0:T(8,128)S(1)} %fusion.6, f32[2,24,16,128]{3,2,1,0:T(8,128)S(1)} %get-tuple-element.81, f32[2,24,16,128]{3,2,1,0:T(8,128)S(1)} %get-tuple-element.82, ...), kind=kLoop, calls=%fused_computation.101 | loop fusion | flops 5570560 | bytes 14548992 | tf_op jit(solution)/shard_map/add | solution.py:90
  32.8 0.1 fusion.176
  32.9 0.1 fusion.181
  33.0 1.9 %collective-permute-start.6 = (f32[2,16,4,128]{3,2,1,0:T(4,128)S(1)}, f32[2,16,4,128]{3,2,1,0:T(4,128)S(1)}, u32[]{:S(2)}, u32[]{:S(2)}) collective-permute-start(f32[2,16,4,128]{3,2,1,0:T(4,128)S(1)} %get-tuple-element.49), channel_id=1, source_target_pairs={{1,0},{2,1},{3,2},{5,4},{6,5},{7,6},{9,8},{10,9},{11,10},{13,12},{... | collective-permute-start | bytes 196616 | tf_op jit(solution)/shard_map/ppermute | solution.py:111
  35.0 2.4 %collective-permute-start.7 = (f32[2,16,4,128]{3,2,1,0:T(4,128)S(1)}, f32[2,16,4,128]{3,2,1,0:T(4,128)S(1)}, u32[]{:S(2)}, u32[]{:S(2)}) collective-permute-start(f32[2,16,4,128]{3,2,1,0:T(4,128)S(1)} %get-tuple-element.48), channel_id=1, source_target_pairs={{0,1},{1,2},{2,3},{4,5},{5,6},{6,7},{8,9},{9,10},{10,11},{12,13},{... | collective-permute-start | bytes 196616 | tf_op jit(solution)/shard_map/ppermute | solution.py:110
  37.4 0.4 fusion.91
  37.8 0.0 collective-permute-done.6
  37.8 2.8 %collective-permute-done.7 = f32[2,16,4,128]{3,2,1,0:T(4,128)S(1)} collective-permute-done((f32[2,16,4,128]{3,2,1,0:T(4,128)S(1)}, f32[2,16,4,128]{3,2,1,0:T(4,128)S(1)}, u32[]{:S(2)}, u32[]{:S(2)}) %collective-permute-start.7) | collective-permute-done | bytes 65568 | tf_op jit(solution)/shard_map/ppermute | solution.py:110
  40.5 0.4 select_maximum_fusion.5
  40.9 0.4 fusion.102
  41.4 0.5 %fusion.27 = f32[2,16,16,128]{3,2,1,0:T(8,128)S(1)} fusion(f32[2,16,24,136]{3,2,1,0:T(8,128)S(1)} %select_maximum_fusion.5), kind=kLoop, calls=%fused_computation.77 | loop fusion | flops 720896 | bytes 2359296 | tf_op jit(solution)/shard_map/add | solution.py:49
  41.9 0.1 pad_maximum_fusion.2
  42.0 0.2 fusion.34
  42.2 0.0 copy-start.10
  42.2 0.6 %fusion.133 = (f32[2,8,16,128]{3,2,1,0:T(8,128)S(1)}, f32[2,8,16,128]{3,2,1,0:T(8,128)S(1)}, f32[2,8,16,128]{3,2,1,0:T(8,128)S(1)}, f32[2,8,16,128]{3,2,1,0:T(8,128)S(1)}) fusion(f32[2,8,24,128]{3,2,1,0:T(8,128)S(1)} %fusion.102, f32[2,16,16,128]{3,2,1,0:T(8,128)S(1)} %fusion.27, f32[2,16,16,128]{3,2,1,0:T(8,128)S(1)} %fusion.34, ...), kind=kLoop, calls=%fused_computation.220 | loop fusion | flops 3080192 | bytes 6422528 | tf_op jit(solution)/shard_map/add | solution.py:90
  42.8 0.3 copy-done.10
  43.1 0.7 %fusion.192 = (f32[8,16,128]{2,1,0:T(8,128)}, f32[8,16,128]{2,1,0:T(8,128)}, f32[8,16,128]{2,1,0:T(8,128)}, f32[8,16,128]{2,1,0:T(8,128)S(1)}) fusion(bf16[2,8,16,128]{3,2,1,0:T(8,128)(2,1)S(1)} %copy-done.10, f32[8,16,128]{2,1,0:T(8,128)S(1)} %fusion.91, f32[8,16,128]{2,1,0:T(8,128)S(1)} %copy-done.3, f32[2,8,16,128]{3,2,1,0:T(8,128)S(1)} %get-tuple-element.11, ...), kind=kLoop, calls=%fused_computation.323 | loop fusion | flops 327680 | bytes 1048576 | tf_op jit(solution)/shard_map/add | solution.py:216
  43.8 0.7 %add_add_fusion = (f32[8,16,128]{2,1,0:T(8,128)}, f32[8,16,128]{2,1,0:T(8,128)}) fusion(f32[8,16,128]{2,1,0:T(8,128)S(1)} %fusion.91, f32[8,16,128]{2,1,0:T(8,128)S(1)} %copy-done.3, f32[8,16,128]{2,1,0:T(8,128)S(1)} %get-tuple-element.8, f32[8,16,128]{2,1,0:T(8,128)S(1)} %copy-done.2, f32[2,8,16,128]{3,2,1,0:T(8,128)S(1)} %get-tuple-element.11, ...), kind=kLoop, calls=%fused_computation.325 | loop fusion | flops 147456 | bytes 589824 | tf_op jit(solution)/shard_map/add | solution.py:99
  (30 shorter events, 0.4 us)
Async XLA Ops:
  0.6 1.5 %copy-start = (f32[1024,128]{1,0:T(8,128)S(1)}, f32[1024,128]{1,0:T(8,128)}, u32[]{:S(2)}) copy-start(f32[1024,128]{1,0:T(8,128)} %param.24) | copy-start | bytes 1572868
  0.7 4.7 %copy-start.8 = (f32[8,16,128]{2,1,0:T(8,128)S(1)}, f32[8,16,128]{2,1,0:T(8,128)}, u32[]{:S(2)}) copy-start(f32[8,16,128]{2,1,0:T(8,128)} %param.16) | copy-start | bytes 196612
  0.7 4.7 %copy-start.9 = (f32[8,16,128]{2,1,0:T(8,128)S(1)}, f32[8,16,128]{2,1,0:T(8,128)}, u32[]{:S(2)}) copy-start(f32[8,16,128]{2,1,0:T(8,128)} %param.17) | copy-start | bytes 196612
  0.7 4.7 %copy-start.3 = (f32[8,16,128]{2,1,0:T(8,128)S(1)}, f32[8,16,128]{2,1,0:T(8,128)}, u32[]{:S(2)}) copy-start(f32[8,16,128]{2,1,0:T(8,128)} %param.18) | copy-start | bytes 196612
  0.7 4.7 %copy-start.5 = (f32[8,16,128]{2,1,0:T(8,128)S(1)}, f32[8,16,128]{2,1,0:T(8,128)}, u32[]{:S(2)}) copy-start(f32[8,16,128]{2,1,0:T(8,128)} %param.19) | copy-start | bytes 196612
  0.7 4.7 %copy-start.4 = (f32[8,16,128]{2,1,0:T(8,128)S(1)}, f32[8,16,128]{2,1,0:T(8,128)}, u32[]{:S(2)}) copy-start(f32[8,16,128]{2,1,0:T(8,128)} %param.20) | copy-start | bytes 196612
  0.7 4.7 %copy-start.6 = (f32[8,16,128]{2,1,0:T(8,128)S(1)}, f32[8,16,128]{2,1,0:T(8,128)}, u32[]{:S(2)}) copy-start(f32[8,16,128]{2,1,0:T(8,128)} %param.21) | copy-start | bytes 196612
  0.7 4.8 %copy-start.7 = (f32[8,16,128]{2,1,0:T(8,128)S(1)}, f32[8,16,128]{2,1,0:T(8,128)}, u32[]{:S(2)}) copy-start(f32[8,16,128]{2,1,0:T(8,128)} %param.22) | copy-start | bytes 196612
  3.1 8.0 %collective-permute-start.4 = (f32[4,128]{1,0:T(4,128)S(1)}, f32[4,128]{1,0:T(4,128)S(1)}, u32[]{:S(2)}, u32[]{:S(2)}) collective-permute-start(f32[4,128]{1,0:T(4,128)S(1)} %pad_maximum_fusion.15), channel_id=1, source_target_pairs={{0,4},{4,0},{8,12},{12,8},{1,5},{5,1},{9,13},{13,9},{2,6},{6,2},{1... | collective-permute-start | bytes 6152 | tf_op jit(solution)/shard_map/ppermute | solution.py:130
  5.5 15.8 %copy-start.1 = (f32[8,16,128]{2,1,0:T(8,128)S(1)}, f32[8,16,128]{2,1,0:T(8,128)}, u32[]{:S(2)}) copy-start(f32[8,16,128]{2,1,0:T(8,128)} %param.14) | copy-start | bytes 196612
  5.5 15.8 %copy-start.2 = (f32[8,16,128]{2,1,0:T(8,128)S(1)}, f32[8,16,128]{2,1,0:T(8,128)}, u32[]{:S(2)}) copy-start(f32[8,16,128]{2,1,0:T(8,128)} %param.15) | copy-start | bytes 196612
  5.5 15.7 %collective-permute-start.1 = (f32[44,16,128]{2,1,0:T(8,128)S(1)}, f32[44,16,128]{2,1,0:T(8,128)S(1)}, u32[]{:S(2)}, u32[]{:S(2)}) collective-permute-start(f32[44,16,128]{2,1,0:T(8,128)S(1)} %get-tuple-element.61), channel_id=1, source_target_pairs={{4,0},{8,4},{12,8},{5,1},{9,5},{13,9},{6,2},{10,6},{14,10},{7,3},{... | collective-permute-start | bytes 1081352 | tf_op jit(solution)/shard_map/ppermute | solution.py:111
  9.2 12.1 %collective-permute-start = (f32[44,16,128]{2,1,0:T(8,128)S(1)}, f32[44,16,128]{2,1,0:T(8,128)S(1)}, u32[]{:S(2)}, u32[]{:S(2)}) collective-permute-start(f32[44,16,128]{2,1,0:T(8,128)S(1)} %get-tuple-element.60), channel_id=1, source_target_pairs={{0,4},{4,8},{8,12},{1,5},{5,9},{9,13},{2,6},{6,10},{10,14},{3,7},{... | collective-permute-start | bytes 1081352 | tf_op jit(solution)/shard_map/ppermute | solution.py:110
  11.1 9.5 %collective-permute-start.5 = (f32[4,256]{1,0:T(4,128)S(1)}, f32[4,256]{1,0:T(4,128)S(1)}, u32[]{:S(2)}, u32[]{:S(2)}) collective-permute-start(f32[4,256]{1,0:T(4,128)S(1)} %pad_maximum_fusion.14), channel_id=1, source_target_pairs={{0,8},{4,12},{8,0},{12,4},{1,9},{5,13},{9,1},{13,5},{2,10},{6,14},... | collective-permute-start | bytes 12296 | tf_op jit(solution)/shard_map/ppermute | solution.py:130
  21.4 5.0 %collective-permute-start.2 = (f32[2,24,4,128]{3,2,1,0:T(4,128)S(1)}, f32[2,24,4,128]{3,2,1,0:T(4,128)S(1)}, u32[]{:S(2)}, u32[]{:S(2)}) collective-permute-start(f32[2,24,4,128]{3,2,1,0:T(4,128)S(1)} %get-tuple-element.27), channel_id=1, source_target_pairs={{1,0},{2,1},{3,2},{5,4},{6,5},{7,6},{9,8},{10,9},{11,10},{13,12},{... | collective-permute-start | bytes 294920 | tf_op jit(solution)/shard_map/ppermute | solution.py:111
  23.3 5.9 %collective-permute-start.3 = (f32[2,24,4,128]{3,2,1,0:T(4,128)S(1)}, f32[2,24,4,128]{3,2,1,0:T(4,128)S(1)}, u32[]{:S(2)}, u32[]{:S(2)}) collective-permute-start(f32[2,24,4,128]{3,2,1,0:T(4,128)S(1)} %get-tuple-element.26), channel_id=1, source_target_pairs={{0,1},{1,2},{2,3},{4,5},{5,6},{6,7},{8,9},{9,10},{10,11},{12,13},{... | collective-permute-start | bytes 294920 | tf_op jit(solution)/shard_map/ppermute | solution.py:110
  33.0 4.7 %collective-permute-start.6 = (f32[2,16,4,128]{3,2,1,0:T(4,128)S(1)}, f32[2,16,4,128]{3,2,1,0:T(4,128)S(1)}, u32[]{:S(2)}, u32[]{:S(2)}) collective-permute-start(f32[2,16,4,128]{3,2,1,0:T(4,128)S(1)} %get-tuple-element.49), channel_id=1, source_target_pairs={{1,0},{2,1},{3,2},{5,4},{6,5},{7,6},{9,8},{10,9},{11,10},{13,12},{... | collective-permute-start | bytes 196616 | tf_op jit(solution)/shard_map/ppermute | solution.py:111
  35.0 5.6 %collective-permute-start.7 = (f32[2,16,4,128]{3,2,1,0:T(4,128)S(1)}, f32[2,16,4,128]{3,2,1,0:T(4,128)S(1)}, u32[]{:S(2)}, u32[]{:S(2)}) collective-permute-start(f32[2,16,4,128]{3,2,1,0:T(4,128)S(1)} %get-tuple-element.48), channel_id=1, source_target_pairs={{0,1},{1,2},{2,3},{4,5},{5,6},{6,7},{8,9},{9,10},{10,11},{12,13},{... | collective-permute-start | bytes 196616 | tf_op jit(solution)/shard_map/ppermute | solution.py:110
  42.2 0.8 %copy-start.10 = (bf16[2,8,16,128]{3,2,1,0:T(8,128)(2,1)S(1)}, bf16[2,8,16,128]{3,2,1,0:T(8,128)(2,1)}, u32[]{:S(2)}) copy-start(bf16[2,8,16,128]{3,2,1,0:T(8,128)(2,1)} %param.23) | copy-start | bytes 196612

commit v9 on v8

--- a/solution.py
+++ b/solution.py
@@ -204,6 +204,7 @@
     now_xy = pad_depth(jnp.concatenate([lo_y, now_x, hi_y], axis=2))
 
     arrived = gather_column(traces, time_steps, rec_owner, rec_local)
+    arrived = arrived + 0.0 * (lo_y[0, 0, 0, 0] + hi_y[0, 0, 0, 0])
     source_0 = sources_over(arrived, arrived[0:1], (sx, sy, sz), -4, sx + 8)[0]
     source_1 = sources_over(arrived, arrived[1:2], (sx, sy, sz), 0, sx)[0]
 

time: 44.9 us -> 48.4 us (1.078)
  starting transfers between devices: 16.2 us -> 18.7 us
  between operations: 1.19 us -> 2.49 us
  waiting for transfers between devices: 13 us -> 11.8 us
  local copies, waits for them, and re-layouts: 2.4 us -> 3.42 us
    ppermute x2, waiting for transfers between devices: 7.41 us -> 0.01 us  [gather_column(): lax.ppermute(arrived, 'gx', [(i, i ^ step) for i in range(groups)])]
    ppermute x3, waiting for transfers between devices: 0.01 us -> 4.34 us  [from_neighbours(): lax.ppermute(high_part, axis, [(i + 1, i) for i in range(count - 1)])]
    ppermute x3, starting transfers between devices: 7.48 us -> 10.9 us  [from_neighbours(): lax.ppermute(high_part, axis, [(i + 1, i) for i in range(count - 1)])]
    ppermute x3, waiting for transfers between devices: 5.61 us -> 7.41 us  [from_neighbours(): below = lax.ppermute(low_part, axis, [(i, i + 1) for i in range(count - 1)])]
    slice x0 -> x2, local copies, waits for them, and re-layouts: none -> 1.02 us  [local(): arrived = arrived + 0.0 * (lo_y[0, 0, 0, 0] + hi_y[0, 0, 0, 0])]
    ppermute x3, starting transfers between devices: 6.1 us -> 5.13 us  [from_neighbours(): below = lax.ppermute(low_part, axis, [(i, i + 1) for i in range(count - 1)])]
  transfers between devices with their start and end apart: 8 -> 8, of which waited for: 3 -> 4; matrix products, arithmetic and copies ran while one was open for 9% -> 9% of each run, Pallas kernels for 0% -> 0%
where the time goes in v9:
time: 48.4 us; the launch traced here: 47.9 us
  starting transfers between devices  18.7 us (39%)
  waiting for transfers between devices  11.8 us (24%)
  other arithmetic  9.75 us (20%)
  local copies, waits for them, and re-layouts  3.42 us (7%)
  between operations  2.49 us (5%)
  matrix products  1.84 us (4%)
    ppermute x3, starting transfers between devices, from_neighbours(): lax.ppermute(high_part, axis, [(i + 1, i) for i in range(count - 1)])  10.9 us
    ppermute x3, waiting for transfers between devices, from_neighbours(): below = lax.ppermute(low_part, axis, [(i, i + 1) for i in range(count - 1)])  7.41 us
    ppermute x3, starting transfers between devices, from_neighbours(): below = lax.ppermute(low_part, axis, [(i, i + 1) for i in range(count - 1)])  5.13 us
    ppermute x3, waiting for transfers between devices, from_neighbours(): lax.ppermute(high_part, axis, [(i + 1, i) for i in range(count - 1)])  4.34 us
    ppermute x2, starting transfers between devices, gather_column(): lax.ppermute(arrived, 'gx', [(i, i ^ step) for i in range(groups)])  2.65 us
    unnamed x32, local copies, waits for them, and re-layouts  2.08 us
    add x2, other arithmetic, advance(): nxx * dxx + nyy * dyy + nzz * dzz + nxy * dxy + nxz * dxz + nyz * dyz  1.61 us
    add x2, other arithmetic, derivatives(): dz_xwide + weight * (padded[:, :, 4:4 + sy, 4 + k:4 + k + sz] - padded[:,...  1.58 us
  transfers between devices with their start and end apart: 8, of which 4 were waited for; matrix products, arithmetic and copies ran while one was open for 9% of the time, Pallas kernels for 0%

profile of v9, /device:TPU:30, one launch (start us, length us, event | category | flops | bytes accessed | tf_op | source)
XLA Modules:
  0.0 47.9 jit_solution(10531574300845566411)
XLA Ops:
  0.6 0.0 copy-start
  0.7 0.0 copy-start.8
  0.7 0.0 copy-start.9
  0.7 0.0 copy-start.3
  0.7 0.0 copy-start.5
  0.7 0.0 copy-start.4
  0.7 0.0 copy-start.6
  0.7 0.0 copy-start.7
  0.7 0.7 %convert_bitcast_fusion = f32[1,128]{1,0:T(1,128)S(1)} fusion(s32[128,1]{0,1:T(1,128)} %param.26), kind=kLoop, calls=%fused_computation.409 | loop fusion | flops 128 | bytes 1024 | tf_op jit(solution)/shard_map/convert_element_type | solution.py:124
  1.4 0.7 %convert_bitcast_fusion.1 = f32[1,128]{1,0:T(1,128)S(1)} fusion(s32[128]{0:T(128)} %param.27), kind=kLoop, calls=%fused_computation.410 | loop fusion | flops 128 | bytes 1024 | tf_op jit(solution)/shard_map/broadcast_in_dim | solution.py:124
  2.1 0.0 copy-done
  2.1 0.9 %fusion.201 = f32[2,128]{1,0:T(2,128)S(1)} fusion(f32[1024,128]{1,0:T(8,128)S(1)} %copy-done, s32[2]{0:T(128)} %param.25), kind=kOutput, calls=%fused_computation.378 | convolution fusion | flops 3147776 | bytes 525320 | tf_op jit(solution)/shard_map/dot_general | solution.py:120
  3.1 0.5 %collective-permute-start.4 = (f32[4,128]{1,0:T(4,128)S(1)}, f32[4,128]{1,0:T(4,128)S(1)}, u32[]{:S(2)}, u32[]{:S(2)}) collective-permute-start(f32[4,128]{1,0:T(4,128)S(1)} %pad_maximum_fusion.14), channel_id=1, source_target_pairs={{0,4},{4,0},{8,12},{12,8},{1,5},{5,1},{9,13},{13,9},{2,6},{6,2},{1... | collective-permute-start | bytes 6152 | tf_op jit(solution)/shard_map/ppermute | solution.py:130
  3.6 0.8 %constant_dynamic-update-slice_fusion.17 = f32[44,16,128]{2,1,0:T(8,128)S(1)} fusion(f32[8,16,128]{2,1,0:T(8,128)} %param.14), kind=kLoop, calls=%fused_computation.351 | loop fusion | bytes 131072
  4.4 0.8 %constant_dynamic-update-slice_fusion.16 = f32[44,16,128]{2,1,0:T(8,128)S(1)} fusion(f32[44,16,128]{2,1,0:T(8,128)S(1)} %constant_dynamic-update-slice_fusion.17, f32[8,16,128]{2,1,0:T(8,128)} %param.15), kind=kLoop, calls=%fused_computation.350 | loop fusion | bytes 131072
  5.3 0.0 copy-done.8
  5.3 0.0 copy-done.9
  5.4 0.0 copy-start.1
  5.4 0.0 copy-start.2
  5.4 0.0 copy-done.3
  5.4 0.0 copy-done.4
  5.5 0.0 copy-done.7
  5.5 3.5 %collective-permute-start.1 = (f32[44,16,128]{2,1,0:T(8,128)S(1)}, f32[44,16,128]{2,1,0:T(8,128)S(1)}, u32[]{:S(2)}, u32[]{:S(2)}) collective-permute-start(f32[44,16,128]{2,1,0:T(8,128)S(1)} %get-tuple-element.61), channel_id=1, source_target_pairs={{4,0},{8,4},{12,8},{5,1},{9,5},{13,9},{6,2},{10,6},{14,10},{7,3},{... | collective-permute-start | bytes 1081352 | tf_op jit(solution)/shard_map/ppermute | solution.py:111
  9.0 1.3 %collective-permute-start = (f32[44,16,128]{2,1,0:T(8,128)S(1)}, f32[44,16,128]{2,1,0:T(8,128)S(1)}, u32[]{:S(2)}, u32[]{:S(2)}) collective-permute-start(f32[44,16,128]{2,1,0:T(8,128)S(1)} %get-tuple-element.60), channel_id=1, source_target_pairs={{0,4},{4,8},{8,12},{1,5},{5,9},{9,13},{2,6},{6,10},{10,14},{3,7},{... | collective-permute-start | bytes 1081352 | tf_op jit(solution)/shard_map/ppermute | solution.py:110
  10.3 0.2 fusion.228
  10.6 0.3 fusion.212
  10.9 0.0 collective-permute-done.4
  10.9 2.1 %collective-permute-start.5 = (f32[4,256]{1,0:T(4,128)S(1)}, f32[4,256]{1,0:T(4,128)S(1)}, u32[]{:S(2)}, u32[]{:S(2)}) collective-permute-start(f32[4,256]{1,0:T(4,128)S(1)} %pad_maximum_fusion.13), channel_id=1, source_target_pairs={{0,8},{4,12},{8,0},{12,4},{1,9},{5,13},{9,1},{13,5},{2,10},{6,14},... | collective-permute-start | bytes 12296 | tf_op jit(solution)/shard_map/ppermute | solution.py:130
  13.1 3.3 %collective-permute-done.1 = f32[44,16,128]{2,1,0:T(8,128)S(1)} collective-permute-done((f32[44,16,128]{2,1,0:T(8,128)S(1)}, f32[44,16,128]{2,1,0:T(8,128)S(1)}, u32[]{:S(2)}, u32[]{:S(2)}) %collective-permute-start.1) | collective-permute-done | bytes 360480 | tf_op jit(solution)/shard_map/ppermute | solution.py:111
  16.4 4.2 %collective-permute-done = f32[44,16,128]{2,1,0:T(8,128)S(1)} collective-permute-done((f32[44,16,128]{2,1,0:T(8,128)S(1)}, f32[44,16,128]{2,1,0:T(8,128)S(1)}, u32[]{:S(2)}, u32[]{:S(2)}) %collective-permute-start) | collective-permute-done | bytes 360480 | tf_op jit(solution)/shard_map/ppermute | solution.py:110
  20.6 0.0 copy-done.1
  20.6 0.0 copy-done.2
  20.7 1.9 %collective-permute-start.3 = (f32[2,24,4,128]{3,2,1,0:T(4,128)S(1)}, f32[2,24,4,128]{3,2,1,0:T(4,128)S(1)}, u32[]{:S(2)}, u32[]{:S(2)}) collective-permute-start(f32[2,24,4,128]{3,2,1,0:T(4,128)S(1)} %get-tuple-element.27), channel_id=1, source_target_pairs={{0,1},{1,2},{2,3},{4,5},{5,6},{6,7},{8,9},{9,10},{10,11},{12,13},{... | collective-permute-start | bytes 294920 | tf_op jit(solution)/shard_map/ppermute | solution.py:110
  22.7 3.6 %collective-permute-start.2 = (f32[2,24,4,128]{3,2,1,0:T(4,128)S(1)}, f32[2,24,4,128]{3,2,1,0:T(4,128)S(1)}, u32[]{:S(2)}, u32[]{:S(2)}) collective-permute-start(f32[2,24,4,128]{3,2,1,0:T(4,128)S(1)} %get-tuple-element.26), channel_id=1, source_target_pairs={{1,0},{2,1},{3,2},{5,4},{6,5},{7,6},{9,8},{10,9},{11,10},{13,12},{... | collective-permute-start | bytes 294920 | tf_op jit(solution)/shard_map/ppermute | solution.py:111
  26.4 0.3 fusion.197
  26.6 0.3 fusion.198
  27.0 0.0 collective-permute-done.3
  27.0 0.5 %slice.990 = f32[1,1,1,1]{3,2,1,0:T(1,128)} slice(f32[2,24,4,128]{3,2,1,0:T(4,128)S(1)} %collective-permute-done.3), slice={[0:1], [0:1], [0:1], [0:1]} | slice | bytes 8 | tf_op jit(solution)/shard_map/slice | solution.py:207
  27.5 1.0 %collective-permute-done.2 = f32[2,24,4,128]{3,2,1,0:T(4,128)S(1)} collective-permute-done((f32[2,24,4,128]{3,2,1,0:T(4,128)S(1)}, f32[2,24,4,128]{3,2,1,0:T(4,128)S(1)}, u32[]{:S(2)}, u32[]{:S(2)}) %collective-permute-start.2) | collective-permute-done | bytes 98336 | tf_op jit(solution)/shard_map/ppermute | solution.py:111
  28.5 0.5 %slice.991 = f32[1,1,1,1]{3,2,1,0:T(1,128)} slice(f32[2,24,4,128]{3,2,1,0:T(4,128)S(1)} %collective-permute-done.2), slice={[0:1], [0:1], [0:1], [0:1]} | slice | bytes 8 | tf_op jit(solution)/shard_map/slice | solution.py:207
  30.3 0.0 collective-permute-done.5
  30.4 0.6 %select_maximum_fusion = f32[2,24,24,136]{3,2,1,0:T(8,128)S(1)} fusion(f32[2,24,4,128]{3,2,1,0:T(4,128)S(1)} %collective-permute-done.2, f32[2,24,4,128]{3,2,1,0:T(4,128)S(1)} %collective-permute-done.3, f32[2,8,16,128]{3,2,1,0:T(8,128)S(1)} %bitcast.75, f32[2,8,16,128]{3,2,1,0:T(8,128)S(1)} %bitcast.79, f32[1,8,16,128]{3,2,1,0:T(8,128)S(1)} %bitcast.87, ...), kind=kLoop, calls=%fused_computation.4 | loop fusion | flops 2193408 | bytes 1216512 | tf_op jit(solution)/shard_map/concatenate | solution.py:204
  31.0 0.8 %fusion.6 = f32[2,16,24,128]{3,2,1,0:T(8,128)S(1)} fusion(f32[2,24,24,136]{3,2,1,0:T(8,128)S(1)} %select_maximum_fusion), kind=kLoop, calls=%fused_computation.41 | loop fusion | flops 1081344 | bytes 3538944 | tf_op jit(solution)/shard_map/add | solution.py:53
  31.8 0.1 pad_maximum_fusion
  31.9 1.0 %fusion.13 = (f32[2,24,16,128]{3,2,1,0:T(8,128)S(1)}, f32[2,24,16,128]{3,2,1,0:T(8,128)S(1)}) fusion(f32[2,24,24,136]{3,2,1,0:T(8,128)S(1)} %select_maximum_fusion, f32[2,24,20,128]{3,2,1,0:T(8,128)S(1)} %get-tuple-element.25, f32[2,24,20,128]{3,2,1,0:T(8,128)S(1)} %get-tuple-element.24), kind=kLoop, calls=%fused_computation.52 | loop fusion | flops 2162688 | bytes 7077888 | tf_op jit(solution)/shard_map/add | solution.py:49
  32.9 0.5 %fusion.2 = f32[16,16,128]{2,1,0:T(8,128)S(1)} fusion(f32[512]{0:T(512)S(1)} %bitcast.97, s32[16,16]{1,0:T(8,128)S(1)} %multiply_add_fusion.1, s32[512]{0:T(512)S(1)} %bitcast.98, s32[512]{0:T(512)S(1)} %add_select_fusion), kind=kOutput, calls=%fused_computation.36 | convolution fusion | flops 201654272 | bytes 138240 | tf_op jit(solution)/shard_map/cpr,rz->cpz/dot_general | solution.py:150
  33.4 1.0 %fusion.43 = (f32[2,16,16,128]{3,2,1,0:T(8,128)S(1)}, f32[2,16,16,128]{3,2,1,0:T(8,128)S(1)}, f32[2,16,16,128]{3,2,1,0:T(8,128)S(1)}, f32[2,16,16,128]{3,2,1,0:T(8,128)S(1)}) fusion(f32[2,16,24,128]{3,2,1,0:T(8,128)S(1)} %fusion.6, f32[2,24,16,128]{3,2,1,0:T(8,128)S(1)} %get-tuple-element.81, f32[2,24,16,128]{3,2,1,0:T(8,128)S(1)} %get-tuple-element.82, ...), kind=kLoop, calls=%fused_computation.101 | loop fusion | flops 5570560 | bytes 14548992 | tf_op jit(solution)/shard_map/add | solution.py:90
  34.5 0.1 fusion.176
  34.6 0.1 fusion.181
  34.7 3.7 %collective-permute-start.6 = (f32[2,16,4,128]{3,2,1,0:T(4,128)S(1)}, f32[2,16,4,128]{3,2,1,0:T(4,128)S(1)}, u32[]{:S(2)}, u32[]{:S(2)}) collective-permute-start(f32[2,16,4,128]{3,2,1,0:T(4,128)S(1)} %get-tuple-element.49), channel_id=1, source_target_pairs={{1,0},{2,1},{3,2},{5,4},{6,5},{7,6},{9,8},{10,9},{11,10},{13,12},{... | collective-permute-start | bytes 196616 | tf_op jit(solution)/shard_map/ppermute | solution.py:111
  38.4 1.9 %collective-permute-start.7 = (f32[2,16,4,128]{3,2,1,0:T(4,128)S(1)}, f32[2,16,4,128]{3,2,1,0:T(4,128)S(1)}, u32[]{:S(2)}, u32[]{:S(2)}) collective-permute-start(f32[2,16,4,128]{3,2,1,0:T(4,128)S(1)} %get-tuple-element.48), channel_id=1, source_target_pairs={{0,1},{1,2},{2,3},{4,5},{5,6},{6,7},{8,9},{9,10},{10,11},{12,13},{... | collective-permute-start | bytes 196616 | tf_op jit(solution)/shard_map/ppermute | solution.py:110
  40.4 0.4 fusion.91
  40.8 0.0 collective-permute-done.6
  40.8 3.2 %collective-permute-done.7 = f32[2,16,4,128]{3,2,1,0:T(4,128)S(1)} collective-permute-done((f32[2,16,4,128]{3,2,1,0:T(4,128)S(1)}, f32[2,16,4,128]{3,2,1,0:T(4,128)S(1)}, u32[]{:S(2)}, u32[]{:S(2)}) %collective-permute-start.7) | collective-permute-done | bytes 65568 | tf_op jit(solution)/shard_map/ppermute | solution.py:110
  44.0 0.4 select_maximum_fusion.5
  44.4 0.4 fusion.102
  44.9 0.5 %fusion.27 = f32[2,16,16,128]{3,2,1,0:T(8,128)S(1)} fusion(f32[2,16,24,136]{3,2,1,0:T(8,128)S(1)} %select_maximum_fusion.5), kind=kLoop, calls=%fused_computation.77 | loop fusion | flops 720896 | bytes 2359296 | tf_op jit(solution)/shard_map/add | solution.py:49
  45.4 0.1 pad_maximum_fusion.2
  45.5 0.2 fusion.34
  45.7 0.0 copy-start.10
  45.7 0.6 %fusion.133 = (f32[2,8,16,128]{3,2,1,0:T(8,128)S(1)}, f32[2,8,16,128]{3,2,1,0:T(8,128)S(1)}, f32[2,8,16,128]{3,2,1,0:T(8,128)S(1)}, f32[2,8,16,128]{3,2,1,0:T(8,128)S(1)}) fusion(f32[2,8,24,128]{3,2,1,0:T(8,128)S(1)} %fusion.102, f32[2,16,16,128]{3,2,1,0:T(8,128)S(1)} %fusion.27, f32[2,16,16,128]{3,2,1,0:T(8,128)S(1)} %fusion.34, ...), kind=kLoop, calls=%fused_computation.220 | loop fusion | flops 3080192 | bytes 6422528 | tf_op jit(solution)/shard_map/add | solution.py:90
  46.3 0.3 copy-done.10
  46.5 0.7 %fusion.192 = (f32[8,16,128]{2,1,0:T(8,128)}, f32[8,16,128]{2,1,0:T(8,128)}, f32[8,16,128]{2,1,0:T(8,128)}, f32[8,16,128]{2,1,0:T(8,128)S(1)}) fusion(bf16[2,8,16,128]{3,2,1,0:T(8,128)(2,1)S(1)} %copy-done.10, f32[8,16,128]{2,1,0:T(8,128)S(1)} %fusion.91, f32[8,16,128]{2,1,0:T(8,128)S(1)} %copy-done.3, f32[2,8,16,128]{3,2,1,0:T(8,128)S(1)} %get-tuple-element.11, ...), kind=kLoop, calls=%fused_computation.323 | loop fusion | flops 327680 | bytes 1048576 | tf_op jit(solution)/shard_map/add | solution.py:217
  47.3 0.7 %add_add_fusion = (f32[8,16,128]{2,1,0:T(8,128)}, f32[8,16,128]{2,1,0:T(8,128)}) fusion(f32[8,16,128]{2,1,0:T(8,128)S(1)} %fusion.91, f32[8,16,128]{2,1,0:T(8,128)S(1)} %copy-done.3, f32[8,16,128]{2,1,0:T(8,128)S(1)} %get-tuple-element.8, f32[8,16,128]{2,1,0:T(8,128)S(1)} %copy-done.2, f32[2,8,16,128]{3,2,1,0:T(8,128)S(1)} %get-tuple-element.11, ...), kind=kLoop, calls=%fused_computation.325 | loop fusion | flops 147456 | bytes 589824 | tf_op jit(solution)/shard_map/add | solution.py:99
  (32 shorter events, 0.4 us)
Async XLA Ops:
  0.6 1.5 %copy-start = (f32[1024,128]{1,0:T(8,128)S(1)}, f32[1024,128]{1,0:T(8,128)}, u32[]{:S(2)}) copy-start(f32[1024,128]{1,0:T(8,128)} %param.24) | copy-start | bytes 1572868
  0.7 4.7 %copy-start.8 = (f32[8,16,128]{2,1,0:T(8,128)S(1)}, f32[8,16,128]{2,1,0:T(8,128)}, u32[]{:S(2)}) copy-start(f32[8,16,128]{2,1,0:T(8,128)} %param.16) | copy-start | bytes 196612
  0.7 4.7 %copy-start.9 = (f32[8,16,128]{2,1,0:T(8,128)S(1)}, f32[8,16,128]{2,1,0:T(8,128)}, u32[]{:S(2)}) copy-start(f32[8,16,128]{2,1,0:T(8,128)} %param.17) | copy-start | bytes 196612
  0.7 4.7 %copy-start.3 = (f32[8,16,128]{2,1,0:T(8,128)S(1)}, f32[8,16,128]{2,1,0:T(8,128)}, u32[]{:S(2)}) copy-start(f32[8,16,128]{2,1,0:T(8,128)} %param.18) | copy-start | bytes 196612
  0.7 4.7 %copy-start.5 = (f32[8,16,128]{2,1,0:T(8,128)S(1)}, f32[8,16,128]{2,1,0:T(8,128)}, u32[]{:S(2)}) copy-start(f32[8,16,128]{2,1,0:T(8,128)} %param.19) | copy-start | bytes 196612
  0.7 4.8 %copy-start.4 = (f32[8,16,128]{2,1,0:T(8,128)S(1)}, f32[8,16,128]{2,1,0:T(8,128)}, u32[]{:S(2)}) copy-start(f32[8,16,128]{2,1,0:T(8,128)} %param.20) | copy-start | bytes 196612
  0.7 4.8 %copy-start.6 = (f32[8,16,128]{2,1,0:T(8,128)S(1)}, f32[8,16,128]{2,1,0:T(8,128)}, u32[]{:S(2)}) copy-start(f32[8,16,128]{2,1,0:T(8,128)} %param.21) | copy-start | bytes 196612
  0.7 4.8 %copy-start.7 = (f32[8,16,128]{2,1,0:T(8,128)S(1)}, f32[8,16,128]{2,1,0:T(8,128)}, u32[]{:S(2)}) copy-start(f32[8,16,128]{2,1,0:T(8,128)} %param.22) | copy-start | bytes 196612
  3.1 7.8 %collective-permute-start.4 = (f32[4,128]{1,0:T(4,128)S(1)}, f32[4,128]{1,0:T(4,128)S(1)}, u32[]{:S(2)}, u32[]{:S(2)}) collective-permute-start(f32[4,128]{1,0:T(4,128)S(1)} %pad_maximum_fusion.14), channel_id=1, source_target_pairs={{0,4},{4,0},{8,12},{12,8},{1,5},{5,1},{9,13},{13,9},{2,6},{6,2},{1... | collective-permute-start | bytes 6152 | tf_op jit(solution)/shard_map/ppermute | solution.py:130
  5.4 15.3 %copy-start.1 = (f32[8,16,128]{2,1,0:T(8,128)S(1)}, f32[8,16,128]{2,1,0:T(8,128)}, u32[]{:S(2)}) copy-start(f32[8,16,128]{2,1,0:T(8,128)} %param.14) | copy-start | bytes 196612
  5.4 15.3 %copy-start.2 = (f32[8,16,128]{2,1,0:T(8,128)S(1)}, f32[8,16,128]{2,1,0:T(8,128)}, u32[]{:S(2)}) copy-start(f32[8,16,128]{2,1,0:T(8,128)} %param.15) | copy-start | bytes 196612
  5.5 10.9 %collective-permute-start.1 = (f32[44,16,128]{2,1,0:T(8,128)S(1)}, f32[44,16,128]{2,1,0:T(8,128)S(1)}, u32[]{:S(2)}, u32[]{:S(2)}) collective-permute-start(f32[44,16,128]{2,1,0:T(8,128)S(1)} %get-tuple-element.61), channel_id=1, source_target_pairs={{4,0},{8,4},{12,8},{5,1},{9,5},{13,9},{6,2},{10,6},{14,10},{7,3},{... | collective-permute-start | bytes 1081352 | tf_op jit(solution)/shard_map/ppermute | solution.py:111
  9.0 11.6 %collective-permute-start = (f32[44,16,128]{2,1,0:T(8,128)S(1)}, f32[44,16,128]{2,1,0:T(8,128)S(1)}, u32[]{:S(2)}, u32[]{:S(2)}) collective-permute-start(f32[44,16,128]{2,1,0:T(8,128)S(1)} %get-tuple-element.60), channel_id=1, source_target_pairs={{0,4},{4,8},{8,12},{1,5},{5,9},{9,13},{2,6},{6,10},{10,14},{3,7},{... | collective-permute-start | bytes 1081352 | tf_op jit(solution)/shard_map/ppermute | solution.py:110
  10.9 19.4 %collective-permute-start.5 = (f32[4,256]{1,0:T(4,128)S(1)}, f32[4,256]{1,0:T(4,128)S(1)}, u32[]{:S(2)}, u32[]{:S(2)}) collective-permute-start(f32[4,256]{1,0:T(4,128)S(1)} %pad_maximum_fusion.13), channel_id=1, source_target_pairs={{0,8},{4,12},{8,0},{12,4},{1,9},{5,13},{9,1},{13,5},{2,10},{6,14},... | collective-permute-start | bytes 12296 | tf_op jit(solution)/shard_map/ppermute | solution.py:130
  20.7 6.3 %collective-permute-start.3 = (f32[2,24,4,128]{3,2,1,0:T(4,128)S(1)}, f32[2,24,4,128]{3,2,1,0:T(4,128)S(1)}, u32[]{:S(2)}, u32[]{:S(2)}) collective-permute-start(f32[2,24,4,128]{3,2,1,0:T(4,128)S(1)} %get-tuple-element.27), channel_id=1, source_target_pairs={{0,1},{1,2},{2,3},{4,5},{5,6},{6,7},{8,9},{9,10},{10,11},{12,13},{... | collective-permute-start | bytes 294920 | tf_op jit(solution)/shard_map/ppermute | solution.py:110
  22.7 5.8 %collective-permute-start.2 = (f32[2,24,4,128]{3,2,1,0:T(4,128)S(1)}, f32[2,24,4,128]{3,2,1,0:T(4,128)S(1)}, u32[]{:S(2)}, u32[]{:S(2)}) collective-permute-start(f32[2,24,4,128]{3,2,1,0:T(4,128)S(1)} %get-tuple-element.26), channel_id=1, source_target_pairs={{1,0},{2,1},{3,2},{5,4},{6,5},{7,6},{9,8},{10,9},{11,10},{13,12},{... | collective-permute-start | bytes 294920 | tf_op jit(solution)/shard_map/ppermute | solution.py:111
  34.7 6.1 %collective-permute-start.6 = (f32[2,16,4,128]{3,2,1,0:T(4,128)S(1)}, f32[2,16,4,128]{3,2,1,0:T(4,128)S(1)}, u32[]{:S(2)}, u32[]{:S(2)}) collective-permute-start(f32[2,16,4,128]{3,2,1,0:T(4,128)S(1)} %get-tuple-element.49), channel_id=1, source_target_pairs={{1,0},{2,1},{3,2},{5,4},{6,5},{7,6},{9,8},{10,9},{11,10},{13,12},{... | collective-permute-start | bytes 196616 | tf_op jit(solution)/shard_map/ppermute | solution.py:111
  38.4 5.6 %collective-permute-start.7 = (f32[2,16,4,128]{3,2,1,0:T(4,128)S(1)}, f32[2,16,4,128]{3,2,1,0:T(4,128)S(1)}, u32[]{:S(2)}, u32[]{:S(2)}) collective-permute-start(f32[2,16,4,128]{3,2,1,0:T(4,128)S(1)} %get-tuple-element.48), channel_id=1, source_target_pairs={{0,1},{1,2},{2,3},{4,5},{5,6},{6,7},{8,9},{9,10},{10,11},{12,13},{... | collective-permute-start | bytes 196616 | tf_op jit(solution)/shard_map/ppermute | solution.py:110
  45.7 0.8 %copy-start.10 = (bf16[2,8,16,128]{3,2,1,0:T(8,128)(2,1)S(1)}, bf16[2,8,16,128]{3,2,1,0:T(8,128)(2,1)}, u32[]{:S(2)}) copy-start(bf16[2,8,16,128]{3,2,1,0:T(8,128)(2,1)} %param.23) | copy-start | bytes 196612

commit v10 on v8

--- a/solution.py
+++ b/solution.py
@@ -1,6 +1,8 @@
 import jax
 import jax.numpy as jnp
 from jax import lax
+from jax.experimental import pallas as pl
+from jax.experimental.pallas import tpu as pltpu
 from jax.sharding import PartitionSpec as P
 
 second_coef = (-205.0 / 72.0, 8.0 / 5.0, -1.0 / 5.0, 8.0 / 315.0, -1.0 / 560.0)
@@ -99,6 +101,73 @@
         2.0 * centre[1] - previous[1] + speed * (root_delta * remainder[0] + rotated[1]) + source
     )
     return jnp.stack([p_new, q_new])
+
+
+def step_kernel(padded_ref, previous_ref, speed_ref, *rest):
+    coef_refs, source_ref, out_ref = rest[:8], rest[8], rest[9]
+    _, sx, sy, sz = out_ref.shape
+    ny = padded_ref.shape[2]
+    padded = padded_ref[...]
+
+    def along_y(values, shift):
+        return pltpu.roll(values, (-shift) % ny, 2)[:, :, 8 : 8 + sy]
+
+    def along_z(values, shift):
+        lane = lax.broadcasted_iota(jnp.int32, values.shape, 3)
+        moved = pltpu.roll(values, (-shift) % sz, 3)
+        return jnp.where((lane + shift >= 0) & (lane + shift < sz), moved, 0.0)
+
+    own_x = padded[:, 4 : 4 + sx]
+    own_y = padded[:, :, 8 : 8 + sy]
+    centre = own_x[:, :, 8 : 8 + sy]
+    dxx = second_coef[0] * centre
+    dyy = second_coef[0] * centre
+    dzz = second_coef[0] * centre
+    for k in range(1, 5):
+        dxx = dxx + second_coef[k] * (own_y[:, 4 + k : 4 + k + sx] + own_y[:, 4 - k : 4 - k + sx])
+        dyy = dyy + second_coef[k] * (along_y(own_x, k) + along_y(own_x, -k))
+        dzz = dzz + second_coef[k] * (along_z(centre, k) + along_z(centre, -k))
+    dy_wide = 0.0
+    dz_xwide = 0.0
+    dz_ywide = 0.0
+    for k in range(1, 5):
+        weight = first_coef[k - 1]
+        dy_wide = dy_wide + weight * (along_y(padded, k) - along_y(padded, -k))
+        dz_xwide = dz_xwide + weight * (along_z(own_y, k) - along_z(own_y, -k))
+        dz_ywide = dz_ywide + weight * (along_z(own_x, k) - along_z(own_x, -k))
+    dxy = 0.0
+    dxz = 0.0
+    dyz = 0.0
+    for k in range(1, 5):
+        weight = first_coef[k - 1]
+        dxy = dxy + weight * (dy_wide[:, 4 + k : 4 + k + sx] - dy_wide[:, 4 - k : 4 - k + sx])
+        dxz = dxz + weight * (dz_xwide[:, 4 + k : 4 + k + sx] - dz_xwide[:, 4 - k : 4 - k + sx])
+        dyz = dyz + weight * (along_y(dz_ywide, k) - along_y(dz_ywide, -k))
+    nxx, nyy, nzz, nxy, nxz, nyz, stretch, root_delta = [ref[...] for ref in coef_refs]
+    rotated = nxx * dxx + nyy * dyy + nzz * dzz + nxy * dxy + nxz * dxz + nyz * dyz
+    remainder = dxx + dyy + dzz - rotated
+    speed = speed_ref[...]
+    source = source_ref[...]
+    out_ref[0] = (
+        2.0 * centre[0]
+        - previous_ref[0]
+        + speed * (stretch * remainder[0] + root_delta * rotated[1])
+        + source
+    )
+    out_ref[1] = (
+        2.0 * centre[1] - previous_ref[1] + speed * (root_delta * remainder[0] + rotated[1]) + source
+    )
+
+
+def advance_kernel(widened_xy, previous, speed, coefs, source):
+    padded = jnp.pad(widened_xy, ((0, 0), (0, 0), (4, 4), (0, 0)))
+    vmem = pl.BlockSpec(memory_space=pltpu.VMEM)
+    return pl.pallas_call(
+        step_kernel,
+        out_shape=jax.ShapeDtypeStruct(previous.shape, jnp.float32),
+        in_specs=[vmem] * 12,
+        out_specs=vmem,
+    )(padded, previous, speed, *coefs, source)
 
 
 def pad_depth(fields):
@@ -201,17 +270,17 @@
     coefs_x = [jnp.concatenate(parts, axis=0) for parts in zip(coefs_lo, coefs, coefs_hi)]
     speed_x = jnp.concatenate([params_lo[0], speed, params_hi[0]], axis=0)
     lo_y, hi_y = from_neighbours(now_x[:, :, sy - 4 :], now_x[:, :, :4], "gy")
-    now_xy = pad_depth(jnp.concatenate([lo_y, now_x, hi_y], axis=2))
+    now_xy = jnp.concatenate([lo_y, now_x, hi_y], axis=2)
 
     arrived = gather_column(traces, time_steps, rec_owner, rec_local)
     source_0 = sources_over(arrived, arrived[0:1], (sx, sy, sz), -4, sx + 8)[0]
     source_1 = sources_over(arrived, arrived[1:2], (sx, sy, sz), 0, sx)[0]
 
-    mid_x = advance(now_xy, prev_x, speed_x, coefs_x, source_0)
+    mid_x = advance_kernel(now_xy, prev_x, speed_x, coefs_x, source_0)
     middle = mid_x[:, 4 : 4 + sx]
     lo_m, hi_m = from_neighbours(mid_x[:, :, sy - 4 :], mid_x[:, :, :4], "gy")
-    mid_xy = pad_depth(jnp.concatenate([lo_m, mid_x, hi_m], axis=2))
-    final = advance(mid_xy, current, speed, coefs, source_1)
+    mid_xy = jnp.concatenate([lo_m, mid_x, hi_m], axis=2)
+    final = advance_kernel(mid_xy, current, speed, coefs, source_1)
     image = (
         snapshots[0].astype(jnp.float32) * middle[0] + snapshots[1].astype(jnp.float32) * final[0]
     )

time: 44.9 us -> 61.2 us (1.36)
  local copies, waits for them, and re-layouts: 2.4 us -> 12.3 us
  Pallas kernels: 0 us -> 7.9 us
  other arithmetic: 9.75 us -> 8.48 us
  waiting for transfers between devices: 13 us -> 12.2 us
    pallas_call x0 -> x2, Pallas kernels: none -> 7.9 us  [advance_kernel(): pl.pallas_call(step_kernel, out_shape=jax.ShapeDtypeStruct(previous.shape...]
    unnamed x32 -> x62, local copies, waits for them, and re-layouts: 2.08 us -> 8 us
    add x8 -> x0, other arithmetic: 5.27 us -> none  [the longest x2 1.61 us: advance(): nxx * dxx + nyy * dyy + nzz * dzz + nxy * dxy + nxz * dxz + nyz * dyz]
    concatenate x3 -> x4, other arithmetic: 0.06 us -> 2.83 us  [local(): jnp.concatenate(parts, axis=0)]
    ppermute x3, waiting for transfers between devices: 5.61 us -> 3.01 us  [from_neighbours(): below = lax.ppermute(low_part, axis, [(i, i + 1) for i in range(count - 1)])]
    squeeze x0 -> x2, local copies, waits for them, and re-layouts: none -> 2.18 us  [local(): return (final[0], final[1], middle[0], middle[1], image)]
    ppermute x2, waiting for transfers between devices: 7.41 us -> 9.14 us  [gather_column(): lax.ppermute(arrived, 'gx', [(i, i ^ step) for i in range(groups)])]
    concatenate x5 -> x3, other arithmetic: 1.17 us -> 2.61 us  [the longest x1 1.01 us: local(): now_xy = jnp.concatenate([lo_y, now_x, hi_y], axis=2)]
  transfers between devices with their start and end apart: 8 -> 8, of which waited for: 3 -> 3; matrix products, arithmetic and copies ran while one was open for 9% -> 15% of each run, Pallas kernels for 0% -> 0%
where the time goes in v10:
time: 61.2 us; the launch traced here: 60.5 us
  starting transfers between devices  16.2 us (26%)
  local copies, waits for them, and re-layouts  12.3 us (20%)
  waiting for transfers between devices  12.2 us (20%)
  other arithmetic  8.48 us (14%)
  Pallas kernels  7.9 us (13%)
  matrix products  2.45 us (4%)
  between operations  1.03 us (2%)
    ppermute x2, waiting for transfers between devices, gather_column(): lax.ppermute(arrived, 'gx', [(i, i ^ step) for i in range(groups)])  9.14 us
    unnamed x62, local copies, waits for them, and re-layouts  8 us
    pallas_call x2, Pallas kernels, advance_kernel(): pl.pallas_call(step_kernel, out_shape=jax.ShapeDtypeStruct(previous.shape...  7.9 us
    ppermute x3, starting transfers between devices, from_neighbours(): lax.ppermute(high_part, axis, [(i + 1, i) for i in range(count - 1)])  7.45 us
    ppermute x3, starting transfers between devices, from_neighbours(): below = lax.ppermute(low_part, axis, [(i, i + 1) for i in range(count - 1)])  5.62 us
    ppermute x2, starting transfers between devices, gather_column(): lax.ppermute(arrived, 'gx', [(i, i ^ step) for i in range(groups)])  3.09 us
    ppermute x3, waiting for transfers between devices, from_neighbours(): below = lax.ppermute(low_part, axis, [(i, i + 1) for i in range(count - 1)])  3.01 us
    concatenate x4, other arithmetic, local(): jnp.concatenate(parts, axis=0)  2.83 us
  transfers between devices with their start and end apart: 8, of which 3 were waited for; matrix products, arithmetic and copies ran while one was open for 15% of the time, Pallas kernels for 0%

profile of v10, /device:TPU:30, one launch (start us, length us, event | category | flops | bytes accessed | tf_op | source)
XLA Modules:
  0.0 60.5 jit_solution(17927664461591235558)
XLA Ops:
  0.6 0.0 copy-start
  0.6 0.0 copy-start.3
  0.7 0.9 %constant_dynamic-update-slice_fusion.17 = f32[44,16,128]{2,1,0:T(8,128)S(1)} fusion(f32[8,16,128]{2,1,0:T(8,128)} %param.14), kind=kLoop, calls=%fused_computation.77 | loop fusion | bytes 131072
  1.6 0.0 copy-done.3
  1.6 0.0 copy-start.20
  1.6 0.8 %copy-done.20 = f32[8,16,128]{2,1,0:T(8,128)S(1)} copy-done((f32[8,16,128]{2,1,0:T(8,128)S(1)}, f32[8,16,128]{2,1,0:T(8,128)}, u32[]{:S(2)}) %copy-start.20) | copy-done | bytes 65560
  2.4 0.8 %copy-done.21 = f32[8,16,128]{2,1,0:T(8,128)S(1)} copy-done((f32[8,16,128]{2,1,0:T(8,128)S(1)}, f32[8,16,128]{2,1,0:T(8,128)}, u32[]{:S(2)}) %copy-start.21) | copy-done | bytes 65560
  3.3 0.8 %copy-done.11 = f32[8,16,128]{2,1,0:T(8,128)S(1)} copy-done((f32[8,16,128]{2,1,0:T(8,128)S(1)}, f32[8,16,128]{2,1,0:T(8,128)}, u32[]{:S(2)}) %copy-start.11) | copy-done | bytes 65560
  4.1 0.8 %copy-done.18 = f32[8,16,128]{2,1,0:T(8,128)S(1)} copy-done((f32[8,16,128]{2,1,0:T(8,128)S(1)}, f32[8,16,128]{2,1,0:T(8,128)}, u32[]{:S(2)}) %copy-start.18) | copy-done | bytes 65560
  5.0 0.8 %copy-done.19 = f32[8,16,128]{2,1,0:T(8,128)S(1)} copy-done((f32[8,16,128]{2,1,0:T(8,128)S(1)}, f32[8,16,128]{2,1,0:T(8,128)}, u32[]{:S(2)}) %copy-start.19) | copy-done | bytes 65560
  5.8 0.8 %copy-done.16 = f32[8,16,128]{2,1,0:T(8,128)S(1)} copy-done((f32[8,16,128]{2,1,0:T(8,128)S(1)}, f32[8,16,128]{2,1,0:T(8,128)}, u32[]{:S(2)}) %copy-start.16) | copy-done | bytes 65560
  6.6 0.8 %copy-done.17 = f32[8,16,128]{2,1,0:T(8,128)S(1)} copy-done((f32[8,16,128]{2,1,0:T(8,128)S(1)}, f32[8,16,128]{2,1,0:T(8,128)}, u32[]{:S(2)}) %copy-start.17) | copy-done | bytes 65560
  7.5 2.4 %collective-permute-start.1 = (f32[44,16,128]{2,1,0:T(8,128)S(1)}, f32[44,16,128]{2,1,0:T(8,128)S(1)}, u32[]{:S(2)}, u32[]{:S(2)}) collective-permute-start(f32[44,16,128]{2,1,0:T(8,128)S(1)} %get-tuple-element.42), channel_id=1, source_target_pairs={{4,0},{8,4},{12,8},{5,1},{9,5},{13,9},{6,2},{10,6},{14,10},{7,3},{... | collective-permute-start | bytes 1081352 | tf_op jit(solution)/shard_map/ppermute | solution.py:180
  9.9 0.0 copy-start.25
  9.9 1.3 %collective-permute-start = (f32[44,16,128]{2,1,0:T(8,128)S(1)}, f32[44,16,128]{2,1,0:T(8,128)S(1)}, u32[]{:S(2)}, u32[]{:S(2)}) collective-permute-start(f32[44,16,128]{2,1,0:T(8,128)S(1)} %get-tuple-element.41), channel_id=1, source_target_pairs={{0,4},{4,8},{8,12},{1,5},{5,9},{9,13},{2,6},{6,10},{10,14},{3,7},{... | collective-permute-start | bytes 1081352 | tf_op jit(solution)/shard_map/ppermute | solution.py:179
  11.2 0.0 copy-done.24
  11.2 0.0 copy-start.23
  11.2 0.6 %copy-done.23 = s32[2]{0:T(128)S(1)} copy-done((s32[2]{0:T(128)S(1)}, s32[2]{0:T(128)}, u32[]{:S(2)}) %copy-start.23) | copy-done | bytes 32
  11.9 0.3 fusion.30
  12.2 2.7 %collective-permute-start.4 = (f32[4,128]{1,0:T(4,128)S(1)}, f32[4,128]{1,0:T(4,128)S(1)}, u32[]{:S(2)}, u32[]{:S(2)}) collective-permute-start(f32[4,128]{1,0:T(4,128)S(1)} %pad_maximum_fusion.17), channel_id=1, source_target_pairs={{0,4},{4,0},{8,12},{12,8},{1,5},{5,1},{9,13},{13,9},{2,6},{6,2},{1... | collective-permute-start | bytes 6152 | tf_op jit(solution)/shard_map/ppermute | solution.py:199
  14.9 0.2 fusion.49
  15.2 0.0 copy-start.2
  15.2 0.3 multiply_multiply_fusion
  15.5 0.0 copy-start.9
  15.5 0.0 copy-start.8
  15.5 0.0 copy-start.10
  15.5 0.0 copy-start.7
  15.5 0.0 copy-start.5
  15.5 0.5 copy-done.2
  16.1 0.7 %pad_maximum_fusion.1.previous_ref = f32[2,8,16,128]{3,2,1,0:T(8,128)} fusion(f32[1,8,16,128]{3,2,1,0:T(8,128)S(1)} %bitcast.45, f32[1,8,16,128]{3,2,1,0:T(8,128)S(1)} %bitcast.42), kind=kLoop, calls=%fused_computation.26 | loop fusion | flops 32768 | bytes 262144 | tf_op jit(solution)/shard_map/stack | solution.py:244
  16.7 5.0 %collective-permute-done.4 = f32[4,128]{1,0:T(4,128)S(1)} collective-permute-done((f32[4,128]{1,0:T(4,128)S(1)}, f32[4,128]{1,0:T(4,128)S(1)}, u32[]{:S(2)}, u32[]{:S(2)}) %collective-permute-start.4) | collective-permute-done | bytes 2080 | tf_op jit(solution)/shard_map/ppermute | solution.py:199
  21.7 0.4 collective-permute-start.5
  22.1 4.2 %collective-permute-done.5 = f32[4,256]{1,0:T(4,128)S(1)} collective-permute-done((f32[4,256]{1,0:T(4,128)S(1)}, f32[4,256]{1,0:T(4,128)S(1)}, u32[]{:S(2)}, u32[]{:S(2)}) %collective-permute-start.5) | collective-permute-done | bytes 4128 | tf_op jit(solution)/shard_map/ppermute | solution.py:199
  26.4 1.0 %fusion.5.rest_8_ = f32[8,16,128]{2,1,0:T(8,128)} fusion(f32[512]{0:T(512)S(1)} %bitcast.55, s32[8,16]{1,0:T(8,128)S(1)} %multiply_add_fusion.2, s32[512]{0:T(512)S(1)} %bitcast.56, s32[512]{0:T(512)S(1)} %add_select_fusion), kind=kOutput, calls=%fused_computation.17 | convolution fusion | flops 100859904 | bytes 72192 | tf_op jit(solution)/shard_map/cpr,rz->cpz/dot_general | solution.py:219
  27.4 1.2 %fusion.1.rest_8_ = f32[16,16,128]{2,1,0:T(8,128)} fusion(f32[512]{0:T(512)S(1)} %bitcast.54, s32[16,16]{1,0:T(8,128)S(1)} %multiply_add_fusion.1, s32[512]{0:T(512)S(1)} %bitcast.53, s32[512]{0:T(512)S(1)} %add_select_fusion), kind=kOutput, calls=%fused_computation.12 | convolution fusion | flops 201654272 | bytes 138240 | tf_op jit(solution)/shard_map/cpr,rz->cpz/dot_general | solution.py:219
  28.5 0.0 collective-permute-done.1
  28.6 0.0 collective-permute-done
  28.6 1.9 %collective-permute-start.3 = (f32[2,24,4,128]{3,2,1,0:T(4,128)S(1)}, f32[2,24,4,128]{3,2,1,0:T(4,128)S(1)}, u32[]{:S(2)}, u32[]{:S(2)}) collective-permute-start(f32[2,24,4,128]{3,2,1,0:T(4,128)S(1)} %get-tuple-element.12), channel_id=1, source_target_pairs={{1,0},{2,1},{3,2},{5,4},{6,5},{7,6},{9,8},{10,9},{11,10},{13,12},{... | collective-permute-start | bytes 294920 | tf_op jit(solution)/shard_map/ppermute | solution.py:180
  30.6 2.4 %collective-permute-start.2 = (f32[2,24,4,128]{3,2,1,0:T(4,128)S(1)}, f32[2,24,4,128]{3,2,1,0:T(4,128)S(1)}, u32[]{:S(2)}, u32[]{:S(2)}) collective-permute-start(f32[2,24,4,128]{3,2,1,0:T(4,128)S(1)} %get-tuple-element.11), channel_id=1, source_target_pairs={{0,1},{1,2},{2,3},{4,5},{5,6},{6,7},{8,9},{9,10},{10,11},{12,13},{... | collective-permute-start | bytes 294920 | tf_op jit(solution)/shard_map/ppermute | solution.py:179
  33.0 0.0 slice-start
  33.0 0.8 %slice-done = f32[8,16,128]{2,1,0:T(8,128)S(1)} async-done(((f32[44,16,128]{2,1,0:T(8,128)}), f32[8,16,128]{2,1,0:T(8,128)S(1)}, s32[]{:S(2)}) %slice-start) | async-done | bytes 65560 | tf_op jit(solution)/shard_map/slice | solution.py:260
  33.8 0.7 %pad_maximum_fusion.previous_ref = f32[2,16,16,128]{3,2,1,0:T(8,128)} fusion(f32[2,4,16,128]{3,2,1,0:T(8,128)S(1)} %bitcast.48, f32[1,8,16,128]{3,2,1,0:T(8,128)S(1)} %bitcast.50, f32[1,8,16,128]{3,2,1,0:T(8,128)S(1)} %bitcast.49, f32[2,4,16,128]{3,2,1,0:T(8,128)S(1)} %bitcast.51), kind=kLoop, calls=%fused_computation.16 | loop fusion | flops 196608 | bytes 524288 | tf_op jit(solution)/shard_map/concatenate | solution.py:266
  34.5 0.3 fusion.23
  34.8 0.3 fusion.25
  35.1 0.7 %pad_maximum_fusion.2 = (f32[16,16,128]{2,1,0:T(8,128)}, f32[16,16,128]{2,1,0:T(8,128)}) fusion(f32[4,16,128]{2,1,0:T(8,128)S(1)} %get-tuple-element.30, f32[8,16,128]{2,1,0:T(8,128)S(1)} %copy-done.11, f32[4,16,128]{2,1,0:T(8,128)S(1)} %get-tuple-element.21, f32[4,16,128]{2,1,0:T(8,128)S(1)} %get-tuple-element.28, ...), kind=kLoop, calls=%fused_computation.27 | loop fusion | flops 131072 | bytes 524288 | tf_op jit(solution)/shard_map/concatenate | solution.py:271
  35.8 0.7 %pad_maximum_fusion.4 = (f32[16,16,128]{2,1,0:T(8,128)}, f32[16,16,128]{2,1,0:T(8,128)}) fusion(f32[4,16,128]{2,1,0:T(8,128)S(1)} %get-tuple-element.26, f32[8,16,128]{2,1,0:T(8,128)S(1)} %get-tuple-element.36.rest_1_, f32[4,16,128]{2,1,0:T(8,128)S(1)} %get-tuple-element.17, f32[4,16,128]{2,1,0:T(8,128)S(1)} %get-tuple-element.29, ...), kind=kLoop, calls=%fused_computation.29 | loop fusion | flops 131072 | bytes 524288 | tf_op jit(solution)/shard_map/concatenate | solution.py:270
  36.5 0.7 %pad_maximum_fusion.6 = (f32[16,16,128]{2,1,0:T(8,128)}, f32[16,16,128]{2,1,0:T(8,128)}) fusion(f32[4,16,128]{2,1,0:T(8,128)S(1)} %get-tuple-element.23, f32[8,16,128]{2,1,0:T(8,128)S(1)} %get-tuple-element.35.rest_3_, f32[4,16,128]{2,1,0:T(8,128)S(1)} %get-tuple-element.14, f32[4,16,128]{2,1,0:T(8,128)S(1)} %get-tuple-element.24, ...), kind=kLoop, calls=%fused_computation.31 | loop fusion | flops 131072 | bytes 524288 | tf_op jit(solution)/shard_map/concatenate | solution.py:270
  37.3 0.7 %pad_maximum_fusion.8 = (f32[16,16,128]{2,1,0:T(8,128)}, f32[16,16,128]{2,1,0:T(8,128)}) fusion(f32[4,16,128]{2,1,0:T(8,128)S(1)} %get-tuple-element.25, f32[8,16,128]{2,1,0:T(8,128)S(1)} %get-tuple-element.33.rest_5_, f32[4,16,128]{2,1,0:T(8,128)S(1)} %get-tuple-element.16, f32[4,16,128]{2,1,0:T(8,128)S(1)} %get-tuple-element.27, ...), kind=kLoop, calls=%fused_computation.33 | loop fusion | flops 131072 | bytes 524288 | tf_op jit(solution)/shard_map/concatenate | solution.py:270
  38.0 0.7 %pad_maximum_fusion.10.rest_7_ = f32[16,16,128]{2,1,0:T(8,128)} fusion(f32[4,16,128]{2,1,0:T(8,128)S(1)} %get-tuple-element.22, f32[8,16,128]{2,1,0:T(8,128)S(1)} %add_sqrt_fusion.rest_7_, f32[4,16,128]{2,1,0:T(8,128)S(1)} %get-tuple-element.13), kind=kLoop, calls=%fused_computation.35 | loop fusion | flops 65536 | bytes 262144 | tf_op jit(solution)/shard_map/concatenate | solution.py:270
  38.7 0.0 collective-permute-done.3
  38.7 0.0 collective-permute-done.2
  38.7 1.0 %select_maximum_fusion.padded_ref = f32[2,24,32,128]{3,2,1,0:T(8,128)} fusion(f32[2,24,4,128]{3,2,1,0:T(4,128)S(1)} %collective-permute-done.3, f32[2,24,4,128]{3,2,1,0:T(4,128)S(1)} %collective-permute-done.2, f32[2,8,16,128]{3,2,1,0:T(8,128)S(1)} %bitcast.39, f32[2,8,16,128]{3,2,1,0:T(8,128)S(1)} %bitcast.41, f32[1,8,16,128]{3,2,1,0:T(8,128)S(1)} %bitcast.47, ...), kind=kLoop, calls=%fused_computation.4 | loop fusion | flops 2752512 | bytes 1376256 | tf_op jit(solution)/shard_map/concatenate | solution.py:273
  39.7 4.6 %shard_map.173 = f32[2,16,16,128]{3,2,1,0:T(8,128)} custom-call(f32[2,24,32,128]{3,2,1,0:T(8,128)} %select_maximum_fusion.padded_ref, f32[2,16,16,128]{3,2,1,0:T(8,128)} %pad_maximum_fusion.previous_ref, f32[16,16,128]{2,1,0:T(8,128)} %get-tuple-element.56.speed_ref, f32[16,16,128]{2,1,0:T(8,128)} %get-tuple-element.57.rest_0_, ...), custom_call_target="tpu_custom_call" | custom-call | tf_op jit(solution)/shard_map/pallas_call | solution.py:165
  44.3 1.0 %fusion.48 = (f32[2,16,4,128]{3,2,1,0:T(4,128)S(1)}, f32[2,16,4,128]{3,2,1,0:T(4,128)S(1)}) fusion(f32[2,16,16,128]{3,2,1,0:T(8,128)} %shard_map.173), kind=kLoop, calls=%fused_computation.145 | loop fusion | bytes 262144 | tf_op jit(solution)/shard_map/slice | solution.py:281
  45.3 3.2 %collective-permute-start.7 = (f32[2,16,4,128]{3,2,1,0:T(4,128)S(1)}, f32[2,16,4,128]{3,2,1,0:T(4,128)S(1)}, u32[]{:S(2)}, u32[]{:S(2)}) collective-permute-start(f32[2,16,4,128]{3,2,1,0:T(4,128)S(1)} %get-tuple-element.32), channel_id=1, source_target_pairs={{1,0},{2,1},{3,2},{5,4},{6,5},{7,6},{9,8},{10,9},{11,10},{13,12},{... | collective-permute-start | bytes 196616 | tf_op jit(solution)/shard_map/ppermute | solution.py:180
  48.5 1.9 %collective-permute-start.6 = (f32[2,16,4,128]{3,2,1,0:T(4,128)S(1)}, f32[2,16,4,128]{3,2,1,0:T(4,128)S(1)}, u32[]{:S(2)}, u32[]{:S(2)}) collective-permute-start(f32[2,16,4,128]{3,2,1,0:T(4,128)S(1)} %get-tuple-element.31), channel_id=1, source_target_pairs={{0,1},{1,2},{2,3},{4,5},{5,6},{6,7},{8,9},{9,10},{10,11},{12,13},{... | collective-permute-start | bytes 196616 | tf_op jit(solution)/shard_map/ppermute | solution.py:179
  50.4 0.6 %slice_bitcast_fusion = f32[8,16,128]{2,1,0:T(8,128)} fusion(f32[2,16,16,128]{3,2,1,0:T(8,128)S(1)} %copy-done.1), kind=kLoop, calls=%fused_computation.46 | loop fusion | bytes 131072 | tf_op jit(solution)/shard_map/squeeze | solution.py:287
  51.1 0.0 collective-permute-done.7
  51.1 3.0 %collective-permute-done.6 = f32[2,16,4,128]{3,2,1,0:T(4,128)S(1)} collective-permute-done((f32[2,16,4,128]{3,2,1,0:T(4,128)S(1)}, f32[2,16,4,128]{3,2,1,0:T(4,128)S(1)}, u32[]{:S(2)}, u32[]{:S(2)}) %collective-permute-start.6) | collective-permute-done | bytes 65568 | tf_op jit(solution)/shard_map/ppermute | solution.py:179
  54.1 0.9 %select_maximum_fusion.5.padded_ref = f32[2,16,32,128]{3,2,1,0:T(8,128)} fusion(f32[2,16,4,128]{3,2,1,0:T(4,128)S(1)} %collective-permute-done.7, f32[2,16,16,128]{3,2,1,0:T(8,128)S(1)} %copy-done.1, f32[2,16,4,128]{3,2,1,0:T(4,128)S(1)} %collective-permute-done.6), kind=kLoop, calls=%fused_computation.10 | loop fusion | flops 1048576 | bytes 917504 | tf_op jit(solution)/shard_map/concatenate | solution.py:282
  54.9 3.3 %shard_map.174 = f32[2,8,16,128]{3,2,1,0:T(8,128)} custom-call(f32[2,16,32,128]{3,2,1,0:T(8,128)} %select_maximum_fusion.5.padded_ref, f32[2,8,16,128]{3,2,1,0:T(8,128)} %pad_maximum_fusion.1.previous_ref, f32[8,16,128]{2,1,0:T(8,128)} %speed_ref.1, f32[8,16,128]{2,1,0:T(8,128)} %copy-done.9, f32[8,16,128]{2,1,0:T(8,128)} %copy-done.8, ...), custom_call_target="tpu_custom_call" | custom-call | tf_op jit(solution)/shard_map/pallas_call | solution.py:165
  58.2 1.5 %slice_bitcast_fusion.2 = f32[8,16,128]{2,1,0:T(8,128)} fusion(f32[2,8,16,128]{3,2,1,0:T(8,128)} %shard_map.174), kind=kLoop, calls=%fused_computation.48 | loop fusion | bytes 131072 | tf_op jit(solution)/shard_map/squeeze | solution.py:287
  59.8 0.0 copy-done.13
  59.8 0.7 %fusion.21 = (f32[8,16,128]{2,1,0:T(8,128)}, f32[8,16,128]{2,1,0:T(8,128)}, f32[8,16,128]{2,1,0:T(8,128)}) fusion(bf16[2,8,16,128]{3,2,1,0:T(8,128)(2,1)S(1)} %copy-done.22, f32[2,16,16,128]{3,2,1,0:T(8,128)S(1)} %copy-done.1, f32[2,8,16,128]{3,2,1,0:T(8,128)S(1)} %copy-done.13), kind=kLoop, calls=%fused_computation.51 | loop fusion | flops 81920 | bytes 393216 | tf_op jit(solution)/shard_map/add | solution.py:285
  (56 shorter events, 0.3 us)
Async XLA Ops:
  0.6 10.6 %copy-start = (f32[1024,128]{1,0:T(8,128)S(1)}, f32[1024,128]{1,0:T(8,128)}, u32[]{:S(2)}) copy-start(f32[1024,128]{1,0:T(8,128)} %param.24) | copy-start | bytes 1572868
  0.6 0.9 %copy-start.3 = (f32[8,16,128]{2,1,0:T(8,128)S(1)}, f32[8,16,128]{2,1,0:T(8,128)}, u32[]{:S(2)}) copy-start(f32[8,16,128]{2,1,0:T(8,128)} %param.15) | copy-start | bytes 196612
  1.6 0.8 %copy-start.20 = (f32[8,16,128]{2,1,0:T(8,128)S(1)}, f32[8,16,128]{2,1,0:T(8,128)}, u32[]{:S(2)}) copy-start(f32[8,16,128]{2,1,0:T(8,128)} %param.16) | copy-start | bytes 196612
  2.4 0.8 %copy-start.21 = (f32[8,16,128]{2,1,0:T(8,128)S(1)}, f32[8,16,128]{2,1,0:T(8,128)}, u32[]{:S(2)}) copy-start(f32[8,16,128]{2,1,0:T(8,128)} %param.17) | copy-start | bytes 196612
  3.3 0.8 %copy-start.11 = (f32[8,16,128]{2,1,0:T(8,128)S(1)}, f32[8,16,128]{2,1,0:T(8,128)}, u32[]{:S(2)}) copy-start(f32[8,16,128]{2,1,0:T(8,128)} %speed_ref.1) | copy-start | bytes 196612
  4.1 0.8 %copy-start.18 = (f32[8,16,128]{2,1,0:T(8,128)S(1)}, f32[8,16,128]{2,1,0:T(8,128)}, u32[]{:S(2)}) copy-start(f32[8,16,128]{2,1,0:T(8,128)} %param.19) | copy-start | bytes 196612
  5.0 0.8 %copy-start.19 = (f32[8,16,128]{2,1,0:T(8,128)S(1)}, f32[8,16,128]{2,1,0:T(8,128)}, u32[]{:S(2)}) copy-start(f32[8,16,128]{2,1,0:T(8,128)} %param.20) | copy-start | bytes 196612
  5.8 0.8 %copy-start.16 = (f32[8,16,128]{2,1,0:T(8,128)S(1)}, f32[8,16,128]{2,1,0:T(8,128)}, u32[]{:S(2)}) copy-start(f32[8,16,128]{2,1,0:T(8,128)} %param.21) | copy-start | bytes 196612
  6.6 0.8 %copy-start.17 = (f32[8,16,128]{2,1,0:T(8,128)S(1)}, f32[8,16,128]{2,1,0:T(8,128)}, u32[]{:S(2)}) copy-start(f32[8,16,128]{2,1,0:T(8,128)} %param.22) | copy-start | bytes 196612
  7.5 3.7 %copy-start.24 = (s32[128,1]{0,1:T(1,128)S(1)}, s32[128,1]{0,1:T(1,128)}, u32[]{:S(2)}) copy-start(s32[128,1]{0,1:T(1,128)} %param.26) | copy-start | bytes 1540
  7.5 21.1 %collective-permute-start.1 = (f32[44,16,128]{2,1,0:T(8,128)S(1)}, f32[44,16,128]{2,1,0:T(8,128)S(1)}, u32[]{:S(2)}, u32[]{:S(2)}) collective-permute-start(f32[44,16,128]{2,1,0:T(8,128)S(1)} %get-tuple-element.42), channel_id=1, source_target_pairs={{4,0},{8,4},{12,8},{5,1},{9,5},{13,9},{6,2},{10,6},{14,10},{7,3},{... | collective-permute-start | bytes 1081352 | tf_op jit(solution)/shard_map/ppermute | solution.py:180
  9.9 1.3 %copy-start.25 = (s32[128]{0:T(128)S(1)}, s32[128]{0:T(128)}, u32[]{:S(2)}) copy-start(s32[128]{0:T(128)} %param.27) | copy-start | bytes 1540
  9.9 18.7 %collective-permute-start = (f32[44,16,128]{2,1,0:T(8,128)S(1)}, f32[44,16,128]{2,1,0:T(8,128)S(1)}, u32[]{:S(2)}, u32[]{:S(2)}) collective-permute-start(f32[44,16,128]{2,1,0:T(8,128)S(1)} %get-tuple-element.41), channel_id=1, source_target_pairs={{0,4},{4,8},{8,12},{1,5},{5,9},{9,13},{2,6},{6,10},{10,14},{3,7},{... | collective-permute-start | bytes 1081352 | tf_op jit(solution)/shard_map/ppermute | solution.py:179
  11.2 0.7 %copy-start.23 = (s32[2]{0:T(128)S(1)}, s32[2]{0:T(128)}, u32[]{:S(2)}) copy-start(s32[2]{0:T(128)} %param.25) | copy-start | bytes 28
  12.2 9.5 %collective-permute-start.4 = (f32[4,128]{1,0:T(4,128)S(1)}, f32[4,128]{1,0:T(4,128)S(1)}, u32[]{:S(2)}, u32[]{:S(2)}) collective-permute-start(f32[4,128]{1,0:T(4,128)S(1)} %pad_maximum_fusion.17), channel_id=1, source_target_pairs={{0,4},{4,0},{8,12},{12,8},{1,5},{5,1},{9,13},{13,9},{2,6},{6,2},{1... | collective-permute-start | bytes 6152 | tf_op jit(solution)/shard_map/ppermute | solution.py:199
  15.1 22.1 %copy-start.12 = (f32[8,16,128]{2,1,0:T(8,128)}, f32[8,16,128]{2,1,0:T(8,128)S(1)}, u32[]{:S(2)}) copy-start(f32[8,16,128]{2,1,0:T(8,128)S(1)} %multiply_add_fusion.rest_6_) | copy-start | bytes 196612
  15.2 22.8 %copy-start.4 = (f32[8,16,128]{2,1,0:T(8,128)}, f32[8,16,128]{2,1,0:T(8,128)S(1)}, u32[]{:S(2)}) copy-start(f32[8,16,128]{2,1,0:T(8,128)S(1)} %add_sqrt_fusion.rest_7_) | copy-start | bytes 196612
  15.2 0.9 %copy-start.2 = (f32[8,16,128]{2,1,0:T(8,128)S(1)}, f32[8,16,128]{2,1,0:T(8,128)}, u32[]{:S(2)}) copy-start(f32[8,16,128]{2,1,0:T(8,128)} %param.14) | copy-start | bytes 196612
  15.5 19.6 %copy-start.9 = (f32[8,16,128]{2,1,0:T(8,128)}, f32[8,16,128]{2,1,0:T(8,128)S(1)}, u32[]{:S(2)}) copy-start(f32[8,16,128]{2,1,0:T(8,128)S(1)} %get-tuple-element.37.rest_0_) | copy-start | bytes 196612
  15.5 20.3 %copy-start.8 = (f32[8,16,128]{2,1,0:T(8,128)}, f32[8,16,128]{2,1,0:T(8,128)S(1)}, u32[]{:S(2)}) copy-start(f32[8,16,128]{2,1,0:T(8,128)S(1)} %get-tuple-element.36.rest_1_) | copy-start | bytes 196612
  15.5 20.3 %copy-start.10 = (f32[8,16,128]{2,1,0:T(8,128)}, f32[8,16,128]{2,1,0:T(8,128)S(1)}, u32[]{:S(2)}) copy-start(f32[8,16,128]{2,1,0:T(8,128)S(1)} %get-tuple-element.38.rest_2_) | copy-start | bytes 196612
  15.5 21.0 %copy-start.6 = (f32[8,16,128]{2,1,0:T(8,128)}, f32[8,16,128]{2,1,0:T(8,128)S(1)}, u32[]{:S(2)}) copy-start(f32[8,16,128]{2,1,0:T(8,128)S(1)} %get-tuple-element.34.rest_4_) | copy-start | bytes 196612
  15.5 21.0 %copy-start.7 = (f32[8,16,128]{2,1,0:T(8,128)}, f32[8,16,128]{2,1,0:T(8,128)S(1)}, u32[]{:S(2)}) copy-start(f32[8,16,128]{2,1,0:T(8,128)S(1)} %get-tuple-element.35.rest_3_) | copy-start | bytes 196612
  15.5 21.8 %copy-start.5 = (f32[8,16,128]{2,1,0:T(8,128)}, f32[8,16,128]{2,1,0:T(8,128)S(1)}, u32[]{:S(2)}) copy-start(f32[8,16,128]{2,1,0:T(8,128)S(1)} %get-tuple-element.33.rest_5_) | copy-start | bytes 196612
  21.7 4.6 %collective-permute-start.5 = (f32[4,256]{1,0:T(4,128)S(1)}, f32[4,256]{1,0:T(4,128)S(1)}, u32[]{:S(2)}, u32[]{:S(2)}) collective-permute-start(f32[4,256]{1,0:T(4,128)S(1)} %pad_maximum_fusion.16), channel_id=1, source_target_pairs={{0,8},{4,12},{8,0},{12,4},{1,9},{5,13},{9,1},{13,5},{2,10},{6,14},... | collective-permute-start | bytes 12296 | tf_op jit(solution)/shard_map/ppermute | solution.py:199
  28.5 4.4 %copy-start.14 = (f32[44,16,128]{2,1,0:T(8,128)}, f32[44,16,128]{2,1,0:T(8,128)S(1)}, u32[]{:S(2)}) copy-start(f32[44,16,128]{2,1,0:T(8,128)S(1)} %collective-permute-done.1) | copy-start | bytes 1081348
  28.6 10.0 %collective-permute-start.3 = (f32[2,24,4,128]{3,2,1,0:T(4,128)S(1)}, f32[2,24,4,128]{3,2,1,0:T(4,128)S(1)}, u32[]{:S(2)}, u32[]{:S(2)}) collective-permute-start(f32[2,24,4,128]{3,2,1,0:T(4,128)S(1)} %get-tuple-element.12), channel_id=1, source_target_pairs={{1,0},{2,1},{3,2},{5,4},{6,5},{7,6},{9,8},{10,9},{11,10},{13,12},{... | collective-permute-start | bytes 294920 | tf_op jit(solution)/shard_map/ppermute | solution.py:180
  30.6 8.1 %collective-permute-start.2 = (f32[2,24,4,128]{3,2,1,0:T(4,128)S(1)}, f32[2,24,4,128]{3,2,1,0:T(4,128)S(1)}, u32[]{:S(2)}, u32[]{:S(2)}) collective-permute-start(f32[2,24,4,128]{3,2,1,0:T(4,128)S(1)} %get-tuple-element.11), channel_id=1, source_target_pairs={{0,1},{1,2},{2,3},{4,5},{5,6},{6,7},{8,9},{9,10},{10,11},{12,13},{... | collective-permute-start | bytes 294920 | tf_op jit(solution)/shard_map/ppermute | solution.py:179
  33.0 0.8 %slice-start = ((f32[44,16,128]{2,1,0:T(8,128)}), f32[8,16,128]{2,1,0:T(8,128)S(1)}, s32[]{:S(2)}) async-start(f32[44,16,128]{2,1,0:T(8,128)} %copy-done.14), calls=%async_computation | async-start | bytes 131072 | tf_op jit(solution)/shard_map/slice | solution.py:260
  33.0 1.5 %copy-start.15 = (f32[44,16,128]{2,1,0:T(8,128)S(1)}, f32[44,16,128]{2,1,0:T(8,128)}, u32[]{:S(2)}) copy-start(f32[44,16,128]{2,1,0:T(8,128)} %copy-done.14) | copy-start | bytes 1081348
  44.3 6.1 %copy-start.1 = (f32[2,16,16,128]{3,2,1,0:T(8,128)S(1)}, f32[2,16,16,128]{3,2,1,0:T(8,128)}, u32[]{:S(2)}) copy-start(f32[2,16,16,128]{3,2,1,0:T(8,128)} %shard_map.173) | copy-start | bytes 786436
  45.3 5.7 %collective-permute-start.7 = (f32[2,16,4,128]{3,2,1,0:T(4,128)S(1)}, f32[2,16,4,128]{3,2,1,0:T(4,128)S(1)}, u32[]{:S(2)}, u32[]{:S(2)}) collective-permute-start(f32[2,16,4,128]{3,2,1,0:T(4,128)S(1)} %get-tuple-element.32), channel_id=1, source_target_pairs={{1,0},{2,1},{3,2},{5,4},{6,5},{7,6},{9,8},{10,9},{11,10},{13,12},{... | collective-permute-start | bytes 196616 | tf_op jit(solution)/shard_map/ppermute | solution.py:180
  48.5 5.6 %collective-permute-start.6 = (f32[2,16,4,128]{3,2,1,0:T(4,128)S(1)}, f32[2,16,4,128]{3,2,1,0:T(4,128)S(1)}, u32[]{:S(2)}, u32[]{:S(2)}) collective-permute-start(f32[2,16,4,128]{3,2,1,0:T(4,128)S(1)} %get-tuple-element.31), channel_id=1, source_target_pairs={{0,1},{1,2},{2,3},{4,5},{5,6},{6,7},{8,9},{9,10},{10,11},{12,13},{... | collective-permute-start | bytes 196616 | tf_op jit(solution)/shard_map/ppermute | solution.py:179
  54.9 4.9 %copy-start.22 = (bf16[2,8,16,128]{3,2,1,0:T(8,128)(2,1)S(1)}, bf16[2,8,16,128]{3,2,1,0:T(8,128)(2,1)}, u32[]{:S(2)}) copy-start(bf16[2,8,16,128]{3,2,1,0:T(8,128)(2,1)} %param.23) | copy-start | bytes 196612
  58.2 1.6 %copy-start.13 = (f32[2,8,16,128]{3,2,1,0:T(8,128)S(1)}, f32[2,8,16,128]{3,2,1,0:T(8,128)}, u32[]{:S(2)}) copy-start(f32[2,8,16,128]{3,2,1,0:T(8,128)} %shard_map.174) | copy-start | bytes 393220

commit v11 on v8

--- a/solution.py
+++ b/solution.py
@@ -112,7 +112,7 @@
     return below, above
 
 
-def gather_column(traces, time_steps, rec_owner, rec_local):
+def gather_column(traces, time_steps, rec_owner, rec_local, block):
     groups = lax.axis_size("gx")
     held = rec_local.shape[0]
     steps = jnp.arange(traces.shape[0], dtype=jnp.int32)
@@ -120,9 +120,9 @@
     samples = jnp.dot(
         chosen, traces, precision=lax.Precision.HIGHEST, preferred_element_type=jnp.float32
     )
-    payload = jnp.concatenate(
-        [samples, rec_local.astype(jnp.float32)[None], rec_owner[:, 0].astype(jnp.float32)[None]]
-    )
+    assert groups * block < 2**24
+    code = (rec_owner[:, 0] * block + rec_local).astype(jnp.float32)
+    payload = jnp.concatenate([samples, code[None]])
     if groups & (groups - 1) == 0:
         arrived = payload
         step = 1
@@ -131,15 +131,16 @@
             arrived = jnp.concatenate([arrived, partner], axis=1)
             step *= 2
         return arrived
-    sent = jnp.broadcast_to(payload[None], (groups, 4, held))
+    sent = jnp.broadcast_to(payload[None], (groups, 3, held))
     arrived = lax.all_to_all(sent, "gx", split_axis=0, concat_axis=0, tiled=True)
-    return jnp.transpose(arrived, (1, 0, 2)).reshape(4, groups * held)
+    return jnp.transpose(arrived, (1, 0, 2)).reshape(3, groups * held)
 
 
 def sources_over(arrived, values, shape, first, rows):
     sx, sy, sz = shape
-    cell = arrived[2].astype(jnp.int32)
-    owner = arrived[3].astype(jnp.int32)
+    code = arrived[2].astype(jnp.int32)
+    cell = code % (sx * sy * sz)
+    owner = code // (sx * sy * sz)
     row = (owner - lax.axis_index("gx")) * sx + cell // (sy * sz) - first
     inside = (row >= 0) & (row < rows)
     plane = jnp.where(inside, row * sy + cell // sz % sy, -1)
@@ -203,7 +204,7 @@
     lo_y, hi_y = from_neighbours(now_x[:, :, sy - 4 :], now_x[:, :, :4], "gy")
     now_xy = pad_depth(jnp.concatenate([lo_y, now_x, hi_y], axis=2))
 
-    arrived = gather_column(traces, time_steps, rec_owner, rec_local)
+    arrived = gather_column(traces, time_steps, rec_owner, rec_local, sx * sy * sz)
     source_0 = sources_over(arrived, arrived[0:1], (sx, sy, sz), -4, sx + 8)[0]
     source_1 = sources_over(arrived, arrived[1:2], (sx, sy, sz), 0, sx)[0]
 

time: 44.9 us -> 44.5 us (level)
  other arithmetic: 9.75 us -> 9.11 us
    convert_element_type x1 -> x0, other arithmetic: 0.73 us -> none  [gather_column(): rec_owner[:, 0].astype(jnp.float32)[None]]
where the time goes in v11:
time: 44.5 us; the launch traced here: 44 us
  starting transfers between devices  16.2 us (36%)
  waiting for transfers between devices  13 us (29%)
  other arithmetic  9.11 us (20%)
  local copies, waits for them, and re-layouts  2.63 us (6%)
  matrix products  1.84 us (4%)
  between operations  1.19 us (3%)
    ppermute x3, starting transfers between devices, from_neighbours(): lax.ppermute(high_part, axis, [(i + 1, i) for i in range(count - 1)])  7.48 us
    ppermute x2, waiting for transfers between devices, gather_column(): lax.ppermute(arrived, 'gx', [(i, i ^ step) for i in range(groups)])  7.41 us
    ppermute x3, starting transfers between devices, from_neighbours(): below = lax.ppermute(low_part, axis, [(i, i + 1) for i in range(count - 1)])  6.1 us
    ppermute x3, waiting for transfers between devices, from_neighbours(): below = lax.ppermute(low_part, axis, [(i, i + 1) for i in range(count - 1)])  5.61 us
    ppermute x2, starting transfers between devices, gather_column(): lax.ppermute(arrived, 'gx', [(i, i ^ step) for i in range(groups)])  2.65 us
    unnamed x32, local copies, waits for them, and re-layouts  2.31 us
    add x2, other arithmetic, advance(): nxx * dxx + nyy * dyy + nzz * dzz + nxy * dxy + nxz * dxz + nyz * dyz  1.61 us
    add x2, other arithmetic, derivatives(): dz_xwide + weight * (padded[:, :, 4:4 + sy, 4 + k:4 + k + sz] - padded[:,...  1.58 us
  transfers between devices with their start and end apart: 8, of which 3 were waited for; matrix products, arithmetic and copies ran while one was open for 9% of the time, Pallas kernels for 0%

profile of v11, /device:TPU:30, one launch (start us, length us, event | category | flops | bytes accessed | tf_op | source)
XLA Modules:
  0.0 44.0 jit_solution(8985739373467493203)
XLA Ops:
  0.6 0.0 copy-start
  0.7 0.0 copy-start.8
  0.7 0.0 copy-start.9
  0.7 0.0 copy-start.3
  0.7 0.0 copy-start.5
  0.7 0.0 copy-start.4
  0.7 0.0 copy-start.6
  0.7 0.0 copy-start.7
  0.7 0.7 %fusion.209 = f32[1,128]{1,0:T(1,128)S(1)} fusion(s32[128]{0:T(128)} %param.27, s32[128,1]{0,1:T(1,128)} %param.26), kind=kLoop, calls=%fused_computation.420 | loop fusion | flops 384 | bytes 1536 | tf_op jit(solution)/shard_map/broadcast_in_dim | solution.py:125
  1.5 0.2 copy-done
  1.7 0.9 %fusion.201 = f32[2,128]{1,0:T(2,128)S(1)} fusion(f32[1024,128]{1,0:T(8,128)S(1)} %copy-done, s32[2]{0:T(128)} %param.25), kind=kOutput, calls=%fused_computation.378 | convolution fusion | flops 3147776 | bytes 525320 | tf_op jit(solution)/shard_map/dot_general | solution.py:120
  2.7 0.5 %collective-permute-start.4 = (f32[3,128]{1,0:T(4,128)S(1)}, f32[3,128]{1,0:T(4,128)S(1)}, u32[]{:S(2)}, u32[]{:S(2)}) collective-permute-start(f32[3,128]{1,0:T(4,128)S(1)} %pad_maximum_fusion.18), channel_id=1, source_target_pairs={{0,4},{4,0},{8,12},{12,8},{1,5},{5,1},{9,13},{13,9},{2,6},{6,2},{1... | collective-permute-start | bytes 4616 | tf_op jit(solution)/shard_map/ppermute | solution.py:130
  3.2 0.8 %constant_dynamic-update-slice_fusion.17 = f32[44,16,128]{2,1,0:T(8,128)S(1)} fusion(f32[8,16,128]{2,1,0:T(8,128)} %param.14), kind=kLoop, calls=%fused_computation.351 | loop fusion | bytes 131072
  4.0 0.8 %constant_dynamic-update-slice_fusion.16 = f32[44,16,128]{2,1,0:T(8,128)S(1)} fusion(f32[44,16,128]{2,1,0:T(8,128)S(1)} %constant_dynamic-update-slice_fusion.17, f32[8,16,128]{2,1,0:T(8,128)} %param.15), kind=kLoop, calls=%fused_computation.350 | loop fusion | bytes 131072
  4.9 0.0 copy-done.8
  4.9 0.0 copy-done.9
  5.0 0.0 copy-done.3
  5.0 0.0 copy-done.5
  5.0 0.0 copy-done.4
  5.0 0.0 copy-done.6
  5.1 0.0 copy-done.7
  5.1 0.0 copy-start.1
  5.1 0.0 copy-start.2
  5.1 3.6 %collective-permute-start.1 = (f32[44,16,128]{2,1,0:T(8,128)S(1)}, f32[44,16,128]{2,1,0:T(8,128)S(1)}, u32[]{:S(2)}, u32[]{:S(2)}) collective-permute-start(f32[44,16,128]{2,1,0:T(8,128)S(1)} %get-tuple-element.62), channel_id=1, source_target_pairs={{4,0},{8,4},{12,8},{5,1},{9,5},{13,9},{6,2},{10,6},{14,10},{7,3},{... | collective-permute-start | bytes 1081352 | tf_op jit(solution)/shard_map/ppermute | solution.py:111
  8.7 1.3 %collective-permute-start = (f32[44,16,128]{2,1,0:T(8,128)S(1)}, f32[44,16,128]{2,1,0:T(8,128)S(1)}, u32[]{:S(2)}, u32[]{:S(2)}) collective-permute-start(f32[44,16,128]{2,1,0:T(8,128)S(1)} %get-tuple-element.61), channel_id=1, source_target_pairs={{0,4},{4,8},{8,12},{1,5},{5,9},{9,13},{2,6},{6,10},{10,14},{3,7},{... | collective-permute-start | bytes 1081352 | tf_op jit(solution)/shard_map/ppermute | solution.py:110
  10.0 0.2 fusion.227
  10.3 0.3 fusion.212
  10.6 0.0 collective-permute-done.4
  10.6 2.1 %collective-permute-start.5 = (f32[3,256]{1,0:T(4,128)S(1)}, f32[3,256]{1,0:T(4,128)S(1)}, u32[]{:S(2)}, u32[]{:S(2)}) collective-permute-start(f32[3,256]{1,0:T(4,128)S(1)} %pad_maximum_fusion.13), channel_id=1, source_target_pairs={{0,8},{4,12},{8,0},{12,4},{1,9},{5,13},{9,1},{13,5},{2,10},{6,14},... | collective-permute-start | bytes 9224 | tf_op jit(solution)/shard_map/ppermute | solution.py:130
  12.8 7.4 %collective-permute-done.5 = f32[3,256]{1,0:T(4,128)S(1)} collective-permute-done((f32[3,256]{1,0:T(4,128)S(1)}, f32[3,256]{1,0:T(4,128)S(1)}, u32[]{:S(2)}, u32[]{:S(2)}) %collective-permute-start.5) | collective-permute-done | bytes 3104 | tf_op jit(solution)/shard_map/ppermute | solution.py:130
  20.2 0.1 and_select_fusion.3
  20.3 0.5 %fusion.2 = f32[16,16,128]{2,1,0:T(8,128)S(1)} fusion(f32[512]{0:T(512)S(1)} %bitcast.100, s32[16,16]{1,0:T(8,128)S(1)} %multiply_add_fusion.1, s32[512]{0:T(512)S(1)} %bitcast.101, s32[512]{0:T(512)S(1)} %add_select_fusion), kind=kOutput, calls=%fused_computation.36 | convolution fusion | flops 201654272 | bytes 138240 | tf_op jit(solution)/shard_map/cpr,rz->cpz/dot_general | solution.py:151
  20.8 0.0 collective-permute-done.1
  20.8 0.0 collective-permute-done
  20.9 0.0 copy-done.1
  20.9 0.0 copy-done.2
  21.0 1.9 %collective-permute-start.2 = (f32[2,24,4,128]{3,2,1,0:T(4,128)S(1)}, f32[2,24,4,128]{3,2,1,0:T(4,128)S(1)}, u32[]{:S(2)}, u32[]{:S(2)}) collective-permute-start(f32[2,24,4,128]{3,2,1,0:T(4,128)S(1)} %get-tuple-element.28), channel_id=1, source_target_pairs={{1,0},{2,1},{3,2},{5,4},{6,5},{7,6},{9,8},{10,9},{11,10},{13,12},{... | collective-permute-start | bytes 294920 | tf_op jit(solution)/shard_map/ppermute | solution.py:111
  22.9 2.4 %collective-permute-start.3 = (f32[2,24,4,128]{3,2,1,0:T(4,128)S(1)}, f32[2,24,4,128]{3,2,1,0:T(4,128)S(1)}, u32[]{:S(2)}, u32[]{:S(2)}) collective-permute-start(f32[2,24,4,128]{3,2,1,0:T(4,128)S(1)} %get-tuple-element.27), channel_id=1, source_target_pairs={{0,1},{1,2},{2,3},{4,5},{5,6},{6,7},{8,9},{9,10},{10,11},{12,13},{... | collective-permute-start | bytes 294920 | tf_op jit(solution)/shard_map/ppermute | solution.py:110
  25.4 0.3 fusion.197
  25.6 0.3 fusion.198
  26.0 0.0 collective-permute-done.2
  26.0 2.8 %collective-permute-done.3 = f32[2,24,4,128]{3,2,1,0:T(4,128)S(1)} collective-permute-done((f32[2,24,4,128]{3,2,1,0:T(4,128)S(1)}, f32[2,24,4,128]{3,2,1,0:T(4,128)S(1)}, u32[]{:S(2)}, u32[]{:S(2)}) %collective-permute-start.3) | collective-permute-done | bytes 98336 | tf_op jit(solution)/shard_map/ppermute | solution.py:110
  28.8 0.6 %select_maximum_fusion = f32[2,24,24,136]{3,2,1,0:T(8,128)S(1)} fusion(f32[2,24,4,128]{3,2,1,0:T(4,128)S(1)} %collective-permute-done.2, f32[2,24,4,128]{3,2,1,0:T(4,128)S(1)} %collective-permute-done.3, f32[2,8,16,128]{3,2,1,0:T(8,128)S(1)} %bitcast.78, f32[2,8,16,128]{3,2,1,0:T(8,128)S(1)} %bitcast.82, f32[1,8,16,128]{3,2,1,0:T(8,128)S(1)} %bitcast.90, ...), kind=kLoop, calls=%fused_computation.4 | loop fusion | flops 2193408 | bytes 1216512 | tf_op jit(solution)/shard_map/concatenate | solution.py:205
  29.4 0.8 %fusion.6 = f32[2,16,24,128]{3,2,1,0:T(8,128)S(1)} fusion(f32[2,24,24,136]{3,2,1,0:T(8,128)S(1)} %select_maximum_fusion), kind=kLoop, calls=%fused_computation.41 | loop fusion | flops 1081344 | bytes 3538944 | tf_op jit(solution)/shard_map/add | solution.py:53
  30.2 0.1 pad_maximum_fusion
  30.3 1.0 %fusion.13 = (f32[2,24,16,128]{3,2,1,0:T(8,128)S(1)}, f32[2,24,16,128]{3,2,1,0:T(8,128)S(1)}) fusion(f32[2,24,24,136]{3,2,1,0:T(8,128)S(1)} %select_maximum_fusion, f32[2,24,20,128]{3,2,1,0:T(8,128)S(1)} %get-tuple-element.26, f32[2,24,20,128]{3,2,1,0:T(8,128)S(1)} %get-tuple-element.25), kind=kLoop, calls=%fused_computation.52 | loop fusion | flops 2162688 | bytes 7077888 | tf_op jit(solution)/shard_map/add | solution.py:49
  31.3 1.0 %fusion.43 = (f32[2,16,16,128]{3,2,1,0:T(8,128)S(1)}, f32[2,16,16,128]{3,2,1,0:T(8,128)S(1)}, f32[2,16,16,128]{3,2,1,0:T(8,128)S(1)}, f32[2,16,16,128]{3,2,1,0:T(8,128)S(1)}) fusion(f32[2,16,24,128]{3,2,1,0:T(8,128)S(1)} %fusion.6, f32[2,24,16,128]{3,2,1,0:T(8,128)S(1)} %get-tuple-element.81, f32[2,24,16,128]{3,2,1,0:T(8,128)S(1)} %get-tuple-element.82, ...), kind=kLoop, calls=%fused_computation.101 | loop fusion | flops 5570560 | bytes 14548992 | tf_op jit(solution)/shard_map/add | solution.py:90
  32.4 0.1 fusion.176
  32.5 0.1 fusion.181
  32.6 1.9 %collective-permute-start.6 = (f32[2,16,4,128]{3,2,1,0:T(4,128)S(1)}, f32[2,16,4,128]{3,2,1,0:T(4,128)S(1)}, u32[]{:S(2)}, u32[]{:S(2)}) collective-permute-start(f32[2,16,4,128]{3,2,1,0:T(4,128)S(1)} %get-tuple-element.50), channel_id=1, source_target_pairs={{1,0},{2,1},{3,2},{5,4},{6,5},{7,6},{9,8},{10,9},{11,10},{13,12},{... | collective-permute-start | bytes 196616 | tf_op jit(solution)/shard_map/ppermute | solution.py:111
  34.5 2.4 %collective-permute-start.7 = (f32[2,16,4,128]{3,2,1,0:T(4,128)S(1)}, f32[2,16,4,128]{3,2,1,0:T(4,128)S(1)}, u32[]{:S(2)}, u32[]{:S(2)}) collective-permute-start(f32[2,16,4,128]{3,2,1,0:T(4,128)S(1)} %get-tuple-element.49), channel_id=1, source_target_pairs={{0,1},{1,2},{2,3},{4,5},{5,6},{6,7},{8,9},{9,10},{10,11},{12,13},{... | collective-permute-start | bytes 196616 | tf_op jit(solution)/shard_map/ppermute | solution.py:110
  36.9 0.4 fusion.91
  37.3 0.0 collective-permute-done.6
  37.3 2.8 %collective-permute-done.7 = f32[2,16,4,128]{3,2,1,0:T(4,128)S(1)} collective-permute-done((f32[2,16,4,128]{3,2,1,0:T(4,128)S(1)}, f32[2,16,4,128]{3,2,1,0:T(4,128)S(1)}, u32[]{:S(2)}, u32[]{:S(2)}) %collective-permute-start.7) | collective-permute-done | bytes 65568 | tf_op jit(solution)/shard_map/ppermute | solution.py:110
  40.1 0.4 select_maximum_fusion.5
  40.5 0.4 fusion.102
  41.0 0.5 %fusion.27 = f32[2,16,16,128]{3,2,1,0:T(8,128)S(1)} fusion(f32[2,16,24,136]{3,2,1,0:T(8,128)S(1)} %select_maximum_fusion.5), kind=kLoop, calls=%fused_computation.77 | loop fusion | flops 720896 | bytes 2359296 | tf_op jit(solution)/shard_map/add | solution.py:49
  41.5 0.1 pad_maximum_fusion.2
  41.6 0.2 fusion.34
  41.8 0.0 copy-start.10
  41.8 0.6 %fusion.133 = (f32[2,8,16,128]{3,2,1,0:T(8,128)S(1)}, f32[2,8,16,128]{3,2,1,0:T(8,128)S(1)}, f32[2,8,16,128]{3,2,1,0:T(8,128)S(1)}, f32[2,8,16,128]{3,2,1,0:T(8,128)S(1)}) fusion(f32[2,8,24,128]{3,2,1,0:T(8,128)S(1)} %fusion.102, f32[2,16,16,128]{3,2,1,0:T(8,128)S(1)} %fusion.27, f32[2,16,16,128]{3,2,1,0:T(8,128)S(1)} %fusion.34, ...), kind=kLoop, calls=%fused_computation.220 | loop fusion | flops 3080192 | bytes 6422528 | tf_op jit(solution)/shard_map/add | solution.py:90
  42.4 0.3 copy-done.10
  42.6 0.7 %fusion.192 = (f32[8,16,128]{2,1,0:T(8,128)}, f32[8,16,128]{2,1,0:T(8,128)}, f32[8,16,128]{2,1,0:T(8,128)}, f32[8,16,128]{2,1,0:T(8,128)S(1)}) fusion(bf16[2,8,16,128]{3,2,1,0:T(8,128)(2,1)S(1)} %copy-done.10, f32[8,16,128]{2,1,0:T(8,128)S(1)} %fusion.91, f32[8,16,128]{2,1,0:T(8,128)S(1)} %copy-done.3, f32[2,8,16,128]{3,2,1,0:T(8,128)S(1)} %get-tuple-element.11, ...), kind=kLoop, calls=%fused_computation.323 | loop fusion | flops 327680 | bytes 1048576 | tf_op jit(solution)/shard_map/add | solution.py:217
  43.3 0.7 %add_add_fusion = (f32[8,16,128]{2,1,0:T(8,128)}, f32[8,16,128]{2,1,0:T(8,128)}) fusion(f32[8,16,128]{2,1,0:T(8,128)S(1)} %fusion.91, f32[8,16,128]{2,1,0:T(8,128)S(1)} %copy-done.3, f32[8,16,128]{2,1,0:T(8,128)S(1)} %get-tuple-element.8, f32[8,16,128]{2,1,0:T(8,128)S(1)} %copy-done.2, f32[2,8,16,128]{3,2,1,0:T(8,128)S(1)} %get-tuple-element.11, ...), kind=kLoop, calls=%fused_computation.325 | loop fusion | flops 147456 | bytes 589824 | tf_op jit(solution)/shard_map/add | solution.py:99
  (28 shorter events, 0.4 us)
Async XLA Ops:
  0.6 1.1 %copy-start = (f32[1024,128]{1,0:T(8,128)S(1)}, f32[1024,128]{1,0:T(8,128)}, u32[]{:S(2)}) copy-start(f32[1024,128]{1,0:T(8,128)} %param.24) | copy-start | bytes 1572868
  0.7 4.2 %copy-start.8 = (f32[8,16,128]{2,1,0:T(8,128)S(1)}, f32[8,16,128]{2,1,0:T(8,128)}, u32[]{:S(2)}) copy-start(f32[8,16,128]{2,1,0:T(8,128)} %param.16) | copy-start | bytes 196612
  0.7 4.3 %copy-start.9 = (f32[8,16,128]{2,1,0:T(8,128)S(1)}, f32[8,16,128]{2,1,0:T(8,128)}, u32[]{:S(2)}) copy-start(f32[8,16,128]{2,1,0:T(8,128)} %param.17) | copy-start | bytes 196612
  0.7 4.3 %copy-start.3 = (f32[8,16,128]{2,1,0:T(8,128)S(1)}, f32[8,16,128]{2,1,0:T(8,128)}, u32[]{:S(2)}) copy-start(f32[8,16,128]{2,1,0:T(8,128)} %param.18) | copy-start | bytes 196612
  0.7 4.3 %copy-start.5 = (f32[8,16,128]{2,1,0:T(8,128)S(1)}, f32[8,16,128]{2,1,0:T(8,128)}, u32[]{:S(2)}) copy-start(f32[8,16,128]{2,1,0:T(8,128)} %param.19) | copy-start | bytes 196612
  0.7 4.3 %copy-start.4 = (f32[8,16,128]{2,1,0:T(8,128)S(1)}, f32[8,16,128]{2,1,0:T(8,128)}, u32[]{:S(2)}) copy-start(f32[8,16,128]{2,1,0:T(8,128)} %param.20) | copy-start | bytes 196612
  0.7 4.3 %copy-start.6 = (f32[8,16,128]{2,1,0:T(8,128)S(1)}, f32[8,16,128]{2,1,0:T(8,128)}, u32[]{:S(2)}) copy-start(f32[8,16,128]{2,1,0:T(8,128)} %param.21) | copy-start | bytes 196612
  0.7 4.3 %copy-start.7 = (f32[8,16,128]{2,1,0:T(8,128)S(1)}, f32[8,16,128]{2,1,0:T(8,128)}, u32[]{:S(2)}) copy-start(f32[8,16,128]{2,1,0:T(8,128)} %param.22) | copy-start | bytes 196612
  2.7 8.0 %collective-permute-start.4 = (f32[3,128]{1,0:T(4,128)S(1)}, f32[3,128]{1,0:T(4,128)S(1)}, u32[]{:S(2)}, u32[]{:S(2)}) collective-permute-start(f32[3,128]{1,0:T(4,128)S(1)} %pad_maximum_fusion.18), channel_id=1, source_target_pairs={{0,4},{4,0},{8,12},{12,8},{1,5},{5,1},{9,13},{13,9},{2,6},{6,2},{1... | collective-permute-start | bytes 4616 | tf_op jit(solution)/shard_map/ppermute | solution.py:130
  5.1 15.8 %copy-start.1 = (f32[8,16,128]{2,1,0:T(8,128)S(1)}, f32[8,16,128]{2,1,0:T(8,128)}, u32[]{:S(2)}) copy-start(f32[8,16,128]{2,1,0:T(8,128)} %param.14) | copy-start | bytes 196612
  5.1 15.8 %copy-start.2 = (f32[8,16,128]{2,1,0:T(8,128)S(1)}, f32[8,16,128]{2,1,0:T(8,128)}, u32[]{:S(2)}) copy-start(f32[8,16,128]{2,1,0:T(8,128)} %param.15) | copy-start | bytes 196612
  5.1 15.7 %collective-permute-start.1 = (f32[44,16,128]{2,1,0:T(8,128)S(1)}, f32[44,16,128]{2,1,0:T(8,128)S(1)}, u32[]{:S(2)}, u32[]{:S(2)}) collective-permute-start(f32[44,16,128]{2,1,0:T(8,128)S(1)} %get-tuple-element.62), channel_id=1, source_target_pairs={{4,0},{8,4},{12,8},{5,1},{9,5},{13,9},{6,2},{10,6},{14,10},{7,3},{... | collective-permute-start | bytes 1081352 | tf_op jit(solution)/shard_map/ppermute | solution.py:111
  8.7 12.1 %collective-permute-start = (f32[44,16,128]{2,1,0:T(8,128)S(1)}, f32[44,16,128]{2,1,0:T(8,128)S(1)}, u32[]{:S(2)}, u32[]{:S(2)}) collective-permute-start(f32[44,16,128]{2,1,0:T(8,128)S(1)} %get-tuple-element.61), channel_id=1, source_target_pairs={{0,4},{4,8},{8,12},{1,5},{5,9},{9,13},{2,6},{6,10},{10,14},{3,7},{... | collective-permute-start | bytes 1081352 | tf_op jit(solution)/shard_map/ppermute | solution.py:110
  10.6 9.5 %collective-permute-start.5 = (f32[3,256]{1,0:T(4,128)S(1)}, f32[3,256]{1,0:T(4,128)S(1)}, u32[]{:S(2)}, u32[]{:S(2)}) collective-permute-start(f32[3,256]{1,0:T(4,128)S(1)} %pad_maximum_fusion.13), channel_id=1, source_target_pairs={{0,8},{4,12},{8,0},{12,4},{1,9},{5,13},{9,1},{13,5},{2,10},{6,14},... | collective-permute-start | bytes 9224 | tf_op jit(solution)/shard_map/ppermute | solution.py:130
  21.0 5.0 %collective-permute-start.2 = (f32[2,24,4,128]{3,2,1,0:T(4,128)S(1)}, f32[2,24,4,128]{3,2,1,0:T(4,128)S(1)}, u32[]{:S(2)}, u32[]{:S(2)}) collective-permute-start(f32[2,24,4,128]{3,2,1,0:T(4,128)S(1)} %get-tuple-element.28), channel_id=1, source_target_pairs={{1,0},{2,1},{3,2},{5,4},{6,5},{7,6},{9,8},{10,9},{11,10},{13,12},{... | collective-permute-start | bytes 294920 | tf_op jit(solution)/shard_map/ppermute | solution.py:111
  22.9 5.9 %collective-permute-start.3 = (f32[2,24,4,128]{3,2,1,0:T(4,128)S(1)}, f32[2,24,4,128]{3,2,1,0:T(4,128)S(1)}, u32[]{:S(2)}, u32[]{:S(2)}) collective-permute-start(f32[2,24,4,128]{3,2,1,0:T(4,128)S(1)} %get-tuple-element.27), channel_id=1, source_target_pairs={{0,1},{1,2},{2,3},{4,5},{5,6},{6,7},{8,9},{9,10},{10,11},{12,13},{... | collective-permute-start | bytes 294920 | tf_op jit(solution)/shard_map/ppermute | solution.py:110
  32.6 4.7 %collective-permute-start.6 = (f32[2,16,4,128]{3,2,1,0:T(4,128)S(1)}, f32[2,16,4,128]{3,2,1,0:T(4,128)S(1)}, u32[]{:S(2)}, u32[]{:S(2)}) collective-permute-start(f32[2,16,4,128]{3,2,1,0:T(4,128)S(1)} %get-tuple-element.50), channel_id=1, source_target_pairs={{1,0},{2,1},{3,2},{5,4},{6,5},{7,6},{9,8},{10,9},{11,10},{13,12},{... | collective-permute-start | bytes 196616 | tf_op jit(solution)/shard_map/ppermute | solution.py:111
  34.5 5.6 %collective-permute-start.7 = (f32[2,16,4,128]{3,2,1,0:T(4,128)S(1)}, f32[2,16,4,128]{3,2,1,0:T(4,128)S(1)}, u32[]{:S(2)}, u32[]{:S(2)}) collective-permute-start(f32[2,16,4,128]{3,2,1,0:T(4,128)S(1)} %get-tuple-element.49), channel_id=1, source_target_pairs={{0,1},{1,2},{2,3},{4,5},{5,6},{6,7},{8,9},{9,10},{10,11},{12,13},{... | collective-permute-start | bytes 196616 | tf_op jit(solution)/shard_map/ppermute | solution.py:110
  41.8 0.8 %copy-start.10 = (bf16[2,8,16,128]{3,2,1,0:T(8,128)(2,1)S(1)}, bf16[2,8,16,128]{3,2,1,0:T(8,128)(2,1)}, u32[]{:S(2)}) copy-start(bf16[2,8,16,128]{3,2,1,0:T(8,128)(2,1)} %param.23) | copy-start | bytes 196612

commit v12 on v11

--- a/solution.py
+++ b/solution.py
@@ -112,7 +112,7 @@
     return below, above
 
 
-def gather_column(traces, time_steps, rec_owner, rec_local, block):
+def gather_column(traces, time_steps, rec_owner, rec_local, block, after):
     groups = lax.axis_size("gx")
     held = rec_local.shape[0]
     steps = jnp.arange(traces.shape[0], dtype=jnp.int32)
@@ -121,7 +121,7 @@
         chosen, traces, precision=lax.Precision.HIGHEST, preferred_element_type=jnp.float32
     )
     assert groups * block < 2**24
-    code = (rec_owner[:, 0] * block + rec_local).astype(jnp.float32)
+    code = (rec_owner[:, 0] * block + rec_local).astype(jnp.float32) + 0.0 * after
     payload = jnp.concatenate([samples, code[None]])
     if groups & (groups - 1) == 0:
         arrived = payload
@@ -184,6 +184,7 @@
         [p_now, q_now, p_prev[sx - 4 :], q_prev[sx - 4 :]] + [f[sx - 4 :] for f in params]
     )
     high_part = slabs([p_now, q_now, p_prev[:4], q_prev[:4]] + [f[:4] for f in params])
+    low_part, high_part = lax.optimization_barrier((low_part, high_part))
     below, above = from_neighbours(low_part, high_part, "gx")
 
     def unpack(got):
@@ -204,7 +205,9 @@
     lo_y, hi_y = from_neighbours(now_x[:, :, sy - 4 :], now_x[:, :, :4], "gy")
     now_xy = pad_depth(jnp.concatenate([lo_y, now_x, hi_y], axis=2))
 
-    arrived = gather_column(traces, time_steps, rec_owner, rec_local, sx * sy * sz)
+    arrived = gather_column(
+        traces, time_steps, rec_owner, rec_local, sx * sy * sz, low_part[0, 0, 0] + high_part[0, 0, 0]
+    )
     source_0 = sources_over(arrived, arrived[0:1], (sx, sy, sz), -4, sx + 8)[0]
     source_1 = sources_over(arrived, arrived[1:2], (sx, sy, sz), 0, sx)[0]
 

time: 44.5 us -> 48.1 us (1.081)
  local copies, waits for them, and re-layouts: 2.63 us -> 5.81 us
  waiting for transfers between devices: 13 us -> 14.3 us
  between operations: 1.19 us -> 2.48 us
  starting transfers between devices: 16.2 us -> 15.4 us
  other arithmetic: 9.11 us -> 8.38 us
  matrix products: 1.84 us -> 1.18 us
    unnamed x32 -> x38, local copies, waits for them, and re-layouts: 2.31 us -> 4.47 us
    ppermute x2, waiting for transfers between devices: 7.41 us -> 8.72 us  [gather_column(): lax.ppermute(arrived, 'gx', [(i, i ^ step) for i in range(groups)])]
    ppermute x3, starting transfers between devices: 7.48 us -> 6.22 us  [from_neighbours(): lax.ppermute(high_part, axis, [(i + 1, i) for i in range(count - 1)])]
    slice x0 -> x2, local copies, waits for them, and re-layouts: none -> 1.02 us  [the longest x1 0.51 us: local(): low_part[0, 0, 0] + high_part[0, 0, 0]]
    broadcast_in_dim x1, other arithmetic: 0.74 us -> 0.01 us  [gather_column(): payload = jnp.concatenate([samples, code[None]])]
    dot_general x1, matrix products: 0.95 us -> 0.29 us  [gather_column(): jnp.dot(chosen, traces, precision=lax.Precision.HIGHEST, preferred_elemen...]
  transfers between devices with their start and end apart: 8 -> 8, of which waited for: 3 -> 4; matrix products, arithmetic and copies ran while one was open for 9% -> 7% of each run, Pallas kernels for 0% -> 0%
where the time goes in v12:
time: 48.1 us; the launch traced here: 47.6 us
  starting transfers between devices  15.4 us (32%)
  waiting for transfers between devices  14.3 us (30%)
  other arithmetic  8.38 us (17%)
  local copies, waits for them, and re-layouts  5.81 us (12%)
  between operations  2.48 us (5%)
  matrix products  1.18 us (2%)
    ppermute x2, waiting for transfers between devices, gather_column(): lax.ppermute(arrived, 'gx', [(i, i ^ step) for i in range(groups)])  8.72 us
    ppermute x3, starting transfers between devices, from_neighbours(): lax.ppermute(high_part, axis, [(i + 1, i) for i in range(count - 1)])  6.22 us
    ppermute x3, starting transfers between devices, from_neighbours(): below = lax.ppermute(low_part, axis, [(i, i + 1) for i in range(count - 1)])  6.1 us
    ppermute x3, waiting for transfers between devices, from_neighbours(): below = lax.ppermute(low_part, axis, [(i, i + 1) for i in range(count - 1)])  5.59 us
    unnamed x38, local copies, waits for them, and re-layouts  4.47 us
    ppermute x2, starting transfers between devices, gather_column(): lax.ppermute(arrived, 'gx', [(i, i ^ step) for i in range(groups)])  3.08 us
    add x2, other arithmetic, advance(): nxx * dxx + nyy * dyy + nzz * dzz + nxy * dxy + nxz * dxz + nyz * dyz  1.61 us
    add x2, other arithmetic, derivatives(): dz_xwide + weight * (padded[:, :, 4:4 + sy, 4 + k:4 + k + sz] - padded[:,...  1.58 us
  transfers between devices with their start and end apart: 8, of which 4 were waited for; matrix products, arithmetic and copies ran while one was open for 7% of the time, Pallas kernels for 0%

profile of v12, /device:TPU:30, one launch (start us, length us, event | category | flops | bytes accessed | tf_op | source)
XLA Modules:
  0.0 47.6 jit_solution(11925583898378124689)
XLA Ops:
  0.6 0.0 copy-start
  0.6 0.0 copy-start.3
  0.7 0.0 copy-start.5
  0.7 0.0 copy-start.4
  0.7 0.0 copy-start.6
  0.7 0.0 copy-start.7
  0.7 0.0 copy-start.11
  0.7 0.9 %constant_dynamic-update-slice_fusion.8 = f32[44,16,128]{2,1,0:T(8,128)S(1)} fusion(f32[8,16,128]{2,1,0:T(8,128)} %param.14), kind=kLoop, calls=%fused_computation.342 | loop fusion | bytes 131072
  1.6 0.9 %constant_dynamic-update-slice_fusion.7 = f32[44,16,128]{2,1,0:T(8,128)S(1)} fusion(f32[44,16,128]{2,1,0:T(8,128)S(1)} %constant_dynamic-update-slice_fusion.8, f32[8,16,128]{2,1,0:T(8,128)} %param.15), kind=kLoop, calls=%fused_computation.341 | loop fusion | bytes 131072
  2.5 0.8 %constant_dynamic-update-slice_fusion.15 = f32[44,16,128]{2,1,0:T(8,128)S(1)} fusion(f32[44,16,128]{2,1,0:T(8,128)S(1)} %constant_dynamic-update-slice_fusion.7, f32[8,16,128]{2,1,0:T(8,128)} %param.16), kind=kLoop, calls=%fused_computation.349 | loop fusion | bytes 65536
  3.3 0.8 %constant_dynamic-update-slice_fusion.6 = f32[44,16,128]{2,1,0:T(8,128)S(1)} fusion(f32[44,16,128]{2,1,0:T(8,128)S(1)} %copy.21, f32[8,16,128]{2,1,0:T(8,128)} %param.16), kind=kLoop, calls=%fused_computation.340 | loop fusion | bytes 65536
  4.0 0.8 %constant_dynamic-update-slice_fusion.14 = (f32[44,16,128]{2,1,0:T(8,128)S(1)}, f32[44,16,128]{2,1,0:T(8,128)S(1)}) fusion(f32[44,16,128]{2,1,0:T(8,128)S(1)} %constant_dynamic-update-slice_fusion.15, f32[8,16,128]{2,1,0:T(8,128)} %param.17, f32[44,16,128]{2,1,0:T(8,128)S(1)} %constant_dynamic-update-slice_fusion.6), kind=kLoop, calls=%fused_computation.348 | loop fusion | bytes 131072
  4.8 0.0 copy-done.3
  4.8 0.0 copy-done.5
  4.9 2.4 %collective-permute-start.1 = (f32[44,16,128]{2,1,0:T(8,128)S(1)}, f32[44,16,128]{2,1,0:T(8,128)S(1)}, u32[]{:S(2)}, u32[]{:S(2)}) collective-permute-start(f32[44,16,128]{2,1,0:T(8,128)S(1)} %get-tuple-element.8), channel_id=1, source_target_pairs={{4,0},{8,4},{12,8},{5,1},{9,5},{13,9},{6,2},{10,6},{14,10},{7,3},{... | collective-permute-start | bytes 1081352 | tf_op jit(solution)/shard_map/ppermute | solution.py:111
  7.3 1.3 %collective-permute-start = (f32[44,16,128]{2,1,0:T(8,128)S(1)}, f32[44,16,128]{2,1,0:T(8,128)S(1)}, u32[]{:S(2)}, u32[]{:S(2)}) collective-permute-start(f32[44,16,128]{2,1,0:T(8,128)S(1)} %get-tuple-element.7), channel_id=1, source_target_pairs={{0,4},{4,8},{8,12},{1,5},{5,9},{9,13},{2,6},{6,10},{10,14},{3,7},{... | collective-permute-start | bytes 1081352 | tf_op jit(solution)/shard_map/ppermute | solution.py:110
  8.6 0.5 %slice.809 = f32[1,1,1]{2,1,0:T(1,128)} slice(f32[44,16,128]{2,1,0:T(8,128)S(1)} %get-tuple-element.7), slice={[0:1], [0:1], [0:1]} | slice | bytes 8 | tf_op jit(solution)/shard_map/slice | solution.py:209
  9.1 0.5 %slice.810 = f32[1,1,1]{2,1,0:T(1,128)} slice(f32[44,16,128]{2,1,0:T(8,128)S(1)} %get-tuple-element.8), slice={[0:1], [0:1], [0:1]} | slice | bytes 8 | tf_op jit(solution)/shard_map/slice | solution.py:209
  11.0 0.0 copy-done
  11.0 0.0 copy-done.11
  11.0 0.3 fusion.201
  11.3 0.0 copy-start.2
  11.3 2.7 %collective-permute-start.4 = (f32[3,128]{1,0:T(4,128)S(1)}, f32[3,128]{1,0:T(4,128)S(1)}, u32[]{:S(2)}, u32[]{:S(2)}) collective-permute-start(f32[3,128]{1,0:T(4,128)S(1)} %pad_maximum_fusion.18), channel_id=1, source_target_pairs={{0,4},{4,0},{8,12},{12,8},{1,5},{5,1},{9,13},{13,9},{2,6},{6,2},{1... | collective-permute-start | bytes 4616 | tf_op jit(solution)/shard_map/ppermute | solution.py:130
  14.0 0.2 fusion.228
  14.3 0.3 fusion.213
  14.6 4.5 %collective-permute-done.4 = f32[3,128]{1,0:T(4,128)S(1)} collective-permute-done((f32[3,128]{1,0:T(4,128)S(1)}, f32[3,128]{1,0:T(4,128)S(1)}, u32[]{:S(2)}, u32[]{:S(2)}) %collective-permute-start.4) | collective-permute-done | bytes 1568 | tf_op jit(solution)/shard_map/ppermute | solution.py:130
  19.1 0.4 collective-permute-start.5
  19.5 4.2 %collective-permute-done.5 = f32[3,256]{1,0:T(4,128)S(1)} collective-permute-done((f32[3,256]{1,0:T(4,128)S(1)}, f32[3,256]{1,0:T(4,128)S(1)}, u32[]{:S(2)}, u32[]{:S(2)}) %collective-permute-start.5) | collective-permute-done | bytes 3104 | tf_op jit(solution)/shard_map/ppermute | solution.py:130
  23.7 0.1 and_select_fusion.3
  23.8 0.0 copy-start.8
  23.8 0.0 copy-start.9
  23.9 0.5 %fusion.2 = f32[16,16,128]{2,1,0:T(8,128)S(1)} fusion(f32[512]{0:T(512)S(1)} %bitcast.103, s32[16,16]{1,0:T(8,128)S(1)} %multiply_add_fusion.1, s32[512]{0:T(512)S(1)} %bitcast.104, s32[512]{0:T(512)S(1)} %add_select_fusion), kind=kOutput, calls=%fused_computation.36 | convolution fusion | flops 201654272 | bytes 138240 | tf_op jit(solution)/shard_map/cpr,rz->cpz/dot_general | solution.py:151
  24.4 0.0 collective-permute-done.1
  24.4 0.0 collective-permute-done
  24.4 0.0 copy-done.1
  24.4 0.0 copy-done.2
  24.5 1.9 %collective-permute-start.2 = (f32[2,24,4,128]{3,2,1,0:T(4,128)S(1)}, f32[2,24,4,128]{3,2,1,0:T(4,128)S(1)}, u32[]{:S(2)}, u32[]{:S(2)}) collective-permute-start(f32[2,24,4,128]{3,2,1,0:T(4,128)S(1)} %get-tuple-element.32), channel_id=1, source_target_pairs={{1,0},{2,1},{3,2},{5,4},{6,5},{7,6},{9,8},{10,9},{11,10},{13,12},{... | collective-permute-start | bytes 294920 | tf_op jit(solution)/shard_map/ppermute | solution.py:111
  26.5 2.4 %collective-permute-start.3 = (f32[2,24,4,128]{3,2,1,0:T(4,128)S(1)}, f32[2,24,4,128]{3,2,1,0:T(4,128)S(1)}, u32[]{:S(2)}, u32[]{:S(2)}) collective-permute-start(f32[2,24,4,128]{3,2,1,0:T(4,128)S(1)} %get-tuple-element.31), channel_id=1, source_target_pairs={{0,1},{1,2},{2,3},{4,5},{5,6},{6,7},{8,9},{9,10},{10,11},{12,13},{... | collective-permute-start | bytes 294920 | tf_op jit(solution)/shard_map/ppermute | solution.py:110
  28.9 0.3 fusion.197
  29.2 0.3 fusion.198
  29.6 0.0 collective-permute-done.2
  29.6 2.8 %collective-permute-done.3 = f32[2,24,4,128]{3,2,1,0:T(4,128)S(1)} collective-permute-done((f32[2,24,4,128]{3,2,1,0:T(4,128)S(1)}, f32[2,24,4,128]{3,2,1,0:T(4,128)S(1)}, u32[]{:S(2)}, u32[]{:S(2)}) %collective-permute-start.3) | collective-permute-done | bytes 98336 | tf_op jit(solution)/shard_map/ppermute | solution.py:110
  32.4 0.6 %select_maximum_fusion = f32[2,24,24,136]{3,2,1,0:T(8,128)S(1)} fusion(f32[2,24,4,128]{3,2,1,0:T(4,128)S(1)} %collective-permute-done.2, f32[2,24,4,128]{3,2,1,0:T(4,128)S(1)} %collective-permute-done.3, f32[2,8,16,128]{3,2,1,0:T(8,128)S(1)} %bitcast.81, f32[2,8,16,128]{3,2,1,0:T(8,128)S(1)} %bitcast.85, f32[1,8,16,128]{3,2,1,0:T(8,128)S(1)} %bitcast.93, ...), kind=kLoop, calls=%fused_computation.4 | loop fusion | flops 2193408 | bytes 1216512 | tf_op jit(solution)/shard_map/concatenate | solution.py:206
  33.0 0.8 %fusion.6 = f32[2,16,24,128]{3,2,1,0:T(8,128)S(1)} fusion(f32[2,24,24,136]{3,2,1,0:T(8,128)S(1)} %select_maximum_fusion), kind=kLoop, calls=%fused_computation.41 | loop fusion | flops 1081344 | bytes 3538944 | tf_op jit(solution)/shard_map/add | solution.py:53
  33.8 0.1 pad_maximum_fusion
  33.9 1.0 %fusion.13 = (f32[2,24,16,128]{3,2,1,0:T(8,128)S(1)}, f32[2,24,16,128]{3,2,1,0:T(8,128)S(1)}) fusion(f32[2,24,24,136]{3,2,1,0:T(8,128)S(1)} %select_maximum_fusion, f32[2,24,20,128]{3,2,1,0:T(8,128)S(1)} %get-tuple-element.30, f32[2,24,20,128]{3,2,1,0:T(8,128)S(1)} %get-tuple-element.29), kind=kLoop, calls=%fused_computation.52 | loop fusion | flops 2162688 | bytes 7077888 | tf_op jit(solution)/shard_map/add | solution.py:49
  34.9 1.0 %fusion.43 = (f32[2,16,16,128]{3,2,1,0:T(8,128)S(1)}, f32[2,16,16,128]{3,2,1,0:T(8,128)S(1)}, f32[2,16,16,128]{3,2,1,0:T(8,128)S(1)}, f32[2,16,16,128]{3,2,1,0:T(8,128)S(1)}) fusion(f32[2,16,24,128]{3,2,1,0:T(8,128)S(1)} %fusion.6, f32[2,24,16,128]{3,2,1,0:T(8,128)S(1)} %get-tuple-element.85, f32[2,24,16,128]{3,2,1,0:T(8,128)S(1)} %get-tuple-element.86, ...), kind=kLoop, calls=%fused_computation.101 | loop fusion | flops 5570560 | bytes 14548992 | tf_op jit(solution)/shard_map/add | solution.py:90
  35.9 0.1 fusion.176
  36.0 0.1 fusion.181
  36.2 1.9 %collective-permute-start.6 = (f32[2,16,4,128]{3,2,1,0:T(4,128)S(1)}, f32[2,16,4,128]{3,2,1,0:T(4,128)S(1)}, u32[]{:S(2)}, u32[]{:S(2)}) collective-permute-start(f32[2,16,4,128]{3,2,1,0:T(4,128)S(1)} %get-tuple-element.54), channel_id=1, source_target_pairs={{1,0},{2,1},{3,2},{5,4},{6,5},{7,6},{9,8},{10,9},{11,10},{13,12},{... | collective-permute-start | bytes 196616 | tf_op jit(solution)/shard_map/ppermute | solution.py:111
  38.1 2.4 %collective-permute-start.7 = (f32[2,16,4,128]{3,2,1,0:T(4,128)S(1)}, f32[2,16,4,128]{3,2,1,0:T(4,128)S(1)}, u32[]{:S(2)}, u32[]{:S(2)}) collective-permute-start(f32[2,16,4,128]{3,2,1,0:T(4,128)S(1)} %get-tuple-element.53), channel_id=1, source_target_pairs={{0,1},{1,2},{2,3},{4,5},{5,6},{6,7},{8,9},{9,10},{10,11},{12,13},{... | collective-permute-start | bytes 196616 | tf_op jit(solution)/shard_map/ppermute | solution.py:110
  40.5 0.4 fusion.91
  40.9 0.0 collective-permute-done.6
  40.9 2.8 %collective-permute-done.7 = f32[2,16,4,128]{3,2,1,0:T(4,128)S(1)} collective-permute-done((f32[2,16,4,128]{3,2,1,0:T(4,128)S(1)}, f32[2,16,4,128]{3,2,1,0:T(4,128)S(1)}, u32[]{:S(2)}, u32[]{:S(2)}) %collective-permute-start.7) | collective-permute-done | bytes 65568 | tf_op jit(solution)/shard_map/ppermute | solution.py:110
  43.7 0.4 select_maximum_fusion.5
  44.1 0.4 fusion.102
  44.5 0.5 %fusion.27 = f32[2,16,16,128]{3,2,1,0:T(8,128)S(1)} fusion(f32[2,16,24,136]{3,2,1,0:T(8,128)S(1)} %select_maximum_fusion.5), kind=kLoop, calls=%fused_computation.77 | loop fusion | flops 720896 | bytes 2359296 | tf_op jit(solution)/shard_map/add | solution.py:49
  45.1 0.1 pad_maximum_fusion.2
  45.1 0.2 fusion.34
  45.3 0.0 copy-start.10
  45.4 0.6 %fusion.133 = (f32[2,8,16,128]{3,2,1,0:T(8,128)S(1)}, f32[2,8,16,128]{3,2,1,0:T(8,128)S(1)}, f32[2,8,16,128]{3,2,1,0:T(8,128)S(1)}, f32[2,8,16,128]{3,2,1,0:T(8,128)S(1)}) fusion(f32[2,8,24,128]{3,2,1,0:T(8,128)S(1)} %fusion.102, f32[2,16,16,128]{3,2,1,0:T(8,128)S(1)} %fusion.27, f32[2,16,16,128]{3,2,1,0:T(8,128)S(1)} %fusion.34, ...), kind=kLoop, calls=%fused_computation.220 | loop fusion | flops 3080192 | bytes 6422528 | tf_op jit(solution)/shard_map/add | solution.py:90
  45.9 0.3 copy-done.10
  46.2 0.7 %fusion.192 = (f32[8,16,128]{2,1,0:T(8,128)}, f32[8,16,128]{2,1,0:T(8,128)}, f32[8,16,128]{2,1,0:T(8,128)}, f32[8,16,128]{2,1,0:T(8,128)S(1)}) fusion(bf16[2,8,16,128]{3,2,1,0:T(8,128)(2,1)S(1)} %copy-done.10, f32[8,16,128]{2,1,0:T(8,128)S(1)} %fusion.91, f32[8,16,128]{2,1,0:T(8,128)S(1)} %copy-done.3, f32[2,8,16,128]{3,2,1,0:T(8,128)S(1)} %get-tuple-element.15, ...), kind=kLoop, calls=%fused_computation.323 | loop fusion | flops 327680 | bytes 1048576 | tf_op jit(solution)/shard_map/add | solution.py:220
  46.9 0.7 %add_add_fusion = (f32[8,16,128]{2,1,0:T(8,128)}, f32[8,16,128]{2,1,0:T(8,128)}) fusion(f32[8,16,128]{2,1,0:T(8,128)S(1)} %fusion.91, f32[8,16,128]{2,1,0:T(8,128)S(1)} %copy-done.3, f32[8,16,128]{2,1,0:T(8,128)S(1)} %get-tuple-element.12, f32[8,16,128]{2,1,0:T(8,128)S(1)} %copy-done.2, f32[2,8,16,128]{3,2,1,0:T(8,128)S(1)} %get-tuple-element.15, ...), kind=kLoop, calls=%fused_computation.325 | loop fusion | flops 147456 | bytes 589824 | tf_op jit(solution)/shard_map/add | solution.py:99
  (36 shorter events, 0.4 us)
Async XLA Ops:
  0.6 10.3 %copy-start = (f32[1024,128]{1,0:T(8,128)S(1)}, f32[1024,128]{1,0:T(8,128)}, u32[]{:S(2)}) copy-start(f32[1024,128]{1,0:T(8,128)} %param.24) | copy-start | bytes 1572868
  0.6 4.2 %copy-start.3 = (f32[8,16,128]{2,1,0:T(8,128)S(1)}, f32[8,16,128]{2,1,0:T(8,128)}, u32[]{:S(2)}) copy-start(f32[8,16,128]{2,1,0:T(8,128)} %param.18) | copy-start | bytes 196612
  0.7 4.2 %copy-start.5 = (f32[8,16,128]{2,1,0:T(8,128)S(1)}, f32[8,16,128]{2,1,0:T(8,128)}, u32[]{:S(2)}) copy-start(f32[8,16,128]{2,1,0:T(8,128)} %param.19) | copy-start | bytes 196612
  0.7 4.2 %copy-start.4 = (f32[8,16,128]{2,1,0:T(8,128)S(1)}, f32[8,16,128]{2,1,0:T(8,128)}, u32[]{:S(2)}) copy-start(f32[8,16,128]{2,1,0:T(8,128)} %param.20) | copy-start | bytes 196612
  0.7 4.2 %copy-start.6 = (f32[8,16,128]{2,1,0:T(8,128)S(1)}, f32[8,16,128]{2,1,0:T(8,128)}, u32[]{:S(2)}) copy-start(f32[8,16,128]{2,1,0:T(8,128)} %param.21) | copy-start | bytes 196612
  0.7 4.2 %copy-start.7 = (f32[8,16,128]{2,1,0:T(8,128)S(1)}, f32[8,16,128]{2,1,0:T(8,128)}, u32[]{:S(2)}) copy-start(f32[8,16,128]{2,1,0:T(8,128)} %param.22) | copy-start | bytes 196612
  0.7 10.3 %copy-start.11 = (s32[2]{0:T(128)S(1)}, s32[2]{0:T(128)}, u32[]{:S(2)}) copy-start(s32[2]{0:T(128)} %param.25) | copy-start | bytes 28
  1.6 9.7 %copy-start.12 = (s32[128]{0:T(128)S(1)}, s32[128]{0:T(128)}, u32[]{:S(2)}) copy-start(s32[128]{0:T(128)} %param.27) | copy-start | bytes 1540
  1.6 9.7 %copy-start.13 = (s32[128,1]{0,1:T(1,128)S(1)}, s32[128,1]{0,1:T(1,128)}, u32[]{:S(2)}) copy-start(s32[128,1]{0,1:T(1,128)} %param.26) | copy-start | bytes 1540
  4.9 19.4 %collective-permute-start.1 = (f32[44,16,128]{2,1,0:T(8,128)S(1)}, f32[44,16,128]{2,1,0:T(8,128)S(1)}, u32[]{:S(2)}, u32[]{:S(2)}) collective-permute-start(f32[44,16,128]{2,1,0:T(8,128)S(1)} %get-tuple-element.8), channel_id=1, source_target_pairs={{4,0},{8,4},{12,8},{5,1},{9,5},{13,9},{6,2},{10,6},{14,10},{7,3},{... | collective-permute-start | bytes 1081352 | tf_op jit(solution)/shard_map/ppermute | solution.py:111
  7.3 17.1 %collective-permute-start = (f32[44,16,128]{2,1,0:T(8,128)S(1)}, f32[44,16,128]{2,1,0:T(8,128)S(1)}, u32[]{:S(2)}, u32[]{:S(2)}) collective-permute-start(f32[44,16,128]{2,1,0:T(8,128)S(1)} %get-tuple-element.7), channel_id=1, source_target_pairs={{0,4},{4,8},{8,12},{1,5},{5,9},{9,13},{2,6},{6,10},{10,14},{3,7},{... | collective-permute-start | bytes 1081352 | tf_op jit(solution)/shard_map/ppermute | solution.py:110
  11.3 13.2 %copy-start.1 = (f32[8,16,128]{2,1,0:T(8,128)S(1)}, f32[8,16,128]{2,1,0:T(8,128)}, u32[]{:S(2)}) copy-start(f32[8,16,128]{2,1,0:T(8,128)} %param.14) | copy-start | bytes 196612
  11.3 13.2 %copy-start.2 = (f32[8,16,128]{2,1,0:T(8,128)S(1)}, f32[8,16,128]{2,1,0:T(8,128)}, u32[]{:S(2)}) copy-start(f32[8,16,128]{2,1,0:T(8,128)} %param.15) | copy-start | bytes 196612
  11.3 7.8 %collective-permute-start.4 = (f32[3,128]{1,0:T(4,128)S(1)}, f32[3,128]{1,0:T(4,128)S(1)}, u32[]{:S(2)}, u32[]{:S(2)}) collective-permute-start(f32[3,128]{1,0:T(4,128)S(1)} %pad_maximum_fusion.18), channel_id=1, source_target_pairs={{0,4},{4,0},{8,12},{12,8},{1,5},{5,1},{9,13},{13,9},{2,6},{6,2},{1... | collective-permute-start | bytes 4616 | tf_op jit(solution)/shard_map/ppermute | solution.py:130
  19.1 4.6 %collective-permute-start.5 = (f32[3,256]{1,0:T(4,128)S(1)}, f32[3,256]{1,0:T(4,128)S(1)}, u32[]{:S(2)}, u32[]{:S(2)}) collective-permute-start(f32[3,256]{1,0:T(4,128)S(1)} %pad_maximum_fusion.13), channel_id=1, source_target_pairs={{0,8},{4,12},{8,0},{12,4},{1,9},{5,13},{9,1},{13,5},{2,10},{6,14},... | collective-permute-start | bytes 9224 | tf_op jit(solution)/shard_map/ppermute | solution.py:130
  23.8 5.1 %copy-start.8 = (f32[8,16,128]{2,1,0:T(8,128)S(1)}, f32[8,16,128]{2,1,0:T(8,128)}, u32[]{:S(2)}) copy-start(f32[8,16,128]{2,1,0:T(8,128)} %param.16) | copy-start | bytes 196612
  23.8 5.1 %copy-start.9 = (f32[8,16,128]{2,1,0:T(8,128)S(1)}, f32[8,16,128]{2,1,0:T(8,128)}, u32[]{:S(2)}) copy-start(f32[8,16,128]{2,1,0:T(8,128)} %param.17) | copy-start | bytes 196612
  24.5 5.0 %collective-permute-start.2 = (f32[2,24,4,128]{3,2,1,0:T(4,128)S(1)}, f32[2,24,4,128]{3,2,1,0:T(4,128)S(1)}, u32[]{:S(2)}, u32[]{:S(2)}) collective-permute-start(f32[2,24,4,128]{3,2,1,0:T(4,128)S(1)} %get-tuple-element.32), channel_id=1, source_target_pairs={{1,0},{2,1},{3,2},{5,4},{6,5},{7,6},{9,8},{10,9},{11,10},{13,12},{... | collective-permute-start | bytes 294920 | tf_op jit(solution)/shard_map/ppermute | solution.py:111
  26.5 5.9 %collective-permute-start.3 = (f32[2,24,4,128]{3,2,1,0:T(4,128)S(1)}, f32[2,24,4,128]{3,2,1,0:T(4,128)S(1)}, u32[]{:S(2)}, u32[]{:S(2)}) collective-permute-start(f32[2,24,4,128]{3,2,1,0:T(4,128)S(1)} %get-tuple-element.31), channel_id=1, source_target_pairs={{0,1},{1,2},{2,3},{4,5},{5,6},{6,7},{8,9},{9,10},{10,11},{12,13},{... | collective-permute-start | bytes 294920 | tf_op jit(solution)/shard_map/ppermute | solution.py:110
  36.2 4.7 %collective-permute-start.6 = (f32[2,16,4,128]{3,2,1,0:T(4,128)S(1)}, f32[2,16,4,128]{3,2,1,0:T(4,128)S(1)}, u32[]{:S(2)}, u32[]{:S(2)}) collective-permute-start(f32[2,16,4,128]{3,2,1,0:T(4,128)S(1)} %get-tuple-element.54), channel_id=1, source_target_pairs={{1,0},{2,1},{3,2},{5,4},{6,5},{7,6},{9,8},{10,9},{11,10},{13,12},{... | collective-permute-start | bytes 196616 | tf_op jit(solution)/shard_map/ppermute | solution.py:111
  38.1 5.6 %collective-permute-start.7 = (f32[2,16,4,128]{3,2,1,0:T(4,128)S(1)}, f32[2,16,4,128]{3,2,1,0:T(4,128)S(1)}, u32[]{:S(2)}, u32[]{:S(2)}) collective-permute-start(f32[2,16,4,128]{3,2,1,0:T(4,128)S(1)} %get-tuple-element.53), channel_id=1, source_target_pairs={{0,1},{1,2},{2,3},{4,5},{5,6},{6,7},{8,9},{9,10},{10,11},{12,13},{... | collective-permute-start | bytes 196616 | tf_op jit(solution)/shard_map/ppermute | solution.py:110
  45.3 0.8 %copy-start.10 = (bf16[2,8,16,128]{3,2,1,0:T(8,128)(2,1)S(1)}, bf16[2,8,16,128]{3,2,1,0:T(8,128)(2,1)}, u32[]{:S(2)}) copy-start(bf16[2,8,16,128]{3,2,1,0:T(8,128)(2,1)} %param.23) | copy-start | bytes 196612

commit v13 on v11

--- a/solution.py
+++ b/solution.py
@@ -125,11 +125,11 @@
     payload = jnp.concatenate([samples, code[None]])
     if groups & (groups - 1) == 0:
         arrived = payload
-        step = 1
-        while step < groups:
+        step = groups // 2
+        while step >= 1:
             partner = lax.ppermute(arrived, "gx", [(i, i ^ step) for i in range(groups)])
             arrived = jnp.concatenate([arrived, partner], axis=1)
-            step *= 2
+            step //= 2
         return arrived
     sent = jnp.broadcast_to(payload[None], (groups, 3, held))
     arrived = lax.all_to_all(sent, "gx", split_axis=0, concat_axis=0, tiled=True)

time: 44.5 us -> 45.6 us (1.025)
  the two profiles are of different devices: /device:TPU:30 before, /device:TPU:14 now
where the time goes in v13:
time: 45.6 us; the launch traced here: 45.1 us
  starting transfers between devices  17.8 us (39%)
  waiting for transfers between devices  12.6 us (28%)
  other arithmetic  9.11 us (20%)
  local copies, waits for them, and re-layouts  2.63 us (6%)
  matrix products  1.84 us (4%)
  between operations  1.19 us (3%)
    ppermute x3, starting transfers between devices, from_neighbours(): below = lax.ppermute(low_part, axis, [(i, i + 1) for i in range(count - 1)])  8.3 us
    ppermute x2, waiting for transfers between devices, gather_column(): lax.ppermute(arrived, 'gx', [(i, i ^ step) for i in range(groups)])  6.95 us
    ppermute x3, starting transfers between devices, from_neighbours(): lax.ppermute(high_part, axis, [(i + 1, i) for i in range(count - 1)])  6.33 us
    ppermute x3, waiting for transfers between devices, from_neighbours(): below = lax.ppermute(low_part, axis, [(i, i + 1) for i in range(count - 1)])  5.61 us
    ppermute x2, starting transfers between devices, gather_column(): lax.ppermute(arrived, 'gx', [(i, i ^ step) for i in range(groups)])  3.19 us
    unnamed x32, local copies, waits for them, and re-layouts  2.31 us
    add x2, other arithmetic, advance(): nxx * dxx + nyy * dyy + nzz * dzz + nxy * dxy + nxz * dxz + nyz * dyz  1.61 us
    add x2, other arithmetic, derivatives(): dz_xwide + weight * (padded[:, :, 4:4 + sy, 4 + k:4 + k + sz] - padded[:,...  1.58 us
  transfers between devices with their start and end apart: 8, of which 3 were waited for; matrix products, arithmetic and copies ran while one was open for 9% of the time, Pallas kernels for 0%

profile of v13, /device:TPU:14, one launch (start us, length us, event | category | flops | bytes accessed | tf_op | source)
XLA Modules:
  0.0 45.1 jit_solution(13804510076285026887)
XLA Ops:
  0.6 0.0 copy-start
  0.7 0.0 copy-start.8
  0.7 0.0 copy-start.9
  0.7 0.0 copy-start.3
  0.7 0.0 copy-start.5
  0.7 0.0 copy-start.4
  0.7 0.0 copy-start.6
  0.7 0.0 copy-start.7
  0.7 0.7 %fusion.209 = f32[1,128]{1,0:T(1,128)S(1)} fusion(s32[128]{0:T(128)} %param.27, s32[128,1]{0,1:T(1,128)} %param.26), kind=kLoop, calls=%fused_computation.420 | loop fusion | flops 384 | bytes 1536 | tf_op jit(solution)/shard_map/broadcast_in_dim | solution.py:125
  1.5 0.2 copy-done
  1.7 0.9 %fusion.201 = f32[2,128]{1,0:T(2,128)S(1)} fusion(f32[1024,128]{1,0:T(8,128)S(1)} %copy-done, s32[2]{0:T(128)} %param.25), kind=kOutput, calls=%fused_computation.378 | convolution fusion | flops 3147776 | bytes 525320 | tf_op jit(solution)/shard_map/dot_general | solution.py:120
  2.7 2.7 %collective-permute-start.4 = (f32[3,128]{1,0:T(4,128)S(1)}, f32[3,128]{1,0:T(4,128)S(1)}, u32[]{:S(2)}, u32[]{:S(2)}) collective-permute-start(f32[3,128]{1,0:T(4,128)S(1)} %pad_maximum_fusion.18), channel_id=1, source_target_pairs={{0,8},{4,12},{8,0},{12,4},{1,9},{5,13},{9,1},{13,5},{2,10},{6,14},... | collective-permute-start | bytes 4616 | tf_op jit(solution)/shard_map/ppermute | solution.py:130
  5.3 0.8 %constant_dynamic-update-slice_fusion.17 = f32[44,16,128]{2,1,0:T(8,128)S(1)} fusion(f32[8,16,128]{2,1,0:T(8,128)} %param.14), kind=kLoop, calls=%fused_computation.351 | loop fusion | bytes 131072
  6.2 0.8 %constant_dynamic-update-slice_fusion.16 = f32[44,16,128]{2,1,0:T(8,128)S(1)} fusion(f32[44,16,128]{2,1,0:T(8,128)S(1)} %constant_dynamic-update-slice_fusion.17, f32[8,16,128]{2,1,0:T(8,128)} %param.15), kind=kLoop, calls=%fused_computation.350 | loop fusion | bytes 131072
  7.0 0.0 copy-done.8
  7.1 0.0 copy-done.9
  7.1 0.0 copy-done.3
  7.1 0.0 copy-done.5
  7.1 0.0 copy-done.4
  7.2 0.0 copy-done.6
  7.2 0.0 copy-done.7
  7.2 0.0 copy-start.1
  7.2 0.0 copy-start.2
  7.2 2.5 %collective-permute-start.1 = (f32[44,16,128]{2,1,0:T(8,128)S(1)}, f32[44,16,128]{2,1,0:T(8,128)S(1)}, u32[]{:S(2)}, u32[]{:S(2)}) collective-permute-start(f32[44,16,128]{2,1,0:T(8,128)S(1)} %get-tuple-element.62), channel_id=1, source_target_pairs={{4,0},{8,4},{12,8},{5,1},{9,5},{13,9},{6,2},{10,6},{14,10},{7,3},{... | collective-permute-start | bytes 1081352 | tf_op jit(solution)/shard_map/ppermute | solution.py:111
  9.7 3.5 %collective-permute-start = (f32[44,16,128]{2,1,0:T(8,128)S(1)}, f32[44,16,128]{2,1,0:T(8,128)S(1)}, u32[]{:S(2)}, u32[]{:S(2)}) collective-permute-start(f32[44,16,128]{2,1,0:T(8,128)S(1)} %get-tuple-element.61), channel_id=1, source_target_pairs={{0,4},{4,8},{8,12},{1,5},{5,9},{9,13},{2,6},{6,10},{10,14},{3,7},{... | collective-permute-start | bytes 1081352 | tf_op jit(solution)/shard_map/ppermute | solution.py:110
  13.2 0.2 fusion.227
  13.5 0.3 fusion.212
  13.8 0.0 collective-permute-done.4
  13.8 0.5 %collective-permute-start.5 = (f32[3,256]{1,0:T(4,128)S(1)}, f32[3,256]{1,0:T(4,128)S(1)}, u32[]{:S(2)}, u32[]{:S(2)}) collective-permute-start(f32[3,256]{1,0:T(4,128)S(1)} %pad_maximum_fusion.13), channel_id=1, source_target_pairs={{0,4},{4,0},{8,12},{12,8},{1,5},{5,1},{9,13},{13,9},{2,6},{6,2},{1... | collective-permute-start | bytes 9224 | tf_op jit(solution)/shard_map/ppermute | solution.py:130
  14.4 6.9 %collective-permute-done.5 = f32[3,256]{1,0:T(4,128)S(1)} collective-permute-done((f32[3,256]{1,0:T(4,128)S(1)}, f32[3,256]{1,0:T(4,128)S(1)}, u32[]{:S(2)}, u32[]{:S(2)}) %collective-permute-start.5) | collective-permute-done | bytes 3104 | tf_op jit(solution)/shard_map/ppermute | solution.py:130
  21.3 0.1 and_select_fusion.3
  21.4 0.5 %fusion.2 = f32[16,16,128]{2,1,0:T(8,128)S(1)} fusion(f32[512]{0:T(512)S(1)} %bitcast.100, s32[16,16]{1,0:T(8,128)S(1)} %multiply_add_fusion.1, s32[512]{0:T(512)S(1)} %bitcast.101, s32[512]{0:T(512)S(1)} %add_select_fusion), kind=kOutput, calls=%fused_computation.36 | convolution fusion | flops 201654272 | bytes 138240 | tf_op jit(solution)/shard_map/cpr,rz->cpz/dot_general | solution.py:151
  21.9 0.0 collective-permute-done.1
  22.0 0.0 collective-permute-done
  22.0 0.0 copy-done.1
  22.0 0.0 copy-done.2
  22.1 1.9 %collective-permute-start.2 = (f32[2,24,4,128]{3,2,1,0:T(4,128)S(1)}, f32[2,24,4,128]{3,2,1,0:T(4,128)S(1)}, u32[]{:S(2)}, u32[]{:S(2)}) collective-permute-start(f32[2,24,4,128]{3,2,1,0:T(4,128)S(1)} %get-tuple-element.28), channel_id=1, source_target_pairs={{1,0},{2,1},{3,2},{5,4},{6,5},{7,6},{9,8},{10,9},{11,10},{13,12},{... | collective-permute-start | bytes 294920 | tf_op jit(solution)/shard_map/ppermute | solution.py:111
  24.0 2.4 %collective-permute-start.3 = (f32[2,24,4,128]{3,2,1,0:T(4,128)S(1)}, f32[2,24,4,128]{3,2,1,0:T(4,128)S(1)}, u32[]{:S(2)}, u32[]{:S(2)}) collective-permute-start(f32[2,24,4,128]{3,2,1,0:T(4,128)S(1)} %get-tuple-element.27), channel_id=1, source_target_pairs={{0,1},{1,2},{2,3},{4,5},{5,6},{6,7},{8,9},{9,10},{10,11},{12,13},{... | collective-permute-start | bytes 294920 | tf_op jit(solution)/shard_map/ppermute | solution.py:110
  26.5 0.3 fusion.197
  26.8 0.3 fusion.198
  27.1 0.0 collective-permute-done.2
  27.1 2.8 %collective-permute-done.3 = f32[2,24,4,128]{3,2,1,0:T(4,128)S(1)} collective-permute-done((f32[2,24,4,128]{3,2,1,0:T(4,128)S(1)}, f32[2,24,4,128]{3,2,1,0:T(4,128)S(1)}, u32[]{:S(2)}, u32[]{:S(2)}) %collective-permute-start.3) | collective-permute-done | bytes 98336 | tf_op jit(solution)/shard_map/ppermute | solution.py:110
  30.0 0.6 %select_maximum_fusion = f32[2,24,24,136]{3,2,1,0:T(8,128)S(1)} fusion(f32[2,24,4,128]{3,2,1,0:T(4,128)S(1)} %collective-permute-done.2, f32[2,24,4,128]{3,2,1,0:T(4,128)S(1)} %collective-permute-done.3, f32[2,8,16,128]{3,2,1,0:T(8,128)S(1)} %bitcast.78, f32[2,8,16,128]{3,2,1,0:T(8,128)S(1)} %bitcast.82, f32[1,8,16,128]{3,2,1,0:T(8,128)S(1)} %bitcast.90, ...), kind=kLoop, calls=%fused_computation.4 | loop fusion | flops 2193408 | bytes 1216512 | tf_op jit(solution)/shard_map/concatenate | solution.py:205
  30.5 0.8 %fusion.6 = f32[2,16,24,128]{3,2,1,0:T(8,128)S(1)} fusion(f32[2,24,24,136]{3,2,1,0:T(8,128)S(1)} %select_maximum_fusion), kind=kLoop, calls=%fused_computation.41 | loop fusion | flops 1081344 | bytes 3538944 | tf_op jit(solution)/shard_map/add | solution.py:53
  31.3 0.1 pad_maximum_fusion
  31.4 1.0 %fusion.13 = (f32[2,24,16,128]{3,2,1,0:T(8,128)S(1)}, f32[2,24,16,128]{3,2,1,0:T(8,128)S(1)}) fusion(f32[2,24,24,136]{3,2,1,0:T(8,128)S(1)} %select_maximum_fusion, f32[2,24,20,128]{3,2,1,0:T(8,128)S(1)} %get-tuple-element.26, f32[2,24,20,128]{3,2,1,0:T(8,128)S(1)} %get-tuple-element.25), kind=kLoop, calls=%fused_computation.52 | loop fusion | flops 2162688 | bytes 7077888 | tf_op jit(solution)/shard_map/add | solution.py:49
  32.5 1.0 %fusion.43 = (f32[2,16,16,128]{3,2,1,0:T(8,128)S(1)}, f32[2,16,16,128]{3,2,1,0:T(8,128)S(1)}, f32[2,16,16,128]{3,2,1,0:T(8,128)S(1)}, f32[2,16,16,128]{3,2,1,0:T(8,128)S(1)}) fusion(f32[2,16,24,128]{3,2,1,0:T(8,128)S(1)} %fusion.6, f32[2,24,16,128]{3,2,1,0:T(8,128)S(1)} %get-tuple-element.81, f32[2,24,16,128]{3,2,1,0:T(8,128)S(1)} %get-tuple-element.82, ...), kind=kLoop, calls=%fused_computation.101 | loop fusion | flops 5570560 | bytes 14548992 | tf_op jit(solution)/shard_map/add | solution.py:90
  33.5 0.1 fusion.176
  33.6 0.1 fusion.181
  33.7 1.9 %collective-permute-start.6 = (f32[2,16,4,128]{3,2,1,0:T(4,128)S(1)}, f32[2,16,4,128]{3,2,1,0:T(4,128)S(1)}, u32[]{:S(2)}, u32[]{:S(2)}) collective-permute-start(f32[2,16,4,128]{3,2,1,0:T(4,128)S(1)} %get-tuple-element.50), channel_id=1, source_target_pairs={{1,0},{2,1},{3,2},{5,4},{6,5},{7,6},{9,8},{10,9},{11,10},{13,12},{... | collective-permute-start | bytes 196616 | tf_op jit(solution)/shard_map/ppermute | solution.py:111
  35.7 2.4 %collective-permute-start.7 = (f32[2,16,4,128]{3,2,1,0:T(4,128)S(1)}, f32[2,16,4,128]{3,2,1,0:T(4,128)S(1)}, u32[]{:S(2)}, u32[]{:S(2)}) collective-permute-start(f32[2,16,4,128]{3,2,1,0:T(4,128)S(1)} %get-tuple-element.49), channel_id=1, source_target_pairs={{0,1},{1,2},{2,3},{4,5},{5,6},{6,7},{8,9},{9,10},{10,11},{12,13},{... | collective-permute-start | bytes 196616 | tf_op jit(solution)/shard_map/ppermute | solution.py:110
  38.1 0.4 fusion.91
  38.5 0.0 collective-permute-done.6
  38.5 2.8 %collective-permute-done.7 = f32[2,16,4,128]{3,2,1,0:T(4,128)S(1)} collective-permute-done((f32[2,16,4,128]{3,2,1,0:T(4,128)S(1)}, f32[2,16,4,128]{3,2,1,0:T(4,128)S(1)}, u32[]{:S(2)}, u32[]{:S(2)}) %collective-permute-start.7) | collective-permute-done | bytes 65568 | tf_op jit(solution)/shard_map/ppermute | solution.py:110
  41.2 0.4 select_maximum_fusion.5
  41.7 0.4 fusion.102
  42.1 0.5 %fusion.27 = f32[2,16,16,128]{3,2,1,0:T(8,128)S(1)} fusion(f32[2,16,24,136]{3,2,1,0:T(8,128)S(1)} %select_maximum_fusion.5), kind=kLoop, calls=%fused_computation.77 | loop fusion | flops 720896 | bytes 2359296 | tf_op jit(solution)/shard_map/add | solution.py:49
  42.6 0.1 pad_maximum_fusion.2
  42.7 0.2 fusion.34
  42.9 0.0 copy-start.10
  42.9 0.6 %fusion.133 = (f32[2,8,16,128]{3,2,1,0:T(8,128)S(1)}, f32[2,8,16,128]{3,2,1,0:T(8,128)S(1)}, f32[2,8,16,128]{3,2,1,0:T(8,128)S(1)}, f32[2,8,16,128]{3,2,1,0:T(8,128)S(1)}) fusion(f32[2,8,24,128]{3,2,1,0:T(8,128)S(1)} %fusion.102, f32[2,16,16,128]{3,2,1,0:T(8,128)S(1)} %fusion.27, f32[2,16,16,128]{3,2,1,0:T(8,128)S(1)} %fusion.34, ...), kind=kLoop, calls=%fused_computation.220 | loop fusion | flops 3080192 | bytes 6422528 | tf_op jit(solution)/shard_map/add | solution.py:90
  43.5 0.3 copy-done.10
  43.8 0.7 %fusion.192 = (f32[8,16,128]{2,1,0:T(8,128)}, f32[8,16,128]{2,1,0:T(8,128)}, f32[8,16,128]{2,1,0:T(8,128)}, f32[8,16,128]{2,1,0:T(8,128)S(1)}) fusion(bf16[2,8,16,128]{3,2,1,0:T(8,128)(2,1)S(1)} %copy-done.10, f32[8,16,128]{2,1,0:T(8,128)S(1)} %fusion.91, f32[8,16,128]{2,1,0:T(8,128)S(1)} %copy-done.3, f32[2,8,16,128]{3,2,1,0:T(8,128)S(1)} %get-tuple-element.11, ...), kind=kLoop, calls=%fused_computation.323 | loop fusion | flops 327680 | bytes 1048576 | tf_op jit(solution)/shard_map/add | solution.py:217
  44.5 0.7 %add_add_fusion = (f32[8,16,128]{2,1,0:T(8,128)}, f32[8,16,128]{2,1,0:T(8,128)}) fusion(f32[8,16,128]{2,1,0:T(8,128)S(1)} %fusion.91, f32[8,16,128]{2,1,0:T(8,128)S(1)} %copy-done.3, f32[8,16,128]{2,1,0:T(8,128)S(1)} %get-tuple-element.8, f32[8,16,128]{2,1,0:T(8,128)S(1)} %copy-done.2, f32[2,8,16,128]{3,2,1,0:T(8,128)S(1)} %get-tuple-element.11, ...), kind=kLoop, calls=%fused_computation.325 | loop fusion | flops 147456 | bytes 589824 | tf_op jit(solution)/shard_map/add | solution.py:99
  (28 shorter events, 0.4 us)
Async XLA Ops:
  0.6 1.1 %copy-start = (f32[1024,128]{1,0:T(8,128)S(1)}, f32[1024,128]{1,0:T(8,128)}, u32[]{:S(2)}) copy-start(f32[1024,128]{1,0:T(8,128)} %param.24) | copy-start | bytes 1572868
  0.7 6.4 %copy-start.8 = (f32[8,16,128]{2,1,0:T(8,128)S(1)}, f32[8,16,128]{2,1,0:T(8,128)}, u32[]{:S(2)}) copy-start(f32[8,16,128]{2,1,0:T(8,128)} %param.16) | copy-start | bytes 196612
  0.7 6.4 %copy-start.9 = (f32[8,16,128]{2,1,0:T(8,128)S(1)}, f32[8,16,128]{2,1,0:T(8,128)}, u32[]{:S(2)}) copy-start(f32[8,16,128]{2,1,0:T(8,128)} %param.17) | copy-start | bytes 196612
  0.7 6.4 %copy-start.3 = (f32[8,16,128]{2,1,0:T(8,128)S(1)}, f32[8,16,128]{2,1,0:T(8,128)}, u32[]{:S(2)}) copy-start(f32[8,16,128]{2,1,0:T(8,128)} %param.18) | copy-start | bytes 196612
  0.7 6.4 %copy-start.5 = (f32[8,16,128]{2,1,0:T(8,128)S(1)}, f32[8,16,128]{2,1,0:T(8,128)}, u32[]{:S(2)}) copy-start(f32[8,16,128]{2,1,0:T(8,128)} %param.19) | copy-start | bytes 196612
  0.7 6.5 %copy-start.4 = (f32[8,16,128]{2,1,0:T(8,128)S(1)}, f32[8,16,128]{2,1,0:T(8,128)}, u32[]{:S(2)}) copy-start(f32[8,16,128]{2,1,0:T(8,128)} %param.20) | copy-start | bytes 196612
  0.7 6.5 %copy-start.6 = (f32[8,16,128]{2,1,0:T(8,128)S(1)}, f32[8,16,128]{2,1,0:T(8,128)}, u32[]{:S(2)}) copy-start(f32[8,16,128]{2,1,0:T(8,128)} %param.21) | copy-start | bytes 196612
  0.7 6.5 %copy-start.7 = (f32[8,16,128]{2,1,0:T(8,128)S(1)}, f32[8,16,128]{2,1,0:T(8,128)}, u32[]{:S(2)}) copy-start(f32[8,16,128]{2,1,0:T(8,128)} %param.22) | copy-start | bytes 196612
  2.7 11.1 %collective-permute-start.4 = (f32[3,128]{1,0:T(4,128)S(1)}, f32[3,128]{1,0:T(4,128)S(1)}, u32[]{:S(2)}, u32[]{:S(2)}) collective-permute-start(f32[3,128]{1,0:T(4,128)S(1)} %pad_maximum_fusion.18), channel_id=1, source_target_pairs={{0,8},{4,12},{8,0},{12,4},{1,9},{5,13},{9,1},{13,5},{2,10},{6,14},... | collective-permute-start | bytes 4616 | tf_op jit(solution)/shard_map/ppermute | solution.py:130
  7.2 14.8 %copy-start.1 = (f32[8,16,128]{2,1,0:T(8,128)S(1)}, f32[8,16,128]{2,1,0:T(8,128)}, u32[]{:S(2)}) copy-start(f32[8,16,128]{2,1,0:T(8,128)} %param.14) | copy-start | bytes 196612
  7.2 14.8 %copy-start.2 = (f32[8,16,128]{2,1,0:T(8,128)S(1)}, f32[8,16,128]{2,1,0:T(8,128)}, u32[]{:S(2)}) copy-start(f32[8,16,128]{2,1,0:T(8,128)} %param.15) | copy-start | bytes 196612
  7.2 14.7 %collective-permute-start.1 = (f32[44,16,128]{2,1,0:T(8,128)S(1)}, f32[44,16,128]{2,1,0:T(8,128)S(1)}, u32[]{:S(2)}, u32[]{:S(2)}) collective-permute-start(f32[44,16,128]{2,1,0:T(8,128)S(1)} %get-tuple-element.62), channel_id=1, source_target_pairs={{4,0},{8,4},{12,8},{5,1},{9,5},{13,9},{6,2},{10,6},{14,10},{7,3},{... | collective-permute-start | bytes 1081352 | tf_op jit(solution)/shard_map/ppermute | solution.py:111
  9.7 12.2 %collective-permute-start = (f32[44,16,128]{2,1,0:T(8,128)S(1)}, f32[44,16,128]{2,1,0:T(8,128)S(1)}, u32[]{:S(2)}, u32[]{:S(2)}) collective-permute-start(f32[44,16,128]{2,1,0:T(8,128)S(1)} %get-tuple-element.61), channel_id=1, source_target_pairs={{0,4},{4,8},{8,12},{1,5},{5,9},{9,13},{2,6},{6,10},{10,14},{3,7},{... | collective-permute-start | bytes 1081352 | tf_op jit(solution)/shard_map/ppermute | solution.py:110
  13.8 7.5 %collective-permute-start.5 = (f32[3,256]{1,0:T(4,128)S(1)}, f32[3,256]{1,0:T(4,128)S(1)}, u32[]{:S(2)}, u32[]{:S(2)}) collective-permute-start(f32[3,256]{1,0:T(4,128)S(1)} %pad_maximum_fusion.13), channel_id=1, source_target_pairs={{0,4},{4,0},{8,12},{12,8},{1,5},{5,1},{9,13},{13,9},{2,6},{6,2},{1... | collective-permute-start | bytes 9224 | tf_op jit(solution)/shard_map/ppermute | solution.py:130
  22.1 5.0 %collective-permute-start.2 = (f32[2,24,4,128]{3,2,1,0:T(4,128)S(1)}, f32[2,24,4,128]{3,2,1,0:T(4,128)S(1)}, u32[]{:S(2)}, u32[]{:S(2)}) collective-permute-start(f32[2,24,4,128]{3,2,1,0:T(4,128)S(1)} %get-tuple-element.28), channel_id=1, source_target_pairs={{1,0},{2,1},{3,2},{5,4},{6,5},{7,6},{9,8},{10,9},{11,10},{13,12},{... | collective-permute-start | bytes 294920 | tf_op jit(solution)/shard_map/ppermute | solution.py:111
  24.0 5.9 %collective-permute-start.3 = (f32[2,24,4,128]{3,2,1,0:T(4,128)S(1)}, f32[2,24,4,128]{3,2,1,0:T(4,128)S(1)}, u32[]{:S(2)}, u32[]{:S(2)}) collective-permute-start(f32[2,24,4,128]{3,2,1,0:T(4,128)S(1)} %get-tuple-element.27), channel_id=1, source_target_pairs={{0,1},{1,2},{2,3},{4,5},{5,6},{6,7},{8,9},{9,10},{10,11},{12,13},{... | collective-permute-start | bytes 294920 | tf_op jit(solution)/shard_map/ppermute | solution.py:110
  33.7 4.7 %collective-permute-start.6 = (f32[2,16,4,128]{3,2,1,0:T(4,128)S(1)}, f32[2,16,4,128]{3,2,1,0:T(4,128)S(1)}, u32[]{:S(2)}, u32[]{:S(2)}) collective-permute-start(f32[2,16,4,128]{3,2,1,0:T(4,128)S(1)} %get-tuple-element.50), channel_id=1, source_target_pairs={{1,0},{2,1},{3,2},{5,4},{6,5},{7,6},{9,8},{10,9},{11,10},{13,12},{... | collective-permute-start | bytes 196616 | tf_op jit(solution)/shard_map/ppermute | solution.py:111
  35.7 5.6 %collective-permute-start.7 = (f32[2,16,4,128]{3,2,1,0:T(4,128)S(1)}, f32[2,16,4,128]{3,2,1,0:T(4,128)S(1)}, u32[]{:S(2)}, u32[]{:S(2)}) collective-permute-start(f32[2,16,4,128]{3,2,1,0:T(4,128)S(1)} %get-tuple-element.49), channel_id=1, source_target_pairs={{0,1},{1,2},{2,3},{4,5},{5,6},{6,7},{8,9},{9,10},{10,11},{12,13},{... | collective-permute-start | bytes 196616 | tf_op jit(solution)/shard_map/ppermute | solution.py:110
  42.9 0.8 %copy-start.10 = (bf16[2,8,16,128]{3,2,1,0:T(8,128)(2,1)S(1)}, bf16[2,8,16,128]{3,2,1,0:T(8,128)(2,1)}, u32[]{:S(2)}) copy-start(bf16[2,8,16,128]{3,2,1,0:T(8,128)(2,1)} %param.23) | copy-start | bytes 196612

commit v14 on v11

--- a/solution.py
+++ b/solution.py
@@ -118,7 +118,7 @@
     steps = jnp.arange(traces.shape[0], dtype=jnp.int32)
     chosen = (time_steps[:, None] == steps[None, :]).astype(jnp.float32)
     samples = jnp.dot(
-        chosen, traces, precision=lax.Precision.HIGHEST, preferred_element_type=jnp.float32
+        chosen, traces, precision=lax.Precision.HIGH, preferred_element_type=jnp.float32
     )
     assert groups * block < 2**24
     code = (rec_owner[:, 0] * block + rec_local).astype(jnp.float32)
@@ -149,7 +149,7 @@
     spread = values[:, None, :] * picks[None, :, :]
     columns = (depth[:, None] == jnp.arange(sz, dtype=jnp.int32)[None, :]).astype(jnp.float32)
     sources = jnp.einsum(
-        "cpr,rz->cpz", spread, columns, precision=lax.Precision.HIGHEST,
+        "cpr,rz->cpz", spread, columns, precision=lax.Precision.HIGH,
         preferred_element_type=jnp.float32,
     )
     return sources.reshape(values.shape[0], rows, sy, sz)

time: 44.5 us -> 44.3 us (level)
  no operation moved by 1% of the time
where the time goes in v14:
time: 44.3 us; the launch traced here: 43.8 us
  starting transfers between devices  16.2 us (37%)
  waiting for transfers between devices  13.1 us (30%)
  other arithmetic  9.11 us (21%)
  local copies, waits for them, and re-layouts  2.63 us (6%)
  matrix products  1.6 us (4%)
  between operations  1.19 us (3%)
    ppermute x3, starting transfers between devices, from_neighbours(): lax.ppermute(high_part, axis, [(i + 1, i) for i in range(count - 1)])  7.48 us
    ppermute x2, waiting for transfers between devices, gather_column(): lax.ppermute(arrived, 'gx', [(i, i ^ step) for i in range(groups)])  7.41 us
    ppermute x3, starting transfers between devices, from_neighbours(): below = lax.ppermute(low_part, axis, [(i, i + 1) for i in range(count - 1)])  6.1 us
    ppermute x3, waiting for transfers between devices, from_neighbours(): below = lax.ppermute(low_part, axis, [(i, i + 1) for i in range(count - 1)])  5.65 us
    ppermute x2, starting transfers between devices, gather_column(): lax.ppermute(arrived, 'gx', [(i, i ^ step) for i in range(groups)])  2.65 us
    unnamed x32, local copies, waits for them, and re-layouts  2.31 us
    add x2, other arithmetic, advance(): nxx * dxx + nyy * dyy + nzz * dzz + nxy * dxy + nxz * dxz + nyz * dyz  1.61 us
    add x2, other arithmetic, derivatives(): dz_xwide + weight * (padded[:, :, 4:4 + sy, 4 + k:4 + k + sz] - padded[:,...  1.58 us
  transfers between devices with their start and end apart: 8, of which 3 were waited for; matrix products, arithmetic and copies ran while one was open for 9% of the time, Pallas kernels for 0%

profile of v14, /device:TPU:30, one launch (start us, length us, event | category | flops | bytes accessed | tf_op | source)
XLA Modules:
  0.0 43.8 jit_solution(5713406870886136156)
XLA Ops:
  0.6 0.0 copy-start
  0.7 0.0 copy-start.8
  0.7 0.0 copy-start.9
  0.7 0.0 copy-start.3
  0.7 0.0 copy-start.5
  0.7 0.0 copy-start.4
  0.7 0.0 copy-start.6
  0.7 0.0 copy-start.7
  0.7 0.7 %fusion.209 = f32[1,128]{1,0:T(1,128)S(1)} fusion(s32[128]{0:T(128)} %param.27, s32[128,1]{0,1:T(1,128)} %param.26), kind=kLoop, calls=%fused_computation.420 | loop fusion | flops 384 | bytes 1536 | tf_op jit(solution)/shard_map/broadcast_in_dim | solution.py:125
  1.5 0.2 copy-done
  1.7 0.9 %fusion.201 = f32[2,128]{1,0:T(2,128)S(1)} fusion(f32[1024,128]{1,0:T(8,128)S(1)} %copy-done, s32[2]{0:T(128)} %param.25), kind=kOutput, calls=%fused_computation.378 | convolution fusion | flops 1574912 | bytes 525320 | tf_op jit(solution)/shard_map/dot_general | solution.py:120
  2.6 0.5 %collective-permute-start.4 = (f32[3,128]{1,0:T(4,128)S(1)}, f32[3,128]{1,0:T(4,128)S(1)}, u32[]{:S(2)}, u32[]{:S(2)}) collective-permute-start(f32[3,128]{1,0:T(4,128)S(1)} %pad_maximum_fusion.18), channel_id=1, source_target_pairs={{0,4},{4,0},{8,12},{12,8},{1,5},{5,1},{9,13},{13,9},{2,6},{6,2},{1... | collective-permute-start | bytes 4616 | tf_op jit(solution)/shard_map/ppermute | solution.py:130
  3.1 0.8 %constant_dynamic-update-slice_fusion.17 = f32[44,16,128]{2,1,0:T(8,128)S(1)} fusion(f32[8,16,128]{2,1,0:T(8,128)} %param.14), kind=kLoop, calls=%fused_computation.351 | loop fusion | bytes 131072
  4.0 0.8 %constant_dynamic-update-slice_fusion.16 = f32[44,16,128]{2,1,0:T(8,128)S(1)} fusion(f32[44,16,128]{2,1,0:T(8,128)S(1)} %constant_dynamic-update-slice_fusion.17, f32[8,16,128]{2,1,0:T(8,128)} %param.15), kind=kLoop, calls=%fused_computation.350 | loop fusion | bytes 131072
  4.8 0.0 copy-done.8
  4.9 0.0 copy-done.9
  4.9 0.0 copy-done.3
  4.9 0.0 copy-done.5
  4.9 0.0 copy-done.4
  5.0 0.0 copy-done.6
  5.0 0.0 copy-done.7
  5.0 0.0 copy-start.1
  5.0 0.0 copy-start.2
  5.0 3.6 %collective-permute-start.1 = (f32[44,16,128]{2,1,0:T(8,128)S(1)}, f32[44,16,128]{2,1,0:T(8,128)S(1)}, u32[]{:S(2)}, u32[]{:S(2)}) collective-permute-start(f32[44,16,128]{2,1,0:T(8,128)S(1)} %get-tuple-element.62), channel_id=1, source_target_pairs={{4,0},{8,4},{12,8},{5,1},{9,5},{13,9},{6,2},{10,6},{14,10},{7,3},{... | collective-permute-start | bytes 1081352 | tf_op jit(solution)/shard_map/ppermute | solution.py:111
  8.7 1.3 %collective-permute-start = (f32[44,16,128]{2,1,0:T(8,128)S(1)}, f32[44,16,128]{2,1,0:T(8,128)S(1)}, u32[]{:S(2)}, u32[]{:S(2)}) collective-permute-start(f32[44,16,128]{2,1,0:T(8,128)S(1)} %get-tuple-element.61), channel_id=1, source_target_pairs={{0,4},{4,8},{8,12},{1,5},{5,9},{9,13},{2,6},{6,10},{10,14},{3,7},{... | collective-permute-start | bytes 1081352 | tf_op jit(solution)/shard_map/ppermute | solution.py:110
  10.0 0.2 fusion.227
  10.3 0.3 fusion.212
  10.6 0.0 collective-permute-done.4
  10.6 2.1 %collective-permute-start.5 = (f32[3,256]{1,0:T(4,128)S(1)}, f32[3,256]{1,0:T(4,128)S(1)}, u32[]{:S(2)}, u32[]{:S(2)}) collective-permute-start(f32[3,256]{1,0:T(4,128)S(1)} %pad_maximum_fusion.13), channel_id=1, source_target_pairs={{0,8},{4,12},{8,0},{12,4},{1,9},{5,13},{9,1},{13,5},{2,10},{6,14},... | collective-permute-start | bytes 9224 | tf_op jit(solution)/shard_map/ppermute | solution.py:130
  12.7 7.4 %collective-permute-done.5 = f32[3,256]{1,0:T(4,128)S(1)} collective-permute-done((f32[3,256]{1,0:T(4,128)S(1)}, f32[3,256]{1,0:T(4,128)S(1)}, u32[]{:S(2)}, u32[]{:S(2)}) %collective-permute-start.5) | collective-permute-done | bytes 3104 | tf_op jit(solution)/shard_map/ppermute | solution.py:130
  20.1 0.1 and_select_fusion.3
  20.2 0.4 fusion.2
  20.6 0.0 collective-permute-done.1
  20.7 0.0 collective-permute-done
  20.7 0.0 copy-done.1
  20.7 0.0 copy-done.2
  20.8 1.9 %collective-permute-start.2 = (f32[2,24,4,128]{3,2,1,0:T(4,128)S(1)}, f32[2,24,4,128]{3,2,1,0:T(4,128)S(1)}, u32[]{:S(2)}, u32[]{:S(2)}) collective-permute-start(f32[2,24,4,128]{3,2,1,0:T(4,128)S(1)} %get-tuple-element.28), channel_id=1, source_target_pairs={{1,0},{2,1},{3,2},{5,4},{6,5},{7,6},{9,8},{10,9},{11,10},{13,12},{... | collective-permute-start | bytes 294920 | tf_op jit(solution)/shard_map/ppermute | solution.py:111
  22.7 2.4 %collective-permute-start.3 = (f32[2,24,4,128]{3,2,1,0:T(4,128)S(1)}, f32[2,24,4,128]{3,2,1,0:T(4,128)S(1)}, u32[]{:S(2)}, u32[]{:S(2)}) collective-permute-start(f32[2,24,4,128]{3,2,1,0:T(4,128)S(1)} %get-tuple-element.27), channel_id=1, source_target_pairs={{0,1},{1,2},{2,3},{4,5},{5,6},{6,7},{8,9},{9,10},{10,11},{12,13},{... | collective-permute-start | bytes 294920 | tf_op jit(solution)/shard_map/ppermute | solution.py:110
  25.2 0.3 fusion.197
  25.5 0.3 fusion.198
  25.8 0.0 collective-permute-done.2
  25.8 2.8 %collective-permute-done.3 = f32[2,24,4,128]{3,2,1,0:T(4,128)S(1)} collective-permute-done((f32[2,24,4,128]{3,2,1,0:T(4,128)S(1)}, f32[2,24,4,128]{3,2,1,0:T(4,128)S(1)}, u32[]{:S(2)}, u32[]{:S(2)}) %collective-permute-start.3) | collective-permute-done | bytes 98336 | tf_op jit(solution)/shard_map/ppermute | solution.py:110
  28.7 0.6 %select_maximum_fusion = f32[2,24,24,136]{3,2,1,0:T(8,128)S(1)} fusion(f32[2,24,4,128]{3,2,1,0:T(4,128)S(1)} %collective-permute-done.2, f32[2,24,4,128]{3,2,1,0:T(4,128)S(1)} %collective-permute-done.3, f32[2,8,16,128]{3,2,1,0:T(8,128)S(1)} %bitcast.78, f32[2,8,16,128]{3,2,1,0:T(8,128)S(1)} %bitcast.82, f32[1,8,16,128]{3,2,1,0:T(8,128)S(1)} %bitcast.90, ...), kind=kLoop, calls=%fused_computation.4 | loop fusion | flops 2193408 | bytes 1216512 | tf_op jit(solution)/shard_map/concatenate | solution.py:205
  29.2 0.8 %fusion.6 = f32[2,16,24,128]{3,2,1,0:T(8,128)S(1)} fusion(f32[2,24,24,136]{3,2,1,0:T(8,128)S(1)} %select_maximum_fusion), kind=kLoop, calls=%fused_computation.41 | loop fusion | flops 1081344 | bytes 3538944 | tf_op jit(solution)/shard_map/add | solution.py:53
  30.0 0.1 pad_maximum_fusion
  30.1 1.0 %fusion.13 = (f32[2,24,16,128]{3,2,1,0:T(8,128)S(1)}, f32[2,24,16,128]{3,2,1,0:T(8,128)S(1)}) fusion(f32[2,24,24,136]{3,2,1,0:T(8,128)S(1)} %select_maximum_fusion, f32[2,24,20,128]{3,2,1,0:T(8,128)S(1)} %get-tuple-element.26, f32[2,24,20,128]{3,2,1,0:T(8,128)S(1)} %get-tuple-element.25), kind=kLoop, calls=%fused_computation.52 | loop fusion | flops 2162688 | bytes 7077888 | tf_op jit(solution)/shard_map/add | solution.py:49
  31.2 1.0 %fusion.43 = (f32[2,16,16,128]{3,2,1,0:T(8,128)S(1)}, f32[2,16,16,128]{3,2,1,0:T(8,128)S(1)}, f32[2,16,16,128]{3,2,1,0:T(8,128)S(1)}, f32[2,16,16,128]{3,2,1,0:T(8,128)S(1)}) fusion(f32[2,16,24,128]{3,2,1,0:T(8,128)S(1)} %fusion.6, f32[2,24,16,128]{3,2,1,0:T(8,128)S(1)} %get-tuple-element.81, f32[2,24,16,128]{3,2,1,0:T(8,128)S(1)} %get-tuple-element.82, ...), kind=kLoop, calls=%fused_computation.101 | loop fusion | flops 5570560 | bytes 14548992 | tf_op jit(solution)/shard_map/add | solution.py:90
  32.2 0.1 fusion.176
  32.3 0.1 fusion.181
  32.4 1.9 %collective-permute-start.6 = (f32[2,16,4,128]{3,2,1,0:T(4,128)S(1)}, f32[2,16,4,128]{3,2,1,0:T(4,128)S(1)}, u32[]{:S(2)}, u32[]{:S(2)}) collective-permute-start(f32[2,16,4,128]{3,2,1,0:T(4,128)S(1)} %get-tuple-element.50), channel_id=1, source_target_pairs={{1,0},{2,1},{3,2},{5,4},{6,5},{7,6},{9,8},{10,9},{11,10},{13,12},{... | collective-permute-start | bytes 196616 | tf_op jit(solution)/shard_map/ppermute | solution.py:111
  34.3 2.4 %collective-permute-start.7 = (f32[2,16,4,128]{3,2,1,0:T(4,128)S(1)}, f32[2,16,4,128]{3,2,1,0:T(4,128)S(1)}, u32[]{:S(2)}, u32[]{:S(2)}) collective-permute-start(f32[2,16,4,128]{3,2,1,0:T(4,128)S(1)} %get-tuple-element.49), channel_id=1, source_target_pairs={{0,1},{1,2},{2,3},{4,5},{5,6},{6,7},{8,9},{9,10},{10,11},{12,13},{... | collective-permute-start | bytes 196616 | tf_op jit(solution)/shard_map/ppermute | solution.py:110
  36.8 0.3 fusion.91
  37.1 0.0 collective-permute-done.6
  37.1 2.8 %collective-permute-done.7 = f32[2,16,4,128]{3,2,1,0:T(4,128)S(1)} collective-permute-done((f32[2,16,4,128]{3,2,1,0:T(4,128)S(1)}, f32[2,16,4,128]{3,2,1,0:T(4,128)S(1)}, u32[]{:S(2)}, u32[]{:S(2)}) %collective-permute-start.7) | collective-permute-done | bytes 65568 | tf_op jit(solution)/shard_map/ppermute | solution.py:110
  39.9 0.4 select_maximum_fusion.5
  40.3 0.4 fusion.102
  40.8 0.5 %fusion.27 = f32[2,16,16,128]{3,2,1,0:T(8,128)S(1)} fusion(f32[2,16,24,136]{3,2,1,0:T(8,128)S(1)} %select_maximum_fusion.5), kind=kLoop, calls=%fused_computation.77 | loop fusion | flops 720896 | bytes 2359296 | tf_op jit(solution)/shard_map/add | solution.py:49
  41.3 0.1 pad_maximum_fusion.2
  41.4 0.2 fusion.34
  41.6 0.0 copy-start.10
  41.6 0.6 %fusion.133 = (f32[2,8,16,128]{3,2,1,0:T(8,128)S(1)}, f32[2,8,16,128]{3,2,1,0:T(8,128)S(1)}, f32[2,8,16,128]{3,2,1,0:T(8,128)S(1)}, f32[2,8,16,128]{3,2,1,0:T(8,128)S(1)}) fusion(f32[2,8,24,128]{3,2,1,0:T(8,128)S(1)} %fusion.102, f32[2,16,16,128]{3,2,1,0:T(8,128)S(1)} %fusion.27, f32[2,16,16,128]{3,2,1,0:T(8,128)S(1)} %fusion.34, ...), kind=kLoop, calls=%fused_computation.220 | loop fusion | flops 3080192 | bytes 6422528 | tf_op jit(solution)/shard_map/add | solution.py:90
  42.2 0.3 copy-done.10
  42.4 0.7 %fusion.192 = (f32[8,16,128]{2,1,0:T(8,128)}, f32[8,16,128]{2,1,0:T(8,128)}, f32[8,16,128]{2,1,0:T(8,128)}, f32[8,16,128]{2,1,0:T(8,128)S(1)}) fusion(bf16[2,8,16,128]{3,2,1,0:T(8,128)(2,1)S(1)} %copy-done.10, f32[8,16,128]{2,1,0:T(8,128)S(1)} %fusion.91, f32[8,16,128]{2,1,0:T(8,128)S(1)} %copy-done.3, f32[2,8,16,128]{3,2,1,0:T(8,128)S(1)} %get-tuple-element.11, ...), kind=kLoop, calls=%fused_computation.323 | loop fusion | flops 327680 | bytes 1048576 | tf_op jit(solution)/shard_map/add | solution.py:217
  43.2 0.7 %add_add_fusion = (f32[8,16,128]{2,1,0:T(8,128)}, f32[8,16,128]{2,1,0:T(8,128)}) fusion(f32[8,16,128]{2,1,0:T(8,128)S(1)} %fusion.91, f32[8,16,128]{2,1,0:T(8,128)S(1)} %copy-done.3, f32[8,16,128]{2,1,0:T(8,128)S(1)} %get-tuple-element.8, f32[8,16,128]{2,1,0:T(8,128)S(1)} %copy-done.2, f32[2,8,16,128]{3,2,1,0:T(8,128)S(1)} %get-tuple-element.11, ...), kind=kLoop, calls=%fused_computation.325 | loop fusion | flops 147456 | bytes 589824 | tf_op jit(solution)/shard_map/add | solution.py:99
  (28 shorter events, 0.4 us)
Async XLA Ops:
  0.6 1.1 %copy-start = (f32[1024,128]{1,0:T(8,128)S(1)}, f32[1024,128]{1,0:T(8,128)}, u32[]{:S(2)}) copy-start(f32[1024,128]{1,0:T(8,128)} %param.24) | copy-start | bytes 1572868
  0.7 4.2 %copy-start.8 = (f32[8,16,128]{2,1,0:T(8,128)S(1)}, f32[8,16,128]{2,1,0:T(8,128)}, u32[]{:S(2)}) copy-start(f32[8,16,128]{2,1,0:T(8,128)} %param.16) | copy-start | bytes 196612
  0.7 4.2 %copy-start.9 = (f32[8,16,128]{2,1,0:T(8,128)S(1)}, f32[8,16,128]{2,1,0:T(8,128)}, u32[]{:S(2)}) copy-start(f32[8,16,128]{2,1,0:T(8,128)} %param.17) | copy-start | bytes 196612
  0.7 4.2 %copy-start.3 = (f32[8,16,128]{2,1,0:T(8,128)S(1)}, f32[8,16,128]{2,1,0:T(8,128)}, u32[]{:S(2)}) copy-start(f32[8,16,128]{2,1,0:T(8,128)} %param.18) | copy-start | bytes 196612
  0.7 4.2 %copy-start.5 = (f32[8,16,128]{2,1,0:T(8,128)S(1)}, f32[8,16,128]{2,1,0:T(8,128)}, u32[]{:S(2)}) copy-start(f32[8,16,128]{2,1,0:T(8,128)} %param.19) | copy-start | bytes 196612
  0.7 4.3 %copy-start.4 = (f32[8,16,128]{2,1,0:T(8,128)S(1)}, f32[8,16,128]{2,1,0:T(8,128)}, u32[]{:S(2)}) copy-start(f32[8,16,128]{2,1,0:T(8,128)} %param.20) | copy-start | bytes 196612
  0.7 4.3 %copy-start.6 = (f32[8,16,128]{2,1,0:T(8,128)S(1)}, f32[8,16,128]{2,1,0:T(8,128)}, u32[]{:S(2)}) copy-start(f32[8,16,128]{2,1,0:T(8,128)} %param.21) | copy-start | bytes 196612
  0.7 4.3 %copy-start.7 = (f32[8,16,128]{2,1,0:T(8,128)S(1)}, f32[8,16,128]{2,1,0:T(8,128)}, u32[]{:S(2)}) copy-start(f32[8,16,128]{2,1,0:T(8,128)} %param.22) | copy-start | bytes 196612
  2.6 8.0 %collective-permute-start.4 = (f32[3,128]{1,0:T(4,128)S(1)}, f32[3,128]{1,0:T(4,128)S(1)}, u32[]{:S(2)}, u32[]{:S(2)}) collective-permute-start(f32[3,128]{1,0:T(4,128)S(1)} %pad_maximum_fusion.18), channel_id=1, source_target_pairs={{0,4},{4,0},{8,12},{12,8},{1,5},{5,1},{9,13},{13,9},{2,6},{6,2},{1... | collective-permute-start | bytes 4616 | tf_op jit(solution)/shard_map/ppermute | solution.py:130
  5.0 15.7 %copy-start.1 = (f32[8,16,128]{2,1,0:T(8,128)S(1)}, f32[8,16,128]{2,1,0:T(8,128)}, u32[]{:S(2)}) copy-start(f32[8,16,128]{2,1,0:T(8,128)} %param.14) | copy-start | bytes 196612
  5.0 15.7 %copy-start.2 = (f32[8,16,128]{2,1,0:T(8,128)S(1)}, f32[8,16,128]{2,1,0:T(8,128)}, u32[]{:S(2)}) copy-start(f32[8,16,128]{2,1,0:T(8,128)} %param.15) | copy-start | bytes 196612
  5.0 15.6 %collective-permute-start.1 = (f32[44,16,128]{2,1,0:T(8,128)S(1)}, f32[44,16,128]{2,1,0:T(8,128)S(1)}, u32[]{:S(2)}, u32[]{:S(2)}) collective-permute-start(f32[44,16,128]{2,1,0:T(8,128)S(1)} %get-tuple-element.62), channel_id=1, source_target_pairs={{4,0},{8,4},{12,8},{5,1},{9,5},{13,9},{6,2},{10,6},{14,10},{7,3},{... | collective-permute-start | bytes 1081352 | tf_op jit(solution)/shard_map/ppermute | solution.py:111
  8.7 12.0 %collective-permute-start = (f32[44,16,128]{2,1,0:T(8,128)S(1)}, f32[44,16,128]{2,1,0:T(8,128)S(1)}, u32[]{:S(2)}, u32[]{:S(2)}) collective-permute-start(f32[44,16,128]{2,1,0:T(8,128)S(1)} %get-tuple-element.61), channel_id=1, source_target_pairs={{0,4},{4,8},{8,12},{1,5},{5,9},{9,13},{2,6},{6,10},{10,14},{3,7},{... | collective-permute-start | bytes 1081352 | tf_op jit(solution)/shard_map/ppermute | solution.py:110
  10.6 9.5 %collective-permute-start.5 = (f32[3,256]{1,0:T(4,128)S(1)}, f32[3,256]{1,0:T(4,128)S(1)}, u32[]{:S(2)}, u32[]{:S(2)}) collective-permute-start(f32[3,256]{1,0:T(4,128)S(1)} %pad_maximum_fusion.13), channel_id=1, source_target_pairs={{0,8},{4,12},{8,0},{12,4},{1,9},{5,13},{9,1},{13,5},{2,10},{6,14},... | collective-permute-start | bytes 9224 | tf_op jit(solution)/shard_map/ppermute | solution.py:130
  20.8 5.0 %collective-permute-start.2 = (f32[2,24,4,128]{3,2,1,0:T(4,128)S(1)}, f32[2,24,4,128]{3,2,1,0:T(4,128)S(1)}, u32[]{:S(2)}, u32[]{:S(2)}) collective-permute-start(f32[2,24,4,128]{3,2,1,0:T(4,128)S(1)} %get-tuple-element.28), channel_id=1, source_target_pairs={{1,0},{2,1},{3,2},{5,4},{6,5},{7,6},{9,8},{10,9},{11,10},{13,12},{... | collective-permute-start | bytes 294920 | tf_op jit(solution)/shard_map/ppermute | solution.py:111
  22.7 5.9 %collective-permute-start.3 = (f32[2,24,4,128]{3,2,1,0:T(4,128)S(1)}, f32[2,24,4,128]{3,2,1,0:T(4,128)S(1)}, u32[]{:S(2)}, u32[]{:S(2)}) collective-permute-start(f32[2,24,4,128]{3,2,1,0:T(4,128)S(1)} %get-tuple-element.27), channel_id=1, source_target_pairs={{0,1},{1,2},{2,3},{4,5},{5,6},{6,7},{8,9},{9,10},{10,11},{12,13},{... | collective-permute-start | bytes 294920 | tf_op jit(solution)/shard_map/ppermute | solution.py:110
  32.4 4.7 %collective-permute-start.6 = (f32[2,16,4,128]{3,2,1,0:T(4,128)S(1)}, f32[2,16,4,128]{3,2,1,0:T(4,128)S(1)}, u32[]{:S(2)}, u32[]{:S(2)}) collective-permute-start(f32[2,16,4,128]{3,2,1,0:T(4,128)S(1)} %get-tuple-element.50), channel_id=1, source_target_pairs={{1,0},{2,1},{3,2},{5,4},{6,5},{7,6},{9,8},{10,9},{11,10},{13,12},{... | collective-permute-start | bytes 196616 | tf_op jit(solution)/shard_map/ppermute | solution.py:111
  34.3 5.6 %collective-permute-start.7 = (f32[2,16,4,128]{3,2,1,0:T(4,128)S(1)}, f32[2,16,4,128]{3,2,1,0:T(4,128)S(1)}, u32[]{:S(2)}, u32[]{:S(2)}) collective-permute-start(f32[2,16,4,128]{3,2,1,0:T(4,128)S(1)} %get-tuple-element.49), channel_id=1, source_target_pairs={{0,1},{1,2},{2,3},{4,5},{5,6},{6,7},{8,9},{9,10},{10,11},{12,13},{... | collective-permute-start | bytes 196616 | tf_op jit(solution)/shard_map/ppermute | solution.py:110
  41.6 0.8 %copy-start.10 = (bf16[2,8,16,128]{3,2,1,0:T(8,128)(2,1)S(1)}, bf16[2,8,16,128]{3,2,1,0:T(8,128)(2,1)}, u32[]{:S(2)}) copy-start(bf16[2,8,16,128]{3,2,1,0:T(8,128)(2,1)} %param.23) | copy-start | bytes 196612
